TPU v7x, 32 devices: a whole 2x2x4 slice. The times are simulated.
32 devices in a mesh: hx: 4 (over z), hy: 4 (over y, x), torso: 2 (over core).
Axes of the slice: x: 2, y: 2, z: 4, core: 2. Of those that a mesh axis runs over, the one named last changes fastest.
Arguments:
- potential: float32 [8, 52, 1024], P('torso', 'hx', 'hy'), may hold values from -4 to 4, as said below
- gating: float32 [40, 8, 52, 1024], P(None, 'torso', 'hx', 'hy'), may hold values from 0 to 1, as said below
- cell_type: int32 [8, 52, 1024], P('torso', 'hx', 'hy'), may hold values from 0 to 2, as said below
- drug_class: int32 [8, 52, 1024], P('torso', 'hx', 'hy'), may hold values from 0 to 3, as said below
- half_point: float32 [3, 40], replicated, may hold values from -3 to 3
- gate_slope: float32 [3, 40], replicated, may hold values from 1 to 4
- time_const: float32 [3, 40], replicated, may hold values from 0.003 to 0.06
- max_conduct: float32 [3, 40], replicated, may hold values from 1 to 16
- reversal: float32 [40], replicated, may hold values from -4 to 4
- drug_block: float32 [4, 40], replicated, may hold values from 0.2 to 1
- heart_cond: float32 [2, 16, 340], P('torso', 'hx', 'hy'), may hold values from 0.5 to 1.5
- torso_cond: float32 [2, 16, 340], P('torso', 'hx', 'hy'), may hold values from 0.5 to 2
- epi_target: int32 [52, 1024], P('hx', 'hy'), may hold values from 0 to 50028, as said below
Outputs:
- new_potential: float32 [8, 52, 1024], P('torso', 'hx', 'hy')
- new_gating: float32 [40, 8, 52, 1024], P(None, 'torso', 'hx', 'hy')
- torso_field: float32 [8, 52, 1024], P('torso', 'hx', 'hy')
Inputs may be any that keep to these rules, and one draw needn't show every extreme that they name: `potential`: copies of a shared node hold equal values. `gating`: copies of a shared node hold equal values. `cell_type`: copies of a shared node hold equal values. `drug_class`: copies of a shared node hold equal values. `epi_target`: the node p * 1021 + q that feeds the torso surface copy at distinct coordinates (a, b) has p within 2 of a and q within 2 of b; copies of a shared node hold equal values.
All inputs are finite; a program needn't handle non-finite values.
Results may differ from a plain program's by a relative error of at most 0.0001.
Values sent between devices are 32-bit elements; how exact they have to be, the bound alone decides.
No kernel may reach another device: no remote copies, remote signals or barrier semaphores. Data moves between devices by JAX's collectives and lax.ppermute only.
A program may use at most 64 MiB of HBM per device.

v0:
```python
import jax
import jax.numpy as jnp
import numpy as np
from jax import lax
from jax.sharding import PartitionSpec as P

TYPES = 3
CLASSES = 4
STEPS = 2
ITERS = 4
REACH = 2


STIFF_LINE = (
    np.array(
        [
            [148.0, -189.0, 54.0, -13.0],
            [-189.0, 432.0, -297.0, 54.0],
            [54.0, -297.0, 432.0, -189.0],
            [-13.0, 54.0, -189.0, 148.0],
        ]
    )
    / 40.0
)
MASS_LINE = (
    np.array(
        [
            [128.0, 99.0, -36.0, 19.0],
            [99.0, 648.0, -81.0, -36.0],
            [-36.0, -81.0, 648.0, 99.0],
            [19.0, -36.0, 99.0, 128.0],
        ]
    )
    / 1680.0
)
ELEMENT_MATRIX = (
    np.kron(np.kron(STIFF_LINE, MASS_LINE), MASS_LINE)
    + np.kron(np.kron(MASS_LINE, STIFF_LINE), MASS_LINE)
    + np.kron(np.kron(MASS_LINE, MASS_LINE), STIFF_LINE)
)
time_step = 0.002
torso_shift = 0.02


def extended_2(cells, sides, width):
    for axis, dim in sides:
        count = lax.axis_size(axis)
        ends = count - 1
        head = lax.slice_in_dim(cells, 0, width, axis=dim)
        tail = lax.slice_in_dim(cells, cells.shape[dim] - width, cells.shape[dim], axis=dim)
        cells = jnp.concatenate(
            [
                lax.ppermute(tail, axis, [(i, (i + 1) % count) for i in range(ends)]),
                cells,
                lax.ppermute(head, axis, [((i + 1) % count, i) for i in range(ends)]),
            ],
            axis=dim,
        )
    return cells


def pick_nodes(values, axis_place, length):
    return jnp.stack(
        [
            lax.slice_in_dim(values, offset, offset + 3 * length - 2, 3, axis_place)
            for offset in range(4)
        ],
        0,
    )


def place_nodes(stacked, axis_place):
    result = None
    for offset in range(4):
        slab_part = stacked[offset]
        config = [(0, 0, 0)] * slab_part.ndim
        config[axis_place] = (offset, 3 - offset, 2)
        placed = lax.pad(slab_part, jnp.zeros((), slab_part.dtype), config)
        result = placed if result is None else result + placed
    return result


def element_products(values, conduct):
    counts = conduct.shape
    picked = pick_nodes(values, 0, counts[0])
    picked = pick_nodes(picked, 2, counts[1])
    picked = pick_nodes(picked, 4, counts[2])
    matrix = jnp.asarray(ELEMENT_MATRIX, values.dtype)
    product = jnp.dot(matrix, picked.reshape(64, -1), precision=lax.Precision.HIGHEST)
    product = (product * conduct.reshape(1, -1)).reshape(picked.shape)
    spread = place_nodes(product, 4)
    spread = place_nodes(spread, 2)
    return place_nodes(spread, 0)


def add_faces(local_sums):
    extended = extended_2(local_sums, (("hx", 1), ("hy", 2), ("torso", 0)), 1)
    summed = extended[1:-1].at[0].add(extended[0]).at[-1].add(extended[-1])
    summed = summed[:, 1:-1].at[:, 0].add(summed[:, 0]).at[:, -1].add(summed[:, -1])
    summed = summed[:, :, 1:-1].at[:, :, 0].add(summed[:, :, 0]).at[:, :, -1].add(summed[:, :, -1])
    return summed


def line_factors(length, block_id, block_count):
    position = jnp.arange(length)
    at_start = (position == 0) & (block_id == 0)
    at_end = (position == length - 1) & (block_id == block_count - 1)
    mass_line = jnp.where(position % 3 == 0, jnp.where(at_start | at_end, 0.125, 0.25), 0.375)
    shared = (position == 0) & (block_id > 0) | (position == length - 1) & (
        block_id < block_count - 1
    )
    weight = jnp.where(shared, 0.5, 1.0)
    return (mass_line.astype(jnp.float32), weight.astype(jnp.float32))


def factor_grid(depth_line, first_line, second_line):
    return depth_line[:, None, None] * first_line[None, :, None] * second_line[None, None, :]


def node_table(matrix, labels, kind_count):
    onehot = (
        labels.reshape(1, -1) == jnp.arange(kind_count, dtype=jnp.int32).reshape(-1, 1)
    ).astype(jnp.float32)
    return jnp.dot(matrix.T, onehot, precision=lax.Precision.HIGHEST)


def ext_index(target, anchor, length_local, rim_width):
    relative = target - anchor
    return jnp.where(
        relative < 0,
        rim_width - 1 + relative,
        jnp.where(relative > length_local - 1, rim_width + relative + 1, rim_width + relative),
    )


def per_device(
    potential,
    gating,
    cell_type,
    drug_class,
    half_point,
    gate_slope,
    time_const,
    max_conduct,
    reversal,
    drug_block,
    heart_cond,
    torso_cond,
    epi_target,
):
    depth_len, first_len, second_len = potential.shape
    torso_len = 3 * torso_cond.shape[0] + 1
    index_torso = lax.axis_index("torso")
    index_first = lax.axis_index("hx")
    index_second = lax.axis_index("hy")
    heart_depth, unused_depth = line_factors(depth_len, index_torso, lax.axis_size("torso"))
    first_mass, first_weight = line_factors(first_len, index_first, lax.axis_size("hx"))
    second_mass, second_weight = line_factors(second_len, index_second, lax.axis_size("hy"))
    torso_depth, torso_depth_weight = line_factors(torso_len, index_torso, lax.axis_size("torso"))
    heart_mass = factor_grid(heart_depth, first_mass, second_mass)
    torso_mass = factor_grid(torso_depth, first_mass, second_mass)
    torso_weight = factor_grid(torso_depth_weight, first_weight, second_weight)
    type_flat = cell_type.reshape(-1)
    half_nodes = node_table(half_point, type_flat, TYPES)
    slope_nodes = node_table(gate_slope, type_flat, TYPES)
    decay_nodes = jnp.exp(-time_step / node_table(time_const, type_flat, TYPES))
    cond_nodes = node_table(max_conduct, type_flat, TYPES) * node_table(
        drug_block, drug_class.reshape(-1), CLASSES
    )
    gate_flat = gating.reshape(gating.shape[0], -1)
    for repeat in range(STEPS):
        volts = potential.reshape(1, -1)
        inf_value = jax.nn.sigmoid((volts - half_nodes) * slope_nodes)
        gate_flat = inf_value + (gate_flat - inf_value) * decay_nodes
        current = jnp.sum(cond_nodes * gate_flat * (volts - reversal[:, None]), 0)
        diffusion = add_faces(element_products(potential, heart_cond))
        potential = potential - time_step * (
            diffusion / heart_mass + current.reshape(potential.shape)
        )
    new_gating = gate_flat.reshape(gating.shape)
    rim_width = REACH + 1
    extended = extended_2(potential[0], (("hx", 0), ("hy", 1)), rim_width)
    distinct_second = lax.axis_size("hy") * (second_len - 1) + 1
    target_first = epi_target // distinct_second
    target_second = epi_target % distinct_second
    place_first = ext_index(target_first, index_first * (first_len - 1), first_len, rim_width)
    place_second = ext_index(target_second, index_second * (second_len - 1), second_len, rim_width)
    flat_place = (place_first * (second_len + 2 * rim_width) + place_second).reshape(-1)
    picked_values = jnp.take(extended.reshape(-1), flat_place).reshape(first_len, second_len)
    plane = jnp.where(index_torso == 0, picked_values, 0.0)
    rhs = jnp.concatenate(
        [plane[None], jnp.zeros((torso_len - 1, first_len, second_len), jnp.float32)], 0
    )

    def torso_apply(values):
        return add_faces(element_products(values, torso_cond)) + torso_shift * torso_mass * values

    def squares(vector):
        return lax.psum(jnp.sum(torso_weight * vector * vector), ("hx", "hy", "torso"))

    def standard_turn(turn_index, state_tuple):
        solution, residual, direction, norm_now = state_tuple
        image = torso_apply(direction)
        curvature = lax.psum(jnp.sum(torso_weight * direction * image), ("hx", "hy", "torso"))
        step_size = norm_now / curvature
        solution = solution + step_size * direction
        residual = residual - step_size * image
        norm_next = squares(residual)
        direction = residual + norm_next / norm_now * direction
        return (solution, residual, direction, norm_next)

    start_state = (jnp.zeros_like(rhs), rhs, rhs, squares(rhs))
    solution = lax.fori_loop(0, ITERS, standard_turn, start_state)[0]
    return (potential, new_gating, solution)


def solution(mesh):
    placed = (
        P("torso", "hx", "hy"),
        P(None, "torso", "hx", "hy"),
        P("torso", "hx", "hy"),
        P("torso", "hx", "hy"),
        P(),
        P(),
        P(),
        P(),
        P(),
        P(),
        P("torso", "hx", "hy"),
        P("torso", "hx", "hy"),
        P("hx", "hy"),
    )
    return jax.shard_map(
        per_device,
        mesh=mesh,
        in_specs=placed,
        out_specs=(P("torso", "hx", "hy"), P(None, "torso", "hx", "hy"), P("torso", "hx", "hy")),
        check_vma=False,
    )
```

profile of v0, /device:TPU:0, one launch (start us, length us, event | category | flops | bytes accessed | tf_op | source)
XLA Modules:
  0.0 674.6 jit_solution(6080765035850276716)
XLA Ops:
  7.7 2.4 pad.208
  10.1 2.4 pad.207
  12.6 2.4 pad.205
  15.0 2.4 pad.206
  19.0 5.6 collective-permute-start.6
  24.7 2.1 copy.72
  26.9 1.9 reshape.766
  28.7 2.6 fusion.15
  31.4 2.4 fusion.20
  33.8 2.4 fusion.21
  36.2 2.4 fusion.22
  38.7 7.0 %multiply_reduce_fusion.1 = (f32[13312]{0:T(1024)S(1)}, f32[40,13312]{1,0:T(8,128)}) fusion(f32[40]{0:T(128)S(1)} %copy-done.11, f32[13312]{0:T(1024)S(1)} %sub.83, f32[40,13312]{1,0:T(8,128)} %fusion.15, f32[40,13312]{1,0:T(8,128)S(1)} %copy-done.1, f32[13312,40]{0,1:T(8,128)} %fusion.20, f32[13312,40]{0,1:T(8,128)} %fusion.21, f32[13312,40]{0,1:T(8,128)} %fusion.22, ...), kind=kOutput, calls=%fused_computation.57 | convolution fusion | flops 32521216 | bytes 12940064 | tf_op jit(solution)/shard_map/dot_general | solution.py:124
  47.1 4.5 collective-permute-start.8
  56.9 1.7 collective-permute-done.11
  64.2 2.4 pad.220
  66.6 2.4 pad.219
  69.1 2.4 pad.217
  71.5 2.4 pad.218
  75.5 4.5 collective-permute-start.12
  82.9 5.4 collective-permute-start.14
  93.4 5.4 multiply_reduce_fusion
  101.2 4.8 collective-permute-start.18
  108.7 5.8 collective-permute-start.20
  114.4 2.0 reshape.770
  116.5 3.2 copy.86
  120.6 17.5 %gather_fusion = f32[3328]{0:T(1024)S(1)} fusion(f32[4978]{0:T(1024)S(1)} %reshape.771, s32[4096]{0:T(1024)S(1)} %pad_clamp_fusion), kind=kCustom, calls=%fused_computation | custom fusion | bytes 39936 | tf_op jit(solution)/shard_map/jit(_take)/gather | solution.py:189
  138.8 42.6 %psum.29 = f32[]{:T(128)} all-reduce(f32[]{:T(128)} %get-tuple-element.558), channel_id=1, replica_groups=mesh['hx'=4,'hy'=4,'torso'=2] {'hx','hy','torso'}, use_global_device_ids=true, to_apply=%region_3.4 | all-reduce | flops 1 | bytes 8 | tf_op jit(solution)/shard_map/psum | solution.py:199
  181.4 492.5 %while.40 = (s32[]{:T(128)}, f32[4,13,256]{2,1,0:T(8,128)S(1)}, f32[4,13,256]{2,1,0:T(8,128)S(1)}, f32[4,13,256]{2,1,0:T(8,128)S(1)}, f32[]{:T(128)}, /*index=5*...) while((s32[]{:T(128)}, f32[4,13,256]{2,1,0:T(8,128)S(1)}, ...), condition=%wide.wide.region_9.10_spmd.clone.clone, body=%wide.wide.region_4.9_spmd.sunk.clone.clone.sunk | while | flops 17425556 | bytes 4695795 | solution.py:213
  186.0 2.4 pad.543
  188.4 2.4 pad.544
  190.9 2.4 pad.545
  193.3 2.4 pad.546
  197.3 4.5 collective-permute-start.1
  204.6 4.8 collective-permute-start.3
  214.5 1.8 collective-permute-done.5
  218.5 43.1 %psum.40 = f32[]{:T(128)} all-reduce(f32[]{:T(128)} %fusion.103), channel_id=1, replica_groups=mesh['hx'=4,'hy'=4,'torso'=2] {'hx','hy','torso'}, use_global_device_ids=true, to_apply=%region_6.6 | all-reduce | flops 1 | bytes 8 | tf_op jit(solution)/shard_map/while/body/eval_jaxpr/psum | solution.py:204
  262.9 41.4 %psum.41 = f32[]{:T(128)} all-reduce(f32[]{:T(128)} %get-tuple-element.762), channel_id=1, replica_groups=mesh['hx'=4,'hy'=4,'torso'=2] {'hx','hy','torso'}, use_global_device_ids=true, to_apply=%region_8.8 | all-reduce | flops 1 | bytes 8 | tf_op jit(solution)/shard_map/while/body/eval_jaxpr/psum | solution.py:199
  309.6 2.4 pad.543
  312.0 2.4 pad.544
  314.4 2.4 pad.545
  316.9 2.4 pad.546
  320.9 4.5 collective-permute-start.1
  328.1 4.8 collective-permute-start.3
  338.1 1.8 collective-permute-done.5
  342.1 43.0 %psum.40 = f32[]{:T(128)} all-reduce(f32[]{:T(128)} %fusion.103), channel_id=1, replica_groups=mesh['hx'=4,'hy'=4,'torso'=2] {'hx','hy','torso'}, use_global_device_ids=true, to_apply=%region_6.6 | all-reduce | flops 1 | bytes 8 | tf_op jit(solution)/shard_map/while/body/eval_jaxpr/psum | solution.py:204
  386.4 40.6 %psum.41 = f32[]{:T(128)} all-reduce(f32[]{:T(128)} %get-tuple-element.762), channel_id=1, replica_groups=mesh['hx'=4,'hy'=4,'torso'=2] {'hx','hy','torso'}, use_global_device_ids=true, to_apply=%region_8.8 | all-reduce | flops 1 | bytes 8 | tf_op jit(solution)/shard_map/while/body/eval_jaxpr/psum | solution.py:199
  432.3 2.4 pad.543
  434.7 2.4 pad.544
  437.1 2.4 pad.545
  439.6 2.4 pad.546
  443.6 4.5 collective-permute-start.1
  450.8 4.8 collective-permute-start.3
  460.8 1.8 collective-permute-done.5
  464.8 43.1 %psum.40 = f32[]{:T(128)} all-reduce(f32[]{:T(128)} %fusion.103), channel_id=1, replica_groups=mesh['hx'=4,'hy'=4,'torso'=2] {'hx','hy','torso'}, use_global_device_ids=true, to_apply=%region_6.6 | all-reduce | flops 1 | bytes 8 | tf_op jit(solution)/shard_map/while/body/eval_jaxpr/psum | solution.py:204
  509.1 40.7 %psum.41 = f32[]{:T(128)} all-reduce(f32[]{:T(128)} %get-tuple-element.762), channel_id=1, replica_groups=mesh['hx'=4,'hy'=4,'torso'=2] {'hx','hy','torso'}, use_global_device_ids=true, to_apply=%region_8.8 | all-reduce | flops 1 | bytes 8 | tf_op jit(solution)/shard_map/while/body/eval_jaxpr/psum | solution.py:199
  555.1 2.4 pad.543
  557.5 2.4 pad.544
  560.0 2.4 pad.545
  562.4 2.4 pad.546
  566.4 4.5 collective-permute-start.1
  573.7 4.8 collective-permute-start.3
  583.6 1.8 collective-permute-done.5
  587.6 43.0 %psum.40 = f32[]{:T(128)} all-reduce(f32[]{:T(128)} %fusion.103), channel_id=1, replica_groups=mesh['hx'=4,'hy'=4,'torso'=2] {'hx','hy','torso'}, use_global_device_ids=true, to_apply=%region_6.6 | all-reduce | flops 1 | bytes 8 | tf_op jit(solution)/shard_map/while/body/eval_jaxpr/psum | solution.py:204
  631.9 41.4 %psum.41 = f32[]{:T(128)} all-reduce(f32[]{:T(128)} %get-tuple-element.762), channel_id=1, replica_groups=mesh['hx'=4,'hy'=4,'torso'=2] {'hx','hy','torso'}, use_global_device_ids=true, to_apply=%region_8.8 | all-reduce | flops 1 | bytes 8 | tf_op jit(solution)/shard_map/while/body/eval_jaxpr/psum | solution.py:199
  (402 shorter events, 102.3 us)
Async XLA Ops:
  0.6 38.1 %copy-start = (f32[4,40]{1,0:T(4,128)S(1)}, f32[4,40]{1,0:T(4,128)}, u32[]{:S(2)}) copy-start(f32[4,40]{1,0:T(4,128)} %param.63) | copy-start | bytes 1924
  0.6 24.0 %copy-start.3 = (f32[4,13,256]{2,0,1:T(4,128)S(1)}, f32[4,13,256]{2,0,1:T(4,128)}, u32[]{:S(2)}) copy-start(f32[4,13,256]{2,0,1:T(4,128)} %param.54) | copy-start | bytes 159748
  1.7 23.0 %copy-start.5 = (s32[4,13,256]{2,0,1:T(4,128)S(1)}, s32[4,13,256]{2,0,1:T(4,128)}, u32[]{:S(2)}) copy-start(s32[4,13,256]{2,0,1:T(4,128)} %param.56) | copy-start | bytes 159748
  17.7 28.0 %collective-permute-start.7 = (f32[4,1,256]{2,1,0:T(1,128)S(1)}, f32[4,1,256]{2,1,0:T(1,128)S(1)}, u32[]{:S(2)}, u32[]{:S(2)}) collective-permute-start(f32[4,1,256]{2,1,0:T(1,128)S(1)} %get-tuple-element.537), channel_id=1, source_target_pairs={{8,0},{16,8},{24,16},{9,1},{17,9},{25,17},{10,2},{18,10},{26,18},{... | collective-permute-start | bytes 12296 | tf_op jit(solution)/shard_map/ppermute | solution.py:55
  19.0 26.7 %collective-permute-start.6 = (f32[4,1,256]{2,1,0:T(1,128)S(1)}, f32[4,1,256]{2,1,0:T(1,128)S(1)}, u32[]{:S(2)}, u32[]{:S(2)}) collective-permute-start(f32[4,1,256]{2,1,0:T(1,128)S(1)} %get-tuple-element.536), channel_id=1, source_target_pairs={{0,8},{8,16},{16,24},{1,9},{9,17},{17,25},{2,10},{10,18},{18,26},{... | collective-permute-start | bytes 12296 | tf_op jit(solution)/shard_map/ppermute | solution.py:53
  26.9 1.9 copy-start.12
  28.7 2.7 copy-start.7
  31.4 2.4 copy-start.8
  31.4 4.8 copy-start.9
  33.8 4.8 copy-start.6
  33.8 4.9 copy-start.4
  33.8 4.9 copy-start.1
  33.8 4.9 copy-start.11
  45.7 18.1 %copy-start.2 = (f32[64,64]{1,0:T(8,128)S(1)}, f32[64,64]{1,0:T(8,128)}, u32[]{:S(2)}) copy-start(f32[64,64]{1,0:T(8,128)} %constant.621.clone) | copy-start | bytes 49156
  45.8 5.9 collective-permute-start.9
  47.1 6.1 collective-permute-start.8
  53.4 2.1 collective-permute-start.10
  55.5 3.1 collective-permute-start.11
  59.6 31.7 %copy-start.10 = (f32[1,4,85]{2,1,0:T(4,128)S(1)}, f32[1,4,85]{2,1,0:T(4,128)}, u32[]{:S(2)}) copy-start(f32[1,4,85]{2,1,0:T(4,128)} %param.65) | copy-start | bytes 4084
  74.2 5.9 collective-permute-start.13
  75.5 5.9 collective-permute-start.12
  81.5 6.8 %collective-permute-start.15 = (f32[4,15,1]{2,1,0:T(8,128)S(1)}, f32[4,15,1]{2,1,0:T(8,128)S(1)}, u32[]{:S(2)}, u32[]{:S(2)}) collective-permute-start(f32[4,15,1]{2,1,0:T(8,128)S(1)} %get-tuple-element.515), channel_id=1, source_target_pairs={{2,0},{4,2},{6,4},{3,1},{5,3},{7,5},{10,8},{12,10},{14,12},{11,9},... | collective-permute-start | bytes 728 | tf_op jit(solution)/shard_map/ppermute | solution.py:55
  82.9 6.9 %collective-permute-start.14 = (f32[4,15,1]{2,1,0:T(8,128)S(1)}, f32[4,15,1]{2,1,0:T(8,128)S(1)}, u32[]{:S(2)}, u32[]{:S(2)}) collective-permute-start(f32[4,15,1]{2,1,0:T(8,128)S(1)} %get-tuple-element.514), channel_id=1, source_target_pairs={{0,2},{2,4},{4,6},{1,3},{3,5},{5,7},{8,10},{10,12},{12,14},{9,11},... | collective-permute-start | bytes 728 | tf_op jit(solution)/shard_map/ppermute | solution.py:53
  90.0 2.1 collective-permute-start.16
  92.1 6.7 collective-permute-start.17
  99.9 6.1 collective-permute-start.19
  101.2 6.1 collective-permute-start.18
  107.4 13.0 %collective-permute-start.21 = (f32[19,3]{1,0:T(8,128)S(1)}, f32[19,3]{1,0:T(8,128)S(1)}, u32[]{:S(2)}, u32[]{:S(2)}) collective-permute-start(f32[19,3]{1,0:T(8,128)S(1)} %get-tuple-element.557), channel_id=1, source_target_pairs={{2,0},{4,2},{6,4},{3,1},{5,3},{7,5},{10,8},{12,10},{14,12},{11,9},... | collective-permute-start | bytes 692 | tf_op jit(solution)/shard_map/ppermute | solution.py:55
  108.7 11.7 %collective-permute-start.20 = (f32[19,3]{1,0:T(8,128)S(1)}, f32[19,3]{1,0:T(8,128)S(1)}, u32[]{:S(2)}, u32[]{:S(2)}) collective-permute-start(f32[19,3]{1,0:T(8,128)S(1)} %get-tuple-element.556), channel_id=1, source_target_pairs={{0,2},{2,4},{4,6},{1,3},{3,5},{5,7},{8,10},{10,12},{12,14},{9,11},... | collective-permute-start | bytes 692 | tf_op jit(solution)/shard_map/ppermute | solution.py:53
  196.0 5.9 collective-permute-start
  197.3 5.9 collective-permute-start.1
  203.3 6.1 collective-permute-start.2
  204.6 6.4 collective-permute-start.3
  211.1 2.1 collective-permute-start.4
  213.2 3.1 collective-permute-start.5
  319.6 5.9 collective-permute-start
  320.9 5.9 collective-permute-start.1
  326.8 6.1 collective-permute-start.2
  328.1 6.4 collective-permute-start.3
  334.7 2.1 collective-permute-start.4
  336.8 3.1 collective-permute-start.5
  442.3 5.9 collective-permute-start
  443.6 5.9 collective-permute-start.1
  449.5 6.1 collective-permute-start.2
  450.8 6.4 collective-permute-start.3
  457.4 2.1 collective-permute-start.4
  459.5 3.1 collective-permute-start.5
  565.1 5.9 collective-permute-start
  566.4 5.9 collective-permute-start.1
  572.4 6.1 collective-permute-start.2
  573.7 6.4 collective-permute-start.3
  580.2 2.1 collective-permute-start.4
  582.3 3.1 collective-permute-start.5
where the time goes:
time: 677 us; the launch traced here: 675 us
  blocking collectives  379 us (56%)
  local copies, waits for them, and re-layouts  119 us (18%)
  starting transfers between devices  102 us (15%)
  waiting for transfers between devices  30.7 us (5%)
  matrix products  18.9 us (3%)
  other arithmetic  15 us (2%)
  loops' own time  8.87 us (1%)
    psum x5, blocking collectives, squares(): lax.psum(jnp.sum(torso_weight * vector * vector), ('hx', 'hy', 'torso'))  207 us
    psum x4, blocking collectives, standard_turn(): lax.psum(jnp.sum(torso_weight * direction * image), ('hx', 'hy', 'torso'))  172 us
    ppermute x20, starting transfers between devices, extended_2(): lax.ppermute(tail, axis, [(i, (i + 1) % count) for i in range(ends)])  75.8 us
    pad x48, local copies, waits for them, and re-layouts, place_nodes(): placed = lax.pad(slab_part, jnp.zeros((), slab_part.dtype), config)  58 us
    ppermute x20, starting transfers between devices, extended_2(): lax.ppermute(head, axis, [((i + 1) % count, i) for i in range(ends)])  25.8 us
    slice x44, local copies, waits for them, and re-layouts, pick_nodes(): lax.slice_in_dim(values, offset, offset + 3 * length - 2, 3, axis_place)  23.2 us
    ppermute x20, waiting for transfers between devices, extended_2(): lax.ppermute(tail, axis, [(i, (i + 1) % count) for i in range(ends)])  21.8 us
    gather x2, local copies, waits for them, and re-layouts, per_device(): jnp.take(extended.reshape(-1), flat_place).reshape(first_len, second_len)  17.5 us
  transfers between devices with their start and end apart: 40, of which 23 were waited for; matrix products, arithmetic and copies ran while one was open for 5% of the time, Pallas kernels for 0%

commit v1 on v0

--- a/solution.py
+++ b/solution.py
@@ -57,6 +57,15 @@
             axis=dim,
         )
     return cells
+
+
+def all_sum(value):
+    axes = ("hx", "hy", "torso")
+    count = 1
+    for axis in axes:
+        count *= lax.axis_size(axis)
+    parts = lax.all_to_all(jnp.broadcast_to(value, (count, 1)), axes, 0, 0, tiled=True)
+    return jnp.sum(parts)
 
 
 def pick_nodes(values, axis_place, length):
@@ -196,12 +205,12 @@
         return add_faces(element_products(values, torso_cond)) + torso_shift * torso_mass * values
 
     def squares(vector):
-        return lax.psum(jnp.sum(torso_weight * vector * vector), ("hx", "hy", "torso"))
+        return all_sum(jnp.sum(torso_weight * vector * vector))
 
     def standard_turn(turn_index, state_tuple):
         solution, residual, direction, norm_now = state_tuple
         image = torso_apply(direction)
-        curvature = lax.psum(jnp.sum(torso_weight * direction * image), ("hx", "hy", "torso"))
+        curvature = all_sum(jnp.sum(torso_weight * direction * image))
         step_size = norm_now / curvature
         solution = solution + step_size * direction
         residual = residual - step_size * image

time: 677 us -> 414 us (0.61)
  blocking collectives: 379 us -> 0 us
  waiting for transfers between devices: 30.7 us -> 87.6 us
  starting transfers between devices: 102 us -> 144 us
  local copies, waits for them, and re-layouts: 119 us -> 130 us
    psum x9 -> x0, blocking collectives: 379 us -> none  [the longest x5 207 us: squares(): lax.psum(jnp.sum(torso_weight * vector * vector), ('hx', 'hy', 'torso'))]
    all_to_all x0 -> x9, waiting for transfers between devices: none -> 55.5 us  [all_sum(): lax.all_to_all(jnp.broadcast_to(value, (count, 1)), axes, 0, 0, tiled=True)]
    all_to_all x0 -> x9, starting transfers between devices: none -> 43.2 us  [all_sum(): lax.all_to_all(jnp.broadcast_to(value, (count, 1)), axes, 0, 0, tiled=True)]
    broadcast_in_dim x0 -> x9, local copies, waits for them, and re-layouts: none -> 10.9 us  [all_sum(): jnp.broadcast_to(value, (count, 1))]
  transfers between devices with their start and end apart: 40 -> 49, of which waited for: 23 -> 33; matrix products, arithmetic and copies ran while one was open for 5% -> 8% of each run, Pallas kernels for 0% -> 0%
where the time goes in v1:
time: 414 us; the launch traced here: 413 us
  starting transfers between devices  144 us (35%)
  local copies, waits for them, and re-layouts  130 us (31%)
  waiting for transfers between devices  87.6 us (21%)
  other arithmetic  21.4 us (5%)
  matrix products  18.9 us (5%)
  loops' own time  9.21 us (2%)
    ppermute x20, starting transfers between devices, extended_2(): lax.ppermute(tail, axis, [(i, (i + 1) % count) for i in range(ends)])  74.7 us
    pad x48, local copies, waits for them, and re-layouts, place_nodes(): placed = lax.pad(slab_part, jnp.zeros((), slab_part.dtype), config)  58 us
    all_to_all x9, waiting for transfers between devices, all_sum(): lax.all_to_all(jnp.broadcast_to(value, (count, 1)), axes, 0, 0, tiled=True)  55.5 us
    all_to_all x9, starting transfers between devices, all_sum(): lax.all_to_all(jnp.broadcast_to(value, (count, 1)), axes, 0, 0, tiled=True)  43.2 us
    ppermute x20, starting transfers between devices, extended_2(): lax.ppermute(head, axis, [((i + 1) % count, i) for i in range(ends)])  25.9 us
    slice x44, local copies, waits for them, and re-layouts, pick_nodes(): lax.slice_in_dim(values, offset, offset + 3 * length - 2, 3, axis_place)  23.2 us
    ppermute x20, waiting for transfers between devices, extended_2(): lax.ppermute(tail, axis, [(i, (i + 1) % count) for i in range(ends)])  23.2 us
    gather x2, local copies, waits for them, and re-layouts, per_device(): jnp.take(extended.reshape(-1), flat_place).reshape(first_len, second_len)  17.5 us
  transfers between devices with their start and end apart: 49, of which 33 were waited for; matrix products, arithmetic and copies ran while one was open for 8% of the time, Pallas kernels for 0%

profile of v1, /device:TPU:0, one launch (start us, length us, event | category | flops | bytes accessed | tf_op | source)
XLA Modules:
  0.0 412.6 jit_solution(13491918838714683338)
XLA Ops:
  7.7 2.4 pad.208
  10.1 2.4 pad.207
  12.6 2.4 pad.205
  15.0 2.4 pad.206
  19.0 5.6 %collective-permute-start.6 = (f32[4,1,256]{2,1,0:T(1,128)S(1)}, f32[4,1,256]{2,1,0:T(1,128)S(1)}, u32[]{:S(2)}, u32[]{:S(2)}) collective-permute-start(f32[4,1,256]{2,1,0:T(1,128)S(1)} %get-tuple-element.542), channel_id=1, source_target_pairs={{0,8},{8,16},{16,24},{1,9},{9,17},{17,25},{2,10},{10,18},{18,26},{... | collective-permute-start | bytes 12296 | tf_op jit(solution)/shard_map/ppermute | solution.py:53
  28.7 2.6 fusion.15
  31.4 2.4 fusion.20
  33.8 2.4 fusion.21
  36.2 2.4 fusion.22
  38.7 6.9 %multiply_reduce_fusion.1 = (f32[13312]{0:T(1024)S(1)}, f32[40,13312]{1,0:T(8,128)}) fusion(f32[40]{0:T(128)S(1)} %copy-done.11, f32[13312]{0:T(1024)S(1)} %sub.83, f32[40,13312]{1,0:T(8,128)} %fusion.15, f32[40,13312]{1,0:T(8,128)S(1)} %copy-done.1, f32[13312,40]{0,1:T(8,128)} %fusion.20, f32[13312,40]{0,1:T(8,128)} %fusion.21, f32[13312,40]{0,1:T(8,128)} %fusion.22, ...), kind=kOutput, calls=%fused_computation.57 | convolution fusion | flops 32521216 | bytes 12940064 | tf_op jit(solution)/shard_map/dot_general | solution.py:133
  47.1 4.5 %collective-permute-start.8 = (f32[4,15,1]{2,1,0:T(8,128)S(1)}, f32[4,15,1]{2,1,0:T(8,128)S(1)}, u32[]{:S(2)}, u32[]{:S(2)}) collective-permute-start(f32[4,15,1]{2,1,0:T(8,128)S(1)} %get-tuple-element.540), channel_id=1, source_target_pairs={{0,2},{2,4},{4,6},{1,3},{3,5},{5,7},{8,10},{10,12},{12,14},{9,11},... | collective-permute-start | bytes 728 | tf_op jit(solution)/shard_map/ppermute | solution.py:53
  64.1 2.4 pad.220
  66.6 2.4 pad.219
  69.0 2.4 pad.217
  71.5 2.4 pad.218
  75.5 4.6 %collective-permute-start.12 = (f32[4,1,256]{2,1,0:T(1,128)S(1)}, f32[4,1,256]{2,1,0:T(1,128)S(1)}, u32[]{:S(2)}, u32[]{:S(2)}) collective-permute-start(f32[4,1,256]{2,1,0:T(1,128)S(1)} %get-tuple-element.522), channel_id=1, source_target_pairs={{0,8},{8,16},{16,24},{1,9},{9,17},{17,25},{2,10},{10,18},{18,26},{... | collective-permute-start | bytes 12296 | tf_op jit(solution)/shard_map/ppermute | solution.py:53
  82.9 5.4 %collective-permute-start.14 = (f32[4,15,1]{2,1,0:T(8,128)S(1)}, f32[4,15,1]{2,1,0:T(8,128)S(1)}, u32[]{:S(2)}, u32[]{:S(2)}) collective-permute-start(f32[4,15,1]{2,1,0:T(8,128)S(1)} %get-tuple-element.520), channel_id=1, source_target_pairs={{0,2},{2,4},{4,6},{1,3},{3,5},{5,7},{8,10},{10,12},{12,14},{9,11},... | collective-permute-start | bytes 728 | tf_op jit(solution)/shard_map/ppermute | solution.py:53
  93.4 5.4 %multiply_reduce_fusion = (f32[13312]{0:T(1024)S(1)}, f32[40,13312]{1,0:T(8,128)}) fusion(f32[40,13312]{1,0:T(8,128)} %get-tuple-element.567, f32[13312]{0:T(1024)S(1)} %sub.91, f32[40]{0:T(128)S(1)} %copy-done.11, f32[40,13312]{1,0:T(8,128)} %fusion.15, f32[40,13312]{1,0:T(8,128)S(1)} %copy-done.1, f32[13312,40]{0,1:T(8,128)} %fusion.20, ...), kind=kLoop, calls=%fused_computation.56 | loop fusion | flops 10636288 | bytes 12939424 | tf_op jit(solution)/shard_map/reduce_sum | solution.py:184
  101.2 4.8 %collective-permute-start.18 = (f32[3,256]{1,0:T(4,128)S(1)}, f32[3,256]{1,0:T(4,128)S(1)}, u32[]{:S(2)}, u32[]{:S(2)}) collective-permute-start(f32[3,256]{1,0:T(4,128)S(1)} %get-tuple-element.518), channel_id=1, source_target_pairs={{0,8},{8,16},{16,24},{1,9},{9,17},{17,25},{2,10},{10,18},{18,26},{... | collective-permute-start | bytes 9224 | tf_op jit(solution)/shard_map/ppermute | solution.py:53
  108.7 5.8 %collective-permute-start.20 = (f32[19,3]{1,0:T(8,128)S(1)}, f32[19,3]{1,0:T(8,128)S(1)}, u32[]{:S(2)}, u32[]{:S(2)}) collective-permute-start(f32[19,3]{1,0:T(8,128)S(1)} %get-tuple-element.562), channel_id=1, source_target_pairs={{0,2},{2,4},{4,6},{1,3},{3,5},{5,7},{8,10},{10,12},{12,14},{9,11},... | collective-permute-start | bytes 692 | tf_op jit(solution)/shard_map/ppermute | solution.py:53
  116.0 17.5 %gather_fusion = f32[3328]{0:T(1024)S(1)} fusion(f32[4978]{0:T(1024)S(1)} %reshape.780, s32[4096]{0:T(1024)S(1)} %pad_clamp_fusion), kind=kCustom, calls=%fused_computation | custom fusion | bytes 39936 | tf_op jit(solution)/shard_map/jit(_take)/gather | solution.py:198
  135.6 10.0 %all-to-all-start.2 = ((f32[32,1,1]{2,1,0:T(1,128)}), f32[32,1,1]{2,1,0:T(1,128)S(1)}, u32[]{:S(2)}, u32[]{:S(2)}) async-start(f32[32,1,1]{2,1,0:T(1,128)} %broadcast_in_dim.113), calls=%async_computation.2 | async-start | bytes 32768 | tf_op jit(solution)/shard_map/all_to_all | solution.py:67
  147.7 3.2 copy.167
  153.4 258.4 %while.40 = (s32[]{:T(128)}, f32[4,13,256]{2,1,0:T(8,128)S(1)}, f32[4,13,256]{2,1,0:T(8,128)S(1)}, f32[4,13,256]{2,1,0:T(8,128)S(1)}, f32[]{:T(128)}, /*index=5*...) while((s32[]{:T(128)}, f32[4,13,256]{2,1,0:T(8,128)S(1)}, ...), condition=%wide.wide.region_9.10_spmd.clone.clone, body=%wide.wide.region_4.9_spmd.sunk.clone.clone.sunk | while | flops 17425620 | bytes 4762163 | solution.py:222
  158.0 2.4 pad.543
  160.4 2.4 pad.544
  162.9 2.4 pad.545
  165.3 2.4 pad.546
  169.3 4.5 %collective-permute-start.1 = (f32[4,1,256]{2,1,0:T(1,128)S(1)}, f32[4,1,256]{2,1,0:T(1,128)S(1)}, u32[]{:S(2)}, u32[]{:S(2)}) collective-permute-start(f32[4,1,256]{2,1,0:T(1,128)S(1)} %get-tuple-element.762), channel_id=1, source_target_pairs={{0,8},{8,16},{16,24},{1,9},{9,17},{17,25},{2,10},{10,18},{18,26},{... | collective-permute-start | bytes 12296 | tf_op jit(solution)/shard_map/while/body/eval_jaxpr/ppermute | solution.py:53
  176.6 4.5 %collective-permute-start.3 = (f32[4,15,1]{2,1,0:T(8,128)S(1)}, f32[4,15,1]{2,1,0:T(8,128)S(1)}, u32[]{:S(2)}, u32[]{:S(2)}) collective-permute-start(f32[4,15,1]{2,1,0:T(8,128)S(1)} %get-tuple-element.764), channel_id=1, source_target_pairs={{0,2},{2,4},{4,6},{1,3},{3,5},{5,7},{8,10},{10,12},{12,14},{9,11},... | collective-permute-start | bytes 728 | tf_op jit(solution)/shard_map/while/body/eval_jaxpr/ppermute | solution.py:53
  190.8 7.1 %all-to-all-start = ((f32[32,1,1]{2,1,0:T(1,128)}), f32[32,1,1]{2,1,0:T(1,128)S(1)}, u32[]{:S(2)}, u32[]{:S(2)}) async-start(f32[32,1,1]{2,1,0:T(1,128)} %broadcast_in_dim.141), calls=%async_computation | async-start | bytes 32768 | tf_op jit(solution)/shard_map/while/body/eval_jaxpr/all_to_all | solution.py:67
  198.6 6.5 %all-to-all-done = f32[32,1,1]{2,1,0:T(1,128)S(1)} async-done(((f32[32,1,1]{2,1,0:T(1,128)}), f32[32,1,1]{2,1,0:T(1,128)S(1)}, u32[]{:S(2)}, u32[]{:S(2)}) %all-to-all-start) | async-done | bytes 160 | tf_op jit(solution)/shard_map/while/body/eval_jaxpr/all_to_all | solution.py:67
  208.4 2.5 all-to-all-start.1
  211.0 7.1 %all-to-all-done.1 = f32[32,1,1]{2,1,0:T(1,128)S(1)} async-done(((f32[32,1,1]{2,1,0:T(1,128)}), f32[32,1,1]{2,1,0:T(1,128)S(1)}, u32[]{:S(2)}, u32[]{:S(2)}) %all-to-all-start.1) | async-done | bytes 160 | tf_op jit(solution)/shard_map/while/body/eval_jaxpr/all_to_all | solution.py:67
  224.0 2.4 pad.543
  226.4 2.4 pad.544
  228.9 2.4 pad.545
  231.3 2.4 pad.546
  235.3 4.5 %collective-permute-start.1 = (f32[4,1,256]{2,1,0:T(1,128)S(1)}, f32[4,1,256]{2,1,0:T(1,128)S(1)}, u32[]{:S(2)}, u32[]{:S(2)}) collective-permute-start(f32[4,1,256]{2,1,0:T(1,128)S(1)} %get-tuple-element.762), channel_id=1, source_target_pairs={{0,8},{8,16},{16,24},{1,9},{9,17},{17,25},{2,10},{10,18},{18,26},{... | collective-permute-start | bytes 12296 | tf_op jit(solution)/shard_map/while/body/eval_jaxpr/ppermute | solution.py:53
  242.6 4.5 %collective-permute-start.3 = (f32[4,15,1]{2,1,0:T(8,128)S(1)}, f32[4,15,1]{2,1,0:T(8,128)S(1)}, u32[]{:S(2)}, u32[]{:S(2)}) collective-permute-start(f32[4,15,1]{2,1,0:T(8,128)S(1)} %get-tuple-element.764), channel_id=1, source_target_pairs={{0,2},{2,4},{4,6},{1,3},{3,5},{5,7},{8,10},{10,12},{12,14},{9,11},... | collective-permute-start | bytes 728 | tf_op jit(solution)/shard_map/while/body/eval_jaxpr/ppermute | solution.py:53
  256.8 5.3 %all-to-all-start = ((f32[32,1,1]{2,1,0:T(1,128)}), f32[32,1,1]{2,1,0:T(1,128)S(1)}, u32[]{:S(2)}, u32[]{:S(2)}) async-start(f32[32,1,1]{2,1,0:T(1,128)} %broadcast_in_dim.141), calls=%async_computation | async-start | bytes 32768 | tf_op jit(solution)/shard_map/while/body/eval_jaxpr/all_to_all | solution.py:67
  262.7 6.5 %all-to-all-done = f32[32,1,1]{2,1,0:T(1,128)S(1)} async-done(((f32[32,1,1]{2,1,0:T(1,128)}), f32[32,1,1]{2,1,0:T(1,128)S(1)}, u32[]{:S(2)}, u32[]{:S(2)}) %all-to-all-start) | async-done | bytes 160 | tf_op jit(solution)/shard_map/while/body/eval_jaxpr/all_to_all | solution.py:67
  272.6 2.5 all-to-all-start.1
  275.1 7.1 %all-to-all-done.1 = f32[32,1,1]{2,1,0:T(1,128)S(1)} async-done(((f32[32,1,1]{2,1,0:T(1,128)}), f32[32,1,1]{2,1,0:T(1,128)S(1)}, u32[]{:S(2)}, u32[]{:S(2)}) %all-to-all-start.1) | async-done | bytes 160 | tf_op jit(solution)/shard_map/while/body/eval_jaxpr/all_to_all | solution.py:67
  288.2 2.4 pad.543
  290.6 2.4 pad.544
  293.0 2.4 pad.545
  295.5 2.4 pad.546
  299.5 4.5 %collective-permute-start.1 = (f32[4,1,256]{2,1,0:T(1,128)S(1)}, f32[4,1,256]{2,1,0:T(1,128)S(1)}, u32[]{:S(2)}, u32[]{:S(2)}) collective-permute-start(f32[4,1,256]{2,1,0:T(1,128)S(1)} %get-tuple-element.762), channel_id=1, source_target_pairs={{0,8},{8,16},{16,24},{1,9},{9,17},{17,25},{2,10},{10,18},{18,26},{... | collective-permute-start | bytes 12296 | tf_op jit(solution)/shard_map/while/body/eval_jaxpr/ppermute | solution.py:53
  306.7 4.5 %collective-permute-start.3 = (f32[4,15,1]{2,1,0:T(8,128)S(1)}, f32[4,15,1]{2,1,0:T(8,128)S(1)}, u32[]{:S(2)}, u32[]{:S(2)}) collective-permute-start(f32[4,15,1]{2,1,0:T(8,128)S(1)} %get-tuple-element.764), channel_id=1, source_target_pairs={{0,2},{2,4},{4,6},{1,3},{3,5},{5,7},{8,10},{10,12},{12,14},{9,11},... | collective-permute-start | bytes 728 | tf_op jit(solution)/shard_map/while/body/eval_jaxpr/ppermute | solution.py:53
  321.0 5.3 %all-to-all-start = ((f32[32,1,1]{2,1,0:T(1,128)}), f32[32,1,1]{2,1,0:T(1,128)S(1)}, u32[]{:S(2)}, u32[]{:S(2)}) async-start(f32[32,1,1]{2,1,0:T(1,128)} %broadcast_in_dim.141), calls=%async_computation | async-start | bytes 32768 | tf_op jit(solution)/shard_map/while/body/eval_jaxpr/all_to_all | solution.py:67
  326.9 6.5 %all-to-all-done = f32[32,1,1]{2,1,0:T(1,128)S(1)} async-done(((f32[32,1,1]{2,1,0:T(1,128)}), f32[32,1,1]{2,1,0:T(1,128)S(1)}, u32[]{:S(2)}, u32[]{:S(2)}) %all-to-all-start) | async-done | bytes 160 | tf_op jit(solution)/shard_map/while/body/eval_jaxpr/all_to_all | solution.py:67
  336.7 2.5 all-to-all-start.1
  339.3 7.1 %all-to-all-done.1 = f32[32,1,1]{2,1,0:T(1,128)S(1)} async-done(((f32[32,1,1]{2,1,0:T(1,128)}), f32[32,1,1]{2,1,0:T(1,128)S(1)}, u32[]{:S(2)}, u32[]{:S(2)}) %all-to-all-start.1) | async-done | bytes 160 | tf_op jit(solution)/shard_map/while/body/eval_jaxpr/all_to_all | solution.py:67
  352.4 2.4 pad.543
  354.7 2.4 pad.544
  357.2 2.4 pad.545
  359.7 2.4 pad.546
  363.7 4.5 %collective-permute-start.1 = (f32[4,1,256]{2,1,0:T(1,128)S(1)}, f32[4,1,256]{2,1,0:T(1,128)S(1)}, u32[]{:S(2)}, u32[]{:S(2)}) collective-permute-start(f32[4,1,256]{2,1,0:T(1,128)S(1)} %get-tuple-element.762), channel_id=1, source_target_pairs={{0,8},{8,16},{16,24},{1,9},{9,17},{17,25},{2,10},{10,18},{18,26},{... | collective-permute-start | bytes 12296 | tf_op jit(solution)/shard_map/while/body/eval_jaxpr/ppermute | solution.py:53
  370.9 4.5 %collective-permute-start.3 = (f32[4,15,1]{2,1,0:T(8,128)S(1)}, f32[4,15,1]{2,1,0:T(8,128)S(1)}, u32[]{:S(2)}, u32[]{:S(2)}) collective-permute-start(f32[4,15,1]{2,1,0:T(8,128)S(1)} %get-tuple-element.764), channel_id=1, source_target_pairs={{0,2},{2,4},{4,6},{1,3},{3,5},{5,7},{8,10},{10,12},{12,14},{9,11},... | collective-permute-start | bytes 728 | tf_op jit(solution)/shard_map/while/body/eval_jaxpr/ppermute | solution.py:53
  385.1 5.3 %all-to-all-start = ((f32[32,1,1]{2,1,0:T(1,128)}), f32[32,1,1]{2,1,0:T(1,128)S(1)}, u32[]{:S(2)}, u32[]{:S(2)}) async-start(f32[32,1,1]{2,1,0:T(1,128)} %broadcast_in_dim.141), calls=%async_computation | async-start | bytes 32768 | tf_op jit(solution)/shard_map/while/body/eval_jaxpr/all_to_all | solution.py:67
  391.1 6.5 %all-to-all-done = f32[32,1,1]{2,1,0:T(1,128)S(1)} async-done(((f32[32,1,1]{2,1,0:T(1,128)}), f32[32,1,1]{2,1,0:T(1,128)S(1)}, u32[]{:S(2)}, u32[]{:S(2)}) %all-to-all-start) | async-done | bytes 160 | tf_op jit(solution)/shard_map/while/body/eval_jaxpr/all_to_all | solution.py:67
  400.9 2.5 all-to-all-start.1
  403.4 7.1 %all-to-all-done.1 = f32[32,1,1]{2,1,0:T(1,128)S(1)} async-done(((f32[32,1,1]{2,1,0:T(1,128)}), f32[32,1,1]{2,1,0:T(1,128)S(1)}, u32[]{:S(2)}, u32[]{:S(2)}) %all-to-all-start.1) | async-done | bytes 160 | tf_op jit(solution)/shard_map/while/body/eval_jaxpr/all_to_all | solution.py:67
  (429 shorter events, 137.2 us)
Async XLA Ops:
  0.6 38.1 %copy-start = (f32[4,40]{1,0:T(4,128)S(1)}, f32[4,40]{1,0:T(4,128)}, u32[]{:S(2)}) copy-start(f32[4,40]{1,0:T(4,128)} %param.63) | copy-start | bytes 1924
  0.6 24.0 %copy-start.3 = (f32[4,13,256]{2,0,1:T(4,128)S(1)}, f32[4,13,256]{2,0,1:T(4,128)}, u32[]{:S(2)}) copy-start(f32[4,13,256]{2,0,1:T(4,128)} %param.54) | copy-start | bytes 159748
  1.7 23.0 %copy-start.5 = (s32[4,13,256]{2,0,1:T(4,128)S(1)}, s32[4,13,256]{2,0,1:T(4,128)}, u32[]{:S(2)}) copy-start(s32[4,13,256]{2,0,1:T(4,128)} %param.56) | copy-start | bytes 159748
  17.7 28.0 %collective-permute-start.7 = (f32[4,1,256]{2,1,0:T(1,128)S(1)}, f32[4,1,256]{2,1,0:T(1,128)S(1)}, u32[]{:S(2)}, u32[]{:S(2)}) collective-permute-start(f32[4,1,256]{2,1,0:T(1,128)S(1)} %get-tuple-element.543), channel_id=1, source_target_pairs={{8,0},{16,8},{24,16},{9,1},{17,9},{25,17},{10,2},{18,10},{26,18},{... | collective-permute-start | bytes 12296 | tf_op jit(solution)/shard_map/ppermute | solution.py:55
  19.0 26.7 %collective-permute-start.6 = (f32[4,1,256]{2,1,0:T(1,128)S(1)}, f32[4,1,256]{2,1,0:T(1,128)S(1)}, u32[]{:S(2)}, u32[]{:S(2)}) collective-permute-start(f32[4,1,256]{2,1,0:T(1,128)S(1)} %get-tuple-element.542), channel_id=1, source_target_pairs={{0,8},{8,16},{16,24},{1,9},{9,17},{17,25},{2,10},{10,18},{18,26},{... | collective-permute-start | bytes 12296 | tf_op jit(solution)/shard_map/ppermute | solution.py:53
  26.9 1.9 copy-start.12
  28.7 2.7 copy-start.7
  31.4 2.4 copy-start.8
  31.4 4.8 %copy-start.9 = (f32[3,40]{1,0:T(4,128)S(1)}, f32[3,40]{1,0:T(4,128)}, u32[]{:S(2)}) copy-start(f32[3,40]{1,0:T(4,128)} %param.61) | copy-start | bytes 1444
  33.8 4.8 %copy-start.6 = (s32[4,13,256]{2,0,1:T(4,128)S(1)}, s32[4,13,256]{2,0,1:T(4,128)}, u32[]{:S(2)}) copy-start(s32[4,13,256]{2,0,1:T(4,128)} %param.57) | copy-start | bytes 159748
  33.8 4.9 %copy-start.4 = (s32[13,256]{1,0:T(8,128)S(1)}, s32[13,256]{1,0:T(8,128)}, u32[]{:S(2)}) copy-start(s32[13,256]{1,0:T(8,128)} %param.66) | copy-start | bytes 39940
  33.8 4.9 %copy-start.1 = (f32[40,13312]{1,0:T(8,128)S(1)}, f32[40,13312]{1,0:T(8,128)}, u32[]{:S(2)}) copy-start(f32[40,13312]{1,0:T(8,128)} %reshape.775) | copy-start | bytes 6389764
  33.8 4.9 %copy-start.11 = (f32[40]{0:T(128)S(1)}, f32[40]{0:T(128)}, u32[]{:S(2)}) copy-start(f32[40]{0:T(128)} %param.62) | copy-start | bytes 484
  45.7 18.1 %copy-start.2 = (f32[64,64]{1,0:T(8,128)S(1)}, f32[64,64]{1,0:T(8,128)}, u32[]{:S(2)}) copy-start(f32[64,64]{1,0:T(8,128)} %constant.621.clone) | copy-start | bytes 49156
  45.8 5.9 %collective-permute-start.9 = (f32[4,15,1]{2,1,0:T(8,128)S(1)}, f32[4,15,1]{2,1,0:T(8,128)S(1)}, u32[]{:S(2)}, u32[]{:S(2)}) collective-permute-start(f32[4,15,1]{2,1,0:T(8,128)S(1)} %get-tuple-element.541), channel_id=1, source_target_pairs={{2,0},{4,2},{6,4},{3,1},{5,3},{7,5},{10,8},{12,10},{14,12},{11,9},... | collective-permute-start | bytes 728 | tf_op jit(solution)/shard_map/ppermute | solution.py:55
  47.1 6.1 %collective-permute-start.8 = (f32[4,15,1]{2,1,0:T(8,128)S(1)}, f32[4,15,1]{2,1,0:T(8,128)S(1)}, u32[]{:S(2)}, u32[]{:S(2)}) collective-permute-start(f32[4,15,1]{2,1,0:T(8,128)S(1)} %get-tuple-element.540), channel_id=1, source_target_pairs={{0,2},{2,4},{4,6},{1,3},{3,5},{5,7},{8,10},{10,12},{12,14},{9,11},... | collective-permute-start | bytes 728 | tf_op jit(solution)/shard_map/ppermute | solution.py:53
  53.4 2.1 collective-permute-start.10
  55.5 3.1 collective-permute-start.11
  74.2 6.0 %collective-permute-start.13 = (f32[4,1,256]{2,1,0:T(1,128)S(1)}, f32[4,1,256]{2,1,0:T(1,128)S(1)}, u32[]{:S(2)}, u32[]{:S(2)}) collective-permute-start(f32[4,1,256]{2,1,0:T(1,128)S(1)} %get-tuple-element.523), channel_id=1, source_target_pairs={{8,0},{16,8},{24,16},{9,1},{17,9},{25,17},{10,2},{18,10},{26,18},{... | collective-permute-start | bytes 12296 | tf_op jit(solution)/shard_map/ppermute | solution.py:55
  75.5 5.9 %collective-permute-start.12 = (f32[4,1,256]{2,1,0:T(1,128)S(1)}, f32[4,1,256]{2,1,0:T(1,128)S(1)}, u32[]{:S(2)}, u32[]{:S(2)}) collective-permute-start(f32[4,1,256]{2,1,0:T(1,128)S(1)} %get-tuple-element.522), channel_id=1, source_target_pairs={{0,8},{8,16},{16,24},{1,9},{9,17},{17,25},{2,10},{10,18},{18,26},{... | collective-permute-start | bytes 12296 | tf_op jit(solution)/shard_map/ppermute | solution.py:53
  81.5 6.9 %collective-permute-start.15 = (f32[4,15,1]{2,1,0:T(8,128)S(1)}, f32[4,15,1]{2,1,0:T(8,128)S(1)}, u32[]{:S(2)}, u32[]{:S(2)}) collective-permute-start(f32[4,15,1]{2,1,0:T(8,128)S(1)} %get-tuple-element.521), channel_id=1, source_target_pairs={{2,0},{4,2},{6,4},{3,1},{5,3},{7,5},{10,8},{12,10},{14,12},{11,9},... | collective-permute-start | bytes 728 | tf_op jit(solution)/shard_map/ppermute | solution.py:55
  82.9 6.9 %collective-permute-start.14 = (f32[4,15,1]{2,1,0:T(8,128)S(1)}, f32[4,15,1]{2,1,0:T(8,128)S(1)}, u32[]{:S(2)}, u32[]{:S(2)}) collective-permute-start(f32[4,15,1]{2,1,0:T(8,128)S(1)} %get-tuple-element.520), channel_id=1, source_target_pairs={{0,2},{2,4},{4,6},{1,3},{3,5},{5,7},{8,10},{10,12},{12,14},{9,11},... | collective-permute-start | bytes 728 | tf_op jit(solution)/shard_map/ppermute | solution.py:53
  90.0 2.1 collective-permute-start.16
  92.1 6.7 %collective-permute-start.17 = (f32[1,15,258]{2,1,0:T(8,128)S(1)}, f32[1,15,258]{2,1,0:T(8,128)S(1)}, u32[]{:S(2)}, u32[]{:S(2)}) collective-permute-start(f32[1,15,258]{2,1,0:T(8,128)S(1)} %get-tuple-element.506), channel_id=1, source_target_pairs={{1,0},{3,2},{5,4},{7,6},{9,8},{11,10},{13,12},{15,14},{17,16},{19,... | collective-permute-start | bytes 46448 | tf_op jit(solution)/shard_map/ppermute | solution.py:55
  93.4 21.0 %copy-start.10 = (f32[1,4,85]{2,1,0:T(4,128)S(1)}, f32[1,4,85]{2,1,0:T(4,128)}, u32[]{:S(2)}) copy-start(f32[1,4,85]{2,1,0:T(4,128)} %param.65) | copy-start | bytes 4084
  99.9 6.1 %collective-permute-start.19 = (f32[3,256]{1,0:T(4,128)S(1)}, f32[3,256]{1,0:T(4,128)S(1)}, u32[]{:S(2)}, u32[]{:S(2)}) collective-permute-start(f32[3,256]{1,0:T(4,128)S(1)} %get-tuple-element.519), channel_id=1, source_target_pairs={{8,0},{16,8},{24,16},{9,1},{17,9},{25,17},{10,2},{18,10},{26,18},{... | collective-permute-start | bytes 9224 | tf_op jit(solution)/shard_map/ppermute | solution.py:55
  101.2 6.1 %collective-permute-start.18 = (f32[3,256]{1,0:T(4,128)S(1)}, f32[3,256]{1,0:T(4,128)S(1)}, u32[]{:S(2)}, u32[]{:S(2)}) collective-permute-start(f32[3,256]{1,0:T(4,128)S(1)} %get-tuple-element.518), channel_id=1, source_target_pairs={{0,8},{8,16},{16,24},{1,9},{9,17},{17,25},{2,10},{10,18},{18,26},{... | collective-permute-start | bytes 9224 | tf_op jit(solution)/shard_map/ppermute | solution.py:53
  107.4 7.2 %collective-permute-start.21 = (f32[19,3]{1,0:T(8,128)S(1)}, f32[19,3]{1,0:T(8,128)S(1)}, u32[]{:S(2)}, u32[]{:S(2)}) collective-permute-start(f32[19,3]{1,0:T(8,128)S(1)} %get-tuple-element.563), channel_id=1, source_target_pairs={{2,0},{4,2},{6,4},{3,1},{5,3},{7,5},{10,8},{12,10},{14,12},{11,9},... | collective-permute-start | bytes 692 | tf_op jit(solution)/shard_map/ppermute | solution.py:55
  108.7 7.1 %collective-permute-start.20 = (f32[19,3]{1,0:T(8,128)S(1)}, f32[19,3]{1,0:T(8,128)S(1)}, u32[]{:S(2)}, u32[]{:S(2)}) collective-permute-start(f32[19,3]{1,0:T(8,128)S(1)} %get-tuple-element.562), channel_id=1, source_target_pairs={{0,2},{2,4},{4,6},{1,3},{3,5},{5,7},{8,10},{10,12},{12,14},{9,11},... | collective-permute-start | bytes 692 | tf_op jit(solution)/shard_map/ppermute | solution.py:53
  135.6 17.1 %all-to-all-start.2 = ((f32[32,1,1]{2,1,0:T(1,128)}), f32[32,1,1]{2,1,0:T(1,128)S(1)}, u32[]{:S(2)}, u32[]{:S(2)}) async-start(f32[32,1,1]{2,1,0:T(1,128)} %broadcast_in_dim.113), calls=%async_computation.2 | async-start | bytes 32768 | tf_op jit(solution)/shard_map/all_to_all | solution.py:67
  168.0 5.9 %collective-permute-start = (f32[4,1,256]{2,1,0:T(1,128)S(1)}, f32[4,1,256]{2,1,0:T(1,128)S(1)}, u32[]{:S(2)}, u32[]{:S(2)}) collective-permute-start(f32[4,1,256]{2,1,0:T(1,128)S(1)} %get-tuple-element.761), channel_id=1, source_target_pairs={{8,0},{16,8},{24,16},{9,1},{17,9},{25,17},{10,2},{18,10},{26,18},{... | collective-permute-start | bytes 12296 | tf_op jit(solution)/shard_map/while/body/eval_jaxpr/ppermute | solution.py:55
  169.3 5.9 %collective-permute-start.1 = (f32[4,1,256]{2,1,0:T(1,128)S(1)}, f32[4,1,256]{2,1,0:T(1,128)S(1)}, u32[]{:S(2)}, u32[]{:S(2)}) collective-permute-start(f32[4,1,256]{2,1,0:T(1,128)S(1)} %get-tuple-element.762), channel_id=1, source_target_pairs={{0,8},{8,16},{16,24},{1,9},{9,17},{17,25},{2,10},{10,18},{18,26},{... | collective-permute-start | bytes 12296 | tf_op jit(solution)/shard_map/while/body/eval_jaxpr/ppermute | solution.py:53
  175.3 5.8 %collective-permute-start.2 = (f32[4,15,1]{2,1,0:T(8,128)S(1)}, f32[4,15,1]{2,1,0:T(8,128)S(1)}, u32[]{:S(2)}, u32[]{:S(2)}) collective-permute-start(f32[4,15,1]{2,1,0:T(8,128)S(1)} %get-tuple-element.763), channel_id=1, source_target_pairs={{2,0},{4,2},{6,4},{3,1},{5,3},{7,5},{10,8},{12,10},{14,12},{11,9},... | collective-permute-start | bytes 728 | tf_op jit(solution)/shard_map/while/body/eval_jaxpr/ppermute | solution.py:55
  176.6 6.1 %collective-permute-start.3 = (f32[4,15,1]{2,1,0:T(8,128)S(1)}, f32[4,15,1]{2,1,0:T(8,128)S(1)}, u32[]{:S(2)}, u32[]{:S(2)}) collective-permute-start(f32[4,15,1]{2,1,0:T(8,128)S(1)} %get-tuple-element.764), channel_id=1, source_target_pairs={{0,2},{2,4},{4,6},{1,3},{3,5},{5,7},{8,10},{10,12},{12,14},{9,11},... | collective-permute-start | bytes 728 | tf_op jit(solution)/shard_map/while/body/eval_jaxpr/ppermute | solution.py:53
  182.9 2.1 collective-permute-start.4
  185.0 3.1 collective-permute-start.5
  190.8 14.2 %all-to-all-start = ((f32[32,1,1]{2,1,0:T(1,128)}), f32[32,1,1]{2,1,0:T(1,128)S(1)}, u32[]{:S(2)}, u32[]{:S(2)}) async-start(f32[32,1,1]{2,1,0:T(1,128)} %broadcast_in_dim.141), calls=%async_computation | async-start | bytes 32768 | tf_op jit(solution)/shard_map/while/body/eval_jaxpr/all_to_all | solution.py:67
  208.4 9.7 %all-to-all-start.1 = ((f32[32,1,1]{2,1,0:T(1,128)}), f32[32,1,1]{2,1,0:T(1,128)S(1)}, u32[]{:S(2)}, u32[]{:S(2)}) async-start(f32[32,1,1]{2,1,0:T(1,128)} %broadcast_in_dim.142), calls=%async_computation.1 | async-start | bytes 32768 | tf_op jit(solution)/shard_map/while/body/eval_jaxpr/all_to_all | solution.py:67
  234.0 5.9 %collective-permute-start = (f32[4,1,256]{2,1,0:T(1,128)S(1)}, f32[4,1,256]{2,1,0:T(1,128)S(1)}, u32[]{:S(2)}, u32[]{:S(2)}) collective-permute-start(f32[4,1,256]{2,1,0:T(1,128)S(1)} %get-tuple-element.761), channel_id=1, source_target_pairs={{8,0},{16,8},{24,16},{9,1},{17,9},{25,17},{10,2},{18,10},{26,18},{... | collective-permute-start | bytes 12296 | tf_op jit(solution)/shard_map/while/body/eval_jaxpr/ppermute | solution.py:55
  235.3 5.9 %collective-permute-start.1 = (f32[4,1,256]{2,1,0:T(1,128)S(1)}, f32[4,1,256]{2,1,0:T(1,128)S(1)}, u32[]{:S(2)}, u32[]{:S(2)}) collective-permute-start(f32[4,1,256]{2,1,0:T(1,128)S(1)} %get-tuple-element.762), channel_id=1, source_target_pairs={{0,8},{8,16},{16,24},{1,9},{9,17},{17,25},{2,10},{10,18},{18,26},{... | collective-permute-start | bytes 12296 | tf_op jit(solution)/shard_map/while/body/eval_jaxpr/ppermute | solution.py:53
  241.3 5.8 %collective-permute-start.2 = (f32[4,15,1]{2,1,0:T(8,128)S(1)}, f32[4,15,1]{2,1,0:T(8,128)S(1)}, u32[]{:S(2)}, u32[]{:S(2)}) collective-permute-start(f32[4,15,1]{2,1,0:T(8,128)S(1)} %get-tuple-element.763), channel_id=1, source_target_pairs={{2,0},{4,2},{6,4},{3,1},{5,3},{7,5},{10,8},{12,10},{14,12},{11,9},... | collective-permute-start | bytes 728 | tf_op jit(solution)/shard_map/while/body/eval_jaxpr/ppermute | solution.py:55
  242.6 6.1 %collective-permute-start.3 = (f32[4,15,1]{2,1,0:T(8,128)S(1)}, f32[4,15,1]{2,1,0:T(8,128)S(1)}, u32[]{:S(2)}, u32[]{:S(2)}) collective-permute-start(f32[4,15,1]{2,1,0:T(8,128)S(1)} %get-tuple-element.764), channel_id=1, source_target_pairs={{0,2},{2,4},{4,6},{1,3},{3,5},{5,7},{8,10},{10,12},{12,14},{9,11},... | collective-permute-start | bytes 728 | tf_op jit(solution)/shard_map/while/body/eval_jaxpr/ppermute | solution.py:53
  248.9 2.1 collective-permute-start.4
  251.0 3.1 collective-permute-start.5
  256.8 12.4 %all-to-all-start = ((f32[32,1,1]{2,1,0:T(1,128)}), f32[32,1,1]{2,1,0:T(1,128)S(1)}, u32[]{:S(2)}, u32[]{:S(2)}) async-start(f32[32,1,1]{2,1,0:T(1,128)} %broadcast_in_dim.141), calls=%async_computation | async-start | bytes 32768 | tf_op jit(solution)/shard_map/while/body/eval_jaxpr/all_to_all | solution.py:67
  272.6 9.7 %all-to-all-start.1 = ((f32[32,1,1]{2,1,0:T(1,128)}), f32[32,1,1]{2,1,0:T(1,128)S(1)}, u32[]{:S(2)}, u32[]{:S(2)}) async-start(f32[32,1,1]{2,1,0:T(1,128)} %broadcast_in_dim.142), calls=%async_computation.1 | async-start | bytes 32768 | tf_op jit(solution)/shard_map/while/body/eval_jaxpr/all_to_all | solution.py:67
  298.2 5.9 %collective-permute-start = (f32[4,1,256]{2,1,0:T(1,128)S(1)}, f32[4,1,256]{2,1,0:T(1,128)S(1)}, u32[]{:S(2)}, u32[]{:S(2)}) collective-permute-start(f32[4,1,256]{2,1,0:T(1,128)S(1)} %get-tuple-element.761), channel_id=1, source_target_pairs={{8,0},{16,8},{24,16},{9,1},{17,9},{25,17},{10,2},{18,10},{26,18},{... | collective-permute-start | bytes 12296 | tf_op jit(solution)/shard_map/while/body/eval_jaxpr/ppermute | solution.py:55
  299.5 5.9 %collective-permute-start.1 = (f32[4,1,256]{2,1,0:T(1,128)S(1)}, f32[4,1,256]{2,1,0:T(1,128)S(1)}, u32[]{:S(2)}, u32[]{:S(2)}) collective-permute-start(f32[4,1,256]{2,1,0:T(1,128)S(1)} %get-tuple-element.762), channel_id=1, source_target_pairs={{0,8},{8,16},{16,24},{1,9},{9,17},{17,25},{2,10},{10,18},{18,26},{... | collective-permute-start | bytes 12296 | tf_op jit(solution)/shard_map/while/body/eval_jaxpr/ppermute | solution.py:53
  305.5 5.8 %collective-permute-start.2 = (f32[4,15,1]{2,1,0:T(8,128)S(1)}, f32[4,15,1]{2,1,0:T(8,128)S(1)}, u32[]{:S(2)}, u32[]{:S(2)}) collective-permute-start(f32[4,15,1]{2,1,0:T(8,128)S(1)} %get-tuple-element.763), channel_id=1, source_target_pairs={{2,0},{4,2},{6,4},{3,1},{5,3},{7,5},{10,8},{12,10},{14,12},{11,9},... | collective-permute-start | bytes 728 | tf_op jit(solution)/shard_map/while/body/eval_jaxpr/ppermute | solution.py:55
  306.7 6.1 %collective-permute-start.3 = (f32[4,15,1]{2,1,0:T(8,128)S(1)}, f32[4,15,1]{2,1,0:T(8,128)S(1)}, u32[]{:S(2)}, u32[]{:S(2)}) collective-permute-start(f32[4,15,1]{2,1,0:T(8,128)S(1)} %get-tuple-element.764), channel_id=1, source_target_pairs={{0,2},{2,4},{4,6},{1,3},{3,5},{5,7},{8,10},{10,12},{12,14},{9,11},... | collective-permute-start | bytes 728 | tf_op jit(solution)/shard_map/while/body/eval_jaxpr/ppermute | solution.py:53
  313.0 2.1 collective-permute-start.4
  315.2 3.1 collective-permute-start.5
  321.0 12.4 %all-to-all-start = ((f32[32,1,1]{2,1,0:T(1,128)}), f32[32,1,1]{2,1,0:T(1,128)S(1)}, u32[]{:S(2)}, u32[]{:S(2)}) async-start(f32[32,1,1]{2,1,0:T(1,128)} %broadcast_in_dim.141), calls=%async_computation | async-start | bytes 32768 | tf_op jit(solution)/shard_map/while/body/eval_jaxpr/all_to_all | solution.py:67
  336.7 9.7 %all-to-all-start.1 = ((f32[32,1,1]{2,1,0:T(1,128)}), f32[32,1,1]{2,1,0:T(1,128)S(1)}, u32[]{:S(2)}, u32[]{:S(2)}) async-start(f32[32,1,1]{2,1,0:T(1,128)} %broadcast_in_dim.142), calls=%async_computation.1 | async-start | bytes 32768 | tf_op jit(solution)/shard_map/while/body/eval_jaxpr/all_to_all | solution.py:67
  362.4 5.9 %collective-permute-start = (f32[4,1,256]{2,1,0:T(1,128)S(1)}, f32[4,1,256]{2,1,0:T(1,128)S(1)}, u32[]{:S(2)}, u32[]{:S(2)}) collective-permute-start(f32[4,1,256]{2,1,0:T(1,128)S(1)} %get-tuple-element.761), channel_id=1, source_target_pairs={{8,0},{16,8},{24,16},{9,1},{17,9},{25,17},{10,2},{18,10},{26,18},{... | collective-permute-start | bytes 12296 | tf_op jit(solution)/shard_map/while/body/eval_jaxpr/ppermute | solution.py:55
  363.7 5.9 %collective-permute-start.1 = (f32[4,1,256]{2,1,0:T(1,128)S(1)}, f32[4,1,256]{2,1,0:T(1,128)S(1)}, u32[]{:S(2)}, u32[]{:S(2)}) collective-permute-start(f32[4,1,256]{2,1,0:T(1,128)S(1)} %get-tuple-element.762), channel_id=1, source_target_pairs={{0,8},{8,16},{16,24},{1,9},{9,17},{17,25},{2,10},{10,18},{18,26},{... | collective-permute-start | bytes 12296 | tf_op jit(solution)/shard_map/while/body/eval_jaxpr/ppermute | solution.py:53
  369.6 5.8 %collective-permute-start.2 = (f32[4,15,1]{2,1,0:T(8,128)S(1)}, f32[4,15,1]{2,1,0:T(8,128)S(1)}, u32[]{:S(2)}, u32[]{:S(2)}) collective-permute-start(f32[4,15,1]{2,1,0:T(8,128)S(1)} %get-tuple-element.763), channel_id=1, source_target_pairs={{2,0},{4,2},{6,4},{3,1},{5,3},{7,5},{10,8},{12,10},{14,12},{11,9},... | collective-permute-start | bytes 728 | tf_op jit(solution)/shard_map/while/body/eval_jaxpr/ppermute | solution.py:55
  370.9 6.1 %collective-permute-start.3 = (f32[4,15,1]{2,1,0:T(8,128)S(1)}, f32[4,15,1]{2,1,0:T(8,128)S(1)}, u32[]{:S(2)}, u32[]{:S(2)}) collective-permute-start(f32[4,15,1]{2,1,0:T(8,128)S(1)} %get-tuple-element.764), channel_id=1, source_target_pairs={{0,2},{2,4},{4,6},{1,3},{3,5},{5,7},{8,10},{10,12},{12,14},{9,11},... | collective-permute-start | bytes 728 | tf_op jit(solution)/shard_map/while/body/eval_jaxpr/ppermute | solution.py:53
  377.2 2.1 collective-permute-start.4
  379.3 3.1 collective-permute-start.5
  385.1 12.4 %all-to-all-start = ((f32[32,1,1]{2,1,0:T(1,128)}), f32[32,1,1]{2,1,0:T(1,128)S(1)}, u32[]{:S(2)}, u32[]{:S(2)}) async-start(f32[32,1,1]{2,1,0:T(1,128)} %broadcast_in_dim.141), calls=%async_computation | async-start | bytes 32768 | tf_op jit(solution)/shard_map/while/body/eval_jaxpr/all_to_all | solution.py:67
  400.9 9.7 %all-to-all-start.1 = ((f32[32,1,1]{2,1,0:T(1,128)}), f32[32,1,1]{2,1,0:T(1,128)S(1)}, u32[]{:S(2)}, u32[]{:S(2)}) async-start(f32[32,1,1]{2,1,0:T(1,128)} %broadcast_in_dim.142), calls=%async_computation.1 | async-start | bytes 32768 | tf_op jit(solution)/shard_map/while/body/eval_jaxpr/all_to_all | solution.py:67

commit v2 on v0

v2 whole, which is shorter than its diff:
```python
import jax
import jax.numpy as jnp
import numpy as np
from jax import lax
from jax.sharding import PartitionSpec as P

TYPES = 3
CLASSES = 4
STEPS = 2
ITERS = 4
REACH = 2


STIFF_LINE = (
    np.array(
        [
            [148.0, -189.0, 54.0, -13.0],
            [-189.0, 432.0, -297.0, 54.0],
            [54.0, -297.0, 432.0, -189.0],
            [-13.0, 54.0, -189.0, 148.0],
        ]
    )
    / 40.0
)
MASS_LINE = (
    np.array(
        [
            [128.0, 99.0, -36.0, 19.0],
            [99.0, 648.0, -81.0, -36.0],
            [-36.0, -81.0, 648.0, 99.0],
            [19.0, -36.0, 99.0, 128.0],
        ]
    )
    / 1680.0
)
time_step = 0.002
torso_shift = 0.02
HIGH = lax.Precision.HIGHEST


def gather_matrix(length, line):
    elements = (length - 1) // 3
    out = np.zeros((length, 4, elements))
    for e in range(elements):
        for a in range(4):
            out[3 * e : 3 * e + 4, a, e] = line[a, :]
    return out.reshape(length, 4 * elements)


def local_products(values, conduct):
    depth, first, second = values.shape
    first_el, second_el = conduct.shape[1], conduct.shape[2]
    mass_d = [[float(MASS_LINE[i, j]) for j in range(4)] for i in range(4)]
    stiff_d = [[float(STIFF_LINE[i, j]) for j in range(4)] for i in range(4)]
    rows = [values[j] for j in range(depth)]
    v_mass = jnp.stack([sum(mass_d[i][j] * rows[j] for j in range(4)) for i in range(4)])
    v_stiff = jnp.stack([sum(stiff_d[i][j] * rows[j] for j in range(4)) for i in range(4)])
    pick_mass = jnp.asarray(gather_matrix(first, MASS_LINE).T, jnp.float32)
    pick_stiff = jnp.asarray(gather_matrix(first, STIFF_LINE).T, jnp.float32)
    along_first_m = jnp.einsum("kx,dxy->dky", pick_mass, v_mass, precision=HIGH)
    along_first_k = jnp.einsum("kx,dxy->dky", pick_stiff, v_mass, precision=HIGH) + jnp.einsum(
        "kx,dxy->dky", pick_mass, v_stiff, precision=HIGH
    )
    lanes_m = jnp.asarray(gather_matrix(second, MASS_LINE), jnp.float32)
    lanes_k = jnp.asarray(gather_matrix(second, STIFF_LINE), jnp.float32)
    flat_m = along_first_m.reshape(-1, second)
    flat_k = along_first_k.reshape(-1, second)
    element = jnp.dot(flat_m, lanes_k, precision=HIGH) + jnp.dot(flat_k, lanes_m, precision=HIGH)
    element = element.reshape(depth, 4, first_el, 4, second_el) * conduct.reshape(
        1, 1, first_el, 1, second_el
    )
    scatter_second = jnp.asarray(gather_matrix(second, np.eye(4)).T, jnp.float32)
    spread = jnp.dot(element.reshape(-1, 4 * second_el), scatter_second, precision=HIGH)
    spread = spread.reshape(depth, 4 * first_el, second)
    scatter_first = jnp.asarray(gather_matrix(first, np.eye(4)), jnp.float32)
    return jnp.einsum("xk,dky->dxy", scatter_first, spread, precision=HIGH)


def torso_stage(values, scalars):
    count = lax.axis_size("torso")
    if count == 1:
        return values, scalars
    if count != 2:
        raise NotImplementedError("torso size")
    me = lax.axis_index("torso")
    face = jnp.where(me == 0, values[-1], values[0])
    extra = None
    if scalars is not None:
        extra = jnp.zeros((1, values.shape[2]), values.dtype).at[0, : scalars.shape[0]].set(scalars)
        face = jnp.concatenate([face, extra], 0)
    got = lax.ppermute(face, "torso", [(0, 1), (1, 0)])
    rows = values.shape[1]
    got_face = got[:rows]
    values = values.at[-1].add(jnp.where(me == 0, got_face, 0.0))
    values = values.at[0].add(jnp.where(me == 1, got_face, 0.0))
    if scalars is not None:
        scalars = scalars + got[rows, : scalars.shape[0]]
    return values, scalars


def plane_exchange(pieces, width, scalars):
    count_x, count_y = lax.axis_size("hx"), lax.axis_size("hy")
    me_x, me_y = lax.axis_index("hx"), lax.axis_index("hy")
    rows = []
    for code in range(9):
        offset = (code // 3 - 1, code % 3 - 1)
        piece = pieces.get(offset)
        row = jnp.zeros((width,), jnp.float32) if piece is None else jnp.pad(piece, (0, width - piece.shape[0]))
        if scalars is not None:
            row = jnp.concatenate([row, scalars])
        rows.append(row)
    table = jnp.stack(rows)
    peers = jnp.arange(count_x * count_y, dtype=jnp.int32)
    off_x = peers // count_y - me_x
    off_y = peers % count_y - me_y
    near = (jnp.abs(off_x) <= 1) & (jnp.abs(off_y) <= 1)
    code_of = jnp.where(near, (off_x + 1) * 3 + (off_y + 1), 4)
    send = jnp.take(table, code_of, axis=0)
    got = lax.all_to_all(send, ("hx", "hy"), 0, 0, tiled=True)
    received = {}
    for offset in pieces:
        src_x, src_y = me_x + offset[0], me_y + offset[1]
        valid = (src_x >= 0) & (src_x < count_x) & (src_y >= 0) & (src_y < count_y)
        src = jnp.clip(src_x, 0, count_x - 1) * count_y + jnp.clip(src_y, 0, count_y - 1)
        row = lax.dynamic_index_in_dim(got, src, 0, keepdims=False)
        received[offset] = jnp.where(valid, row[: pieces[offset].shape[0]], 0.0)
    total = None
    if scalars is not None:
        total = jnp.sum(got[:, width:], axis=0)
    return received, total


def face_sums(values, scalars=None):
    values, scalars = torso_stage(values, scalars)
    depth, first, second = values.shape
    pieces = {
        (1, 0): values[:, -1, :].reshape(-1),
        (-1, 0): values[:, 0, :].reshape(-1),
        (0, 1): values[:, :, -1].reshape(-1),
        (0, -1): values[:, :, 0].reshape(-1),
        (1, 1): values[:, -1, -1],
        (1, -1): values[:, -1, 0],
        (-1, 1): values[:, 0, -1],
        (-1, -1): values[:, 0, 0],
    }
    got, total = plane_exchange(pieces, depth * second, scalars)
    low_second = got[(0, -1)].reshape(depth, first)
    low_second = low_second.at[:, 0].add(got[(-1, -1)]).at[:, -1].add(got[(1, -1)])
    high_second = got[(0, 1)].reshape(depth, first)
    high_second = high_second.at[:, 0].add(got[(-1, 1)]).at[:, -1].add(got[(1, 1)])
    values = values.at[:, 0, :].add(got[(-1, 0)].reshape(depth, second))
    values = values.at[:, -1, :].add(got[(1, 0)].reshape(depth, second))
    values = values.at[:, :, 0].add(low_second).at[:, :, -1].add(high_second)
    return values, total


def rim_plane(plane, rim):
    first, second = plane.shape
    pieces = {
        (1, 0): plane[-rim:, :].reshape(-1),
        (-1, 0): plane[:rim, :].reshape(-1),
        (0, 1): plane[:, -rim:].reshape(-1),
        (0, -1): plane[:, :rim].reshape(-1),
        (1, 1): plane[-rim:, -rim:].reshape(-1),
        (1, -1): plane[-rim:, :rim].reshape(-1),
        (-1, 1): plane[:rim, -rim:].reshape(-1),
        (-1, -1): plane[:rim, :rim].reshape(-1),
    }
    got, _ = plane_exchange(pieces, rim * second, None)
    top = jnp.concatenate(
        [got[(-1, -1)].reshape(rim, rim), got[(-1, 0)].reshape(rim, second), got[(-1, 1)].reshape(rim, rim)], 1
    )
    middle = jnp.concatenate(
        [got[(0, -1)].reshape(first, rim), plane, got[(0, 1)].reshape(first, rim)], 1
    )
    bottom = jnp.concatenate(
        [got[(1, -1)].reshape(rim, rim), got[(1, 0)].reshape(rim, second), got[(1, 1)].reshape(rim, rim)], 1
    )
    return jnp.concatenate([top, middle, bottom], 0)


def line_factors(length, block_id, block_count):
    position = jnp.arange(length)
    at_start = (position == 0) & (block_id == 0)
    at_end = (position == length - 1) & (block_id == block_count - 1)
    mass_line = jnp.where(position % 3 == 0, jnp.where(at_start | at_end, 0.125, 0.25), 0.375)
    shared = (position == 0) & (block_id > 0) | (position == length - 1) & (
        block_id < block_count - 1
    )
    weight = jnp.where(shared, 0.5, 1.0)
    return (mass_line.astype(jnp.float32), weight.astype(jnp.float32))


def factor_grid(depth_line, first_line, second_line):
    return depth_line[:, None, None] * first_line[None, :, None] * second_line[None, None, :]


def node_table(matrix, labels, kind_count):
    onehot = (
        labels.reshape(1, -1) == jnp.arange(kind_count, dtype=jnp.int32).reshape(-1, 1)
    ).astype(jnp.float32)
    return jnp.dot(matrix.T, onehot, precision=HIGH)


def ext_index(target, anchor, length_local, rim_width):
    relative = target - anchor
    return jnp.where(
        relative < 0,
        rim_width - 1 + relative,
        jnp.where(relative > length_local - 1, rim_width + relative + 1, rim_width + relative),
    )


def per_device(
    potential,
    gating,
    cell_type,
    drug_class,
    half_point,
    gate_slope,
    time_const,
    max_conduct,
    reversal,
    drug_block,
    heart_cond,
    torso_cond,
    epi_target,
):
    depth_len, first_len, second_len = potential.shape
    torso_len = 3 * torso_cond.shape[0] + 1
    index_torso = lax.axis_index("torso")
    index_first = lax.axis_index("hx")
    index_second = lax.axis_index("hy")
    heart_depth, unused_depth = line_factors(depth_len, index_torso, lax.axis_size("torso"))
    first_mass, first_weight = line_factors(first_len, index_first, lax.axis_size("hx"))
    second_mass, second_weight = line_factors(second_len, index_second, lax.axis_size("hy"))
    torso_depth, torso_depth_weight = line_factors(torso_len, index_torso, lax.axis_size("torso"))
    heart_mass = factor_grid(heart_depth, first_mass, second_mass)
    torso_mass = factor_grid(torso_depth, first_mass, second_mass)
    torso_weight = factor_grid(torso_depth_weight, first_weight, second_weight)
    type_flat = cell_type.reshape(-1)
    half_nodes = node_table(half_point, type_flat, TYPES)
    slope_nodes = node_table(gate_slope, type_flat, TYPES)
    decay_nodes = jnp.exp(-time_step / node_table(time_const, type_flat, TYPES))
    cond_nodes = node_table(max_conduct, type_flat, TYPES) * node_table(
        drug_block, drug_class.reshape(-1), CLASSES
    )
    gate_flat = gating.reshape(gating.shape[0], -1)
    for repeat in range(STEPS):
        volts = potential.reshape(1, -1)
        inf_value = jax.nn.sigmoid((volts - half_nodes) * slope_nodes)
        gate_flat = inf_value + (gate_flat - inf_value) * decay_nodes
        current = jnp.sum(cond_nodes * gate_flat * (volts - reversal[:, None]), 0)
        diffusion, _ = face_sums(local_products(potential, heart_cond))
        potential = potential - time_step * (
            diffusion / heart_mass + current.reshape(potential.shape)
        )
    new_gating = gate_flat.reshape(gating.shape)

    rim_width = REACH + 1
    extended = rim_plane(potential[0], rim_width)
    distinct_second = lax.axis_size("hy") * (second_len - 1) + 1
    target_first = epi_target // distinct_second
    target_second = epi_target % distinct_second
    place_first = ext_index(target_first, index_first * (first_len - 1), first_len, rim_width)
    place_second = ext_index(target_second, index_second * (second_len - 1), second_len, rim_width)
    shift_first = place_first - rim_width - jnp.arange(first_len)[:, None]
    shift_second = place_second - rim_width - jnp.arange(second_len)[None, :]
    picked_values = jnp.zeros((first_len, second_len), jnp.float32)
    for step_first in range(-rim_width, rim_width + 1):
        rows = extended[rim_width + step_first : rim_width + step_first + first_len]
        along = jnp.zeros((first_len, second_len), jnp.float32)
        for step_second in range(-rim_width, rim_width + 1):
            window = rows[:, rim_width + step_second : rim_width + step_second + second_len]
            along = jnp.where(shift_second == step_second, window, along)
        picked_values = jnp.where(shift_first == step_first, along, picked_values)
    plane = jnp.where(index_torso == 0, picked_values, 0.0)
    rhs = jnp.concatenate(
        [plane[None], jnp.zeros((torso_len - 1, first_len, second_len), jnp.float32)], 0
    )

    mass_shift = torso_shift * torso_mass
    weighted_mass = torso_weight * mass_shift

    def exchange(residual, extra):
        local = local_products(residual, torso_cond)
        partial = jnp.stack(
            [
                jnp.sum(torso_weight * residual * residual),
                jnp.sum(residual * local) + jnp.sum(weighted_mass * residual * residual),
            ]
            + extra(local)
        )
        summed, sums = face_sums(local, partial)
        return summed + mass_shift * residual, sums

    image, sums = exchange(rhs, lambda local: [])
    norm_now = sums[0]
    curvature = sums[1]
    step_size = norm_now / curvature
    solution = step_size * rhs
    direction = rhs
    residual = rhs - step_size * image

    def later_turn(turn_index, state_tuple):
        solution, residual, direction, image, norm_now, curvature = state_tuple
        s_image, sums = exchange(
            residual,
            lambda local: [
                jnp.sum(torso_weight * residual * image),
                jnp.sum(direction * local) + jnp.sum(weighted_mass * direction * residual),
            ],
        )
        norm_next = sums[0]
        ratio = norm_next / norm_now
        curvature = sums[1] + ratio * (sums[2] + sums[3]) + ratio * ratio * curvature
        direction = residual + ratio * direction
        image = s_image + ratio * image
        step_size = norm_next / curvature
        solution = solution + step_size * direction
        residual = residual - step_size * image
        return (solution, residual, direction, image, norm_next, curvature)

    state = (solution, residual, direction, image, norm_now, curvature)
    solution = lax.fori_loop(1, ITERS, later_turn, state)[0]
    return (potential, new_gating, solution)


def solution(mesh):
    placed = (
        P("torso", "hx", "hy"),
        P(None, "torso", "hx", "hy"),
        P("torso", "hx", "hy"),
        P("torso", "hx", "hy"),
        P(),
        P(),
        P(),
        P(),
        P(),
        P(),
        P("torso", "hx", "hy"),
        P("torso", "hx", "hy"),
        P("hx", "hy"),
    )
    return jax.shard_map(
        per_device,
        mesh=mesh,
        in_specs=placed,
        out_specs=(P("torso", "hx", "hy"), P(None, "torso", "hx", "hy"), P("torso", "hx", "hy")),
        check_vma=False,
    )
```

time: 677 us -> 244 us (0.36)
  blocking collectives: 379 us -> 0 us
  starting transfers between devices: 102 us -> 35 us
  local copies, waits for them, and re-layouts: 119 us -> 52.3 us
  other arithmetic: 15 us -> 49.7 us
  matrix products: 18.9 us -> 38 us
  loops' own time: 8.87 us -> 23 us
  waiting for transfers between devices: 30.7 us -> 39.6 us
    psum x9 -> x0, blocking collectives: 379 us -> none  [the longest x5 207 us: squares(): lax.psum(jnp.sum(torso_weight * vector * vector), ('hx', 'hy', 'torso'))]
    ppermute x40 -> x6, starting transfers between devices: 102 us -> 0.93 us  [torso_stage(): got = lax.ppermute(face, 'torso', [(0, 1), (1, 0)])]
    pad x48 -> x18, local copies, waits for them, and re-layouts: 58 us -> 3.01 us  [plane_exchange(): jnp.pad(piece, (0, width - piece.shape[0]))]
    all_to_all x0 -> x7, waiting for transfers between devices: none -> 35.3 us  [plane_exchange(): got = lax.all_to_all(send, ('hx', 'hy'), 0, 0, tiled=True)]
    all_to_all x0 -> x7, starting transfers between devices: none -> 34.1 us  [plane_exchange(): got = lax.all_to_all(send, ('hx', 'hy'), 0, 0, tiled=True)]
    ppermute x40 -> x6, waiting for transfers between devices: 30.7 us -> 4.31 us  [torso_stage(): got = lax.ppermute(face, 'torso', [(0, 1), (1, 0)])]
    another operation x24 -> x29, other arithmetic: 0.51 us -> 23.4 us  [the longest x18 0.48 us: pick_nodes(): jnp.stack([lax.slice_in_dim(values, offset, offset + 3 * length - 2, 3, a...]
    dot_general x11 -> x47, matrix products: 18.9 us -> 38 us  [the longest x5 17.2 us: node_table(): return jnp.dot(matrix.T, onehot, precision=HIGH)]
  transfers between devices with their start and end apart: 40 -> 13, of which waited for: 23 -> 10; matrix products, arithmetic and copies ran while one was open for 5% -> 17% of each run, Pallas kernels for 0% -> 0%
where the time goes in v2:
time: 244 us; the launch traced here: 242 us
  local copies, waits for them, and re-layouts  52.3 us (21%)
  other arithmetic  49.7 us (20%)
  waiting for transfers between devices  39.6 us (16%)
  matrix products  38 us (16%)
  starting transfers between devices  35 us (14%)
  loops' own time  23 us (9%)
  between operations  4.43 us (2%)
    all_to_all x7, waiting for transfers between devices, plane_exchange(): got = lax.all_to_all(send, ('hx', 'hy'), 0, 0, tiled=True)  35.3 us
    all_to_all x7, starting transfers between devices, plane_exchange(): got = lax.all_to_all(send, ('hx', 'hy'), 0, 0, tiled=True)  34.1 us
    another operation x27, other arithmetic  23.1 us
    another operation x1, loops' own time, per_device(): solution = lax.fori_loop(1, ITERS, later_turn, state)[0]  23 us
    dot_general x5, matrix products, node_table(): return jnp.dot(matrix.T, onehot, precision=HIGH)  17.2 us
    unnamed x82, local copies, waits for them, and re-layouts  10.1 us
    gather x7, local copies, waits for them, and re-layouts, plane_exchange(): send = jnp.take(table, code_of, axis=0)  6.43 us
    reduce_sum x1, other arithmetic, per_device(): current = jnp.sum(cond_nodes * gate_flat * (volts - reversal[:, None]), 0)  5.43 us
  transfers between devices with their start and end apart: 13, of which 10 were waited for; matrix products, arithmetic and copies ran while one was open for 17% of the time, Pallas kernels for 0%

profile of v2, /device:TPU:0, one launch (start us, length us, event | category | flops | bytes accessed | tf_op | source)
XLA Modules:
  0.0 242.1 jit_solution(13525357416584418689)
XLA Ops:
  0.7 1.0 copy.151
  2.6 0.9 fusion.98
  3.5 0.9 fusion.97
  4.4 1.3 fusion.250
  5.8 0.9 convolution_add_fusion.7
  6.7 1.3 fusion.51
  9.8 2.0 copy.150
  11.8 2.0 reshape.2392
  13.8 2.6 %fusion.48 = f32[40,13312]{1,0:T(8,128)} fusion(f32[3,40]{1,0:T(4,128)S(1)} %copy-done.33, s32[13312]{0:T(1024)S(1)} %eq.316), kind=kOutput, calls=%fused_computation.139 | convolution fusion | flops 19741696 | bytes 2183648 | tf_op jit(solution)/shard_map/dot_general | solution.py:202
  16.5 2.4 fusion.54
  18.8 2.4 fusion.55
  21.2 2.4 fusion.56
  24.4 7.5 %multiply_reduce_fusion.3 = (f32[13312]{0:T(1024)}, f32[40,13312]{1,0:T(8,128)}) fusion(f32[40]{0:T(128)S(1)} %copy-done.31, f32[13312]{0:T(1024)S(1)} %sub.236, f32[40,13312]{1,0:T(8,128)} %fusion.48, f32[40,13312]{1,0:T(8,128)S(1)} %reshape.2392, f32[13312,40]{0,1:T(8,128)} %fusion.54, f32[13312,40]{0,1:T(8,128)} %fusion.55, f32[13312,40]{0,1:T(8,128)} %fusion.56, ...), kind=kOutput, calls=%fused_computation.147 | convolution fusion | flops 32521216 | bytes 12940064 | tf_op jit(solution)/shard_map/dot_general | solution.py:202
  33.9 1.3 gather_fusion.3
  35.2 0.9 select_bitcast_fusion.1
  36.8 7.9 %all-to-all-start.1 = ((f32[16,1,1024]{2,1,0:T(1,128)}), f32[16,1,1024]{2,1,0:T(1,128)S(1)}, u32[]{:S(2)}, u32[]{:S(2)}) async-start(f32[16,1,1024]{2,1,0:T(1,128)} %copy.138), calls=%async_computation.1 | async-start | bytes 131072 | tf_op jit(solution)/shard_map/all_to_all | solution.py:119
  45.2 0.8 reshape.2393
  46.8 5.4 %all-to-all-done.1 = f32[16,1,1024]{2,1,0:T(1,128)S(1)} async-done(((f32[16,1,1024]{2,1,0:T(1,128)}), f32[16,1,1024]{2,1,0:T(1,128)S(1)}, u32[]{:S(2)}, u32[]{:S(2)}) %all-to-all-start.1) | async-done | bytes 65568 | tf_op jit(solution)/shard_map/all_to_all | solution.py:119
  52.9 1.3 fusion.199
  56.9 0.8 select_n.1311
  61.2 1.2 fusion.52
  62.8 0.9 fusion.255
  65.6 1.6 mul.1148
  72.8 1.4 stack.359
  74.3 1.3 gather_fusion.4
  75.6 0.9 select_bitcast_fusion
  77.2 4.1 %all-to-all-start.2 = ((f32[16,1,1024]{2,1,0:T(1,128)}), f32[16,1,1024]{2,1,0:T(1,128)}, u32[]{:S(2)}, u32[]{:S(2)}) async-start(f32[16,1,1024]{2,1,0:T(1,128)} %copy.152), calls=%async_computation.2 | async-start | bytes 131072 | tf_op jit(solution)/shard_map/all_to_all | solution.py:119
  81.3 5.4 %multiply_reduce_fusion.2 = (f32[13312]{0:T(1024)S(1)}, f32[40,13312]{1,0:T(8,128)}) fusion(f32[40,13312]{1,0:T(8,128)} %get-tuple-element.1260, f32[13312]{0:T(1024)S(1)} %sub.244, f32[40]{0:T(128)} %param.133, f32[40,13312]{1,0:T(8,128)} %fusion.48, f32[40,13312]{1,0:T(8,128)S(1)} %reshape.2392, f32[13312,40]{0,1:T(8,128)} %fusion.54, ...), kind=kLoop, calls=%fused_computation.146 | loop fusion | flops 10636288 | bytes 12939424 | tf_op jit(solution)/shard_map/reduce_sum | solution.py:253
  86.8 2.2 all-to-all-done.2
  88.9 0.8 fusion.188
  95.9 4.7 %all-to-all-start.3 = ((f32[16,1,768]{2,1,0:T(1,128)}), f32[16,1,768]{2,1,0:T(1,128)S(1)}, u32[]{:S(2)}, u32[]{:S(2)}) async-start(f32[16,1,768]{2,1,0:T(1,128)} %copy.161), calls=%async_computation.3 | async-start | bytes 98304 | tf_op jit(solution)/shard_map/all_to_all | solution.py:119
  101.1 6.9 %all-to-all-done.3 = f32[16,1,768]{2,1,0:T(1,128)S(1)} async-done(((f32[16,1,768]{2,1,0:T(1,128)}), f32[16,1,768]{2,1,0:T(1,128)S(1)}, u32[]{:S(2)}, u32[]{:S(2)}) %all-to-all-start.3) | async-done | bytes 49184 | tf_op jit(solution)/shard_map/all_to_all | solution.py:119
  110.1 1.3 fusion.53
  111.8 1.6 fusion.68
  114.6 1.4 broadcast_select_fusion.17
  116.1 1.2 collective-permute-done.3
  118.8 1.3 gather_fusion.2
  120.1 1.0 bitcast_select_fusion.1
  121.8 3.5 %all-to-all-start.4 = ((f32[16,1,1026]{2,1,0:T(1,128)}), f32[16,1,1026]{2,1,0:T(1,128)S(1)}, u32[]{:S(2)}, u32[]{:S(2)}) async-start(f32[16,1,1026]{2,1,0:T(1,128)} %copy.162), calls=%async_computation.4 | async-start | bytes 147456 | tf_op jit(solution)/shard_map/all_to_all | solution.py:119
  125.3 2.1 reshape.2403
  127.4 5.0 %copy.172 = f32[40,4,13,256]{3,1,2,0:T(4,128)} copy(f32[40,4,13,256]{3,2,1,0:T(8,128)} %reshape.2403) | data formatting | bytes 4259840
  138.5 103.0 %while.69 = (s32[]{:T(128)}, f32[4,13,256]{2,1,0:T(8,128)S(1)}, f32[4,13,256]{2,1,0:T(8,128)S(1)}, f32[4,13,256]{2,1,0:T(8,128)S(1)}, f32[4,13,256]{2,1,0:T(8,12...) while((s32[]{:T(128)}, f32[4,13,256]{2,1,0:T(8,128)S(1)}, ...), condition=%wide.region_19.21_spmd.clone.clone.clone, body=%wide.region_9.20_spmd.sunk.clone.clone.clone.sunk | while | flops 211608112 | bytes 4754102 | solution.py:325
  141.1 0.8 fusion.355
  144.4 2.0 broadcast_select_fusion.45
  146.7 1.0 collective-permute-done
  148.2 1.3 fusion.357
  151.0 6.9 %all-to-all-start = ((f32[16,1,1028]{2,1,0:T(1,128)}), f32[16,1,1028]{2,1,0:T(1,128)S(1)}, u32[]{:S(2)}, u32[]{:S(2)}) async-start(f32[16,1,1028]{2,1,0:T(1,128)} %copy.191), calls=%async_computation | async-start | bytes 147456 | tf_op jit(solution)/shard_map/while/body/eval_jaxpr/all_to_all | solution.py:119
  158.5 7.0 %all-to-all-done = f32[16,1,1028]{2,1,0:T(1,128)S(1)} async-done(((f32[16,1,1028]{2,1,0:T(1,128)}), f32[16,1,1028]{2,1,0:T(1,128)S(1)}, u32[]{:S(2)}, u32[]{:S(2)}) %all-to-all-start) | async-done | bytes 65824 | tf_op jit(solution)/shard_map/while/body/eval_jaxpr/all_to_all | solution.py:119
  171.2 0.8 add_select_fusion.17
  177.7 0.8 fusion.355
  181.0 2.0 broadcast_select_fusion.45
  183.1 1.1 collective-permute-done
  184.8 1.3 fusion.357
  187.6 3.5 %all-to-all-start = ((f32[16,1,1028]{2,1,0:T(1,128)}), f32[16,1,1028]{2,1,0:T(1,128)S(1)}, u32[]{:S(2)}, u32[]{:S(2)}) async-start(f32[16,1,1028]{2,1,0:T(1,128)} %copy.191), calls=%async_computation | async-start | bytes 147456 | tf_op jit(solution)/shard_map/while/body/eval_jaxpr/all_to_all | solution.py:119
  191.7 6.9 %all-to-all-done = f32[16,1,1028]{2,1,0:T(1,128)S(1)} async-done(((f32[16,1,1028]{2,1,0:T(1,128)}), f32[16,1,1028]{2,1,0:T(1,128)S(1)}, u32[]{:S(2)}, u32[]{:S(2)}) %all-to-all-start) | async-done | bytes 65824 | tf_op jit(solution)/shard_map/while/body/eval_jaxpr/all_to_all | solution.py:119
  204.4 0.8 add_select_fusion.17
  206.4 0.8 add_select_fusion.19
  210.9 0.8 fusion.355
  214.2 2.0 broadcast_select_fusion.45
  216.3 1.1 collective-permute-done
  217.9 1.3 fusion.357
  220.8 3.5 %all-to-all-start = ((f32[16,1,1028]{2,1,0:T(1,128)}), f32[16,1,1028]{2,1,0:T(1,128)S(1)}, u32[]{:S(2)}, u32[]{:S(2)}) async-start(f32[16,1,1028]{2,1,0:T(1,128)} %copy.191), calls=%async_computation | async-start | bytes 147456 | tf_op jit(solution)/shard_map/while/body/eval_jaxpr/all_to_all | solution.py:119
  224.9 6.9 %all-to-all-done = f32[16,1,1028]{2,1,0:T(1,128)S(1)} async-done(((f32[16,1,1028]{2,1,0:T(1,128)}), f32[16,1,1028]{2,1,0:T(1,128)S(1)}, u32[]{:S(2)}, u32[]{:S(2)}) %all-to-all-start) | async-done | bytes 65824 | tf_op jit(solution)/shard_map/while/body/eval_jaxpr/all_to_all | solution.py:119
  237.6 0.8 add_select_fusion.17
  (539 shorter events, 65.8 us)
Async XLA Ops:
  0.6 23.8 %copy-start = (f32[4,40]{1,0:T(4,128)S(1)}, f32[4,40]{1,0:T(4,128)}, u32[]{:S(2)}) copy-start(f32[4,40]{1,0:T(4,128)} %param.134) | copy-start | bytes 1924
  0.6 7.4 %copy-start.3 = (f32[340,256,1]{1,0,2:T(8,128)S(1)}, f32[340,256,1]{1,0,2:T(8,128)}, u32[]{:S(2)}) copy-start(f32[340,256,1]{1,0,2:T(8,128)} %constant.1719) | copy-start | bytes 1044484
  0.7 7.7 %copy-start.19 = (f32[13,16,1]{1,0,2:T(8,128)S(1)}, f32[13,16,1]{1,0,2:T(8,128)}, u32[]{:S(2)}) copy-start(f32[13,16,1]{1,0,2:T(8,128)} %constant.1720) | copy-start | bytes 2500
  0.7 9.1 %copy-start.17 = (s32[4,13,256]{2,0,1:T(4,128)S(1)}, s32[4,13,256]{2,0,1:T(4,128)}, u32[]{:S(2)}) copy-start(s32[4,13,256]{2,0,1:T(4,128)} %param.127) | copy-start | bytes 159748
  0.7 9.1 %copy-start.5 = (f32[40,4,13,256]{3,1,2,0:T(4,128)S(1)}, f32[40,4,13,256]{3,1,2,0:T(4,128)}, u32[]{:S(2)}) copy-start(f32[40,4,13,256]{3,1,2,0:T(4,128)} %param.126) | copy-start | bytes 6389764
  2.6 9.2 %copy-start.7 = (f32[64,340]{1,0:T(8,128)}, f32[64,340]{1,0:T(8,128)S(1)}, u32[]{:S(2)}) copy-start(f32[64,340]{1,0:T(8,128)S(1)} %mul.1078) | copy-start | bytes 261124
  9.2 23.3 %collective-permute-start.1 = (f32[13,256]{1,0:T(8,128)}, f32[13,256]{1,0:T(8,128)}, u32[]{:S(2)}, u32[]{:S(2)}) collective-permute-start(f32[13,256]{1,0:T(8,128)} %fusion.165), channel_id=1, source_target_pairs={{0,1},{1,0},{2,3},{3,2},{4,5},{5,4},{6,7},{7,6},{8,9},{9,8},{10,11... | collective-permute-start | bytes 39944 | tf_op jit(solution)/shard_map/ppermute | solution.py:91
  9.7 14.7 %copy-start.11 = (f32[13312]{0:T(1024)}, f32[13312]{0:T(1024)S(1)}, u32[]{:S(2)}) copy-start(f32[13312]{0:T(1024)S(1)} %sub.236) | copy-start | bytes 159748
  11.8 2.0 copy-start.33
  13.8 2.7 %copy-start.25 = (f32[3,40]{1,0:T(4,128)S(1)}, f32[3,40]{1,0:T(4,128)}, u32[]{:S(2)}) copy-start(f32[3,40]{1,0:T(4,128)} %param.130) | copy-start | bytes 1444
  16.4 2.4 copy-start.26
  16.5 4.7 %copy-start.27 = (f32[3,40]{1,0:T(4,128)S(1)}, f32[3,40]{1,0:T(4,128)}, u32[]{:S(2)}) copy-start(f32[3,40]{1,0:T(4,128)} %param.132) | copy-start | bytes 1444
  18.8 4.7 %copy-start.18 = (s32[4,13,256]{2,0,1:T(4,128)S(1)}, s32[4,13,256]{2,0,1:T(4,128)}, u32[]{:S(2)}) copy-start(s32[4,13,256]{2,0,1:T(4,128)} %param.128) | copy-start | bytes 159748
  18.8 5.6 %copy-start.31 = (f32[40]{0:T(128)S(1)}, f32[40]{0:T(128)}, u32[]{:S(2)}) copy-start(f32[40]{0:T(128)} %param.133) | copy-start | bytes 484
  23.6 11.6 %copy-start.23 = (pred[16]{0:T(512)(128)(4,1)}, pred[16]{0:T(512)(128)(4,1)S(1)}, u32[]{:S(2)}) copy-start(pred[16]{0:T(512)(128)(4,1)S(1)} %get-tuple-element.1135) | copy-start | bytes 52
  31.9 28.2 %copy-start.12 = (f32[4,13,256]{2,0,1:T(4,128)S(1)}, f32[4,13,256]{2,0,1:T(4,128)}, u32[]{:S(2)}) copy-start(f32[4,13,256]{2,0,1:T(4,128)} %param.125) | copy-start | bytes 159748
  31.9 28.3 %copy-start.6 = (f32[16,13,1]{1,0,2:T(8,128)S(1)}, f32[16,13,1]{1,0,2:T(8,128)}, u32[]{:S(2)}) copy-start(f32[16,13,1]{1,0,2:T(8,128)} %constant.1717) | copy-start | bytes 2500
  31.9 28.5 %copy-start.8 = (f32[16,13,1]{1,0,2:T(8,128)S(1)}, f32[16,13,1]{1,0,2:T(8,128)}, u32[]{:S(2)}) copy-start(f32[16,13,1]{1,0,2:T(8,128)} %constant.1718) | copy-start | bytes 2500
  31.9 28.8 %copy-start.2 = (f32[256,340]{1,0:T(8,128)S(1)}, f32[256,340]{1,0:T(8,128)}, u32[]{:S(2)}) copy-start(f32[256,340]{1,0:T(8,128)} %constant.1637.clone) | copy-start | bytes 1044484
  31.9 29.3 %copy-start.1 = (f32[256,340]{1,0:T(8,128)S(1)}, f32[256,340]{1,0:T(8,128)}, u32[]{:S(2)}) copy-start(f32[256,340]{1,0:T(8,128)} %constant.1636.clone) | copy-start | bytes 1044484
  36.2 28.8 %copy-start.15 = (f32[1,4,85]{2,1,0:T(4,128)S(1)}, f32[1,4,85]{2,1,0:T(4,128)}, u32[]{:S(2)}) copy-start(f32[1,4,85]{2,1,0:T(4,128)} %param.136) | copy-start | bytes 4084
  36.8 15.4 %all-to-all-start.1 = ((f32[16,1,1024]{2,1,0:T(1,128)}), f32[16,1,1024]{2,1,0:T(1,128)S(1)}, u32[]{:S(2)}, u32[]{:S(2)}) async-start(f32[16,1,1024]{2,1,0:T(1,128)} %copy.138), calls=%async_computation.1 | async-start | bytes 131072 | tf_op jit(solution)/shard_map/all_to_all | solution.py:119
  60.0 4.3 %copy-start.32 = (s32[16]{0:T(128)S(1)}, s32[16]{0:T(128)}, u32[]{:S(2)}) copy-start(s32[16]{0:T(128)} %fusion.225) | copy-start | bytes 196
  64.3 3.7 %collective-permute-start.2 = (f32[13,256]{1,0:T(8,128)}, f32[13,256]{1,0:T(8,128)}, u32[]{:S(2)}, u32[]{:S(2)}) collective-permute-start(f32[13,256]{1,0:T(8,128)} %fusion.161), channel_id=1, source_target_pairs={{0,1},{1,0},{2,3},{3,2},{4,5},{5,4},{6,7},{7,6},{8,9},{9,8},{10,11... | collective-permute-start | bytes 39944 | tf_op jit(solution)/shard_map/ppermute | solution.py:91
  77.2 11.8 %all-to-all-start.2 = ((f32[16,1,1024]{2,1,0:T(1,128)}), f32[16,1,1024]{2,1,0:T(1,128)}, u32[]{:S(2)}, u32[]{:S(2)}) async-start(f32[16,1,1024]{2,1,0:T(1,128)} %copy.152), calls=%async_computation.2 | async-start | bytes 131072 | tf_op jit(solution)/shard_map/all_to_all | solution.py:119
  81.3 13.8 %copy-start.24 = (pred[16]{0:T(512)(128)(4,1)S(1)}, pred[16]{0:T(512)(128)(4,1)}, u32[]{:S(2)}) copy-start(pred[16]{0:T(512)(128)(4,1)} %copy-done.23) | copy-start | bytes 52
  86.8 22.1 %copy-start.22 = (s32[13,256]{1,0:T(8,128)S(1)}, s32[13,256]{1,0:T(8,128)}, u32[]{:S(2)}) copy-start(s32[13,256]{1,0:T(8,128)} %param.137) | copy-start | bytes 39940
  92.9 0.6 copy-start.9
  94.3 17.5 %copy-start.20 = (f32[13,16,1]{1,0,2:T(8,128)S(1)}, f32[13,16,1]{1,0,2:T(8,128)}, u32[]{:S(2)}) copy-start(f32[13,16,1]{1,0,2:T(8,128)} %constant.1720) | copy-start | bytes 2500
  95.9 12.1 %all-to-all-start.3 = ((f32[16,1,768]{2,1,0:T(1,128)}), f32[16,1,768]{2,1,0:T(1,128)S(1)}, u32[]{:S(2)}, u32[]{:S(2)}) async-start(f32[16,1,768]{2,1,0:T(1,128)} %copy.161), calls=%async_computation.3 | async-start | bytes 98304 | tf_op jit(solution)/shard_map/all_to_all | solution.py:119
  108.6 3.2 %copy-start.29 = (f32[256]{0:T(256)S(1)}, f32[256]{0:T(256)}, u32[]{:S(2)}) copy-start(f32[256]{0:T(256)} %or_select_fusion) | copy-start | bytes 3076
  109.1 2.7 %copy-start.13 = (f32[13,256]{1,0:T(8,128)}, f32[13,256]{1,0:T(8,128)S(1)}, u32[]{:S(2)}) copy-start(f32[13,256]{1,0:T(8,128)S(1)} %get-tuple-element.1132) | copy-start | bytes 39940
  109.6 15.7 %copy-start.4 = (f32[40,13312]{1,0:T(8,128)S(1)}, f32[40,13312]{1,0:T(8,128)}, u32[]{:S(2)}) copy-start(f32[40,13312]{1,0:T(8,128)} %get-tuple-element.1134) | copy-start | bytes 6389764
  116.1 1.2 collective-permute-start.3
  121.8 11.3 %all-to-all-start.4 = ((f32[16,1,1026]{2,1,0:T(1,128)}), f32[16,1,1026]{2,1,0:T(1,128)S(1)}, u32[]{:S(2)}, u32[]{:S(2)}) async-start(f32[16,1,1026]{2,1,0:T(1,128)} %copy.162), calls=%async_computation.4 | async-start | bytes 147456 | tf_op jit(solution)/shard_map/all_to_all | solution.py:119
  127.4 5.0 %copy-start.10 = (f32[4,13,256]{2,1,0:T(8,128)S(1)}, f32[4,13,256]{2,1,0:T(8,128)}, u32[]{:S(2)}) copy-start(f32[4,13,256]{2,1,0:T(8,128)} %copy-done.9) | copy-start | bytes 159748
  127.4 10.9 %copy-start.14 = (f32[13,256]{1,0:T(8,128)S(1)}, f32[13,256]{1,0:T(8,128)}, u32[]{:S(2)}) copy-start(f32[13,256]{1,0:T(8,128)} %copy-done.13) | copy-start | bytes 39940
  127.4 11.0 %copy-start.16 = (f32[1,4,85]{2,1,0:T(4,128)S(1)}, f32[1,4,85]{2,1,0:T(4,128)}, u32[]{:S(2)}) copy-start(f32[1,4,85]{2,1,0:T(4,128)} %param.136) | copy-start | bytes 4084
  127.4 11.1 %copy-start.21 = (f32[13,16,1]{1,0,2:T(8,128)S(1)}, f32[13,16,1]{1,0,2:T(8,128)}, u32[]{:S(2)}) copy-start(f32[13,16,1]{1,0,2:T(8,128)} %constant.1720) | copy-start | bytes 2500
  127.4 11.1 %copy-start.28 = (f32[4,13]{1,0:T(4,128)S(1)}, f32[4,13]{1,0:T(4,128)}, u32[]{:S(2)}) copy-start(f32[4,13]{1,0:T(4,128)} %broadcast_multiply_fusion) | copy-start | bytes 628
  127.4 11.1 %copy-start.30 = (f32[256]{0:T(256)S(1)}, f32[256]{0:T(256)}, u32[]{:S(2)}) copy-start(f32[256]{0:T(256)} %or_select_fusion) | copy-start | bytes 3076
  146.4 1.2 collective-permute-start
  151.0 14.4 %all-to-all-start = ((f32[16,1,1028]{2,1,0:T(1,128)}), f32[16,1,1028]{2,1,0:T(1,128)S(1)}, u32[]{:S(2)}, u32[]{:S(2)}) async-start(f32[16,1,1028]{2,1,0:T(1,128)} %copy.191), calls=%async_computation | async-start | bytes 147456 | tf_op jit(solution)/shard_map/while/body/eval_jaxpr/all_to_all | solution.py:119
  183.0 1.2 collective-permute-start
  187.6 11.0 %all-to-all-start = ((f32[16,1,1028]{2,1,0:T(1,128)}), f32[16,1,1028]{2,1,0:T(1,128)S(1)}, u32[]{:S(2)}, u32[]{:S(2)}) async-start(f32[16,1,1028]{2,1,0:T(1,128)} %copy.191), calls=%async_computation | async-start | bytes 147456 | tf_op jit(solution)/shard_map/while/body/eval_jaxpr/all_to_all | solution.py:119
  216.1 1.2 collective-permute-start
  220.8 11.0 %all-to-all-start = ((f32[16,1,1028]{2,1,0:T(1,128)}), f32[16,1,1028]{2,1,0:T(1,128)S(1)}, u32[]{:S(2)}, u32[]{:S(2)}) async-start(f32[16,1,1028]{2,1,0:T(1,128)} %copy.191), calls=%async_computation | async-start | bytes 147456 | tf_op jit(solution)/shard_map/while/body/eval_jaxpr/all_to_all | solution.py:119

commit v3 on v2

--- a/solution.py
+++ b/solution.py
@@ -40,10 +40,15 @@
 
 def gather_matrix(length, line):
     elements = (length - 1) // 3
-    out = np.zeros((length, 4, elements))
-    for e in range(elements):
-        for a in range(4):
-            out[3 * e : 3 * e + 4, a, e] = line[a, :]
+    shape = (length, 4, elements)
+    node = lax.broadcasted_iota(jnp.int32, shape, 0)
+    offset = lax.broadcasted_iota(jnp.int32, shape, 1)
+    local = node - 3 * lax.broadcasted_iota(jnp.int32, shape, 2)
+    out = jnp.zeros(shape, jnp.float32)
+    for a in range(4):
+        for j in range(4):
+            if line[a, j] != 0.0:
+                out = jnp.where((offset == a) & (local == j), jnp.float32(line[a, j]), out)
     return out.reshape(length, 4 * elements)
 
 
@@ -55,24 +60,24 @@
     rows = [values[j] for j in range(depth)]
     v_mass = jnp.stack([sum(mass_d[i][j] * rows[j] for j in range(4)) for i in range(4)])
     v_stiff = jnp.stack([sum(stiff_d[i][j] * rows[j] for j in range(4)) for i in range(4)])
-    pick_mass = jnp.asarray(gather_matrix(first, MASS_LINE).T, jnp.float32)
-    pick_stiff = jnp.asarray(gather_matrix(first, STIFF_LINE).T, jnp.float32)
+    pick_mass = gather_matrix(first, MASS_LINE).T
+    pick_stiff = gather_matrix(first, STIFF_LINE).T
     along_first_m = jnp.einsum("kx,dxy->dky", pick_mass, v_mass, precision=HIGH)
     along_first_k = jnp.einsum("kx,dxy->dky", pick_stiff, v_mass, precision=HIGH) + jnp.einsum(
         "kx,dxy->dky", pick_mass, v_stiff, precision=HIGH
     )
-    lanes_m = jnp.asarray(gather_matrix(second, MASS_LINE), jnp.float32)
-    lanes_k = jnp.asarray(gather_matrix(second, STIFF_LINE), jnp.float32)
+    lanes_m = gather_matrix(second, MASS_LINE)
+    lanes_k = gather_matrix(second, STIFF_LINE)
     flat_m = along_first_m.reshape(-1, second)
     flat_k = along_first_k.reshape(-1, second)
     element = jnp.dot(flat_m, lanes_k, precision=HIGH) + jnp.dot(flat_k, lanes_m, precision=HIGH)
     element = element.reshape(depth, 4, first_el, 4, second_el) * conduct.reshape(
         1, 1, first_el, 1, second_el
     )
-    scatter_second = jnp.asarray(gather_matrix(second, np.eye(4)).T, jnp.float32)
+    scatter_second = gather_matrix(second, np.eye(4)).T
     spread = jnp.dot(element.reshape(-1, 4 * second_el), scatter_second, precision=HIGH)
     spread = spread.reshape(depth, 4 * first_el, second)
-    scatter_first = jnp.asarray(gather_matrix(first, np.eye(4)), jnp.float32)
+    scatter_first = gather_matrix(first, np.eye(4))
     return jnp.einsum("xk,dky->dxy", scatter_first, spread, precision=HIGH)
 
 
@@ -196,10 +201,10 @@
 
 
 def node_table(matrix, labels, kind_count):
-    onehot = (
-        labels.reshape(1, -1) == jnp.arange(kind_count, dtype=jnp.int32).reshape(-1, 1)
-    ).astype(jnp.float32)
-    return jnp.dot(matrix.T, onehot, precision=HIGH)
+    out = matrix[kind_count - 1][:, None]
+    for kind in range(kind_count - 2, -1, -1):
+        out = jnp.where(labels == kind, matrix[kind][:, None], out)
+    return out
 
 
 def ext_index(target, anchor, length_local, rim_width):
@@ -238,12 +243,13 @@
     heart_mass = factor_grid(heart_depth, first_mass, second_mass)
     torso_mass = factor_grid(torso_depth, first_mass, second_mass)
     torso_weight = factor_grid(torso_depth_weight, first_weight, second_weight)
-    type_flat = cell_type.reshape(-1)
+    type_flat = cell_type.reshape(1, -1)
+    class_flat = drug_class.reshape(1, -1)
     half_nodes = node_table(half_point, type_flat, TYPES)
     slope_nodes = node_table(gate_slope, type_flat, TYPES)
-    decay_nodes = jnp.exp(-time_step / node_table(time_const, type_flat, TYPES))
+    decay_nodes = node_table(jnp.exp(-time_step / time_const), type_flat, TYPES)
     cond_nodes = node_table(max_conduct, type_flat, TYPES) * node_table(
-        drug_block, drug_class.reshape(-1), CLASSES
+        drug_block, class_flat, CLASSES
     )
     gate_flat = gating.reshape(gating.shape[0], -1)
     for repeat in range(STEPS):

time: 244 us -> 220 us (0.902)
  matrix products: 38 us -> 18.6 us
  local copies, waits for them, and re-layouts: 52.3 us -> 34.8 us
  other arithmetic: 49.7 us -> 57.1 us
  waiting for transfers between devices: 39.6 us -> 45.7 us
    dot_general x5 -> x0, matrix products: 17.2 us -> none  [node_table(): return jnp.dot(matrix.T, onehot, precision=HIGH)]
    reduce_sum x1 -> x2, other arithmetic: 5.43 us -> 15.8 us  [per_device(): current = jnp.sum(cond_nodes * gate_flat * (volts - reversal[:, None]), 0)]
    unnamed x82 -> x104, local copies, waits for them, and re-layouts: 10.1 us -> 2.39 us
    all_to_all x7, waiting for transfers between devices: 35.3 us -> 41.2 us  [plane_exchange(): got = lax.all_to_all(send, ('hx', 'hy'), 0, 0, tiled=True)]
    reshape x4 -> x0, local copies, waits for them, and re-layouts: 4.89 us -> none  [the longest x1 2.09 us: per_device(): new_gating = gate_flat.reshape(gating.shape)]
    select_n x0 -> x4, other arithmetic: none -> 3.59 us  [gather_matrix(): out = jnp.where((offset == a) & (local == j), jnp.float32(line[a, j]), out)]
    pad x18, local copies, waits for them, and re-layouts: 3.01 us -> 0.09 us  [plane_exchange(): jnp.pad(piece, (0, width - piece.shape[0]))]
    iota x0 -> x40, local copies, waits for them, and re-layouts: none -> 2.92 us  [the longest x32 2.58 us: gather_matrix(): offset = lax.broadcasted_iota(jnp.int32, shape, 1)]
  transfers between devices with their start and end apart: 13 -> 13, of which waited for: 10 -> 10; matrix products, arithmetic and copies ran while one was open for 17% -> 10% of each run, Pallas kernels for 0% -> 0%
where the time goes in v3:
time: 220 us; the launch traced here: 218 us
  other arithmetic  57.1 us (26%)
  waiting for transfers between devices  45.7 us (21%)
  local copies, waits for them, and re-layouts  34.8 us (16%)
  starting transfers between devices  33 us (15%)
  loops' own time  23.7 us (11%)
  matrix products  18.6 us (8%)
  between operations  4.96 us (2%)
    all_to_all x7, waiting for transfers between devices, plane_exchange(): got = lax.all_to_all(send, ('hx', 'hy'), 0, 0, tiled=True)  41.2 us
    all_to_all x7, starting transfers between devices, plane_exchange(): got = lax.all_to_all(send, ('hx', 'hy'), 0, 0, tiled=True)  32.2 us
    another operation x1, loops' own time, per_device(): solution = lax.fori_loop(1, ITERS, later_turn, state)[0]  23.7 us
    another operation x27, other arithmetic  21.9 us
    reduce_sum x2, other arithmetic, per_device(): current = jnp.sum(cond_nodes * gate_flat * (volts - reversal[:, None]), 0)  15.8 us
    gather x7, local copies, waits for them, and re-layouts, plane_exchange(): send = jnp.take(table, code_of, axis=0)  4.73 us
    add x4, other arithmetic, torso_stage(): scalars = scalars + got[rows, :scalars.shape[0]]  4.57 us
    ppermute x6, waiting for transfers between devices, torso_stage(): got = lax.ppermute(face, 'torso', [(0, 1), (1, 0)])  4.45 us
  transfers between devices with their start and end apart: 13, of which 10 were waited for; matrix products, arithmetic and copies ran while one was open for 10% of the time, Pallas kernels for 0%

profile of v3, /device:TPU:0, one launch (start us, length us, event | category | flops | bytes accessed | tf_op | source)
XLA Modules:
  0.0 217.8 jit_solution(13298688711616201008)
XLA Ops:
  0.7 0.8 copy.149
  2.9 0.7 mul.1184
  3.7 0.9 select_select_fusion.9
  9.0 7.7 %multiply_reduce_fusion.3 = (f32[4,13,256]{2,0,1:T(4,128)}, f32[40,4,13,256]{3,1,2,0:T(4,128)S(1)}) fusion(f32[40]{0:T(128)} %param.109, f32[4,13,256]{2,0,1:T(4,128)S(1)} %copy-done, f32[40]{0:T(128)S(1)} %get-tuple-element.1150, f32[40]{0:T(128)S(1)} %get-tuple-element.1149, f32[40]{0:T(128)S(1)} %get-tuple-element.1151, f32[40]{0:T(128)S(1)} %get-tuple-element.1152, ...), kind=kLoop, calls=%fused_computation.280 | loop fusion | flops 12766208 | bytes 4435616 | tf_op jit(solution)/shard_map/reduce_sum | solution.py:259
  17.5 0.7 fusion.325
  18.9 0.7 gather_fusion.3
  20.4 7.9 %all-to-all-start.1 = ((f32[16,1,1024]{2,1,0:T(1,128)}), f32[16,1,1024]{2,1,0:T(1,128)S(1)}, u32[]{:S(2)}, u32[]{:S(2)}) async-start(f32[16,1,1024]{2,1,0:T(1,128)} %copy.139), calls=%async_computation.1 | async-start | bytes 131072 | tf_op jit(solution)/shard_map/all_to_all | solution.py:124
  29.5 6.3 %all-to-all-done.1 = f32[16,1,1024]{2,1,0:T(1,128)S(1)} async-done(((f32[16,1,1024]{2,1,0:T(1,128)}), f32[16,1,1024]{2,1,0:T(1,128)S(1)}, u32[]{:S(2)}, u32[]{:S(2)}) %all-to-all-start.1) | async-done | bytes 65568 | tf_op jit(solution)/shard_map/all_to_all | solution.py:124
  38.7 0.9 fusion.222
  39.7 0.9 fusion.254
  40.6 0.9 fusion.253
  42.0 1.0 convolution_add_fusion.6
  43.8 0.9 fusion.329
  47.4 0.7 fusion.321
  48.7 0.7 stack.359
  49.5 0.7 gather_fusion.4
  50.2 0.7 select_bitcast_fusion
  51.6 3.5 %all-to-all-start.2 = ((f32[16,1,1024]{2,1,0:T(1,128)}), f32[16,1,1024]{2,1,0:T(1,128)S(1)}, u32[]{:S(2)}, u32[]{:S(2)}) async-start(f32[16,1,1024]{2,1,0:T(1,128)} %copy.153), calls=%async_computation.2 | async-start | bytes 131072 | tf_op jit(solution)/shard_map/all_to_all | solution.py:124
  55.1 8.1 %multiply_reduce_fusion.2 = (f32[4,13,256]{2,0,1:T(4,128)S(1)}, f32[40,4,13,256]{3,1,2,0:T(4,128)}) fusion(f32[4,13,256]{2,0,1:T(4,128)} %copy.162, f32[40]{0:T(128)} %param.109, f32[40]{0:T(128)} %copy-done.18, f32[40]{0:T(128)} %copy-done.17, f32[40]{0:T(128)} %copy-done.19, f32[40]{0:T(128)} %copy-done.20, f32[40]{0:T(128)} %copy-done.30, ...), kind=kLoop, calls=%fused_computation.278 | loop fusion | flops 12766208 | bytes 4435616 | tf_op jit(solution)/shard_map/reduce_sum | solution.py:259
  67.3 0.8 gather_fusion.1
  68.2 0.7 bitcast_select_fusion.2
  69.6 6.9 %all-to-all-start.3 = ((f32[16,1,768]{2,1,0:T(1,128)}), f32[16,1,768]{2,1,0:T(1,128)S(1)}, u32[]{:S(2)}, u32[]{:S(2)}) async-start(f32[16,1,768]{2,1,0:T(1,128)} %copy.164), calls=%async_computation.3 | async-start | bytes 98304 | tf_op jit(solution)/shard_map/all_to_all | solution.py:124
  76.5 7.5 %all-to-all-done.3 = f32[16,1,768]{2,1,0:T(1,128)S(1)} async-done(((f32[16,1,768]{2,1,0:T(1,128)}), f32[16,1,768]{2,1,0:T(1,128)S(1)}, u32[]{:S(2)}, u32[]{:S(2)}) %all-to-all-start.3) | async-done | bytes 49184 | tf_op jit(solution)/shard_map/all_to_all | solution.py:124
  87.2 0.9 fusion.226
  89.3 1.3 broadcast_select_fusion.17
  90.7 1.2 collective-permute-done.3
  92.4 0.7 fusion.431
  93.4 0.7 gather_fusion.2
  94.2 0.7 copy.168
  94.9 3.5 %all-to-all-start.4 = ((f32[16,1,1026]{2,1,0:T(1,128)}), f32[16,1,1026]{2,1,0:T(1,128)S(1)}, u32[]{:S(2)}, u32[]{:S(2)}) async-start(f32[16,1,1026]{2,1,0:T(1,128)} %copy.168), calls=%async_computation.4 | async-start | bytes 147456 | tf_op jit(solution)/shard_map/all_to_all | solution.py:124
  99.1 6.9 %all-to-all-done.4 = f32[16,1,1026]{2,1,0:T(1,128)S(1)} async-done(((f32[16,1,1026]{2,1,0:T(1,128)}), f32[16,1,1026]{2,1,0:T(1,128)S(1)}, u32[]{:S(2)}, u32[]{:S(2)}) %all-to-all-start.4) | async-done | bytes 65696 | tf_op jit(solution)/shard_map/all_to_all | solution.py:124
  111.0 106.1 %while.68 = (s32[]{:T(128)}, f32[4,13,256]{2,1,0:T(8,128)S(1)}, f32[4,13,256]{2,1,0:T(8,128)S(1)}, f32[4,13,256]{2,1,0:T(8,128)S(1)}, f32[4,13,256]{2,1,0:T(8,12...) while((s32[]{:T(128)}, f32[4,13,256]{2,1,0:T(8,128)S(1)}, ...), condition=%wide.region_19.21_spmd.clone.clone, body=%wide.region_9.20_spmd.clone.clone.sunk | while | flops 216595312 | bytes 7885822 | solution.py:331
  111.0 0.7 compare_reduce_fusion.6
  113.3 0.9 select_select_fusion.28
  115.9 0.8 fusion.640
  119.1 2.0 broadcast_select_fusion.45
  121.3 1.1 collective-permute-done
  122.9 1.3 fusion.642
  125.1 0.7 copy.222
  125.8 3.5 %all-to-all-start = ((f32[16,1,1028]{2,1,0:T(1,128)}), f32[16,1,1028]{2,1,0:T(1,128)S(1)}, u32[]{:S(2)}, u32[]{:S(2)}) async-start(f32[16,1,1028]{2,1,0:T(1,128)} %copy.222), calls=%async_computation | async-start | bytes 147456 | tf_op jit(solution)/shard_map/while/body/eval_jaxpr/all_to_all | solution.py:124
  130.0 6.9 %all-to-all-done = f32[16,1,1028]{2,1,0:T(1,128)S(1)} async-done(((f32[16,1,1028]{2,1,0:T(1,128)}), f32[16,1,1028]{2,1,0:T(1,128)S(1)}, u32[]{:S(2)}, u32[]{:S(2)}) %all-to-all-start) | async-done | bytes 65824 | tf_op jit(solution)/shard_map/while/body/eval_jaxpr/all_to_all | solution.py:124
  142.6 0.7 add_select_fusion.17
  144.6 0.7 add_select_fusion.19
  146.4 0.7 compare_reduce_fusion.6
  148.7 0.9 select_select_fusion.28
  151.2 0.8 fusion.640
  154.5 2.0 broadcast_select_fusion.45
  156.6 1.1 collective-permute-done
  158.3 1.3 fusion.642
  160.4 0.7 copy.222
  161.1 3.5 %all-to-all-start = ((f32[16,1,1028]{2,1,0:T(1,128)}), f32[16,1,1028]{2,1,0:T(1,128)S(1)}, u32[]{:S(2)}, u32[]{:S(2)}) async-start(f32[16,1,1028]{2,1,0:T(1,128)} %copy.222), calls=%async_computation | async-start | bytes 147456 | tf_op jit(solution)/shard_map/while/body/eval_jaxpr/all_to_all | solution.py:124
  165.3 6.9 %all-to-all-done = f32[16,1,1028]{2,1,0:T(1,128)S(1)} async-done(((f32[16,1,1028]{2,1,0:T(1,128)}), f32[16,1,1028]{2,1,0:T(1,128)S(1)}, u32[]{:S(2)}, u32[]{:S(2)}) %all-to-all-start) | async-done | bytes 65824 | tf_op jit(solution)/shard_map/while/body/eval_jaxpr/all_to_all | solution.py:124
  178.0 0.7 add_select_fusion.17
  180.0 0.7 add_select_fusion.19
  181.8 0.7 compare_reduce_fusion.6
  184.1 0.9 select_select_fusion.28
  186.6 0.8 fusion.640
  189.9 2.0 broadcast_select_fusion.45
  192.0 1.1 collective-permute-done
  193.6 1.3 fusion.642
  196.5 3.5 %all-to-all-start = ((f32[16,1,1028]{2,1,0:T(1,128)}), f32[16,1,1028]{2,1,0:T(1,128)S(1)}, u32[]{:S(2)}, u32[]{:S(2)}) async-start(f32[16,1,1028]{2,1,0:T(1,128)} %copy.222), calls=%async_computation | async-start | bytes 147456 | tf_op jit(solution)/shard_map/while/body/eval_jaxpr/all_to_all | solution.py:124
  200.7 6.9 %all-to-all-done = f32[16,1,1028]{2,1,0:T(1,128)S(1)} async-done(((f32[16,1,1028]{2,1,0:T(1,128)}), f32[16,1,1028]{2,1,0:T(1,128)S(1)}, u32[]{:S(2)}, u32[]{:S(2)}) %all-to-all-start) | async-done | bytes 65824 | tf_op jit(solution)/shard_map/while/body/eval_jaxpr/all_to_all | solution.py:124
  213.4 0.7 add_select_fusion.17
  215.3 0.7 add_select_fusion.19
  (629 shorter events, 55.5 us)
Async XLA Ops:
  1.7 4.7 %copy-start.21 = (s32[16]{0:T(128)}, s32[16]{0:T(128)S(1)}, u32[]{:S(2)}) copy-start(s32[16]{0:T(128)S(1)} %iota.1070) | copy-start | bytes 196
  1.8 4.6 %copy-start.32 = (pred[16]{0:T(512)(128)(4,1)}, pred[16]{0:T(512)(128)(4,1)S(1)}, u32[]{:S(2)}) copy-start(pred[16]{0:T(512)(128)(4,1)S(1)} %iota.1079) | copy-start | bytes 52
  2.0 4.4 %copy-start.34 = (pred[16]{0:T(512)(128)(4,1)}, pred[16]{0:T(512)(128)(4,1)S(1)}, u32[]{:S(2)}) copy-start(pred[16]{0:T(512)(128)(4,1)S(1)} %iota.1076) | copy-start | bytes 52
  2.1 4.3 %copy-start.36 = (pred[16]{0:T(512)(128)(4,1)}, pred[16]{0:T(512)(128)(4,1)S(1)}, u32[]{:S(2)}) copy-start(pred[16]{0:T(512)(128)(4,1)S(1)} %iota.1073) | copy-start | bytes 52
  2.3 4.1 %copy-start.38 = (pred[16]{0:T(512)(128)(4,1)}, pred[16]{0:T(512)(128)(4,1)S(1)}, u32[]{:S(2)}) copy-start(pred[16]{0:T(512)(128)(4,1)S(1)} %iota.1065) | copy-start | bytes 52
  4.6 3.1 %copy-start.44 = (f32[3,40]{1,0:T(4,128)S(1)}, f32[3,40]{1,0:T(4,128)}, u32[]{:S(2)}) copy-start(f32[3,40]{1,0:T(4,128)} %param.108) | copy-start | bytes 1444
  4.7 3.2 %copy-start.42 = (f32[3,40]{1,0:T(4,128)S(1)}, f32[3,40]{1,0:T(4,128)}, u32[]{:S(2)}) copy-start(f32[3,40]{1,0:T(4,128)} %param.107) | copy-start | bytes 1444
  4.7 3.2 %copy-start.40 = (f32[4,40]{1,0:T(4,128)S(1)}, f32[4,40]{1,0:T(4,128)}, u32[]{:S(2)}) copy-start(f32[4,40]{1,0:T(4,128)} %param.110) | copy-start | bytes 1924
  4.7 3.2 %copy-start.43 = (f32[3,40]{1,0:T(4,128)S(1)}, f32[3,40]{1,0:T(4,128)}, u32[]{:S(2)}) copy-start(f32[3,40]{1,0:T(4,128)} %param.105) | copy-start | bytes 1444
  4.7 3.2 %copy-start.8 = (s32[4,13,256]{2,0,1:T(4,128)S(1)}, s32[4,13,256]{2,0,1:T(4,128)}, u32[]{:S(2)}) copy-start(s32[4,13,256]{2,0,1:T(4,128)} %param.104) | copy-start | bytes 159748
  4.7 3.2 %copy-start.9 = (s32[4,13,256]{2,0,1:T(4,128)S(1)}, s32[4,13,256]{2,0,1:T(4,128)}, u32[]{:S(2)}) copy-start(s32[4,13,256]{2,0,1:T(4,128)} %param.103) | copy-start | bytes 159748
  4.7 3.4 %copy-start.45 = (f32[3,40]{1,0:T(4,128)S(1)}, f32[3,40]{1,0:T(4,128)}, u32[]{:S(2)}) copy-start(f32[3,40]{1,0:T(4,128)} %param.106) | copy-start | bytes 1444
  4.7 4.2 %copy-start = (f32[4,13,256]{2,0,1:T(4,128)S(1)}, f32[4,13,256]{2,0,1:T(4,128)}, u32[]{:S(2)}) copy-start(f32[4,13,256]{2,0,1:T(4,128)} %param.101) | copy-start | bytes 159748
  7.3 10.2 %collective-permute-start.1 = (f32[13,256]{1,0:T(8,128)}, f32[13,256]{1,0:T(8,128)}, u32[]{:S(2)}, u32[]{:S(2)}) collective-permute-start(f32[13,256]{1,0:T(8,128)} %fusion.323), channel_id=1, source_target_pairs={{0,1},{1,0},{2,3},{3,2},{4,5},{5,4},{6,7},{7,6},{8,9},{9,8},{10,11... | collective-permute-start | bytes 39944 | tf_op jit(solution)/shard_map/ppermute | solution.py:96
  7.8 11.8 %copy-start.12 = (pred[16]{0:T(512)(128)(4,1)}, pred[16]{0:T(512)(128)(4,1)S(1)}, u32[]{:S(2)}) copy-start(pred[16]{0:T(512)(128)(4,1)S(1)} %get-tuple-element.980) | copy-start | bytes 52
  7.8 8.9 %copy-start.29 = (f32[40]{0:T(128)}, f32[40]{0:T(128)S(1)}, u32[]{:S(2)}) copy-start(f32[40]{0:T(128)S(1)} %get-tuple-element.1117) | copy-start | bytes 484
  7.8 8.9 %copy-start.30 = (f32[40]{0:T(128)}, f32[40]{0:T(128)S(1)}, u32[]{:S(2)}) copy-start(f32[40]{0:T(128)S(1)} %get-tuple-element.1118) | copy-start | bytes 484
  7.8 8.9 %copy-start.31 = (f32[40]{0:T(128)}, f32[40]{0:T(128)S(1)}, u32[]{:S(2)}) copy-start(f32[40]{0:T(128)S(1)} %get-tuple-element.1119) | copy-start | bytes 484
  7.9 8.8 %copy-start.14 = (f32[40]{0:T(128)}, f32[40]{0:T(128)S(1)}, u32[]{:S(2)}) copy-start(f32[40]{0:T(128)S(1)} %get-tuple-element.1108) | copy-start | bytes 484
  7.9 8.8 %copy-start.15 = (f32[40]{0:T(128)}, f32[40]{0:T(128)S(1)}, u32[]{:S(2)}) copy-start(f32[40]{0:T(128)S(1)} %get-tuple-element.1109) | copy-start | bytes 484
  8.0 8.8 %copy-start.16 = (f32[40]{0:T(128)}, f32[40]{0:T(128)S(1)}, u32[]{:S(2)}) copy-start(f32[40]{0:T(128)S(1)} %get-tuple-element.1110) | copy-start | bytes 484
  8.0 8.8 %copy-start.17 = (f32[40]{0:T(128)}, f32[40]{0:T(128)S(1)}, u32[]{:S(2)}) copy-start(f32[40]{0:T(128)S(1)} %get-tuple-element.1149) | copy-start | bytes 484
  8.0 8.8 %copy-start.18 = (f32[40]{0:T(128)}, f32[40]{0:T(128)S(1)}, u32[]{:S(2)}) copy-start(f32[40]{0:T(128)S(1)} %get-tuple-element.1150) | copy-start | bytes 484
  8.0 8.8 %copy-start.19 = (f32[40]{0:T(128)}, f32[40]{0:T(128)S(1)}, u32[]{:S(2)}) copy-start(f32[40]{0:T(128)S(1)} %get-tuple-element.1151) | copy-start | bytes 484
  8.0 8.8 %copy-start.20 = (f32[40]{0:T(128)}, f32[40]{0:T(128)S(1)}, u32[]{:S(2)}) copy-start(f32[40]{0:T(128)S(1)} %get-tuple-element.1152) | copy-start | bytes 484
  8.1 8.7 %copy-start.2 = (pred[4,13,256]{2,0,1:T(4,128)(4,1)}, pred[4,13,256]{2,0,1:T(4,128)(4,1)S(1)}, u32[]{:S(2)}) copy-start(pred[4,13,256]{2,0,1:T(4,128)(4,1)S(1)} %get-tuple-element.1076) | copy-start | bytes 39940
  8.1 8.7 %copy-start.3 = (pred[4,13,256]{2,0,1:T(4,128)(4,1)}, pred[4,13,256]{2,0,1:T(4,128)(4,1)S(1)}, u32[]{:S(2)}) copy-start(pred[4,13,256]{2,0,1:T(4,128)(4,1)S(1)} %get-tuple-element.1077) | copy-start | bytes 39940
  8.1 8.7 %copy-start.4 = (pred[4,13,256]{2,0,1:T(4,128)(4,1)}, pred[4,13,256]{2,0,1:T(4,128)(4,1)S(1)}, u32[]{:S(2)}) copy-start(pred[4,13,256]{2,0,1:T(4,128)(4,1)S(1)} %get-tuple-element.1144) | copy-start | bytes 39940
  8.1 8.7 %copy-start.5 = (pred[4,13,256]{2,0,1:T(4,128)(4,1)}, pred[4,13,256]{2,0,1:T(4,128)(4,1)S(1)}, u32[]{:S(2)}) copy-start(pred[4,13,256]{2,0,1:T(4,128)(4,1)S(1)} %get-tuple-element.1145) | copy-start | bytes 39940
  8.1 10.7 %copy-start.1 = (pred[4,13,256]{2,0,1:T(4,128)(4,1)}, pred[4,13,256]{2,0,1:T(4,128)(4,1)S(1)}, u32[]{:S(2)}) copy-start(pred[4,13,256]{2,0,1:T(4,128)(4,1)S(1)} %get-tuple-element.1075) | copy-start | bytes 39940
  8.2 8.6 %copy-start.23 = (f32[40]{0:T(128)}, f32[40]{0:T(128)S(1)}, u32[]{:S(2)}) copy-start(f32[40]{0:T(128)S(1)} %get-tuple-element.1114) | copy-start | bytes 484
  8.2 8.6 %copy-start.24 = (f32[40]{0:T(128)}, f32[40]{0:T(128)S(1)}, u32[]{:S(2)}) copy-start(f32[40]{0:T(128)S(1)} %get-tuple-element.1115) | copy-start | bytes 484
  8.2 8.6 %copy-start.25 = (f32[40]{0:T(128)}, f32[40]{0:T(128)S(1)}, u32[]{:S(2)}) copy-start(f32[40]{0:T(128)S(1)} %get-tuple-element.1116) | copy-start | bytes 484
  8.2 8.6 %copy-start.26 = (f32[40]{0:T(128)}, f32[40]{0:T(128)S(1)}, u32[]{:S(2)}) copy-start(f32[40]{0:T(128)S(1)} %get-tuple-element.1146) | copy-start | bytes 484
  8.2 8.6 %copy-start.27 = (f32[40]{0:T(128)}, f32[40]{0:T(128)S(1)}, u32[]{:S(2)}) copy-start(f32[40]{0:T(128)S(1)} %get-tuple-element.1147) | copy-start | bytes 484
  8.2 8.6 %copy-start.28 = (f32[40]{0:T(128)}, f32[40]{0:T(128)S(1)}, u32[]{:S(2)}) copy-start(f32[40]{0:T(128)S(1)} %get-tuple-element.1148) | copy-start | bytes 484
  18.8 0.8 copy-start.10
  19.6 26.3 %copy-start.6 = (f32[1,4,85]{2,1,0:T(4,128)S(1)}, f32[1,4,85]{2,1,0:T(4,128)}, u32[]{:S(2)}) copy-start(f32[1,4,85]{2,1,0:T(4,128)} %param.112) | copy-start | bytes 4084
  20.4 15.4 %all-to-all-start.1 = ((f32[16,1,1024]{2,1,0:T(1,128)}), f32[16,1,1024]{2,1,0:T(1,128)S(1)}, u32[]{:S(2)}, u32[]{:S(2)}) async-start(f32[16,1,1024]{2,1,0:T(1,128)} %copy.139), calls=%async_computation.1 | async-start | bytes 131072 | tf_op jit(solution)/shard_map/all_to_all | solution.py:124
  38.3 7.0 %copy-start.46 = (s32[16]{0:T(128)S(1)}, s32[16]{0:T(128)}, u32[]{:S(2)}) copy-start(s32[16]{0:T(128)} %fusion.430) | copy-start | bytes 196
  45.3 2.1 collective-permute-start.2
  51.6 11.6 %all-to-all-start.2 = ((f32[16,1,1024]{2,1,0:T(1,128)}), f32[16,1,1024]{2,1,0:T(1,128)S(1)}, u32[]{:S(2)}, u32[]{:S(2)}) async-start(f32[16,1,1024]{2,1,0:T(1,128)} %copy.153), calls=%async_computation.2 | async-start | bytes 131072 | tf_op jit(solution)/shard_map/all_to_all | solution.py:124
  63.2 21.6 %copy-start.11 = (s32[13,256]{1,0:T(8,128)S(1)}, s32[13,256]{1,0:T(8,128)}, u32[]{:S(2)}) copy-start(s32[13,256]{1,0:T(8,128)} %param.113) | copy-start | bytes 39940
  63.2 21.9 %copy-start.22 = (s32[16]{0:T(128)S(1)}, s32[16]{0:T(128)}, u32[]{:S(2)}) copy-start(s32[16]{0:T(128)} %copy-done.21) | copy-start | bytes 196
  63.2 21.9 %copy-start.33 = (pred[16]{0:T(512)(128)(4,1)S(1)}, pred[16]{0:T(512)(128)(4,1)}, u32[]{:S(2)}) copy-start(pred[16]{0:T(512)(128)(4,1)} %copy-done.32) | copy-start | bytes 52
  63.2 21.9 %copy-start.35 = (pred[16]{0:T(512)(128)(4,1)S(1)}, pred[16]{0:T(512)(128)(4,1)}, u32[]{:S(2)}) copy-start(pred[16]{0:T(512)(128)(4,1)} %copy-done.34) | copy-start | bytes 52
  63.2 21.9 %copy-start.37 = (pred[16]{0:T(512)(128)(4,1)S(1)}, pred[16]{0:T(512)(128)(4,1)}, u32[]{:S(2)}) copy-start(pred[16]{0:T(512)(128)(4,1)} %copy-done.36) | copy-start | bytes 52
  63.2 21.9 %copy-start.39 = (pred[16]{0:T(512)(128)(4,1)S(1)}, pred[16]{0:T(512)(128)(4,1)}, u32[]{:S(2)}) copy-start(pred[16]{0:T(512)(128)(4,1)} %copy-done.38) | copy-start | bytes 52
  67.3 19.8 %copy-start.41 = (f32[4,13]{1,0:T(4,128)S(1)}, f32[4,13]{1,0:T(4,128)}, u32[]{:S(2)}) copy-start(f32[4,13]{1,0:T(4,128)} %broadcast_multiply_fusion) | copy-start | bytes 628
  69.6 14.3 %all-to-all-start.3 = ((f32[16,1,768]{2,1,0:T(1,128)}), f32[16,1,768]{2,1,0:T(1,128)S(1)}, u32[]{:S(2)}, u32[]{:S(2)}) async-start(f32[16,1,768]{2,1,0:T(1,128)} %copy.164), calls=%async_computation.3 | async-start | bytes 98304 | tf_op jit(solution)/shard_map/all_to_all | solution.py:124
  85.0 9.1 %copy-start.13 = (pred[16]{0:T(512)(128)(4,1)S(1)}, pred[16]{0:T(512)(128)(4,1)}, u32[]{:S(2)}) copy-start(pred[16]{0:T(512)(128)(4,1)} %copy-done.12) | copy-start | bytes 52
  86.8 24.2 %copy-start.7 = (f32[1,4,85]{2,1,0:T(4,128)S(1)}, f32[1,4,85]{2,1,0:T(4,128)}, u32[]{:S(2)}) copy-start(f32[1,4,85]{2,1,0:T(4,128)} %param.112) | copy-start | bytes 4084
  90.7 1.2 collective-permute-start.3
  94.9 11.0 %all-to-all-start.4 = ((f32[16,1,1026]{2,1,0:T(1,128)}), f32[16,1,1026]{2,1,0:T(1,128)S(1)}, u32[]{:S(2)}, u32[]{:S(2)}) async-start(f32[16,1,1026]{2,1,0:T(1,128)} %copy.168), calls=%async_computation.4 | async-start | bytes 147456 | tf_op jit(solution)/shard_map/all_to_all | solution.py:124
  121.1 1.2 collective-permute-start
  125.8 11.0 %all-to-all-start = ((f32[16,1,1028]{2,1,0:T(1,128)}), f32[16,1,1028]{2,1,0:T(1,128)S(1)}, u32[]{:S(2)}, u32[]{:S(2)}) async-start(f32[16,1,1028]{2,1,0:T(1,128)} %copy.222), calls=%async_computation | async-start | bytes 147456 | tf_op jit(solution)/shard_map/while/body/eval_jaxpr/all_to_all | solution.py:124
  156.5 1.2 collective-permute-start
  161.1 11.0 %all-to-all-start = ((f32[16,1,1028]{2,1,0:T(1,128)}), f32[16,1,1028]{2,1,0:T(1,128)S(1)}, u32[]{:S(2)}, u32[]{:S(2)}) async-start(f32[16,1,1028]{2,1,0:T(1,128)} %copy.222), calls=%async_computation | async-start | bytes 147456 | tf_op jit(solution)/shard_map/while/body/eval_jaxpr/all_to_all | solution.py:124
  191.8 1.2 collective-permute-start
  196.5 11.0 %all-to-all-start = ((f32[16,1,1028]{2,1,0:T(1,128)}), f32[16,1,1028]{2,1,0:T(1,128)S(1)}, u32[]{:S(2)}, u32[]{:S(2)}) async-start(f32[16,1,1028]{2,1,0:T(1,128)} %copy.222), calls=%async_computation | async-start | bytes 147456 | tf_op jit(solution)/shard_map/while/body/eval_jaxpr/all_to_all | solution.py:124

commit v4 on v3

--- a/solution.py
+++ b/solution.py
@@ -52,7 +52,18 @@
     return out.reshape(length, 4 * elements)
 
 
-def local_products(values, conduct):
+def element_matrices(first, second):
+    return dict(
+        pick_mass=gather_matrix(first, MASS_LINE).T,
+        pick_stiff=gather_matrix(first, STIFF_LINE).T,
+        lanes_m=gather_matrix(second, MASS_LINE),
+        lanes_k=gather_matrix(second, STIFF_LINE),
+        scatter_second=gather_matrix(second, np.eye(4)).T,
+        scatter_first=gather_matrix(first, np.eye(4)),
+    )
+
+
+def local_products(values, conduct, mats):
     depth, first, second = values.shape
     first_el, second_el = conduct.shape[1], conduct.shape[2]
     mass_d = [[float(MASS_LINE[i, j]) for j in range(4)] for i in range(4)]
@@ -60,24 +71,24 @@
     rows = [values[j] for j in range(depth)]
     v_mass = jnp.stack([sum(mass_d[i][j] * rows[j] for j in range(4)) for i in range(4)])
     v_stiff = jnp.stack([sum(stiff_d[i][j] * rows[j] for j in range(4)) for i in range(4)])
-    pick_mass = gather_matrix(first, MASS_LINE).T
-    pick_stiff = gather_matrix(first, STIFF_LINE).T
+    pick_mass = mats["pick_mass"]
+    pick_stiff = mats["pick_stiff"]
     along_first_m = jnp.einsum("kx,dxy->dky", pick_mass, v_mass, precision=HIGH)
     along_first_k = jnp.einsum("kx,dxy->dky", pick_stiff, v_mass, precision=HIGH) + jnp.einsum(
         "kx,dxy->dky", pick_mass, v_stiff, precision=HIGH
     )
-    lanes_m = gather_matrix(second, MASS_LINE)
-    lanes_k = gather_matrix(second, STIFF_LINE)
+    lanes_m = mats["lanes_m"]
+    lanes_k = mats["lanes_k"]
     flat_m = along_first_m.reshape(-1, second)
     flat_k = along_first_k.reshape(-1, second)
     element = jnp.dot(flat_m, lanes_k, precision=HIGH) + jnp.dot(flat_k, lanes_m, precision=HIGH)
     element = element.reshape(depth, 4, first_el, 4, second_el) * conduct.reshape(
         1, 1, first_el, 1, second_el
     )
-    scatter_second = gather_matrix(second, np.eye(4)).T
+    scatter_second = mats["scatter_second"]
     spread = jnp.dot(element.reshape(-1, 4 * second_el), scatter_second, precision=HIGH)
     spread = spread.reshape(depth, 4 * first_el, second)
-    scatter_first = gather_matrix(first, np.eye(4))
+    scatter_first = mats["scatter_first"]
     return jnp.einsum("xk,dky->dxy", scatter_first, spread, precision=HIGH)
 
 
@@ -91,7 +102,7 @@
     face = jnp.where(me == 0, values[-1], values[0])
     extra = None
     if scalars is not None:
-        extra = jnp.zeros((1, values.shape[2]), values.dtype).at[0, : scalars.shape[0]].set(scalars)
+        extra = jnp.pad(scalars, (0, values.shape[2] - scalars.shape[0]))[None, :]
         face = jnp.concatenate([face, extra], 0)
     got = lax.ppermute(face, "torso", [(0, 1), (1, 0)])
     rows = values.shape[1]
@@ -252,12 +263,13 @@
         drug_block, class_flat, CLASSES
     )
     gate_flat = gating.reshape(gating.shape[0], -1)
+    mats = element_matrices(first_len, second_len)
     for repeat in range(STEPS):
         volts = potential.reshape(1, -1)
         inf_value = jax.nn.sigmoid((volts - half_nodes) * slope_nodes)
         gate_flat = inf_value + (gate_flat - inf_value) * decay_nodes
         current = jnp.sum(cond_nodes * gate_flat * (volts - reversal[:, None]), 0)
-        diffusion, _ = face_sums(local_products(potential, heart_cond))
+        diffusion, _ = face_sums(local_products(potential, heart_cond, mats))
         potential = potential - time_step * (
             diffusion / heart_mass + current.reshape(potential.shape)
         )
@@ -287,18 +299,17 @@
 
     mass_shift = torso_shift * torso_mass
     weighted_mass = torso_weight * mass_shift
+    zero_lanes = 0.0 * torso_weight[0, 0]
 
     def exchange(residual, extra):
-        local = local_products(residual, torso_cond)
-        partial = jnp.stack(
-            [
-                jnp.sum(torso_weight * residual * residual),
-                jnp.sum(residual * local) + jnp.sum(weighted_mass * residual * residual),
-            ]
-            + extra(local)
-        )
+        local = local_products(residual, torso_cond, mats)
+        terms = [
+            torso_weight * residual * residual,
+            residual * local + weighted_mass * residual * residual,
+        ] + extra(local)
+        partial = jnp.sum(jnp.sum(jnp.stack(terms), axis=(1, 2)), axis=1)
         summed, sums = face_sums(local, partial)
-        return summed + mass_shift * residual, sums
+        return summed + mass_shift * residual, sums[:, None] + zero_lanes[None, :]
 
     image, sums = exchange(rhs, lambda local: [])
     norm_now = sums[0]
@@ -313,8 +324,8 @@
         s_image, sums = exchange(
             residual,
             lambda local: [
-                jnp.sum(torso_weight * residual * image),
-                jnp.sum(direction * local) + jnp.sum(weighted_mass * direction * residual),
+                torso_weight * residual * image,
+                direction * local + weighted_mass * direction * residual,
             ],
         )
         norm_next = sums[0]

time: 220 us -> 177 us (0.80)
  loops' own time: 23.7 us -> 1.32 us
  other arithmetic: 57.1 us -> 42.5 us
  local copies, waits for them, and re-layouts: 34.8 us -> 30.2 us
  between operations: 4.96 us -> 2.48 us
  matrix products: 18.6 us -> 20.9 us
    another operation x1, loops' own time: 23.7 us -> 1.32 us  [per_device(): solution = lax.fori_loop(1, ITERS, later_turn, state)[0]]
    another operation x27 -> x23, other arithmetic: 21.9 us -> 12.6 us
    add x4, other arithmetic: 4.57 us -> 0.02 us  [torso_stage(): scalars = scalars + got[rows, :scalars.shape[0]]]
    select_n x4 -> x1, other arithmetic: 3.59 us -> 0.9 us  [gather_matrix(): out = jnp.where((offset == a) & (local == j), jnp.float32(line[a, j]), out)]
    dot_general x6, matrix products: 4.44 us -> 1.91 us  [local_products(): return jnp.einsum('xk,dky->dxy', scatter_first, spread, precision=HIGH)]
  transfers between devices with their start and end apart: 13 -> 13, of which waited for: 10 -> 10; matrix products, arithmetic and copies ran while one was open for 10% -> 13% of each run, Pallas kernels for 0% -> 0%
where the time goes in v4:
time: 177 us; the launch traced here: 176 us
  waiting for transfers between devices  45.2 us (26%)
  other arithmetic  42.5 us (24%)
  starting transfers between devices  33.6 us (19%)
  local copies, waits for them, and re-layouts  30.2 us (17%)
  matrix products  20.9 us (12%)
  between operations  2.48 us (1%)
    all_to_all x7, waiting for transfers between devices, plane_exchange(): got = lax.all_to_all(send, ('hx', 'hy'), 0, 0, tiled=True)  41.8 us
    all_to_all x7, starting transfers between devices, plane_exchange(): got = lax.all_to_all(send, ('hx', 'hy'), 0, 0, tiled=True)  32.8 us
    reduce_sum x2, other arithmetic, per_device(): current = jnp.sum(cond_nodes * gate_flat * (volts - reversal[:, None]), 0)  15.7 us
    another operation x19, other arithmetic  12.1 us
    gather x7, local copies, waits for them, and re-layouts, plane_exchange(): send = jnp.take(table, code_of, axis=0)  4.6 us
    dot_general x6, matrix products, local_products(): jnp.dot(flat_k, lanes_m, precision=HIGH)  4.55 us
    dot_general x6, matrix products, local_products(): jnp.dot(flat_m, lanes_k, precision=HIGH)  4.52 us
    select_n x44, local copies, waits for them, and re-layouts, plane_exchange(): received[offset] = jnp.where(valid, row[:pieces[offset].shape[0]], 0.0)  3.81 us
  transfers between devices with their start and end apart: 13, of which 10 were waited for; matrix products, arithmetic and copies ran while one was open for 13% of the time, Pallas kernels for 0%

profile of v4, /device:TPU:0, one launch (start us, length us, event | category | flops | bytes accessed | tf_op | source)
XLA Modules:
  0.0 176.2 jit_solution(3490912292530270046)
XLA Ops:
  0.7 0.8 copy.140
  3.0 0.7 mul.1179
  3.8 0.9 select_select_fusion.6
  9.0 7.7 %multiply_reduce_fusion.1 = (f32[4,13,256]{2,0,1:T(4,128)}, f32[40,4,13,256]{3,1,2,0:T(4,128)S(1)}) fusion(f32[40]{0:T(128)} %param.105, f32[4,13,256]{2,0,1:T(4,128)S(1)} %copy-done, f32[40]{0:T(128)S(1)} %get-tuple-element.1443, f32[40]{0:T(128)S(1)} %get-tuple-element.1442, f32[40]{0:T(128)S(1)} %get-tuple-element.1444, f32[40]{0:T(128)S(1)} %get-tuple-element.1445, ...), kind=kLoop, calls=%fused_computation.407 | loop fusion | flops 12766208 | bytes 4435616 | tf_op jit(solution)/shard_map/reduce_sum | solution.py:271
  17.5 0.7 fusion.504
  18.9 0.7 gather_fusion.3
  19.7 0.7 select_bitcast_fusion.1
  20.3 0.7 copy.130
  21.0 7.9 %all-to-all-start.1 = ((f32[16,1,1024]{2,1,0:T(1,128)}), f32[16,1,1024]{2,1,0:T(1,128)S(1)}, u32[]{:S(2)}, u32[]{:S(2)}) async-start(f32[16,1,1024]{2,1,0:T(1,128)} %copy.130), calls=%async_computation.1 | async-start | bytes 131072 | tf_op jit(solution)/shard_map/all_to_all | solution.py:135
  29.5 0.7 compare_reduce_fusion.1
  30.2 6.2 %all-to-all-done.1 = f32[16,1,1024]{2,1,0:T(1,128)S(1)} async-done(((f32[16,1,1024]{2,1,0:T(1,128)}), f32[16,1,1024]{2,1,0:T(1,128)S(1)}, u32[]{:S(2)}, u32[]{:S(2)}) %all-to-all-start.1) | async-done | bytes 65568 | tf_op jit(solution)/shard_map/all_to_all | solution.py:135
  39.5 0.9 fusion.401
  40.4 1.0 fusion.433
  41.4 1.0 fusion.432
  42.9 1.0 convolution_add_fusion.6
  44.6 0.9 fusion.508
  46.8 0.7 mul.1249
  47.7 0.7 fusion.500
  49.0 0.8 stack.343
  49.7 0.7 gather_fusion.4
  50.4 0.7 select_bitcast_fusion
  51.1 0.7 copy.144
  51.8 4.1 %all-to-all-start.2 = ((f32[16,1,1024]{2,1,0:T(1,128)}), f32[16,1,1024]{2,1,0:T(1,128)}, u32[]{:S(2)}, u32[]{:S(2)}) async-start(f32[16,1,1024]{2,1,0:T(1,128)} %copy.144), calls=%async_computation.2 | async-start | bytes 131072 | tf_op jit(solution)/shard_map/all_to_all | solution.py:135
  56.0 7.9 %multiply_reduce_fusion = (f32[4,13,256]{2,0,1:T(4,128)S(1)}, f32[40,4,13,256]{3,1,2,0:T(4,128)}) fusion(f32[4,13,256]{2,0,1:T(4,128)S(1)} %copy.153, f32[40]{0:T(128)} %param.105, f32[40]{0:T(128)} %copy-done.27, f32[40]{0:T(128)} %copy-done.26, f32[40]{0:T(128)} %copy-done.28, f32[40]{0:T(128)} %copy-done.29, f32[40]{0:T(128)} %copy-done.37, ...), kind=kLoop, calls=%fused_computation.405 | loop fusion | flops 12766208 | bytes 4435616 | tf_op jit(solution)/shard_map/reduce_sum | solution.py:271
  64.0 0.8 fusion.560
  69.0 0.7 gather_fusion.1
  69.7 0.7 bitcast_select_fusion.2
  70.4 0.7 copy.155
  71.1 6.8 %all-to-all-start.3 = ((f32[16,1,768]{2,1,0:T(1,128)}), f32[16,1,768]{2,1,0:T(1,128)S(1)}, u32[]{:S(2)}, u32[]{:S(2)}) async-start(f32[16,1,768]{2,1,0:T(1,128)} %copy.155), calls=%async_computation.3 | async-start | bytes 98304 | tf_op jit(solution)/shard_map/all_to_all | solution.py:135
  77.9 7.4 %all-to-all-done.3 = f32[16,1,768]{2,1,0:T(1,128)S(1)} async-done(((f32[16,1,768]{2,1,0:T(1,128)}), f32[16,1,768]{2,1,0:T(1,128)S(1)}, u32[]{:S(2)}, u32[]{:S(2)}) %all-to-all-start.3) | async-done | bytes 49184 | tf_op jit(solution)/shard_map/all_to_all | solution.py:135
  89.9 0.7 copy.168
  91.3 0.7 gather_fusion.2
  92.1 0.7 copy.159
  92.8 3.5 %all-to-all-start.4 = ((f32[16,1,1026]{2,1,0:T(1,128)}), f32[16,1,1026]{2,1,0:T(1,128)S(1)}, u32[]{:S(2)}, u32[]{:S(2)}) async-start(f32[16,1,1026]{2,1,0:T(1,128)} %copy.159), calls=%async_computation.4 | async-start | bytes 147456 | tf_op jit(solution)/shard_map/all_to_all | solution.py:135
  96.4 7.6 %all-to-all-done.4 = f32[16,1,1026]{2,1,0:T(1,128)S(1)} async-done(((f32[16,1,1026]{2,1,0:T(1,128)}), f32[16,1,1026]{2,1,0:T(1,128)S(1)}, u32[]{:S(2)}, u32[]{:S(2)}) %all-to-all-start.4) | async-done | bytes 65696 | tf_op jit(solution)/shard_map/all_to_all | solution.py:135
  107.3 68.2 %while.67 = (s32[]{:T(128)}, f32[4,13,256]{2,1,0:T(8,128)S(1)}, f32[4,13,256]{2,1,0:T(8,128)S(1)}, f32[4,13,256]{2,1,0:T(8,128)S(1)}, f32[4,13,256]{2,1,0:T(8,12...) while((s32[]{:T(128)}, f32[4,13,256]{2,1,0:T(8,128)S(1)}, ...), condition=%wide.region_10.12_spmd.clone.clone.clone, body=%wide.region_6.11_spmd.clone.clone.clone.sunk | while | flops 219348720 | bytes 4220679 | solution.py:342
  108.4 1.1 fusion.812
  109.5 1.1 fusion.814
  110.6 0.6 fusion.815
  111.8 1.1 collective-permute-done
  114.4 0.7 copy.207
  115.1 3.5 %all-to-all-start = ((f32[16,1,1028]{2,1,0:T(1,128)}), f32[16,1,1028]{2,1,0:T(1,128)S(1)}, u32[]{:S(2)}, u32[]{:S(2)}) async-start(f32[16,1,1028]{2,1,0:T(1,128)} %copy.207), calls=%async_computation | async-start | bytes 147456 | tf_op jit(solution)/shard_map/while/body/eval_jaxpr/all_to_all | solution.py:135
  118.7 0.6 compare_reduce_fusion.4
  119.3 6.8 %all-to-all-done = f32[16,1,1028]{2,1,0:T(1,128)S(1)} async-done(((f32[16,1,1028]{2,1,0:T(1,128)}), f32[16,1,1028]{2,1,0:T(1,128)S(1)}, u32[]{:S(2)}, u32[]{:S(2)}) %all-to-all-start) | async-done | bytes 65824 | tf_op jit(solution)/shard_map/while/body/eval_jaxpr/all_to_all | solution.py:135
  128.5 0.7 add_select_fusion.17
  131.1 1.1 fusion.812
  132.2 1.1 fusion.814
  133.3 0.6 fusion.815
  134.6 1.1 collective-permute-done
  137.1 0.7 copy.207
  137.8 3.5 %all-to-all-start = ((f32[16,1,1028]{2,1,0:T(1,128)}), f32[16,1,1028]{2,1,0:T(1,128)S(1)}, u32[]{:S(2)}, u32[]{:S(2)}) async-start(f32[16,1,1028]{2,1,0:T(1,128)} %copy.207), calls=%async_computation | async-start | bytes 147456 | tf_op jit(solution)/shard_map/while/body/eval_jaxpr/all_to_all | solution.py:135
  141.4 0.6 compare_reduce_fusion.4
  142.0 6.8 %all-to-all-done = f32[16,1,1028]{2,1,0:T(1,128)S(1)} async-done(((f32[16,1,1028]{2,1,0:T(1,128)}), f32[16,1,1028]{2,1,0:T(1,128)S(1)}, u32[]{:S(2)}, u32[]{:S(2)}) %all-to-all-start) | async-done | bytes 65824 | tf_op jit(solution)/shard_map/while/body/eval_jaxpr/all_to_all | solution.py:135
  151.2 0.7 add_select_fusion.17
  153.8 1.1 fusion.812
  154.9 1.1 fusion.814
  156.0 0.6 fusion.815
  157.3 1.1 collective-permute-done
  159.8 0.7 copy.207
  160.5 3.5 %all-to-all-start = ((f32[16,1,1028]{2,1,0:T(1,128)}), f32[16,1,1028]{2,1,0:T(1,128)S(1)}, u32[]{:S(2)}, u32[]{:S(2)}) async-start(f32[16,1,1028]{2,1,0:T(1,128)} %copy.207), calls=%async_computation | async-start | bytes 147456 | tf_op jit(solution)/shard_map/while/body/eval_jaxpr/all_to_all | solution.py:135
  164.1 0.6 compare_reduce_fusion.4
  164.8 6.8 %all-to-all-done = f32[16,1,1028]{2,1,0:T(1,128)S(1)} async-done(((f32[16,1,1028]{2,1,0:T(1,128)}), f32[16,1,1028]{2,1,0:T(1,128)S(1)}, u32[]{:S(2)}, u32[]{:S(2)}) %all-to-all-start) | async-done | bytes 65824 | tf_op jit(solution)/shard_map/while/body/eval_jaxpr/all_to_all | solution.py:135
  174.0 0.7 add_select_fusion.17
  175.5 0.7 copy.169
  (614 shorter events, 43.7 us)
Async XLA Ops:
  0.7 4.0 %copy-start.46 = (pred[4]{0:T(512)(128)(4,1)}, pred[4]{0:T(512)(128)(4,1)S(1)}, u32[]{:S(2)}) copy-start(pred[4]{0:T(512)(128)(4,1)S(1)} %iota_compare_fusion.2) | copy-start | bytes 16
  0.7 4.0 %copy-start.48 = (pred[4]{0:T(512)(128)(4,1)}, pred[4]{0:T(512)(128)(4,1)S(1)}, u32[]{:S(2)}) copy-start(pred[4]{0:T(512)(128)(4,1)S(1)} %iota_compare_fusion.3) | copy-start | bytes 16
  0.7 4.0 %copy-start.50 = (pred[4]{0:T(512)(128)(4,1)}, pred[4]{0:T(512)(128)(4,1)S(1)}, u32[]{:S(2)}) copy-start(pred[4]{0:T(512)(128)(4,1)S(1)} %iota_compare_fusion.4) | copy-start | bytes 16
  0.7 4.0 %copy-start.52 = (pred[4]{0:T(512)(128)(4,1)}, pred[4]{0:T(512)(128)(4,1)S(1)}, u32[]{:S(2)}) copy-start(pred[4]{0:T(512)(128)(4,1)S(1)} %iota_compare_fusion.5) | copy-start | bytes 16
  0.7 4.0 %copy-start.39 = (s32[85]{0:T(128)}, s32[85]{0:T(128)S(1)}, u32[]{:S(2)}) copy-start(s32[85]{0:T(128)S(1)} %iota_multiply_fusion.1) | copy-start | bytes 1024
  1.9 4.6 %copy-start.13 = (pred[16]{0:T(512)(128)(4,1)}, pred[16]{0:T(512)(128)(4,1)S(1)}, u32[]{:S(2)}) copy-start(pred[16]{0:T(512)(128)(4,1)S(1)} %iota.993) | copy-start | bytes 52
  2.0 4.5 %copy-start.15 = (pred[16]{0:T(512)(128)(4,1)}, pred[16]{0:T(512)(128)(4,1)S(1)}, u32[]{:S(2)}) copy-start(pred[16]{0:T(512)(128)(4,1)S(1)} %iota.990) | copy-start | bytes 52
  2.2 4.3 %copy-start.17 = (pred[16]{0:T(512)(128)(4,1)}, pred[16]{0:T(512)(128)(4,1)S(1)}, u32[]{:S(2)}) copy-start(pred[16]{0:T(512)(128)(4,1)S(1)} %iota.987) | copy-start | bytes 52
  2.4 4.2 %copy-start.19 = (pred[16]{0:T(512)(128)(4,1)}, pred[16]{0:T(512)(128)(4,1)S(1)}, u32[]{:S(2)}) copy-start(pred[16]{0:T(512)(128)(4,1)S(1)} %iota.979) | copy-start | bytes 52
  4.8 3.7 %copy-start.10 = (s32[4,13,256]{2,0,1:T(4,128)S(1)}, s32[4,13,256]{2,0,1:T(4,128)}, u32[]{:S(2)}) copy-start(s32[4,13,256]{2,0,1:T(4,128)} %param.100) | copy-start | bytes 159748
  4.8 3.7 %copy-start.11 = (s32[4,13,256]{2,0,1:T(4,128)S(1)}, s32[4,13,256]{2,0,1:T(4,128)}, u32[]{:S(2)}) copy-start(s32[4,13,256]{2,0,1:T(4,128)} %param.99) | copy-start | bytes 159748
  4.8 3.9 %copy-start.45 = (f32[3,40]{1,0:T(4,128)S(1)}, f32[3,40]{1,0:T(4,128)}, u32[]{:S(2)}) copy-start(f32[3,40]{1,0:T(4,128)} %param.102) | copy-start | bytes 1444
  4.8 4.2 %copy-start = (f32[4,13,256]{2,0,1:T(4,128)S(1)}, f32[4,13,256]{2,0,1:T(4,128)}, u32[]{:S(2)}) copy-start(f32[4,13,256]{2,0,1:T(4,128)} %param.97) | copy-start | bytes 159748
  7.4 10.1 %collective-permute-start.1 = (f32[13,256]{1,0:T(8,128)}, f32[13,256]{1,0:T(8,128)}, u32[]{:S(2)}, u32[]{:S(2)}) collective-permute-start(f32[13,256]{1,0:T(8,128)} %fusion.502), channel_id=1, source_target_pairs={{0,1},{1,0},{2,3},{3,2},{4,5},{5,4},{6,7},{7,6},{8,9},{9,8},{10,11... | collective-permute-start | bytes 39944 | tf_op jit(solution)/shard_map/ppermute | solution.py:107
  8.4 8.3 %copy-start.36 = (f32[40]{0:T(128)}, f32[40]{0:T(128)S(1)}, u32[]{:S(2)}) copy-start(f32[40]{0:T(128)S(1)} %get-tuple-element.1413) | copy-start | bytes 484
  8.4 8.3 %copy-start.37 = (f32[40]{0:T(128)}, f32[40]{0:T(128)S(1)}, u32[]{:S(2)}) copy-start(f32[40]{0:T(128)S(1)} %get-tuple-element.1414) | copy-start | bytes 484
  8.4 8.3 %copy-start.38 = (f32[40]{0:T(128)}, f32[40]{0:T(128)S(1)}, u32[]{:S(2)}) copy-start(f32[40]{0:T(128)S(1)} %get-tuple-element.1415) | copy-start | bytes 484
  8.5 8.2 %copy-start.23 = (f32[40]{0:T(128)}, f32[40]{0:T(128)S(1)}, u32[]{:S(2)}) copy-start(f32[40]{0:T(128)S(1)} %get-tuple-element.1404) | copy-start | bytes 484
  8.5 8.2 %copy-start.24 = (f32[40]{0:T(128)}, f32[40]{0:T(128)S(1)}, u32[]{:S(2)}) copy-start(f32[40]{0:T(128)S(1)} %get-tuple-element.1405) | copy-start | bytes 484
  8.5 8.2 %copy-start.25 = (f32[40]{0:T(128)}, f32[40]{0:T(128)S(1)}, u32[]{:S(2)}) copy-start(f32[40]{0:T(128)S(1)} %get-tuple-element.1406) | copy-start | bytes 484
  8.5 8.2 %copy-start.26 = (f32[40]{0:T(128)}, f32[40]{0:T(128)S(1)}, u32[]{:S(2)}) copy-start(f32[40]{0:T(128)S(1)} %get-tuple-element.1442) | copy-start | bytes 484
  8.6 8.2 %copy-start.27 = (f32[40]{0:T(128)}, f32[40]{0:T(128)S(1)}, u32[]{:S(2)}) copy-start(f32[40]{0:T(128)S(1)} %get-tuple-element.1443) | copy-start | bytes 484
  8.6 8.2 %copy-start.28 = (f32[40]{0:T(128)}, f32[40]{0:T(128)S(1)}, u32[]{:S(2)}) copy-start(f32[40]{0:T(128)S(1)} %get-tuple-element.1444) | copy-start | bytes 484
  8.6 8.2 %copy-start.29 = (f32[40]{0:T(128)}, f32[40]{0:T(128)S(1)}, u32[]{:S(2)}) copy-start(f32[40]{0:T(128)S(1)} %get-tuple-element.1445) | copy-start | bytes 484
  8.7 8.1 %copy-start.2 = (pred[4,13,256]{2,0,1:T(4,128)(4,1)}, pred[4,13,256]{2,0,1:T(4,128)(4,1)S(1)}, u32[]{:S(2)}) copy-start(pred[4,13,256]{2,0,1:T(4,128)(4,1)S(1)} %get-tuple-element.1368) | copy-start | bytes 39940
  8.7 8.1 %copy-start.4 = (pred[4,13,256]{2,0,1:T(4,128)(4,1)}, pred[4,13,256]{2,0,1:T(4,128)(4,1)S(1)}, u32[]{:S(2)}) copy-start(pred[4,13,256]{2,0,1:T(4,128)(4,1)S(1)} %get-tuple-element.1369) | copy-start | bytes 39940
  8.7 8.1 %copy-start.8 = (pred[4,13,256]{2,0,1:T(4,128)(4,1)}, pred[4,13,256]{2,0,1:T(4,128)(4,1)S(1)}, u32[]{:S(2)}) copy-start(pred[4,13,256]{2,0,1:T(4,128)(4,1)S(1)} %get-tuple-element.1438) | copy-start | bytes 39940
  8.7 10.1 %copy-start.6 = (pred[4,13,256]{2,0,1:T(4,128)(4,1)}, pred[4,13,256]{2,0,1:T(4,128)(4,1)S(1)}, u32[]{:S(2)}) copy-start(pred[4,13,256]{2,0,1:T(4,128)(4,1)S(1)} %get-tuple-element.1370) | copy-start | bytes 39940
  8.7 10.1 %copy-start.7 = (pred[4,13,256]{2,0,1:T(4,128)(4,1)}, pred[4,13,256]{2,0,1:T(4,128)(4,1)S(1)}, u32[]{:S(2)}) copy-start(pred[4,13,256]{2,0,1:T(4,128)(4,1)S(1)} %get-tuple-element.1437) | copy-start | bytes 39940
  8.7 8.1 %copy-start.30 = (f32[40]{0:T(128)}, f32[40]{0:T(128)S(1)}, u32[]{:S(2)}) copy-start(f32[40]{0:T(128)S(1)} %get-tuple-element.1410) | copy-start | bytes 484
  8.8 8.1 %copy-start.31 = (f32[40]{0:T(128)}, f32[40]{0:T(128)S(1)}, u32[]{:S(2)}) copy-start(f32[40]{0:T(128)S(1)} %get-tuple-element.1411) | copy-start | bytes 484
  8.8 8.1 %copy-start.32 = (f32[40]{0:T(128)}, f32[40]{0:T(128)S(1)}, u32[]{:S(2)}) copy-start(f32[40]{0:T(128)S(1)} %get-tuple-element.1412) | copy-start | bytes 484
  8.8 8.1 %copy-start.33 = (f32[40]{0:T(128)}, f32[40]{0:T(128)S(1)}, u32[]{:S(2)}) copy-start(f32[40]{0:T(128)S(1)} %get-tuple-element.1439) | copy-start | bytes 484
  8.8 8.1 %copy-start.34 = (f32[40]{0:T(128)}, f32[40]{0:T(128)S(1)}, u32[]{:S(2)}) copy-start(f32[40]{0:T(128)S(1)} %get-tuple-element.1440) | copy-start | bytes 484
  8.8 8.1 %copy-start.35 = (f32[40]{0:T(128)}, f32[40]{0:T(128)S(1)}, u32[]{:S(2)}) copy-start(f32[40]{0:T(128)S(1)} %get-tuple-element.1441) | copy-start | bytes 484
  18.8 10.7 %copy-start.12 = (f32[1,1024]{1,0:T(1,128)}, f32[1,1024]{1,0:T(1,128)S(1)}, u32[]{:S(2)}) copy-start(f32[1,1024]{1,0:T(1,128)S(1)} %broadcast.6035) | copy-start | bytes 12292
  19.6 27.1 %copy-start.9 = (f32[1,4,85]{2,1,0:T(4,128)S(1)}, f32[1,4,85]{2,1,0:T(4,128)}, u32[]{:S(2)}) copy-start(f32[1,4,85]{2,1,0:T(4,128)} %param.108) | copy-start | bytes 4084
  21.0 15.4 %all-to-all-start.1 = ((f32[16,1,1024]{2,1,0:T(1,128)}), f32[16,1,1024]{2,1,0:T(1,128)S(1)}, u32[]{:S(2)}, u32[]{:S(2)}) async-start(f32[16,1,1024]{2,1,0:T(1,128)} %copy.130), calls=%async_computation.1 | async-start | bytes 131072 | tf_op jit(solution)/shard_map/all_to_all | solution.py:135
  39.5 6.6 %copy-start.54 = (s32[16]{0:T(128)S(1)}, s32[16]{0:T(128)}, u32[]{:S(2)}) copy-start(s32[16]{0:T(128)} %fusion.609) | copy-start | bytes 196
  42.4 13.6 %copy-start.3 = (pred[4,13,256]{2,0,1:T(4,128)(4,1)S(1)}, pred[4,13,256]{2,0,1:T(4,128)(4,1)}, u32[]{:S(2)}) copy-start(pred[4,13,256]{2,0,1:T(4,128)(4,1)} %copy-done.2) | copy-start | bytes 39940
  42.4 13.6 %copy-start.5 = (pred[4,13,256]{2,0,1:T(4,128)(4,1)S(1)}, pred[4,13,256]{2,0,1:T(4,128)(4,1)}, u32[]{:S(2)}) copy-start(pred[4,13,256]{2,0,1:T(4,128)(4,1)} %copy-done.4) | copy-start | bytes 39940
  46.1 1.5 collective-permute-start.2
  51.8 12.2 %all-to-all-start.2 = ((f32[16,1,1024]{2,1,0:T(1,128)}), f32[16,1,1024]{2,1,0:T(1,128)}, u32[]{:S(2)}, u32[]{:S(2)}) async-start(f32[16,1,1024]{2,1,0:T(1,128)} %copy.144), calls=%async_computation.2 | async-start | bytes 131072 | tf_op jit(solution)/shard_map/all_to_all | solution.py:135
  63.9 22.2 %copy-start.21 = (s32[13,256]{1,0:T(8,128)S(1)}, s32[13,256]{1,0:T(8,128)}, u32[]{:S(2)}) copy-start(s32[13,256]{1,0:T(8,128)} %param.109) | copy-start | bytes 39940
  63.9 22.5 %copy-start.14 = (pred[16]{0:T(512)(128)(4,1)S(1)}, pred[16]{0:T(512)(128)(4,1)}, u32[]{:S(2)}) copy-start(pred[16]{0:T(512)(128)(4,1)} %copy-done.13) | copy-start | bytes 52
  63.9 22.5 %copy-start.16 = (pred[16]{0:T(512)(128)(4,1)S(1)}, pred[16]{0:T(512)(128)(4,1)}, u32[]{:S(2)}) copy-start(pred[16]{0:T(512)(128)(4,1)} %copy-done.15) | copy-start | bytes 52
  63.9 22.5 %copy-start.18 = (pred[16]{0:T(512)(128)(4,1)S(1)}, pred[16]{0:T(512)(128)(4,1)}, u32[]{:S(2)}) copy-start(pred[16]{0:T(512)(128)(4,1)} %copy-done.17) | copy-start | bytes 52
  64.0 22.5 %copy-start.20 = (pred[16]{0:T(512)(128)(4,1)S(1)}, pred[16]{0:T(512)(128)(4,1)}, u32[]{:S(2)}) copy-start(pred[16]{0:T(512)(128)(4,1)} %copy-done.19) | copy-start | bytes 52
  64.0 23.8 %copy-start.1 = (f32[64,340]{1,0:T(8,128)S(1)}, f32[64,340]{1,0:T(8,128)}, u32[]{:S(2)}) copy-start(f32[64,340]{1,0:T(8,128)} %mul.1249) | copy-start | bytes 261124
  71.1 14.3 %all-to-all-start.3 = ((f32[16,1,768]{2,1,0:T(1,128)}), f32[16,1,768]{2,1,0:T(1,128)S(1)}, u32[]{:S(2)}, u32[]{:S(2)}) async-start(f32[16,1,768]{2,1,0:T(1,128)} %copy.155), calls=%async_computation.3 | async-start | bytes 98304 | tf_op jit(solution)/shard_map/all_to_all | solution.py:135
  77.9 11.2 %copy-start.53 = (pred[4]{0:T(512)(128)(4,1)S(1)}, pred[4]{0:T(512)(128)(4,1)}, u32[]{:S(2)}) copy-start(pred[4]{0:T(512)(128)(4,1)} %copy-done.52) | copy-start | bytes 16
  77.9 11.4 %copy-start.51 = (pred[4]{0:T(512)(128)(4,1)S(1)}, pred[4]{0:T(512)(128)(4,1)}, u32[]{:S(2)}) copy-start(pred[4]{0:T(512)(128)(4,1)} %copy-done.50) | copy-start | bytes 16
  77.9 11.5 %copy-start.49 = (pred[4]{0:T(512)(128)(4,1)S(1)}, pred[4]{0:T(512)(128)(4,1)}, u32[]{:S(2)}) copy-start(pred[4]{0:T(512)(128)(4,1)} %copy-done.48) | copy-start | bytes 16
  77.9 11.7 %copy-start.40 = (s32[85]{0:T(128)S(1)}, s32[85]{0:T(128)}, u32[]{:S(2)}) copy-start(s32[85]{0:T(128)} %copy-done.39) | copy-start | bytes 1024
  77.9 11.8 %copy-start.47 = (pred[4]{0:T(512)(128)(4,1)S(1)}, pred[4]{0:T(512)(128)(4,1)}, u32[]{:S(2)}) copy-start(pred[4]{0:T(512)(128)(4,1)} %copy-done.46) | copy-start | bytes 16
  87.1 5.0 %copy-start.22 = (pred[16]{0:T(512)(128)(4,1)S(1)}, pred[16]{0:T(512)(128)(4,1)}, u32[]{:S(2)}) copy-start(pred[16]{0:T(512)(128)(4,1)} %get-tuple-element.1276) | copy-start | bytes 52
  89.0 1.5 collective-permute-start.3
  92.8 11.2 %all-to-all-start.4 = ((f32[16,1,1026]{2,1,0:T(1,128)}), f32[16,1,1026]{2,1,0:T(1,128)S(1)}, u32[]{:S(2)}, u32[]{:S(2)}) async-start(f32[16,1,1026]{2,1,0:T(1,128)} %copy.159), calls=%async_computation.4 | async-start | bytes 147456 | tf_op jit(solution)/shard_map/all_to_all | solution.py:135
  111.7 1.2 collective-permute-start
  115.1 11.0 %all-to-all-start = ((f32[16,1,1028]{2,1,0:T(1,128)}), f32[16,1,1028]{2,1,0:T(1,128)S(1)}, u32[]{:S(2)}, u32[]{:S(2)}) async-start(f32[16,1,1028]{2,1,0:T(1,128)} %copy.207), calls=%async_computation | async-start | bytes 147456 | tf_op jit(solution)/shard_map/while/body/eval_jaxpr/all_to_all | solution.py:135
  134.4 1.2 collective-permute-start
  137.8 11.0 %all-to-all-start = ((f32[16,1,1028]{2,1,0:T(1,128)}), f32[16,1,1028]{2,1,0:T(1,128)S(1)}, u32[]{:S(2)}, u32[]{:S(2)}) async-start(f32[16,1,1028]{2,1,0:T(1,128)} %copy.207), calls=%async_computation | async-start | bytes 147456 | tf_op jit(solution)/shard_map/while/body/eval_jaxpr/all_to_all | solution.py:135
  157.1 1.2 collective-permute-start
  160.5 11.0 %all-to-all-start = ((f32[16,1,1028]{2,1,0:T(1,128)}), f32[16,1,1028]{2,1,0:T(1,128)S(1)}, u32[]{:S(2)}, u32[]{:S(2)}) async-start(f32[16,1,1028]{2,1,0:T(1,128)} %copy.207), calls=%async_computation | async-start | bytes 147456 | tf_op jit(solution)/shard_map/while/body/eval_jaxpr/all_to_all | solution.py:135
  (4 other events, 14.7 us)

commit v5 on v4

--- a/solution.py
+++ b/solution.py
@@ -131,7 +131,10 @@
     off_y = peers % count_y - me_y
     near = (jnp.abs(off_x) <= 1) & (jnp.abs(off_y) <= 1)
     code_of = jnp.where(near, (off_x + 1) * 3 + (off_y + 1), 4)
-    send = jnp.take(table, code_of, axis=0)
+    send = jnp.broadcast_to(table[4][None, :], (count_x * count_y, table.shape[1]))
+    for code in range(9):
+        if code != 4:
+            send = jnp.where(code_of[:, None] == code, table[code][None, :], send)
     got = lax.all_to_all(send, ("hx", "hy"), 0, 0, tiled=True)
     received = {}
     for offset in pieces:
@@ -160,14 +163,26 @@
         (-1, -1): values[:, 0, 0],
     }
     got, total = plane_exchange(pieces, depth * second, scalars)
+    row = lax.broadcasted_iota(jnp.int32, (1, first, 1), 1)
+    col = lax.broadcasted_iota(jnp.int32, (1, 1, second), 2)
+    row_2d = row[:, :, 0]
     low_second = got[(0, -1)].reshape(depth, first)
-    low_second = low_second.at[:, 0].add(got[(-1, -1)]).at[:, -1].add(got[(1, -1)])
+    low_second = low_second + jnp.where(row_2d == 0, got[(-1, -1)][:, None], 0.0)
+    low_second = low_second + jnp.where(row_2d == first - 1, got[(1, -1)][:, None], 0.0)
     high_second = got[(0, 1)].reshape(depth, first)
-    high_second = high_second.at[:, 0].add(got[(-1, 1)]).at[:, -1].add(got[(1, 1)])
-    values = values.at[:, 0, :].add(got[(-1, 0)].reshape(depth, second))
-    values = values.at[:, -1, :].add(got[(1, 0)].reshape(depth, second))
-    values = values.at[:, :, 0].add(low_second).at[:, :, -1].add(high_second)
-    return values, total
+    high_second = high_second + jnp.where(row_2d == 0, got[(-1, 1)][:, None], 0.0)
+    high_second = high_second + jnp.where(row_2d == first - 1, got[(1, 1)][:, None], 0.0)
+    along_first = jnp.where(
+        row == 0,
+        got[(-1, 0)].reshape(depth, 1, second),
+        jnp.where(row == first - 1, got[(1, 0)].reshape(depth, 1, second), 0.0),
+    )
+    along_second = jnp.where(
+        col == 0,
+        low_second[:, :, None],
+        jnp.where(col == second - 1, high_second[:, :, None], 0.0),
+    )
+    return values + along_first + along_second, total
 
 
 def rim_plane(plane, rim):

time: 177 us -> 158 us (0.89)
  local copies, waits for them, and re-layouts: 30.2 us -> 11.2 us
  waiting for transfers between devices: 45.2 us -> 48 us
  other arithmetic: 42.5 us -> 39.8 us
    another operation x19 -> x0, other arithmetic: 12.1 us -> none
    select_n x9 -> x7, other arithmetic: 1.64 us -> 8.58 us  [plane_exchange(): send = jnp.where(code_of[:, None] == code, table[code][None, :], send)]
    gather x7 -> x0, local copies, waits for them, and re-layouts: 4.6 us -> none  [plane_exchange(): send = jnp.take(table, code_of, axis=0)]
    scatter-add x48 -> x0, local copies, waits for them, and re-layouts: 4.15 us -> none  [the longest x12 2.55 us: face_sums(): values = values.at[:, :, 0].add(low_second).at[:, :, -1].add(high_second)]
    select_n x5 -> x0, local copies, waits for them, and re-layouts: 3.47 us -> none  [plane_exchange(): send = jnp.take(table, code_of, axis=0)]
    eq x0 -> x18, other arithmetic: none -> 3.45 us  [the longest x8 1.24 us: plane_exchange(): send = jnp.where(code_of[:, None] == code, table[code][None, :], send)]
    another operation x63 -> x0, local copies, waits for them, and re-layouts: 2.84 us -> none  [the longest x50 1.47 us: plane_exchange(): table = jnp.stack(rows)]
    select_n x44 -> x36, other arithmetic: 0.5 us -> 3.14 us  [plane_exchange(): received[offset] = jnp.where(valid, row[:pieces[offset].shape[0]], 0.0)]
  transfers between devices with their start and end apart: 13 -> 13, of which waited for: 10 -> 10; matrix products, arithmetic and copies ran while one was open for 13% -> 14% of each run, Pallas kernels for 0% -> 0%
where the time goes in v5:
time: 158 us; the launch traced here: 157 us
  waiting for transfers between devices  48 us (30%)
  other arithmetic  39.8 us (25%)
  starting transfers between devices  33.1 us (21%)
  matrix products  21.6 us (14%)
  local copies, waits for them, and re-layouts  11.2 us (7%)
  between operations  2.36 us (1%)
    all_to_all x7, waiting for transfers between devices, plane_exchange(): got = lax.all_to_all(send, ('hx', 'hy'), 0, 0, tiled=True)  44.4 us
    all_to_all x7, starting transfers between devices, plane_exchange(): got = lax.all_to_all(send, ('hx', 'hy'), 0, 0, tiled=True)  32.2 us
    reduce_sum x2, other arithmetic, per_device(): current = jnp.sum(cond_nodes * gate_flat * (volts - reversal[:, None]), 0)  15.1 us
    select_n x7, other arithmetic, plane_exchange(): send = jnp.where(code_of[:, None] == code, table[code][None, :], send)  8.58 us
    dot_general x6, matrix products, local_products(): jnp.dot(flat_k, lanes_m, precision=HIGH)  4.54 us
    dot_general x6, matrix products, local_products(): jnp.dot(flat_m, lanes_k, precision=HIGH)  4.52 us
    ppermute x6, waiting for transfers between devices, torso_stage(): got = lax.ppermute(face, 'torso', [(0, 1), (1, 0)])  3.62 us
  transfers between devices with their start and end apart: 13, of which 10 were waited for; matrix products, arithmetic and copies ran while one was open for 14% of the time, Pallas kernels for 0%

profile of v5, /device:TPU:0, one launch (start us, length us, event | category | flops | bytes accessed | tf_op | source)
XLA Modules:
  0.0 156.9 jit_solution(4628780417097607262)
XLA Ops:
  0.7 0.8 copy.97
  3.0 0.9 select_select_fusion.6
  6.1 0.6 fusion.501
  6.7 0.5 collective-permute-start.1
  7.2 0.5 iota_compare_fusion.12
  7.7 0.5 iota_compare_fusion.13
  8.3 0.6 iota_compare_fusion.10
  8.8 0.5 iota_compare_fusion.11
  9.4 0.6 broadcast_compare_fusion.15
  9.9 0.6 broadcast_compare_fusion.14
  11.3 7.1 %multiply_reduce_fusion.1 = (f32[4,13,256]{2,0,1:T(4,128)S(1)}, f32[40,4,13,256]{3,1,2,0:T(4,128)S(1)}) fusion(f32[40]{0:T(128)} %param.39, f32[4,13,256]{2,0,1:T(4,128)S(1)} %copy-done, f32[40]{0:T(128)S(1)} %get-tuple-element.850, f32[40]{0:T(128)S(1)} %get-tuple-element.851, f32[40]{0:T(128)S(1)} %get-tuple-element.849, f32[40]{0:T(128)S(1)} %get-tuple-element.848, ...), kind=kLoop, calls=%fused_computation.403 | loop fusion | flops 12766208 | bytes 4435616 | tf_op jit(solution)/shard_map/reduce_sum | solution.py:286
  18.6 0.5 or_select_fusion.1
  19.8 1.6 %broadcast_select_fusion.37 = f32[16,1,1024]{2,1,0:T(1,128)} fusion(pred[16]{0:T(512)(128)(4,1)} %get-tuple-element.873, pred[16]{0:T(512)(128)(4,1)} %get-tuple-element.872, pred[16]{0:T(512)(128)(4,1)} %get-tuple-element.868, pred[16]{0:T(512)(128)(4,1)} %get-tuple-element.869, pred[16]{0:T(512)(128)(4,1)} %get-tuple-element.870, ...), kind=kLoop, calls=%fused_computation.471 | loop fusion | flops 131072 | bytes 98432 | tf_op jit(solution)/shard_map/jit(_where)/select_n | solution.py:137
  21.4 7.8 %all-to-all-start.1 = ((f32[16,1,1024]{2,1,0:T(1,128)}), f32[16,1,1024]{2,1,0:T(1,128)S(1)}, u32[]{:S(2)}, u32[]{:S(2)}) async-start(f32[16,1,1024]{2,1,0:T(1,128)} %broadcast_select_fusion.37), calls=%async_computation.1 | async-start | bytes 131072 | tf_op jit(solution)/shard_map/all_to_all | solution.py:138
  29.2 0.5 or_select_fusion.2
  29.8 7.0 %all-to-all-done.1 = f32[16,1,1024]{2,1,0:T(1,128)S(1)} async-done(((f32[16,1,1024]{2,1,0:T(1,128)}), f32[16,1,1024]{2,1,0:T(1,128)S(1)}, u32[]{:S(2)}, u32[]{:S(2)}) %all-to-all-start.1) | async-done | bytes 65568 | tf_op jit(solution)/shard_map/all_to_all | solution.py:138
  36.8 0.6 fusion.548
  37.6 0.7 fusion.599
  38.3 0.7 fusion.602
  39.0 0.7 fusion.590
  39.6 0.7 select_add_fusion.7
  40.3 0.8 fusion.400
  41.2 1.0 fusion.431
  42.1 1.0 fusion.432
  43.5 1.0 convolution_add_fusion.6
  45.3 0.9 fusion.507
  46.4 0.7 mul.1178
  48.1 1.6 %broadcast_select_fusion.36 = f32[16,1,1024]{2,1,0:T(1,128)} fusion(pred[16]{0:T(512)(128)(4,1)} %get-tuple-element.873, pred[16]{0:T(512)(128)(4,1)} %get-tuple-element.872, pred[16]{0:T(512)(128)(4,1)} %get-tuple-element.868, pred[16]{0:T(512)(128)(4,1)} %get-tuple-element.869, pred[16]{0:T(512)(128)(4,1)} %get-tuple-element.870, ...), kind=kLoop, calls=%fused_computation.470 | loop fusion | flops 131072 | bytes 98432 | tf_op jit(solution)/shard_map/jit(_where)/select_n | solution.py:137
  49.6 3.5 %all-to-all-start.2 = ((f32[16,1,1024]{2,1,0:T(1,128)}), f32[16,1,1024]{2,1,0:T(1,128)S(1)}, u32[]{:S(2)}, u32[]{:S(2)}) async-start(f32[16,1,1024]{2,1,0:T(1,128)} %broadcast_select_fusion.36), calls=%async_computation.2 | async-start | bytes 131072 | tf_op jit(solution)/shard_map/all_to_all | solution.py:138
  53.1 8.0 %multiply_reduce_fusion = (f32[4,13,256]{2,0,1:T(4,128)S(1)}, f32[40,4,13,256]{3,1,2,0:T(4,128)}) fusion(f32[4,13,256]{2,0,1:T(4,128)S(1)} %copy.101, f32[40]{0:T(128)} %param.39, f32[40]{0:T(128)} %copy-done.44, f32[40]{0:T(128)} %copy-done.45, f32[40]{0:T(128)} %copy-done.43, f32[40]{0:T(128)} %copy-done.42, f32[40]{0:T(128)} %copy-done.40, ...), kind=kLoop, calls=%fused_computation.401 | loop fusion | flops 12766208 | bytes 4435616 | tf_op jit(solution)/shard_map/reduce_sum | solution.py:286
  61.5 0.7 select_add_fusion.5
  62.2 0.8 fusion.403
  63.7 1.5 broadcast_select_fusion.46
  65.2 6.9 %all-to-all-start.3 = ((f32[16,1,768]{2,1,0:T(1,128)}), f32[16,1,768]{2,1,0:T(1,128)S(1)}, u32[]{:S(2)}, u32[]{:S(2)}) async-start(f32[16,1,768]{2,1,0:T(1,128)} %broadcast_select_fusion.46), calls=%async_computation.3 | async-start | bytes 98304 | tf_op jit(solution)/shard_map/all_to_all | solution.py:138
  72.2 7.4 %all-to-all-done.3 = f32[16,1,768]{2,1,0:T(1,128)S(1)} async-done(((f32[16,1,768]{2,1,0:T(1,128)}), f32[16,1,768]{2,1,0:T(1,128)S(1)}, u32[]{:S(2)}, u32[]{:S(2)}) %all-to-all-start.3) | async-done | bytes 49184 | tf_op jit(solution)/shard_map/all_to_all | solution.py:138
  80.5 1.0 multiply_bitcast_fusion.3
  81.5 1.0 fusion.429
  85.6 0.7 copy.107
  87.0 1.0 broadcast_select_fusion.22
  87.9 3.5 %all-to-all-start.4 = ((f32[16,1,1026]{2,1,0:T(1,128)}), f32[16,1,1026]{2,1,0:T(1,128)S(1)}, u32[]{:S(2)}, u32[]{:S(2)}) async-start(f32[16,1,1026]{2,1,0:T(1,128)} %broadcast_select_fusion.22), calls=%async_computation.4 | async-start | bytes 147456 | tf_op jit(solution)/shard_map/all_to_all | solution.py:138
  91.4 7.6 %all-to-all-done.4 = f32[16,1,1026]{2,1,0:T(1,128)S(1)} async-done(((f32[16,1,1026]{2,1,0:T(1,128)}), f32[16,1,1026]{2,1,0:T(1,128)S(1)}, u32[]{:S(2)}, u32[]{:S(2)}) %all-to-all-start.4) | async-done | bytes 65696 | tf_op jit(solution)/shard_map/all_to_all | solution.py:138
  99.7 56.6 %while.33 = (s32[]{:T(128)}, f32[4,13,256]{2,1,0:T(8,128)S(1)}, f32[4,13,256]{2,1,0:T(8,128)S(1)}, f32[4,13,256]{2,1,0:T(8,128)S(1)}, f32[4,13,256]{2,1,0:T(8,12...) while((s32[]{:T(128)}, f32[4,13,256]{2,1,0:T(8,128)S(1)}, ...), condition=%wide.region_7.8_spmd.clone.clone.clone, body=%wide.region_4.7_spmd.clone.clone.clone.sunk | while | flops 219541120 | bytes 3759361 | solution.py:357
  100.7 1.1 fusion.812
  101.8 1.1 fusion.814
  102.9 0.6 fusion.815
  104.2 1.1 collective-permute-done
  105.9 1.0 broadcast_select_fusion.81
  106.9 3.5 %all-to-all-start = ((f32[16,1,1028]{2,1,0:T(1,128)}), f32[16,1,1028]{2,1,0:T(1,128)S(1)}, u32[]{:S(2)}, u32[]{:S(2)}) async-start(f32[16,1,1028]{2,1,0:T(1,128)} %broadcast_select_fusion.81), calls=%async_computation | async-start | bytes 147456 | tf_op jit(solution)/shard_map/while/body/eval_jaxpr/all_to_all | solution.py:138
  110.5 7.5 %all-to-all-done = f32[16,1,1028]{2,1,0:T(1,128)S(1)} async-done(((f32[16,1,1028]{2,1,0:T(1,128)}), f32[16,1,1028]{2,1,0:T(1,128)S(1)}, u32[]{:S(2)}, u32[]{:S(2)}) %all-to-all-start) | async-done | bytes 65824 | tf_op jit(solution)/shard_map/while/body/eval_jaxpr/all_to_all | solution.py:138
  119.6 1.1 fusion.812
  120.7 1.1 fusion.814
  121.8 0.6 fusion.815
  123.0 1.1 collective-permute-done
  124.7 1.0 broadcast_select_fusion.81
  125.7 3.5 %all-to-all-start = ((f32[16,1,1028]{2,1,0:T(1,128)}), f32[16,1,1028]{2,1,0:T(1,128)S(1)}, u32[]{:S(2)}, u32[]{:S(2)}) async-start(f32[16,1,1028]{2,1,0:T(1,128)} %broadcast_select_fusion.81), calls=%async_computation | async-start | bytes 147456 | tf_op jit(solution)/shard_map/while/body/eval_jaxpr/all_to_all | solution.py:138
  129.3 7.5 %all-to-all-done = f32[16,1,1028]{2,1,0:T(1,128)S(1)} async-done(((f32[16,1,1028]{2,1,0:T(1,128)}), f32[16,1,1028]{2,1,0:T(1,128)S(1)}, u32[]{:S(2)}, u32[]{:S(2)}) %all-to-all-start) | async-done | bytes 65824 | tf_op jit(solution)/shard_map/while/body/eval_jaxpr/all_to_all | solution.py:138
  138.4 1.1 fusion.812
  139.5 1.1 fusion.814
  140.6 0.6 fusion.815
  141.9 1.1 collective-permute-done
  143.6 1.0 broadcast_select_fusion.81
  144.6 3.5 %all-to-all-start = ((f32[16,1,1028]{2,1,0:T(1,128)}), f32[16,1,1028]{2,1,0:T(1,128)S(1)}, u32[]{:S(2)}, u32[]{:S(2)}) async-start(f32[16,1,1028]{2,1,0:T(1,128)} %broadcast_select_fusion.81), calls=%async_computation | async-start | bytes 147456 | tf_op jit(solution)/shard_map/while/body/eval_jaxpr/all_to_all | solution.py:138
  148.2 7.5 %all-to-all-done = f32[16,1,1028]{2,1,0:T(1,128)S(1)} async-done(((f32[16,1,1028]{2,1,0:T(1,128)}), f32[16,1,1028]{2,1,0:T(1,128)S(1)}, u32[]{:S(2)}, u32[]{:S(2)}) %all-to-all-start) | async-done | bytes 65824 | tf_op jit(solution)/shard_map/while/body/eval_jaxpr/all_to_all | solution.py:138
  156.2 0.7 copy.108
  (450 shorter events, 21.0 us)
Async XLA Ops:
  4.0 6.6 %copy-start.49 = (f32[4,40]{1,0:T(4,128)S(1)}, f32[4,40]{1,0:T(4,128)}, u32[]{:S(2)}) copy-start(f32[4,40]{1,0:T(4,128)} %param.40) | copy-start | bytes 1924
  4.0 6.6 %copy-start.9 = (s32[4,13,256]{2,0,1:T(4,128)S(1)}, s32[4,13,256]{2,0,1:T(4,128)}, u32[]{:S(2)}) copy-start(s32[4,13,256]{2,0,1:T(4,128)} %param.34) | copy-start | bytes 159748
  4.0 6.7 %copy-start.50 = (f32[3,40]{1,0:T(4,128)S(1)}, f32[3,40]{1,0:T(4,128)}, u32[]{:S(2)}) copy-start(f32[3,40]{1,0:T(4,128)} %param.37) | copy-start | bytes 1444
  4.0 6.7 %copy-start.51 = (f32[3,40]{1,0:T(4,128)S(1)}, f32[3,40]{1,0:T(4,128)}, u32[]{:S(2)}) copy-start(f32[3,40]{1,0:T(4,128)} %param.35) | copy-start | bytes 1444
  4.0 6.8 %copy-start.52 = (f32[3,40]{1,0:T(4,128)S(1)}, f32[3,40]{1,0:T(4,128)}, u32[]{:S(2)}) copy-start(f32[3,40]{1,0:T(4,128)} %param.36) | copy-start | bytes 1444
  4.0 6.8 %copy-start.53 = (f32[3,40]{1,0:T(4,128)S(1)}, f32[3,40]{1,0:T(4,128)}, u32[]{:S(2)}) copy-start(f32[3,40]{1,0:T(4,128)} %param.38) | copy-start | bytes 1444
  4.0 6.8 %copy-start.8 = (s32[4,13,256]{2,0,1:T(4,128)S(1)}, s32[4,13,256]{2,0,1:T(4,128)}, u32[]{:S(2)}) copy-start(s32[4,13,256]{2,0,1:T(4,128)} %param.33) | copy-start | bytes 159748
  4.0 7.3 %copy-start = (f32[4,13,256]{2,0,1:T(4,128)S(1)}, f32[4,13,256]{2,0,1:T(4,128)}, u32[]{:S(2)}) copy-start(f32[4,13,256]{2,0,1:T(4,128)} %param.31) | copy-start | bytes 159748
  6.7 12.5 %collective-permute-start.1 = (f32[13,256]{1,0:T(8,128)}, f32[13,256]{1,0:T(8,128)S(1)}, u32[]{:S(2)}, u32[]{:S(2)}) collective-permute-start(f32[13,256]{1,0:T(8,128)} %fusion.501), channel_id=1, source_target_pairs={{0,1},{1,0},{2,3},{3,2},{4,5},{5,4},{6,7},{7,6},{8,9},{9,8},{10,11... | collective-permute-start | bytes 39944 | tf_op jit(solution)/shard_map/ppermute | solution.py:107
  10.6 7.9 %copy-start.42 = (f32[40]{0:T(128)}, f32[40]{0:T(128)S(1)}, u32[]{:S(2)}) copy-start(f32[40]{0:T(128)S(1)} %get-tuple-element.848) | copy-start | bytes 484
  10.6 7.9 %copy-start.43 = (f32[40]{0:T(128)}, f32[40]{0:T(128)S(1)}, u32[]{:S(2)}) copy-start(f32[40]{0:T(128)S(1)} %get-tuple-element.849) | copy-start | bytes 484
  10.6 7.9 %copy-start.44 = (f32[40]{0:T(128)}, f32[40]{0:T(128)S(1)}, u32[]{:S(2)}) copy-start(f32[40]{0:T(128)S(1)} %get-tuple-element.850) | copy-start | bytes 484
  10.6 7.9 %copy-start.45 = (f32[40]{0:T(128)}, f32[40]{0:T(128)S(1)}, u32[]{:S(2)}) copy-start(f32[40]{0:T(128)S(1)} %get-tuple-element.851) | copy-start | bytes 484
  10.7 7.8 %copy-start.4 = (pred[4,13,256]{2,0,1:T(4,128)(4,1)}, pred[4,13,256]{2,0,1:T(4,128)(4,1)S(1)}, u32[]{:S(2)}) copy-start(pred[4,13,256]{2,0,1:T(4,128)(4,1)S(1)} %get-tuple-element.800) | copy-start | bytes 39940
  10.7 7.8 %copy-start.5 = (pred[4,13,256]{2,0,1:T(4,128)(4,1)}, pred[4,13,256]{2,0,1:T(4,128)(4,1)S(1)}, u32[]{:S(2)}) copy-start(pred[4,13,256]{2,0,1:T(4,128)(4,1)S(1)} %get-tuple-element.801) | copy-start | bytes 39940
  10.7 7.8 %copy-start.6 = (pred[4,13,256]{2,0,1:T(4,128)(4,1)}, pred[4,13,256]{2,0,1:T(4,128)(4,1)S(1)}, u32[]{:S(2)}) copy-start(pred[4,13,256]{2,0,1:T(4,128)(4,1)S(1)} %get-tuple-element.802) | copy-start | bytes 39940
  10.7 7.8 %copy-start.30 = (f32[40]{0:T(128)}, f32[40]{0:T(128)S(1)}, u32[]{:S(2)}) copy-start(f32[40]{0:T(128)S(1)} %get-tuple-element.842) | copy-start | bytes 484
  10.7 7.8 %copy-start.31 = (f32[40]{0:T(128)}, f32[40]{0:T(128)S(1)}, u32[]{:S(2)}) copy-start(f32[40]{0:T(128)S(1)} %get-tuple-element.843) | copy-start | bytes 484
  10.8 7.8 %copy-start.32 = (f32[40]{0:T(128)}, f32[40]{0:T(128)S(1)}, u32[]{:S(2)}) copy-start(f32[40]{0:T(128)S(1)} %get-tuple-element.844) | copy-start | bytes 484
  10.8 7.7 %copy-start.34 = (f32[40]{0:T(128)}, f32[40]{0:T(128)S(1)}, u32[]{:S(2)}) copy-start(f32[40]{0:T(128)S(1)} %get-tuple-element.837) | copy-start | bytes 484
  10.8 7.7 %copy-start.35 = (f32[40]{0:T(128)}, f32[40]{0:T(128)S(1)}, u32[]{:S(2)}) copy-start(f32[40]{0:T(128)S(1)} %get-tuple-element.838) | copy-start | bytes 484
  10.8 7.7 %copy-start.36 = (f32[40]{0:T(128)}, f32[40]{0:T(128)S(1)}, u32[]{:S(2)}) copy-start(f32[40]{0:T(128)S(1)} %get-tuple-element.839) | copy-start | bytes 484
  10.8 7.7 %copy-start.37 = (f32[40]{0:T(128)}, f32[40]{0:T(128)S(1)}, u32[]{:S(2)}) copy-start(f32[40]{0:T(128)S(1)} %get-tuple-element.840) | copy-start | bytes 484
  10.9 7.7 %copy-start.38 = (f32[40]{0:T(128)}, f32[40]{0:T(128)S(1)}, u32[]{:S(2)}) copy-start(f32[40]{0:T(128)S(1)} %get-tuple-element.841) | copy-start | bytes 484
  10.9 7.7 %copy-start.39 = (f32[40]{0:T(128)}, f32[40]{0:T(128)S(1)}, u32[]{:S(2)}) copy-start(f32[40]{0:T(128)S(1)} %get-tuple-element.845) | copy-start | bytes 484
  10.9 7.7 %copy-start.40 = (f32[40]{0:T(128)}, f32[40]{0:T(128)S(1)}, u32[]{:S(2)}) copy-start(f32[40]{0:T(128)S(1)} %get-tuple-element.846) | copy-start | bytes 484
  10.9 7.7 %copy-start.41 = (f32[40]{0:T(128)}, f32[40]{0:T(128)S(1)}, u32[]{:S(2)}) copy-start(f32[40]{0:T(128)S(1)} %get-tuple-element.847) | copy-start | bytes 484
  11.0 7.7 %copy-start.2 = (pred[4,13,256]{2,0,1:T(4,128)(4,1)}, pred[4,13,256]{2,0,1:T(4,128)(4,1)S(1)}, u32[]{:S(2)}) copy-start(pred[4,13,256]{2,0,1:T(4,128)(4,1)S(1)} %get-tuple-element.798) | copy-start | bytes 39940
  11.0 7.7 %copy-start.3 = (pred[4,13,256]{2,0,1:T(4,128)(4,1)}, pred[4,13,256]{2,0,1:T(4,128)(4,1)S(1)}, u32[]{:S(2)}) copy-start(pred[4,13,256]{2,0,1:T(4,128)(4,1)S(1)} %get-tuple-element.799) | copy-start | bytes 39940
  18.6 27.7 %copy-start.7 = (f32[1,4,85]{2,1,0:T(4,128)S(1)}, f32[1,4,85]{2,1,0:T(4,128)}, u32[]{:S(2)}) copy-start(f32[1,4,85]{2,1,0:T(4,128)} %param.42) | copy-start | bytes 4084
  21.4 15.4 %all-to-all-start.1 = ((f32[16,1,1024]{2,1,0:T(1,128)}), f32[16,1,1024]{2,1,0:T(1,128)S(1)}, u32[]{:S(2)}, u32[]{:S(2)}) async-start(f32[16,1,1024]{2,1,0:T(1,128)} %broadcast_select_fusion.37), calls=%async_computation.1 | async-start | bytes 131072 | tf_op jit(solution)/shard_map/all_to_all | solution.py:138
  37.6 8.7 %copy-start.62 = (f32[13]{0:T(128)S(1)}, f32[13]{0:T(128)}, u32[]{:S(2)}) copy-start(f32[13]{0:T(128)} %or_select_fusion.1) | copy-start | bytes 160
  37.6 8.7 %copy-start.63 = (f32[4]{0:T(128)S(1)}, f32[4]{0:T(128)}, u32[]{:S(2)}) copy-start(f32[4]{0:T(128)} %or_select_fusion.2) | copy-start | bytes 52
  46.2 1.2 collective-permute-start.2
  49.6 11.5 %all-to-all-start.2 = ((f32[16,1,1024]{2,1,0:T(1,128)}), f32[16,1,1024]{2,1,0:T(1,128)S(1)}, u32[]{:S(2)}, u32[]{:S(2)}) async-start(f32[16,1,1024]{2,1,0:T(1,128)} %broadcast_select_fusion.36), calls=%async_computation.2 | async-start | bytes 131072 | tf_op jit(solution)/shard_map/all_to_all | solution.py:138
  61.1 21.4 %copy-start.11 = (pred[16]{0:T(512)(128)(4,1)S(1)}, pred[16]{0:T(512)(128)(4,1)}, u32[]{:S(2)}) copy-start(pred[16]{0:T(512)(128)(4,1)} %copy-done.10) | copy-start | bytes 52
  61.1 21.4 %copy-start.13 = (pred[16]{0:T(512)(128)(4,1)S(1)}, pred[16]{0:T(512)(128)(4,1)}, u32[]{:S(2)}) copy-start(pred[16]{0:T(512)(128)(4,1)} %copy-done.12) | copy-start | bytes 52
  61.1 21.4 %copy-start.15 = (pred[16]{0:T(512)(128)(4,1)S(1)}, pred[16]{0:T(512)(128)(4,1)}, u32[]{:S(2)}) copy-start(pred[16]{0:T(512)(128)(4,1)} %copy-done.14) | copy-start | bytes 52
  61.1 21.4 %copy-start.17 = (pred[16]{0:T(512)(128)(4,1)S(1)}, pred[16]{0:T(512)(128)(4,1)}, u32[]{:S(2)}) copy-start(pred[16]{0:T(512)(128)(4,1)} %copy-done.16) | copy-start | bytes 52
  61.1 22.4 %copy-start.1 = (f32[64,340]{1,0:T(8,128)S(1)}, f32[64,340]{1,0:T(8,128)}, u32[]{:S(2)}) copy-start(f32[64,340]{1,0:T(8,128)} %mul.1178) | copy-start | bytes 261124
  65.2 14.3 %all-to-all-start.3 = ((f32[16,1,768]{2,1,0:T(1,128)}), f32[16,1,768]{2,1,0:T(1,128)S(1)}, u32[]{:S(2)}, u32[]{:S(2)}) async-start(f32[16,1,768]{2,1,0:T(1,128)} %broadcast_select_fusion.46), calls=%async_computation.3 | async-start | bytes 98304 | tf_op jit(solution)/shard_map/all_to_all | solution.py:138
  72.1 12.7 %copy-start.61 = (pred[4]{0:T(512)(128)(4,1)S(1)}, pred[4]{0:T(512)(128)(4,1)}, u32[]{:S(2)}) copy-start(pred[4]{0:T(512)(128)(4,1)} %copy-done.60) | copy-start | bytes 16
  72.2 12.9 %copy-start.59 = (pred[4]{0:T(512)(128)(4,1)S(1)}, pred[4]{0:T(512)(128)(4,1)}, u32[]{:S(2)}) copy-start(pred[4]{0:T(512)(128)(4,1)} %copy-done.58) | copy-start | bytes 16
  72.2 13.0 %copy-start.57 = (pred[4]{0:T(512)(128)(4,1)S(1)}, pred[4]{0:T(512)(128)(4,1)}, u32[]{:S(2)}) copy-start(pred[4]{0:T(512)(128)(4,1)} %copy-done.56) | copy-start | bytes 16
  72.2 13.2 %copy-start.55 = (pred[4]{0:T(512)(128)(4,1)S(1)}, pred[4]{0:T(512)(128)(4,1)}, u32[]{:S(2)}) copy-start(pred[4]{0:T(512)(128)(4,1)} %copy-done.54) | copy-start | bytes 16
  72.2 13.3 %copy-start.48 = (s32[85]{0:T(128)S(1)}, s32[85]{0:T(128)}, u32[]{:S(2)}) copy-start(s32[85]{0:T(128)} %copy-done.47) | copy-start | bytes 1024
  80.4 6.5 %copy-start.20 = (pred[16]{0:T(512)(128)(4,1)S(1)}, pred[16]{0:T(512)(128)(4,1)}, u32[]{:S(2)}) copy-start(pred[16]{0:T(512)(128)(4,1)} %get-tuple-element.693) | copy-start | bytes 52
  80.4 6.5 %copy-start.21 = (pred[16]{0:T(512)(128)(4,1)S(1)}, pred[16]{0:T(512)(128)(4,1)}, u32[]{:S(2)}) copy-start(pred[16]{0:T(512)(128)(4,1)} %get-tuple-element.867) | copy-start | bytes 52
  80.4 6.5 %copy-start.22 = (pred[16]{0:T(512)(128)(4,1)S(1)}, pred[16]{0:T(512)(128)(4,1)}, u32[]{:S(2)}) copy-start(pred[16]{0:T(512)(128)(4,1)} %get-tuple-element.868) | copy-start | bytes 52
  80.4 6.5 %copy-start.23 = (pred[16]{0:T(512)(128)(4,1)S(1)}, pred[16]{0:T(512)(128)(4,1)}, u32[]{:S(2)}) copy-start(pred[16]{0:T(512)(128)(4,1)} %get-tuple-element.869) | copy-start | bytes 52
  80.4 6.5 %copy-start.24 = (pred[16]{0:T(512)(128)(4,1)S(1)}, pred[16]{0:T(512)(128)(4,1)}, u32[]{:S(2)}) copy-start(pred[16]{0:T(512)(128)(4,1)} %get-tuple-element.870) | copy-start | bytes 52
  80.4 6.5 %copy-start.25 = (pred[16]{0:T(512)(128)(4,1)S(1)}, pred[16]{0:T(512)(128)(4,1)}, u32[]{:S(2)}) copy-start(pred[16]{0:T(512)(128)(4,1)} %get-tuple-element.871) | copy-start | bytes 52
  81.5 18.0 %copy-start.18 = (pred[13]{0:T(512)(128)(4,1)S(1)}, pred[13]{0:T(512)(128)(4,1)}, u32[]{:S(2)}) copy-start(pred[13]{0:T(512)(128)(4,1)} %iota_compare_fusion.12) | copy-start | bytes 43
  81.5 18.0 %copy-start.19 = (pred[13]{0:T(512)(128)(4,1)S(1)}, pred[13]{0:T(512)(128)(4,1)}, u32[]{:S(2)}) copy-start(pred[13]{0:T(512)(128)(4,1)} %iota_compare_fusion.13) | copy-start | bytes 43
  82.5 17.1 %copy-start.28 = (pred[256]{0:T(512)(128)(4,1)S(1)}, pred[256]{0:T(512)(128)(4,1)}, u32[]{:S(2)}) copy-start(pred[256]{0:T(512)(128)(4,1)} %iota_compare_fusion.10) | copy-start | bytes 772
  82.5 17.1 %copy-start.29 = (pred[256]{0:T(512)(128)(4,1)S(1)}, pred[256]{0:T(512)(128)(4,1)}, u32[]{:S(2)}) copy-start(pred[256]{0:T(512)(128)(4,1)} %iota_compare_fusion.11) | copy-start | bytes 772
  84.8 1.5 collective-permute-start.3
  87.9 11.2 %all-to-all-start.4 = ((f32[16,1,1026]{2,1,0:T(1,128)}), f32[16,1,1026]{2,1,0:T(1,128)S(1)}, u32[]{:S(2)}, u32[]{:S(2)}) async-start(f32[16,1,1026]{2,1,0:T(1,128)} %broadcast_select_fusion.22), calls=%async_computation.4 | async-start | bytes 147456 | tf_op jit(solution)/shard_map/all_to_all | solution.py:138
  104.1 1.2 collective-permute-start
  106.9 11.0 %all-to-all-start = ((f32[16,1,1028]{2,1,0:T(1,128)}), f32[16,1,1028]{2,1,0:T(1,128)S(1)}, u32[]{:S(2)}, u32[]{:S(2)}) async-start(f32[16,1,1028]{2,1,0:T(1,128)} %broadcast_select_fusion.81), calls=%async_computation | async-start | bytes 147456 | tf_op jit(solution)/shard_map/while/body/eval_jaxpr/all_to_all | solution.py:138
  122.9 1.2 collective-permute-start
  125.7 11.0 %all-to-all-start = ((f32[16,1,1028]{2,1,0:T(1,128)}), f32[16,1,1028]{2,1,0:T(1,128)S(1)}, u32[]{:S(2)}, u32[]{:S(2)}) async-start(f32[16,1,1028]{2,1,0:T(1,128)} %broadcast_select_fusion.81), calls=%async_computation | async-start | bytes 147456 | tf_op jit(solution)/shard_map/while/body/eval_jaxpr/all_to_all | solution.py:138
  141.8 1.2 collective-permute-start
  144.6 11.0 %all-to-all-start = ((f32[16,1,1028]{2,1,0:T(1,128)}), f32[16,1,1028]{2,1,0:T(1,128)S(1)}, u32[]{:S(2)}, u32[]{:S(2)}) async-start(f32[16,1,1028]{2,1,0:T(1,128)} %broadcast_select_fusion.81), calls=%async_computation | async-start | bytes 147456 | tf_op jit(solution)/shard_map/while/body/eval_jaxpr/all_to_all | solution.py:138
  (13 other events, 47.1 us)

commit v6 on v4

--- a/solution.py
+++ b/solution.py
@@ -114,7 +114,7 @@
     return values, scalars
 
 
-def plane_exchange(pieces, width, scalars):
+def plane_exchange(pieces, width, scalars, tie=None):
     count_x, count_y = lax.axis_size("hx"), lax.axis_size("hy")
     me_x, me_y = lax.axis_index("hx"), lax.axis_index("hy")
     rows = []
@@ -131,7 +131,12 @@
     off_y = peers % count_y - me_y
     near = (jnp.abs(off_x) <= 1) & (jnp.abs(off_y) <= 1)
     code_of = jnp.where(near, (off_x + 1) * 3 + (off_y + 1), 4)
-    send = jnp.take(table, code_of, axis=0)
+    send = jnp.broadcast_to(table[4][None, :], (count_x * count_y, table.shape[1]))
+    for code in range(9):
+        if code != 4:
+            send = jnp.where(code_of[:, None] == code, table[code][None, :], send)
+    if tie is not None:
+        send, tie = lax.optimization_barrier((send, tie))
     got = lax.all_to_all(send, ("hx", "hy"), 0, 0, tiled=True)
     received = {}
     for offset in pieces:
@@ -143,10 +148,10 @@
     total = None
     if scalars is not None:
         total = jnp.sum(got[:, width:], axis=0)
-    return received, total
-
-
-def face_sums(values, scalars=None):
+    return received, total, tie
+
+
+def face_sums(values, scalars=None, tie=None):
     values, scalars = torso_stage(values, scalars)
     depth, first, second = values.shape
     pieces = {
@@ -159,15 +164,27 @@
         (-1, 1): values[:, 0, -1],
         (-1, -1): values[:, 0, 0],
     }
-    got, total = plane_exchange(pieces, depth * second, scalars)
+    got, total, tie = plane_exchange(pieces, depth * second, scalars, tie)
+    at_low = ((0, 0), (0, first - 1))
+    at_high = ((0, 0), (first - 1, 0))
     low_second = got[(0, -1)].reshape(depth, first)
-    low_second = low_second.at[:, 0].add(got[(-1, -1)]).at[:, -1].add(got[(1, -1)])
+    low_second = low_second + jnp.pad(got[(-1, -1)][:, None], at_low)
+    low_second = low_second + jnp.pad(got[(1, -1)][:, None], at_high)
     high_second = got[(0, 1)].reshape(depth, first)
-    high_second = high_second.at[:, 0].add(got[(-1, 1)]).at[:, -1].add(got[(1, 1)])
-    values = values.at[:, 0, :].add(got[(-1, 0)].reshape(depth, second))
-    values = values.at[:, -1, :].add(got[(1, 0)].reshape(depth, second))
-    values = values.at[:, :, 0].add(low_second).at[:, :, -1].add(high_second)
-    return values, total
+    high_second = high_second + jnp.pad(got[(-1, 1)][:, None], at_low)
+    high_second = high_second + jnp.pad(got[(1, 1)][:, None], at_high)
+    along_first = jnp.pad(got[(-1, 0)].reshape(depth, 1, second), ((0, 0), (0, first - 1), (0, 0)))
+    along_first = along_first + jnp.pad(
+        got[(1, 0)].reshape(depth, 1, second), ((0, 0), (first - 1, 0), (0, 0))
+    )
+    along_second = jnp.pad(low_second[:, :, None], ((0, 0), (0, 0), (0, second - 1)))
+    along_second = along_second + jnp.pad(
+        high_second[:, :, None], ((0, 0), (0, 0), (second - 1, 0))
+    )
+    summed = values + along_first + along_second
+    if tie is None:
+        return summed, total
+    return summed, total, tie
 
 
 def rim_plane(plane, rim):
@@ -182,7 +199,7 @@
         (-1, 1): plane[:rim, -rim:].reshape(-1),
         (-1, -1): plane[:rim, :rim].reshape(-1),
     }
-    got, _ = plane_exchange(pieces, rim * second, None)
+    got, _, _ = plane_exchange(pieces, rim * second, None)
     top = jnp.concatenate(
         [got[(-1, -1)].reshape(rim, rim), got[(-1, 0)].reshape(rim, second), got[(-1, 1)].reshape(rim, rim)], 1
     )
@@ -265,11 +282,11 @@
     gate_flat = gating.reshape(gating.shape[0], -1)
     mats = element_matrices(first_len, second_len)
     for repeat in range(STEPS):
-        volts = potential.reshape(1, -1)
+        diffusion, _, tied = face_sums(local_products(potential, heart_cond, mats), tie=potential)
+        volts = tied.reshape(1, -1)
         inf_value = jax.nn.sigmoid((volts - half_nodes) * slope_nodes)
         gate_flat = inf_value + (gate_flat - inf_value) * decay_nodes
         current = jnp.sum(cond_nodes * gate_flat * (volts - reversal[:, None]), 0)
-        diffusion, _ = face_sums(local_products(potential, heart_cond, mats))
         potential = potential - time_step * (
             diffusion / heart_mass + current.reshape(potential.shape)
         )

time: 177 us -> 156 us (0.88)
  local copies, waits for them, and re-layouts: 30.2 us -> 19.4 us
  other arithmetic: 42.5 us -> 33.8 us
  waiting for transfers between devices: 45.2 us -> 40.8 us
  starting transfers between devices: 33.6 us -> 36.6 us
    another operation x19 -> x0, other arithmetic: 12.1 us -> none
    select_n x9 -> x7, other arithmetic: 1.64 us -> 6.33 us  [plane_exchange(): send = jnp.where(code_of[:, None] == code, table[code][None, :], send)]
    gather x7 -> x0, local copies, waits for them, and re-layouts: 4.6 us -> none  [plane_exchange(): send = jnp.take(table, code_of, axis=0)]
    all_to_all x7, waiting for transfers between devices: 41.8 us -> 37.5 us  [plane_exchange(): got = lax.all_to_all(send, ('hx', 'hy'), 0, 0, tiled=True)]
    scatter-add x48 -> x0, local copies, waits for them, and re-layouts: 4.15 us -> none  [the longest x12 2.55 us: face_sums(): values = values.at[:, :, 0].add(low_second).at[:, :, -1].add(high_second)]
    select_n x5 -> x0, local copies, waits for them, and re-layouts: 3.47 us -> none  [plane_exchange(): send = jnp.take(table, code_of, axis=0)]
    another operation x63 -> x0, local copies, waits for them, and re-layouts: 2.84 us -> none  [the longest x50 1.47 us: plane_exchange(): table = jnp.stack(rows)]
    select_n x44 -> x37, other arithmetic: 0.5 us -> 3.21 us  [plane_exchange(): received[offset] = jnp.where(valid, row[:pieces[offset].shape[0]], 0.0)]
  transfers between devices with their start and end apart: 13 -> 13, of which waited for: 10 -> 8; matrix products, arithmetic and copies ran while one was open for 13% -> 14% of each run, Pallas kernels for 0% -> 0%
where the time goes in v6:
time: 156 us; the launch traced here: 155 us
  waiting for transfers between devices  40.8 us (26%)
  starting transfers between devices  36.6 us (23%)
  other arithmetic  33.8 us (22%)
  matrix products  21.6 us (14%)
  local copies, waits for them, and re-layouts  19.4 us (12%)
  between operations  2.11 us (1%)
    all_to_all x7, waiting for transfers between devices, plane_exchange(): got = lax.all_to_all(send, ('hx', 'hy'), 0, 0, tiled=True)  37.5 us
    all_to_all x7, starting transfers between devices, plane_exchange(): got = lax.all_to_all(send, ('hx', 'hy'), 0, 0, tiled=True)  35.5 us
    reduce_sum x2, other arithmetic, per_device(): current = jnp.sum(cond_nodes * gate_flat * (volts - reversal[:, None]), 0)  15.4 us
    select_n x7, other arithmetic, plane_exchange(): send = jnp.where(code_of[:, None] == code, table[code][None, :], send)  6.33 us
    dot_general x6, matrix products, local_products(): jnp.dot(flat_k, lanes_m, precision=HIGH)  4.55 us
    dot_general x6, matrix products, local_products(): jnp.dot(flat_m, lanes_k, precision=HIGH)  4.52 us
    select_n x44, local copies, waits for them, and re-layouts, plane_exchange(): received[offset] = jnp.where(valid, row[:pieces[offset].shape[0]], 0.0)  3.77 us
    ppermute x6, waiting for transfers between devices, torso_stage(): got = lax.ppermute(face, 'torso', [(0, 1), (1, 0)])  3.35 us
  transfers between devices with their start and end apart: 13, of which 8 were waited for; matrix products, arithmetic and copies ran while one was open for 14% of the time, Pallas kernels for 0%

profile of v6, /device:TPU:0, one launch (start us, length us, event | category | flops | bytes accessed | tf_op | source)
XLA Modules:
  0.0 155.2 jit_solution(4795676317746590761)
XLA Ops:
  0.7 0.8 copy.209
  3.0 0.7 mul.1109
  3.8 0.9 select_select_fusion.6
  5.7 0.4 fusion.374
  6.8 0.6 collective-permute-start.1
  7.5 0.6 slice_bitcast_fusion.22
  8.1 0.6 slice_bitcast_fusion.15
  8.7 0.7 broadcast_compare_fusion.11
  9.4 0.6 slice_bitcast_fusion.9
  10.1 0.6 or_select_fusion.1
  10.7 0.5 or_select_fusion.2
  11.9 0.7 all_to_all.31
  12.6 7.9 %all-to-all-start.1 = ((f32[16,1,1024]{2,1,0:T(1,128)}), f32[16,1,1024]{2,1,0:T(1,128)S(1)}, u32[]{:S(2)}, u32[]{:S(2)}) async-start(f32[16,1,1024]{2,1,0:T(1,128)} %all_to_all.31), calls=%async_computation.1 | async-start | bytes 131072 | tf_op jit(solution)/shard_map/all_to_all | solution.py:140
  20.6 7.5 %multiply_reduce_fusion.1 = (f32[4,13,256]{2,0,1:T(4,128)S(1)}, f32[40,4,13,256]{3,1,2,0:T(4,128)S(1)}) fusion(f32[40]{0:T(128)} %param.39, f32[4,13,256]{2,0,1:T(4,128)S(1)} %copy-done, f32[40]{0:T(128)} %get-tuple-element.878, f32[40]{0:T(128)} %get-tuple-element.877, f32[40]{0:T(128)} %get-tuple-element.879, f32[40]{0:T(128)} %get-tuple-element.880, ...), kind=kLoop, calls=%fused_computation.397 | loop fusion | flops 12766208 | bytes 4435616 | tf_op jit(solution)/shard_map/reduce_sum | solution.py:289
  28.1 0.6 broadcast_select_fusion.37
  28.8 0.7 fusion.579
  29.8 0.7 copy.207
  30.5 0.7 fusion.582
  31.5 0.7 copy.204
  32.3 0.9 fusion.398
  33.2 1.0 fusion.430
  34.1 1.0 fusion.429
  35.6 1.0 convolution_add_fusion.6
  37.3 0.9 fusion.505
  38.5 0.7 broadcast_multiply_fusion.1
  39.3 0.7 mul.1178
  40.6 0.8 select_select_fusion.9
  41.5 0.7 copy.213
  42.2 6.8 %all-to-all-start.2 = ((f32[16,1,1024]{2,1,0:T(1,128)}), f32[16,1,1024]{2,1,0:T(1,128)}, u32[]{:S(2)}, u32[]{:S(2)}) async-start(f32[16,1,1024]{2,1,0:T(1,128)} %copy.213), calls=%async_computation.2 | async-start | bytes 131072 | tf_op jit(solution)/shard_map/all_to_all | solution.py:140
  48.9 7.9 %multiply_reduce_fusion = (f32[4,13,256]{2,0,1:T(4,128)S(1)}, f32[40,4,13,256]{3,1,2,0:T(4,128)}) fusion(f32[4,13,256]{2,0,1:T(4,128)S(1)} %copy.220, f32[40]{0:T(128)} %param.39, f32[40]{0:T(128)} %get-tuple-element.878, f32[40]{0:T(128)} %get-tuple-element.877, f32[40]{0:T(128)} %get-tuple-element.879, f32[40]{0:T(128)} %get-tuple-element.880, ...), kind=kLoop, calls=%fused_computation.395 | loop fusion | flops 12766208 | bytes 4435616 | tf_op jit(solution)/shard_map/reduce_sum | solution.py:289
  56.9 0.8 broadcast_select_fusion.36
  59.6 1.5 broadcast_select_fusion.30
  61.1 6.8 %all-to-all-start.3 = ((f32[16,1,768]{2,1,0:T(1,128)}), f32[16,1,768]{2,1,0:T(1,128)S(1)}, u32[]{:S(2)}, u32[]{:S(2)}) async-start(f32[16,1,768]{2,1,0:T(1,128)} %broadcast_select_fusion.30), calls=%async_computation.3 | async-start | bytes 98304 | tf_op jit(solution)/shard_map/all_to_all | solution.py:140
  68.1 7.4 %all-to-all-done.3 = f32[16,1,768]{2,1,0:T(1,128)S(1)} async-done(((f32[16,1,768]{2,1,0:T(1,128)}), f32[16,1,768]{2,1,0:T(1,128)S(1)}, u32[]{:S(2)}, u32[]{:S(2)}) %all-to-all-start.3) | async-done | bytes 49184 | tf_op jit(solution)/shard_map/all_to_all | solution.py:140
  76.3 1.0 multiply_bitcast_fusion.3
  77.3 1.0 fusion.428
  79.4 0.4 fusion.372
  81.4 0.7 copy.232
  82.8 1.0 broadcast_select_fusion.22
  83.8 3.5 %all-to-all-start.4 = ((f32[16,1,1026]{2,1,0:T(1,128)}), f32[16,1,1026]{2,1,0:T(1,128)S(1)}, u32[]{:S(2)}, u32[]{:S(2)}) async-start(f32[16,1,1026]{2,1,0:T(1,128)} %broadcast_select_fusion.22), calls=%async_computation.4 | async-start | bytes 147456 | tf_op jit(solution)/shard_map/all_to_all | solution.py:140
  87.3 7.6 %all-to-all-done.4 = f32[16,1,1026]{2,1,0:T(1,128)S(1)} async-done(((f32[16,1,1026]{2,1,0:T(1,128)}), f32[16,1,1026]{2,1,0:T(1,128)S(1)}, u32[]{:S(2)}, u32[]{:S(2)}) %all-to-all-start.4) | async-done | bytes 65696 | tf_op jit(solution)/shard_map/all_to_all | solution.py:140
  96.2 58.4 %while.33 = (s32[]{:T(128)}, f32[4,13,256]{2,1,0:T(8,128)S(1)}, f32[4,13,256]{2,1,0:T(8,128)S(1)}, f32[4,13,256]{2,1,0:T(8,128)S(1)}, f32[4,13,256]{2,1,0:T(8,12...) while((s32[]{:T(128)}, f32[4,13,256]{2,1,0:T(8,128)S(1)}, ...), condition=%wide.region_7.8_spmd.clone.clone.clone, body=%wide.region_4.7_spmd.clone.clone.clone.sunk | while | flops 219513728 | bytes 3742835 | solution.py:359
  97.2 1.1 fusion.803
  98.3 1.1 fusion.805
  99.4 0.6 fusion.806
  100.7 1.1 collective-permute-done
  102.4 1.0 broadcast_select_fusion.66
  103.4 3.5 %all-to-all-start = ((f32[16,1,1028]{2,1,0:T(1,128)}), f32[16,1,1028]{2,1,0:T(1,128)S(1)}, u32[]{:S(2)}, u32[]{:S(2)}) async-start(f32[16,1,1028]{2,1,0:T(1,128)} %broadcast_select_fusion.66), calls=%async_computation | async-start | bytes 147456 | tf_op jit(solution)/shard_map/while/body/eval_jaxpr/all_to_all | solution.py:140
  106.9 7.5 %all-to-all-done = f32[16,1,1028]{2,1,0:T(1,128)S(1)} async-done(((f32[16,1,1028]{2,1,0:T(1,128)}), f32[16,1,1028]{2,1,0:T(1,128)S(1)}, u32[]{:S(2)}, u32[]{:S(2)}) %all-to-all-start) | async-done | bytes 65824 | tf_op jit(solution)/shard_map/while/body/eval_jaxpr/all_to_all | solution.py:140
  116.7 1.1 fusion.803
  117.8 1.1 fusion.805
  118.9 0.6 fusion.806
  120.2 1.1 collective-permute-done
  121.8 1.0 broadcast_select_fusion.66
  122.8 3.5 %all-to-all-start = ((f32[16,1,1028]{2,1,0:T(1,128)}), f32[16,1,1028]{2,1,0:T(1,128)S(1)}, u32[]{:S(2)}, u32[]{:S(2)}) async-start(f32[16,1,1028]{2,1,0:T(1,128)} %broadcast_select_fusion.66), calls=%async_computation | async-start | bytes 147456 | tf_op jit(solution)/shard_map/while/body/eval_jaxpr/all_to_all | solution.py:140
  126.4 7.5 %all-to-all-done = f32[16,1,1028]{2,1,0:T(1,128)S(1)} async-done(((f32[16,1,1028]{2,1,0:T(1,128)}), f32[16,1,1028]{2,1,0:T(1,128)S(1)}, u32[]{:S(2)}, u32[]{:S(2)}) %all-to-all-start) | async-done | bytes 65824 | tf_op jit(solution)/shard_map/while/body/eval_jaxpr/all_to_all | solution.py:140
  136.2 1.1 fusion.803
  137.3 1.1 fusion.805
  138.4 0.6 fusion.806
  139.6 1.1 collective-permute-done
  141.3 1.0 broadcast_select_fusion.66
  142.3 3.5 %all-to-all-start = ((f32[16,1,1028]{2,1,0:T(1,128)}), f32[16,1,1028]{2,1,0:T(1,128)S(1)}, u32[]{:S(2)}, u32[]{:S(2)}) async-start(f32[16,1,1028]{2,1,0:T(1,128)} %broadcast_select_fusion.66), calls=%async_computation | async-start | bytes 147456 | tf_op jit(solution)/shard_map/while/body/eval_jaxpr/all_to_all | solution.py:140
  145.9 7.5 %all-to-all-done = f32[16,1,1028]{2,1,0:T(1,128)S(1)} async-done(((f32[16,1,1028]{2,1,0:T(1,128)}), f32[16,1,1028]{2,1,0:T(1,128)S(1)}, u32[]{:S(2)}, u32[]{:S(2)}) %all-to-all-start) | async-done | bytes 65824 | tf_op jit(solution)/shard_map/while/body/eval_jaxpr/all_to_all | solution.py:140
  154.6 0.7 copy.233
  (436 shorter events, 23.5 us)
Async XLA Ops:
  0.7 4.0 %copy-start.39 = (pred[4]{0:T(512)(128)(4,1)}, pred[4]{0:T(512)(128)(4,1)S(1)}, u32[]{:S(2)}) copy-start(pred[4]{0:T(512)(128)(4,1)S(1)} %iota_compare_fusion.2) | copy-start | bytes 16
  0.7 4.0 %copy-start.41 = (pred[4]{0:T(512)(128)(4,1)}, pred[4]{0:T(512)(128)(4,1)S(1)}, u32[]{:S(2)}) copy-start(pred[4]{0:T(512)(128)(4,1)S(1)} %iota_compare_fusion.3) | copy-start | bytes 16
  0.7 4.0 %copy-start.43 = (pred[4]{0:T(512)(128)(4,1)}, pred[4]{0:T(512)(128)(4,1)S(1)}, u32[]{:S(2)}) copy-start(pred[4]{0:T(512)(128)(4,1)S(1)} %iota_compare_fusion.4) | copy-start | bytes 16
  0.7 4.0 %copy-start.45 = (pred[4]{0:T(512)(128)(4,1)}, pred[4]{0:T(512)(128)(4,1)S(1)}, u32[]{:S(2)}) copy-start(pred[4]{0:T(512)(128)(4,1)S(1)} %iota_compare_fusion.5) | copy-start | bytes 16
  0.7 4.2 %copy-start.32 = (s32[85]{0:T(128)}, s32[85]{0:T(128)S(1)}, u32[]{:S(2)}) copy-start(s32[85]{0:T(128)S(1)} %iota_multiply_fusion) | copy-start | bytes 1024
  1.7 35.6 %copy-start.5 = (s32[16]{0:T(128)}, s32[16]{0:T(128)S(1)}, u32[]{:S(2)}) copy-start(s32[16]{0:T(128)S(1)} %iota.1005) | copy-start | bytes 196
  1.9 4.6 %copy-start.7 = (pred[16]{0:T(512)(128)(4,1)}, pred[16]{0:T(512)(128)(4,1)S(1)}, u32[]{:S(2)}) copy-start(pred[16]{0:T(512)(128)(4,1)S(1)} %iota.1014) | copy-start | bytes 52
  2.0 4.5 %copy-start.9 = (pred[16]{0:T(512)(128)(4,1)}, pred[16]{0:T(512)(128)(4,1)S(1)}, u32[]{:S(2)}) copy-start(pred[16]{0:T(512)(128)(4,1)S(1)} %iota.1011) | copy-start | bytes 52
  2.2 4.3 %copy-start.11 = (pred[16]{0:T(512)(128)(4,1)}, pred[16]{0:T(512)(128)(4,1)S(1)}, u32[]{:S(2)}) copy-start(pred[16]{0:T(512)(128)(4,1)S(1)} %iota.1008) | copy-start | bytes 52
  2.4 4.2 %copy-start.13 = (pred[16]{0:T(512)(128)(4,1)}, pred[16]{0:T(512)(128)(4,1)S(1)}, u32[]{:S(2)}) copy-start(pred[16]{0:T(512)(128)(4,1)S(1)} %iota.1000) | copy-start | bytes 52
  4.7 2.7 %copy-start.37 = (f32[3,40]{1,0:T(4,128)S(1)}, f32[3,40]{1,0:T(4,128)}, u32[]{:S(2)}) copy-start(f32[3,40]{1,0:T(4,128)} %param.38) | copy-start | bytes 1444
  4.7 3.3 %copy-start.35 = (f32[3,40]{1,0:T(4,128)S(1)}, f32[3,40]{1,0:T(4,128)}, u32[]{:S(2)}) copy-start(f32[3,40]{1,0:T(4,128)} %param.37) | copy-start | bytes 1444
  4.8 3.3 %copy-start.34 = (f32[4,40]{1,0:T(4,128)S(1)}, f32[4,40]{1,0:T(4,128)}, u32[]{:S(2)}) copy-start(f32[4,40]{1,0:T(4,128)} %param.40) | copy-start | bytes 1924
  4.8 3.3 %copy-start.36 = (f32[3,40]{1,0:T(4,128)S(1)}, f32[3,40]{1,0:T(4,128)}, u32[]{:S(2)}) copy-start(f32[3,40]{1,0:T(4,128)} %param.35) | copy-start | bytes 1444
  4.8 3.9 %copy-start.3 = (s32[4,13,256]{2,0,1:T(4,128)S(1)}, s32[4,13,256]{2,0,1:T(4,128)}, u32[]{:S(2)}) copy-start(s32[4,13,256]{2,0,1:T(4,128)} %param.34) | copy-start | bytes 159748
  4.8 3.9 %copy-start.4 = (s32[4,13,256]{2,0,1:T(4,128)S(1)}, s32[4,13,256]{2,0,1:T(4,128)}, u32[]{:S(2)}) copy-start(s32[4,13,256]{2,0,1:T(4,128)} %param.33) | copy-start | bytes 159748
  4.8 4.6 %copy-start.38 = (f32[3,40]{1,0:T(4,128)S(1)}, f32[3,40]{1,0:T(4,128)}, u32[]{:S(2)}) copy-start(f32[3,40]{1,0:T(4,128)} %param.36) | copy-start | bytes 1444
  4.9 15.7 %copy-start = (f32[4,13,256]{2,0,1:T(4,128)S(1)}, f32[4,13,256]{2,0,1:T(4,128)}, u32[]{:S(2)}) copy-start(f32[4,13,256]{2,0,1:T(4,128)} %param.31) | copy-start | bytes 159748
  6.8 4.5 %collective-permute-start.1 = (f32[13,256]{1,0:T(8,128)S(1)}, f32[13,256]{1,0:T(8,128)S(1)}, u32[]{:S(2)}, u32[]{:S(2)}) collective-permute-start(f32[13,256]{1,0:T(8,128)S(1)} %fusion.499), channel_id=1, source_target_pairs={{0,1},{1,0},{2,3},{3,2},{4,5},{5,4},{6,7},{7,6},{8,9},{9,8},{10,11... | collective-permute-start | bytes 39944 | tf_op jit(solution)/shard_map/ppermute | solution.py:107
  7.3 13.2 %copy-start.15 = (pred[16]{0:T(512)(128)(4,1)}, pred[16]{0:T(512)(128)(4,1)S(1)}, u32[]{:S(2)}) copy-start(pred[16]{0:T(512)(128)(4,1)S(1)} %get-tuple-element.699) | copy-start | bytes 52
  7.4 13.1 %copy-start.17 = (pred[16]{0:T(512)(128)(4,1)}, pred[16]{0:T(512)(128)(4,1)S(1)}, u32[]{:S(2)}) copy-start(pred[16]{0:T(512)(128)(4,1)S(1)} %get-tuple-element.863) | copy-start | bytes 52
  7.4 13.1 %copy-start.19 = (pred[16]{0:T(512)(128)(4,1)}, pred[16]{0:T(512)(128)(4,1)S(1)}, u32[]{:S(2)}) copy-start(pred[16]{0:T(512)(128)(4,1)S(1)} %get-tuple-element.864) | copy-start | bytes 52
  7.4 13.1 %copy-start.21 = (pred[16]{0:T(512)(128)(4,1)}, pred[16]{0:T(512)(128)(4,1)S(1)}, u32[]{:S(2)}) copy-start(pred[16]{0:T(512)(128)(4,1)S(1)} %get-tuple-element.865) | copy-start | bytes 52
  7.4 13.1 %copy-start.23 = (pred[16]{0:T(512)(128)(4,1)}, pred[16]{0:T(512)(128)(4,1)S(1)}, u32[]{:S(2)}) copy-start(pred[16]{0:T(512)(128)(4,1)S(1)} %get-tuple-element.866) | copy-start | bytes 52
  7.4 13.1 %copy-start.25 = (pred[16]{0:T(512)(128)(4,1)}, pred[16]{0:T(512)(128)(4,1)S(1)}, u32[]{:S(2)}) copy-start(pred[16]{0:T(512)(128)(4,1)S(1)} %get-tuple-element.867) | copy-start | bytes 52
  7.4 13.1 %copy-start.27 = (pred[16]{0:T(512)(128)(4,1)}, pred[16]{0:T(512)(128)(4,1)S(1)}, u32[]{:S(2)}) copy-start(pred[16]{0:T(512)(128)(4,1)S(1)} %get-tuple-element.868) | copy-start | bytes 52
  7.5 13.1 %copy-start.29 = (pred[16]{0:T(512)(128)(4,1)}, pred[16]{0:T(512)(128)(4,1)S(1)}, u32[]{:S(2)}) copy-start(pred[16]{0:T(512)(128)(4,1)S(1)} %get-tuple-element.869) | copy-start | bytes 52
  8.7 11.9 %copy-start.31 = (f32[40]{0:T(128)}, f32[40]{0:T(128)S(1)}, u32[]{:S(2)}) copy-start(f32[40]{0:T(128)S(1)} %get-tuple-element.838) | copy-start | bytes 484
  12.6 15.5 %all-to-all-start.1 = ((f32[16,1,1024]{2,1,0:T(1,128)}), f32[16,1,1024]{2,1,0:T(1,128)S(1)}, u32[]{:S(2)}, u32[]{:S(2)}) async-start(f32[16,1,1024]{2,1,0:T(1,128)} %all_to_all.31), calls=%async_computation.1 | async-start | bytes 131072 | tf_op jit(solution)/shard_map/all_to_all | solution.py:140
  28.1 11.1 %copy-start.2 = (f32[1,4,85]{2,1,0:T(4,128)S(1)}, f32[1,4,85]{2,1,0:T(4,128)}, u32[]{:S(2)}) copy-start(f32[1,4,85]{2,1,0:T(4,128)} %param.42) | copy-start | bytes 4084
  38.2 1.8 %collective-permute-start.2 = (f32[13,256]{1,0:T(8,128)S(1)}, f32[13,256]{1,0:T(8,128)S(1)}, u32[]{:S(2)}, u32[]{:S(2)}) collective-permute-start(f32[13,256]{1,0:T(8,128)S(1)} %fusion.495), channel_id=1, source_target_pairs={{0,1},{1,0},{2,3},{3,2},{4,5},{5,4},{6,7},{7,6},{8,9},{9,8},{10,11... | collective-permute-start | bytes 39944 | tf_op jit(solution)/shard_map/ppermute | solution.py:107
  42.2 14.7 %all-to-all-start.2 = ((f32[16,1,1024]{2,1,0:T(1,128)}), f32[16,1,1024]{2,1,0:T(1,128)}, u32[]{:S(2)}, u32[]{:S(2)}) async-start(f32[16,1,1024]{2,1,0:T(1,128)} %copy.213), calls=%async_computation.2 | async-start | bytes 131072 | tf_op jit(solution)/shard_map/all_to_all | solution.py:140
  56.9 21.5 %copy-start.6 = (s32[16]{0:T(128)S(1)}, s32[16]{0:T(128)}, u32[]{:S(2)}) copy-start(s32[16]{0:T(128)} %copy-done.5) | copy-start | bytes 196
  56.9 21.5 %copy-start.8 = (pred[16]{0:T(512)(128)(4,1)S(1)}, pred[16]{0:T(512)(128)(4,1)}, u32[]{:S(2)}) copy-start(pred[16]{0:T(512)(128)(4,1)} %copy-done.7) | copy-start | bytes 52
  56.9 21.5 %copy-start.10 = (pred[16]{0:T(512)(128)(4,1)S(1)}, pred[16]{0:T(512)(128)(4,1)}, u32[]{:S(2)}) copy-start(pred[16]{0:T(512)(128)(4,1)} %copy-done.9) | copy-start | bytes 52
  56.9 21.5 %copy-start.12 = (pred[16]{0:T(512)(128)(4,1)S(1)}, pred[16]{0:T(512)(128)(4,1)}, u32[]{:S(2)}) copy-start(pred[16]{0:T(512)(128)(4,1)} %copy-done.11) | copy-start | bytes 52
  56.9 21.5 %copy-start.14 = (pred[16]{0:T(512)(128)(4,1)S(1)}, pred[16]{0:T(512)(128)(4,1)}, u32[]{:S(2)}) copy-start(pred[16]{0:T(512)(128)(4,1)} %copy-done.13) | copy-start | bytes 52
  56.9 22.5 %copy-start.1 = (f32[64,340]{1,0:T(8,128)S(1)}, f32[64,340]{1,0:T(8,128)}, u32[]{:S(2)}) copy-start(f32[64,340]{1,0:T(8,128)} %mul.1178) | copy-start | bytes 261124
  61.1 14.3 %all-to-all-start.3 = ((f32[16,1,768]{2,1,0:T(1,128)}), f32[16,1,768]{2,1,0:T(1,128)S(1)}, u32[]{:S(2)}, u32[]{:S(2)}) async-start(f32[16,1,768]{2,1,0:T(1,128)} %broadcast_select_fusion.30), calls=%async_computation.3 | async-start | bytes 98304 | tf_op jit(solution)/shard_map/all_to_all | solution.py:140
  68.0 12.7 %copy-start.46 = (pred[4]{0:T(512)(128)(4,1)S(1)}, pred[4]{0:T(512)(128)(4,1)}, u32[]{:S(2)}) copy-start(pred[4]{0:T(512)(128)(4,1)} %copy-done.45) | copy-start | bytes 16
  68.0 12.8 %copy-start.44 = (pred[4]{0:T(512)(128)(4,1)S(1)}, pred[4]{0:T(512)(128)(4,1)}, u32[]{:S(2)}) copy-start(pred[4]{0:T(512)(128)(4,1)} %copy-done.43) | copy-start | bytes 16
  68.0 13.0 %copy-start.42 = (pred[4]{0:T(512)(128)(4,1)S(1)}, pred[4]{0:T(512)(128)(4,1)}, u32[]{:S(2)}) copy-start(pred[4]{0:T(512)(128)(4,1)} %copy-done.41) | copy-start | bytes 16
  68.0 13.1 %copy-start.33 = (s32[85]{0:T(128)S(1)}, s32[85]{0:T(128)}, u32[]{:S(2)}) copy-start(s32[85]{0:T(128)} %copy-done.32) | copy-start | bytes 1024
  68.0 13.2 %copy-start.40 = (pred[4]{0:T(512)(128)(4,1)S(1)}, pred[4]{0:T(512)(128)(4,1)}, u32[]{:S(2)}) copy-start(pred[4]{0:T(512)(128)(4,1)} %copy-done.39) | copy-start | bytes 16
  76.3 6.5 %copy-start.16 = (pred[16]{0:T(512)(128)(4,1)S(1)}, pred[16]{0:T(512)(128)(4,1)}, u32[]{:S(2)}) copy-start(pred[16]{0:T(512)(128)(4,1)} %copy-done.15) | copy-start | bytes 52
  76.3 6.5 %copy-start.18 = (pred[16]{0:T(512)(128)(4,1)S(1)}, pred[16]{0:T(512)(128)(4,1)}, u32[]{:S(2)}) copy-start(pred[16]{0:T(512)(128)(4,1)} %copy-done.17) | copy-start | bytes 52
  76.3 6.5 %copy-start.20 = (pred[16]{0:T(512)(128)(4,1)S(1)}, pred[16]{0:T(512)(128)(4,1)}, u32[]{:S(2)}) copy-start(pred[16]{0:T(512)(128)(4,1)} %copy-done.19) | copy-start | bytes 52
  76.3 6.5 %copy-start.22 = (pred[16]{0:T(512)(128)(4,1)S(1)}, pred[16]{0:T(512)(128)(4,1)}, u32[]{:S(2)}) copy-start(pred[16]{0:T(512)(128)(4,1)} %copy-done.21) | copy-start | bytes 52
  76.3 6.5 %copy-start.24 = (pred[16]{0:T(512)(128)(4,1)S(1)}, pred[16]{0:T(512)(128)(4,1)}, u32[]{:S(2)}) copy-start(pred[16]{0:T(512)(128)(4,1)} %copy-done.23) | copy-start | bytes 52
  76.3 6.5 %copy-start.26 = (pred[16]{0:T(512)(128)(4,1)S(1)}, pred[16]{0:T(512)(128)(4,1)}, u32[]{:S(2)}) copy-start(pred[16]{0:T(512)(128)(4,1)} %copy-done.25) | copy-start | bytes 52
  76.3 6.5 %copy-start.28 = (pred[16]{0:T(512)(128)(4,1)S(1)}, pred[16]{0:T(512)(128)(4,1)}, u32[]{:S(2)}) copy-start(pred[16]{0:T(512)(128)(4,1)} %copy-done.27) | copy-start | bytes 52
  76.3 6.5 %copy-start.30 = (pred[16]{0:T(512)(128)(4,1)S(1)}, pred[16]{0:T(512)(128)(4,1)}, u32[]{:S(2)}) copy-start(pred[16]{0:T(512)(128)(4,1)} %copy-done.29) | copy-start | bytes 52
  80.6 1.5 collective-permute-start.3
  83.8 11.2 %all-to-all-start.4 = ((f32[16,1,1026]{2,1,0:T(1,128)}), f32[16,1,1026]{2,1,0:T(1,128)S(1)}, u32[]{:S(2)}, u32[]{:S(2)}) async-start(f32[16,1,1026]{2,1,0:T(1,128)} %broadcast_select_fusion.22), calls=%async_computation.4 | async-start | bytes 147456 | tf_op jit(solution)/shard_map/all_to_all | solution.py:140
  100.6 1.2 collective-permute-start
  103.4 11.0 %all-to-all-start = ((f32[16,1,1028]{2,1,0:T(1,128)}), f32[16,1,1028]{2,1,0:T(1,128)S(1)}, u32[]{:S(2)}, u32[]{:S(2)}) async-start(f32[16,1,1028]{2,1,0:T(1,128)} %broadcast_select_fusion.66), calls=%async_computation | async-start | bytes 147456 | tf_op jit(solution)/shard_map/while/body/eval_jaxpr/all_to_all | solution.py:140
  120.0 1.2 collective-permute-start
  122.8 11.0 %all-to-all-start = ((f32[16,1,1028]{2,1,0:T(1,128)}), f32[16,1,1028]{2,1,0:T(1,128)S(1)}, u32[]{:S(2)}, u32[]{:S(2)}) async-start(f32[16,1,1028]{2,1,0:T(1,128)} %broadcast_select_fusion.66), calls=%async_computation | async-start | bytes 147456 | tf_op jit(solution)/shard_map/while/body/eval_jaxpr/all_to_all | solution.py:140
  139.5 1.2 collective-permute-start
  142.3 11.0 %all-to-all-start = ((f32[16,1,1028]{2,1,0:T(1,128)}), f32[16,1,1028]{2,1,0:T(1,128)S(1)}, u32[]{:S(2)}, u32[]{:S(2)}) async-start(f32[16,1,1028]{2,1,0:T(1,128)} %broadcast_select_fusion.66), calls=%async_computation | async-start | bytes 147456 | tf_op jit(solution)/shard_map/while/body/eval_jaxpr/all_to_all | solution.py:140

commit v7 on v6

--- a/solution.py
+++ b/solution.py
@@ -90,28 +90,6 @@
     spread = spread.reshape(depth, 4 * first_el, second)
     scatter_first = mats["scatter_first"]
     return jnp.einsum("xk,dky->dxy", scatter_first, spread, precision=HIGH)
-
-
-def torso_stage(values, scalars):
-    count = lax.axis_size("torso")
-    if count == 1:
-        return values, scalars
-    if count != 2:
-        raise NotImplementedError("torso size")
-    me = lax.axis_index("torso")
-    face = jnp.where(me == 0, values[-1], values[0])
-    extra = None
-    if scalars is not None:
-        extra = jnp.pad(scalars, (0, values.shape[2] - scalars.shape[0]))[None, :]
-        face = jnp.concatenate([face, extra], 0)
-    got = lax.ppermute(face, "torso", [(0, 1), (1, 0)])
-    rows = values.shape[1]
-    got_face = got[:rows]
-    values = values.at[-1].add(jnp.where(me == 0, got_face, 0.0))
-    values = values.at[0].add(jnp.where(me == 1, got_face, 0.0))
-    if scalars is not None:
-        scalars = scalars + got[rows, : scalars.shape[0]]
-    return values, scalars
 
 
 def plane_exchange(pieces, width, scalars, tie=None):
@@ -151,10 +129,49 @@
     return received, total, tie
 
 
+def edge_pieces(plane):
+    return {
+        (1, 0): plane[-1, :],
+        (-1, 0): plane[0, :],
+        (0, 1): plane[:, -1],
+        (0, -1): plane[:, 0],
+        (1, 1): plane[-1, -1][None],
+        (1, -1): plane[-1, 0][None],
+        (-1, 1): plane[0, -1][None],
+        (-1, -1): plane[0, 0][None],
+    }
+
+
+def rim_sum(got, depth, first, second):
+    at_low = ((0, 0), (0, first - 1))
+    at_high = ((0, 0), (first - 1, 0))
+    low_second = got[(0, -1)].reshape(depth, first)
+    low_second = low_second + jnp.pad(got[(-1, -1)].reshape(depth, 1), at_low)
+    low_second = low_second + jnp.pad(got[(1, -1)].reshape(depth, 1), at_high)
+    high_second = got[(0, 1)].reshape(depth, first)
+    high_second = high_second + jnp.pad(got[(-1, 1)].reshape(depth, 1), at_low)
+    high_second = high_second + jnp.pad(got[(1, 1)].reshape(depth, 1), at_high)
+    along_first = jnp.pad(got[(-1, 0)].reshape(depth, 1, second), ((0, 0), (0, first - 1), (0, 0)))
+    along_first = along_first + jnp.pad(
+        got[(1, 0)].reshape(depth, 1, second), ((0, 0), (first - 1, 0), (0, 0))
+    )
+    along_second = jnp.pad(low_second[:, :, None], ((0, 0), (0, 0), (0, second - 1)))
+    along_second = along_second + jnp.pad(
+        high_second[:, :, None], ((0, 0), (0, 0), (second - 1, 0))
+    )
+    return along_first + along_second
+
+
 def face_sums(values, scalars=None, tie=None):
-    values, scalars = torso_stage(values, scalars)
     depth, first, second = values.shape
-    pieces = {
+    count_t, count_x, count_y = lax.axis_size("torso"), lax.axis_size("hx"), lax.axis_size("hy")
+    if count_t != 2:
+        raise NotImplementedError("torso size")
+    me_t, me_x, me_y = lax.axis_index("torso"), lax.axis_index("hx"), lax.axis_index("hy")
+    my_face = jnp.where(me_t == 0, values[-1], values[0])
+    got_face = lax.ppermute(my_face, "torso", [(0, 1), (1, 0)])
+    width = depth * second
+    in_plane = {
         (1, 0): values[:, -1, :].reshape(-1),
         (-1, 0): values[:, 0, :].reshape(-1),
         (0, 1): values[:, :, -1].reshape(-1),
@@ -164,24 +181,50 @@
         (-1, 1): values[:, 0, -1],
         (-1, -1): values[:, 0, 0],
     }
-    got, total, tie = plane_exchange(pieces, depth * second, scalars, tie)
-    at_low = ((0, 0), (0, first - 1))
-    at_high = ((0, 0), (first - 1, 0))
-    low_second = got[(0, -1)].reshape(depth, first)
-    low_second = low_second + jnp.pad(got[(-1, -1)][:, None], at_low)
-    low_second = low_second + jnp.pad(got[(1, -1)][:, None], at_high)
-    high_second = got[(0, 1)].reshape(depth, first)
-    high_second = high_second + jnp.pad(got[(-1, 1)][:, None], at_low)
-    high_second = high_second + jnp.pad(got[(1, 1)][:, None], at_high)
-    along_first = jnp.pad(got[(-1, 0)].reshape(depth, 1, second), ((0, 0), (0, first - 1), (0, 0)))
-    along_first = along_first + jnp.pad(
-        got[(1, 0)].reshape(depth, 1, second), ((0, 0), (first - 1, 0), (0, 0))
-    )
-    along_second = jnp.pad(low_second[:, :, None], ((0, 0), (0, 0), (0, second - 1)))
-    along_second = along_second + jnp.pad(
-        high_second[:, :, None], ((0, 0), (0, 0), (second - 1, 0))
-    )
-    summed = values + along_first + along_second
+    across = edge_pieces(my_face)
+    rows = []
+    for code in range(27):
+        off_t, off_x, off_y = code // 9 - 1, code // 3 % 3 - 1, code % 3 - 1
+        if off_t == 0:
+            piece = in_plane.get((off_x, off_y))
+        else:
+            piece = across.get((off_x, off_y))
+        row = jnp.zeros((width,), jnp.float32) if piece is None else jnp.pad(piece, (0, width - piece.shape[0]))
+        if scalars is not None:
+            row = jnp.concatenate([row, scalars])
+        rows.append(row)
+    peers = jnp.arange(count_t * count_x * count_y, dtype=jnp.int32)
+    peer_t = peers % count_t
+    peer_x = peers // (count_t * count_y)
+    peer_y = peers // count_t % count_y
+    off_t, off_x, off_y = peer_t - me_t, peer_x - me_x, peer_y - me_y
+    near = (jnp.abs(off_x) <= 1) & (jnp.abs(off_y) <= 1)
+    code_of = jnp.where(near, (off_t + 1) * 9 + (off_x + 1) * 3 + (off_y + 1), 13)
+    send = jnp.broadcast_to(rows[13][None, :], (peers.shape[0], rows[13].shape[0]))
+    for code in range(27):
+        if code != 13:
+            send = jnp.where(code_of[:, None] == code, rows[code][None, :], send)
+    if tie is not None:
+        send, tie = lax.optimization_barrier((send, tie))
+    got = lax.all_to_all(send, ("hx", "hy", "torso"), 0, 0, tiled=True)
+
+    def received(offset, length, torso_of):
+        src_x, src_y = me_x + offset[0], me_y + offset[1]
+        valid = (src_x >= 0) & (src_x < count_x) & (src_y >= 0) & (src_y < count_y)
+        src = (jnp.clip(src_x, 0, count_x - 1) * count_y + jnp.clip(src_y, 0, count_y - 1)) * count_t + torso_of
+        row = lax.dynamic_index_in_dim(got, src, 0, keepdims=False)
+        return jnp.where(valid, row[:length], 0.0)
+
+    got_in = {o: received(o, p.shape[0], me_t) for o, p in in_plane.items()}
+    got_across = {o: received(o, p.shape[0], 1 - me_t) for o, p in across.items()}
+    summed = values + rim_sum(got_in, depth, first, second)
+    face_term = got_face + rim_sum(got_across, 1, first, second)[0]
+    depth_index = lax.broadcasted_iota(jnp.int32, (depth, 1, 1), 0)
+    face_at = jnp.where(me_t == 0, depth - 1, 0)
+    summed = summed + jnp.where(depth_index == face_at, face_term[None], 0.0)
+    total = None
+    if scalars is not None:
+        total = jnp.sum(got[:, width:], axis=0)
     if tie is None:
         return summed, total
     return summed, total, tie

time: 156 us -> 218 us (1.40)
  local copies, waits for them, and re-layouts: 19.4 us -> 44.9 us
  other arithmetic: 33.8 us -> 58.7 us
  between operations: 2.11 us -> 10.3 us
  starting transfers between devices: 36.6 us -> 29 us
  loops' own time: 0.86 us -> 8.22 us
  waiting for transfers between devices: 40.8 us -> 44.5 us
    all_to_all x0 -> x6, waiting for transfers between devices: none -> 37.1 us  [face_sums(): got = lax.all_to_all(send, ('hx', 'hy', 'torso'), 0, 0, tiled=True)]
    all_to_all x7 -> x1, waiting for transfers between devices: 37.5 us -> 7.45 us  [plane_exchange(): got = lax.all_to_all(send, ('hx', 'hy'), 0, 0, tiled=True)]
    all_to_all x7 -> x1, starting transfers between devices: 35.5 us -> 6.64 us  [plane_exchange(): got = lax.all_to_all(send, ('hx', 'hy'), 0, 0, tiled=True)]
    all_to_all x0 -> x6, starting transfers between devices: none -> 21.1 us  [face_sums(): got = lax.all_to_all(send, ('hx', 'hy', 'torso'), 0, 0, tiled=True)]
    slice x0 -> x42, local copies, waits for them, and re-layouts: none -> 20.9 us  [the longest x24 13 us: received(): return jnp.where(valid, row[:length], 0.0)]
    select_n x6 -> x55, other arithmetic: 0.03 us -> 15.7 us  [the longest x6 14.1 us: face_sums(): send = jnp.where(code_of[:, None] == code, rows[code][None, :], send)]
    concatenate x8, other arithmetic: 0.09 us -> 10.3 us  [face_sums(): row = jnp.concatenate([row, scalars])]
    another operation x1, loops' own time: 0.86 us -> 8.22 us  [per_device(): solution = lax.fori_loop(1, ITERS, later_turn, state)[0]]
  transfers between devices with their start and end apart: 13 -> 13, of which waited for: 8 -> 6; matrix products, arithmetic and copies ran while one was open for 14% -> 26% of each run, Pallas kernels for 0% -> 0%
where the time goes in v7:
time: 218 us; the launch traced here: 216 us
  other arithmetic  58.7 us (27%)
  local copies, waits for them, and re-layouts  44.9 us (21%)
  waiting for transfers between devices  44.5 us (20%)
  starting transfers between devices  29 us (13%)
  matrix products  20.9 us (10%)
  between operations  10.3 us (5%)
  loops' own time  8.22 us (4%)
    all_to_all x6, waiting for transfers between devices, face_sums(): got = lax.all_to_all(send, ('hx', 'hy', 'torso'), 0, 0, tiled=True)  37.1 us
    all_to_all x6, starting transfers between devices, face_sums(): got = lax.all_to_all(send, ('hx', 'hy', 'torso'), 0, 0, tiled=True)  21.1 us
    reduce_sum x2, other arithmetic, per_device(): current = jnp.sum(cond_nodes * gate_flat * (volts - reversal[:, None]), 0)  16.5 us
    select_n x6, other arithmetic, face_sums(): send = jnp.where(code_of[:, None] == code, rows[code][None, :], send)  14.1 us
    slice x24, local copies, waits for them, and re-layouts, received(): return jnp.where(valid, row[:length], 0.0)  13 us
    concatenate x8, other arithmetic, face_sums(): row = jnp.concatenate([row, scalars])  10.3 us
    another operation x1, loops' own time, per_device(): solution = lax.fori_loop(1, ITERS, later_turn, state)[0]  8.22 us
    all_to_all x1, waiting for transfers between devices, plane_exchange(): got = lax.all_to_all(send, ('hx', 'hy'), 0, 0, tiled=True)  7.45 us
  transfers between devices with their start and end apart: 13, of which 6 were waited for; matrix products, arithmetic and copies ran while one was open for 26% of the time, Pallas kernels for 0%

profile of v7, /device:TPU:0, one launch (start us, length us, event | category | flops | bytes accessed | tf_op | source)
XLA Modules:
  0.0 216.5 jit_solution(5562555575374932210)
XLA Ops:
  0.7 0.8 copy.245
  3.0 0.9 select_select_fusion.6
  7.2 1.4 fusion.771
  8.6 0.9 slice_reduce_fusion.21
  10.4 0.6 pad.556
  11.7 0.7 pad.561
  12.4 0.7 pad.563
  13.9 0.7 all_to_all.32
  16.8 8.0 %multiply_reduce_fusion.1 = (f32[4,13,256]{2,0,1:T(4,128)}, f32[40,4,13,256]{3,1,2,0:T(4,128)S(1)}) fusion(f32[40]{0:T(128)S(1)} %copy-done.81, f32[4,13,256]{2,0,1:T(4,128)S(1)} %copy-done, f32[40]{0:T(128)S(1)} %get-tuple-element.967, f32[40]{0:T(128)S(1)} %get-tuple-element.966, f32[40]{0:T(128)S(1)} %get-tuple-element.968, ...), kind=kLoop, calls=%fused_computation.466 | loop fusion | flops 12766208 | bytes 4435616 | tf_op jit(solution)/shard_map/reduce_sum | solution.py:332
  24.8 7.1 %all-to-all-start.1 = ((f32[32,1,1024]{2,1,0:T(1,128)}), f32[32,1,1024]{2,1,0:T(1,128)}, u32[]{:S(2)}, u32[]{:S(2)}) async-start(f32[32,1,1024]{2,1,0:T(1,128)} %all_to_all.32), calls=%async_computation.1 | async-start | bytes 262144 | tf_op jit(solution)/shard_map/all_to_all | solution.py:209
  32.5 0.8 mul.1837
  33.2 1.2 broadcast_compare_fusion.32
  34.4 5.6 %all-to-all-done.1 = f32[32,1,1024]{2,1,0:T(1,128)} async-done(((f32[32,1,1024]{2,1,0:T(1,128)}), f32[32,1,1024]{2,1,0:T(1,128)}, u32[]{:S(2)}, u32[]{:S(2)}) %all-to-all-start.1) | async-done | bytes 131104 | tf_op jit(solution)/shard_map/all_to_all | solution.py:209
  40.0 1.5 fusion.551
  47.2 0.8 bitcast_add_fusion.3
  48.0 0.9 fusion.404
  49.1 1.0 fusion.435
  50.0 1.0 fusion.436
  51.4 1.0 convolution_add_fusion.6
  53.2 0.9 convolution_bitcast_fusion.2
  54.7 1.3 fusion.769
  56.0 0.9 slice_reduce_fusion.19
  57.6 0.6 pad.586
  58.2 0.7 pad.588
  59.5 0.7 pad.593
  60.4 1.0 select_select_fusion.9
  61.5 0.8 copy.249
  62.3 3.5 %all-to-all-start.2 = ((f32[32,1,1024]{2,1,0:T(1,128)}), f32[32,1,1024]{2,1,0:T(1,128)}, u32[]{:S(2)}, u32[]{:S(2)}) async-start(f32[32,1,1024]{2,1,0:T(1,128)} %copy.249), calls=%async_computation.2 | async-start | bytes 262144 | tf_op jit(solution)/shard_map/all_to_all | solution.py:209
  65.8 8.6 %multiply_reduce_fusion = (f32[4,13,256]{2,0,1:T(4,128)}, f32[40,4,13,256]{3,1,2,0:T(4,128)}) fusion(f32[4,13,256]{2,0,1:T(4,128)S(1)} %copy.258, f32[40]{0:T(128)} %param.23, f32[40]{0:T(128)} %copy-done.75, f32[40]{0:T(128)} %copy-done.74, f32[40]{0:T(128)} %copy-done.76, f32[40]{0:T(128)} %copy-done.77, f32[40]{0:T(128)} %get-tuple-element.904, ...), kind=kLoop, calls=%fused_computation.464 | loop fusion | flops 12766208 | bytes 4435616 | tf_op jit(solution)/shard_map/reduce_sum | solution.py:332
  74.4 0.9 fusion.565
  81.3 0.8 bitcast_add_fusion.2
  82.1 0.9 fusion.407
  83.8 1.5 broadcast_select_fusion.70
  85.3 6.6 %all-to-all-start.3 = ((f32[16,1,768]{2,1,0:T(1,128)}), f32[16,1,768]{2,1,0:T(1,128)S(1)}, u32[]{:S(2)}, u32[]{:S(2)}) async-start(f32[16,1,768]{2,1,0:T(1,128)} %broadcast_select_fusion.70), calls=%async_computation.3 | async-start | bytes 98304 | tf_op jit(solution)/shard_map/all_to_all | solution.py:118
  92.0 7.5 %all-to-all-done.3 = f32[16,1,768]{2,1,0:T(1,128)S(1)} async-done(((f32[16,1,768]{2,1,0:T(1,128)}), f32[16,1,768]{2,1,0:T(1,128)S(1)}, u32[]{:S(2)}, u32[]{:S(2)}) %all-to-all-start.3) | async-done | bytes 49184 | tf_op jit(solution)/shard_map/all_to_all | solution.py:118
  100.5 1.0 multiply_bitcast_fusion.3
  105.5 2.5 %pad_maximum_fusion.37 = (f32[1026]{0:T(1024)S(1)}, f32[1026]{0:T(1024)S(1)}, f32[1026]{0:T(1024)S(1)}, f32[1026]{0:T(1024)S(1)}, f32[1026]{0:T(1024)S(1)}, /*in...) fusion(f32[2]{0:T(128)S(1)} %maximum_reduce_fusion.1, f32[1]{0:T(128)} %bitcast.155, ...), kind=kLoop, calls=%fused_computation.606 | loop fusion | flops 19494 | bytes 39128 | tf_op jit(solution)/shard_map/concatenate | solution.py:194
  108.3 3.2 %broadcast_select_fusion.62 = f32[32,1,1026]{2,1,0:T(1,128)} fusion(pred[32]{0:T(512)(128)(4,1)S(1)} %copy-done.20, pred[32]{0:T(512)(128)(4,1)S(1)} %copy-done.70, pred[32]{0:T(512)(128)(4,1)S(1)} %copy-done.24, pred[32]{0:T(512)(128)(4,1)S(1)} %copy-done.26, pred[32]{0:T(512)(128)(4,1)S(1)} %copy-done.28, pred[32]{0:T(512)(128)(4,1)S(1)} %copy-done.30, ...), kind=kLoop, calls=%fused_computation.532 | loop fusion | flops 853632 | bytes 201928 | tf_op jit(solution)/shard_map/jit(_where)/select_n | solution.py:206
  111.4 2.8 %all-to-all-start.4 = ((f32[32,1,1026]{2,1,0:T(1,128)}), f32[32,1,1026]{2,1,0:T(1,128)S(1)}, u32[]{:S(2)}, u32[]{:S(2)}) async-start(f32[32,1,1026]{2,1,0:T(1,128)} %broadcast_select_fusion.62), calls=%async_computation.4 | async-start | bytes 294912 | tf_op jit(solution)/shard_map/all_to_all | solution.py:209
  115.0 0.7 copy.272
  115.7 6.8 %all-to-all-done.4 = f32[32,1,1026]{2,1,0:T(1,128)S(1)} async-done(((f32[32,1,1026]{2,1,0:T(1,128)}), f32[32,1,1026]{2,1,0:T(1,128)S(1)}, u32[]{:S(2)}, u32[]{:S(2)}) %all-to-all-start.4) | async-done | bytes 131360 | tf_op jit(solution)/shard_map/all_to_all | solution.py:209
  128.9 86.9 %while.26 = (s32[]{:T(128)}, f32[4,13,256]{2,1,0:T(8,128)S(1)}, f32[4,13,256]{2,1,0:T(8,128)S(1)}, f32[4,13,256]{2,1,0:T(8,128)S(1)}, f32[4,13,256]{2,1,0:T(8,12...) while((s32[]{:T(128)}, f32[4,13,256]{2,1,0:T(8,128)S(1)}, ...), condition=%wide.region_7.8_spmd.clone.clone.clone, body=%wide.region_4.7_spmd.clone.clone.clone.sunk | while | flops 220283680 | bytes 4141966 | solution.py:402
  130.0 1.1 fusion.864
  131.1 1.1 fusion.866
  133.1 0.7 fusion.872
  134.8 2.6 %pad_maximum_fusion.51 = (f32[1028]{0:T(1024)S(1)}, f32[1028]{0:T(1024)S(1)}, f32[1028]{0:T(1024)S(1)}, f32[1028]{0:T(1024)S(1)}, f32[1028]{0:T(1024)S(1)}, /*in...) fusion(f32[4]{0:T(128)S(1)} %maximum_reduce_fusion.3, f32[1]{0:T(128)} %bitcast.578, ...), kind=kLoop, calls=%fused_computation.197.clone.1 | loop fusion | flops 19532 | bytes 39208 | tf_op jit(solution)/shard_map/while/body/eval_jaxpr/concatenate | solution.py:194
  137.4 3.2 %broadcast_select_fusion.118 = f32[32,1,1028]{2,1,0:T(1,128)} fusion(pred[32]{0:T(512)(128)(4,1)S(1)} %get-tuple-element.1228, pred[32]{0:T(512)(128)(4,1)S(1)} %get-tuple-element.1229, pred[32]{0:T(512)(128)(4,1)S(1)} %get-tuple-element.1230, pred[32]{0:T(512)(128)(4,1)S(1)} %get-tuple-element.1231, pred[32]{0:T(512)(128)(4,1)S(1)} %get-tuple-element.1232, ...), kind=kLoop, calls=%fused_computation.106.clone.1 | loop fusion | flops 855296 | bytes 202320 | tf_op jit(solution)/shard_map/while/body/eval_jaxpr/jit(_where)/select_n | solution.py:206
  140.6 2.6 %all-to-all-start = ((f32[32,1,1028]{2,1,0:T(1,128)}), f32[32,1,1028]{2,1,0:T(1,128)S(1)}, u32[]{:S(2)}, u32[]{:S(2)}) async-start(f32[32,1,1028]{2,1,0:T(1,128)} %broadcast_select_fusion.118), calls=%async_computation | async-start | bytes 294912 | tf_op jit(solution)/shard_map/while/body/eval_jaxpr/all_to_all | solution.py:209
  143.3 8.2 %all-to-all-done = f32[32,1,1028]{2,1,0:T(1,128)S(1)} async-done(((f32[32,1,1028]{2,1,0:T(1,128)}), f32[32,1,1028]{2,1,0:T(1,128)S(1)}, u32[]{:S(2)}, u32[]{:S(2)}) %all-to-all-start) | async-done | bytes 131616 | tf_op jit(solution)/shard_map/while/body/eval_jaxpr/all_to_all | solution.py:209
  159.0 1.1 fusion.864
  160.1 1.1 fusion.866
  162.0 0.7 fusion.872
  163.7 2.6 %pad_maximum_fusion.51 = (f32[1028]{0:T(1024)S(1)}, f32[1028]{0:T(1024)S(1)}, f32[1028]{0:T(1024)S(1)}, f32[1028]{0:T(1024)S(1)}, f32[1028]{0:T(1024)S(1)}, /*in...) fusion(f32[4]{0:T(128)S(1)} %maximum_reduce_fusion.3, f32[1]{0:T(128)} %bitcast.578, ...), kind=kLoop, calls=%fused_computation.197.clone.1 | loop fusion | flops 19532 | bytes 39208 | tf_op jit(solution)/shard_map/while/body/eval_jaxpr/concatenate | solution.py:194
  166.3 3.2 %broadcast_select_fusion.118 = f32[32,1,1028]{2,1,0:T(1,128)} fusion(pred[32]{0:T(512)(128)(4,1)S(1)} %get-tuple-element.1228, pred[32]{0:T(512)(128)(4,1)S(1)} %get-tuple-element.1229, pred[32]{0:T(512)(128)(4,1)S(1)} %get-tuple-element.1230, pred[32]{0:T(512)(128)(4,1)S(1)} %get-tuple-element.1231, pred[32]{0:T(512)(128)(4,1)S(1)} %get-tuple-element.1232, ...), kind=kLoop, calls=%fused_computation.106.clone.1 | loop fusion | flops 855296 | bytes 202320 | tf_op jit(solution)/shard_map/while/body/eval_jaxpr/jit(_where)/select_n | solution.py:206
  169.5 2.6 %all-to-all-start = ((f32[32,1,1028]{2,1,0:T(1,128)}), f32[32,1,1028]{2,1,0:T(1,128)S(1)}, u32[]{:S(2)}, u32[]{:S(2)}) async-start(f32[32,1,1028]{2,1,0:T(1,128)} %broadcast_select_fusion.118), calls=%async_computation | async-start | bytes 294912 | tf_op jit(solution)/shard_map/while/body/eval_jaxpr/all_to_all | solution.py:209
  172.3 8.2 %all-to-all-done = f32[32,1,1028]{2,1,0:T(1,128)S(1)} async-done(((f32[32,1,1028]{2,1,0:T(1,128)}), f32[32,1,1028]{2,1,0:T(1,128)S(1)}, u32[]{:S(2)}, u32[]{:S(2)}) %all-to-all-start) | async-done | bytes 131616 | tf_op jit(solution)/shard_map/while/body/eval_jaxpr/all_to_all | solution.py:209
  187.9 1.1 fusion.864
  189.0 1.1 fusion.866
  191.0 0.7 fusion.872
  192.7 2.6 %pad_maximum_fusion.51 = (f32[1028]{0:T(1024)S(1)}, f32[1028]{0:T(1024)S(1)}, f32[1028]{0:T(1024)S(1)}, f32[1028]{0:T(1024)S(1)}, f32[1028]{0:T(1024)S(1)}, /*in...) fusion(f32[4]{0:T(128)S(1)} %maximum_reduce_fusion.3, f32[1]{0:T(128)} %bitcast.578, ...), kind=kLoop, calls=%fused_computation.197.clone.1 | loop fusion | flops 19532 | bytes 39208 | tf_op jit(solution)/shard_map/while/body/eval_jaxpr/concatenate | solution.py:194
  195.3 3.2 %broadcast_select_fusion.118 = f32[32,1,1028]{2,1,0:T(1,128)} fusion(pred[32]{0:T(512)(128)(4,1)S(1)} %get-tuple-element.1228, pred[32]{0:T(512)(128)(4,1)S(1)} %get-tuple-element.1229, pred[32]{0:T(512)(128)(4,1)S(1)} %get-tuple-element.1230, pred[32]{0:T(512)(128)(4,1)S(1)} %get-tuple-element.1231, pred[32]{0:T(512)(128)(4,1)S(1)} %get-tuple-element.1232, ...), kind=kLoop, calls=%fused_computation.106.clone.1 | loop fusion | flops 855296 | bytes 202320 | tf_op jit(solution)/shard_map/while/body/eval_jaxpr/jit(_where)/select_n | solution.py:206
  198.5 2.6 %all-to-all-start = ((f32[32,1,1028]{2,1,0:T(1,128)}), f32[32,1,1028]{2,1,0:T(1,128)S(1)}, u32[]{:S(2)}, u32[]{:S(2)}) async-start(f32[32,1,1028]{2,1,0:T(1,128)} %broadcast_select_fusion.118), calls=%async_computation | async-start | bytes 294912 | tf_op jit(solution)/shard_map/while/body/eval_jaxpr/all_to_all | solution.py:209
  201.2 8.2 %all-to-all-done = f32[32,1,1028]{2,1,0:T(1,128)S(1)} async-done(((f32[32,1,1028]{2,1,0:T(1,128)}), f32[32,1,1028]{2,1,0:T(1,128)S(1)}, u32[]{:S(2)}, u32[]{:S(2)}) %all-to-all-start) | async-done | bytes 131616 | tf_op jit(solution)/shard_map/while/body/eval_jaxpr/all_to_all | solution.py:209
  215.8 0.7 copy.273
  (614 shorter events, 49.5 us)
Async XLA Ops:
  4.0 10.7 %copy-start.85 = (f32[3,40]{1,0:T(4,128)S(1)}, f32[3,40]{1,0:T(4,128)}, u32[]{:S(2)}) copy-start(f32[3,40]{1,0:T(4,128)} %param.21) | copy-start | bytes 1444
  4.0 10.7 %copy-start.87 = (f32[3,40]{1,0:T(4,128)S(1)}, f32[3,40]{1,0:T(4,128)}, u32[]{:S(2)}) copy-start(f32[3,40]{1,0:T(4,128)} %param.22) | copy-start | bytes 1444
  4.0 11.3 %copy-start.84 = (f32[4,40]{1,0:T(4,128)S(1)}, f32[4,40]{1,0:T(4,128)}, u32[]{:S(2)}) copy-start(f32[4,40]{1,0:T(4,128)} %param.24) | copy-start | bytes 1924
  4.0 11.3 %copy-start.86 = (f32[3,40]{1,0:T(4,128)S(1)}, f32[3,40]{1,0:T(4,128)}, u32[]{:S(2)}) copy-start(f32[3,40]{1,0:T(4,128)} %param.19) | copy-start | bytes 1444
  4.0 11.3 %copy-start.88 = (f32[3,40]{1,0:T(4,128)S(1)}, f32[3,40]{1,0:T(4,128)}, u32[]{:S(2)}) copy-start(f32[3,40]{1,0:T(4,128)} %param.20) | copy-start | bytes 1444
  4.0 12.0 %copy-start.9 = (s32[4,13,256]{2,0,1:T(4,128)S(1)}, s32[4,13,256]{2,0,1:T(4,128)}, u32[]{:S(2)}) copy-start(s32[4,13,256]{2,0,1:T(4,128)} %param.18) | copy-start | bytes 159748
  4.0 12.0 %copy-start.10 = (s32[4,13,256]{2,0,1:T(4,128)S(1)}, s32[4,13,256]{2,0,1:T(4,128)}, u32[]{:S(2)}) copy-start(s32[4,13,256]{2,0,1:T(4,128)} %param.17) | copy-start | bytes 159748
  4.1 12.6 %copy-start = (f32[4,13,256]{2,0,1:T(4,128)S(1)}, f32[4,13,256]{2,0,1:T(4,128)}, u32[]{:S(2)}) copy-start(f32[4,13,256]{2,0,1:T(4,128)} %param.15) | copy-start | bytes 159748
  4.2 12.6 %copy-start.81 = (f32[40]{0:T(128)S(1)}, f32[40]{0:T(128)}, u32[]{:S(2)}) copy-start(f32[40]{0:T(128)} %param.23) | copy-start | bytes 484
  6.7 40.5 %collective-permute-start.1 = (f32[13,256]{1,0:T(8,128)}, f32[13,256]{1,0:T(8,128)}, u32[]{:S(2)}, u32[]{:S(2)}) collective-permute-start(f32[13,256]{1,0:T(8,128)} %fusion.821), channel_id=1, source_target_pairs={{0,1},{1,0},{2,3},{3,2},{4,5},{5,4},{6,7},{7,6},{8,9},{9,8},{10,11... | collective-permute-start | bytes 39944 | tf_op jit(solution)/shard_map/ppermute | solution.py:172
  15.3 9.4 %copy-start.71 = (f32[40]{0:T(128)}, f32[40]{0:T(128)S(1)}, u32[]{:S(2)}) copy-start(f32[40]{0:T(128)S(1)} %get-tuple-element.894) | copy-start | bytes 484
  15.3 9.4 %copy-start.72 = (f32[40]{0:T(128)}, f32[40]{0:T(128)S(1)}, u32[]{:S(2)}) copy-start(f32[40]{0:T(128)S(1)} %get-tuple-element.895) | copy-start | bytes 484
  15.3 9.4 %copy-start.73 = (f32[40]{0:T(128)}, f32[40]{0:T(128)S(1)}, u32[]{:S(2)}) copy-start(f32[40]{0:T(128)S(1)} %get-tuple-element.896) | copy-start | bytes 484
  15.4 9.4 %copy-start.74 = (f32[40]{0:T(128)}, f32[40]{0:T(128)S(1)}, u32[]{:S(2)}) copy-start(f32[40]{0:T(128)S(1)} %get-tuple-element.966) | copy-start | bytes 484
  15.4 9.4 %copy-start.75 = (f32[40]{0:T(128)}, f32[40]{0:T(128)S(1)}, u32[]{:S(2)}) copy-start(f32[40]{0:T(128)S(1)} %get-tuple-element.967) | copy-start | bytes 484
  15.4 9.4 %copy-start.76 = (f32[40]{0:T(128)}, f32[40]{0:T(128)S(1)}, u32[]{:S(2)}) copy-start(f32[40]{0:T(128)S(1)} %get-tuple-element.968) | copy-start | bytes 484
  15.4 9.4 %copy-start.77 = (f32[40]{0:T(128)}, f32[40]{0:T(128)S(1)}, u32[]{:S(2)}) copy-start(f32[40]{0:T(128)S(1)} %get-tuple-element.969) | copy-start | bytes 484
  16.0 8.7 %copy-start.78 = (f32[40]{0:T(128)}, f32[40]{0:T(128)S(1)}, u32[]{:S(2)}) copy-start(f32[40]{0:T(128)S(1)} %get-tuple-element.900) | copy-start | bytes 484
  16.7 15.7 %copy-start.8 = (f32[1,4,85]{2,1,0:T(4,128)S(1)}, f32[1,4,85]{2,1,0:T(4,128)}, u32[]{:S(2)}) copy-start(f32[1,4,85]{2,1,0:T(4,128)} %param.26) | copy-start | bytes 4084
  24.8 15.3 %all-to-all-start.1 = ((f32[32,1,1024]{2,1,0:T(1,128)}), f32[32,1,1024]{2,1,0:T(1,128)}, u32[]{:S(2)}, u32[]{:S(2)}) async-start(f32[32,1,1024]{2,1,0:T(1,128)} %all_to_all.32), calls=%async_computation.1 | async-start | bytes 262144 | tf_op jit(solution)/shard_map/all_to_all | solution.py:209
  49.0 16.8 %copy-start.3 = (pred[4,13,256]{2,0,1:T(4,128)(4,1)S(1)}, pred[4,13,256]{2,0,1:T(4,128)(4,1)}, u32[]{:S(2)}) copy-start(pred[4,13,256]{2,0,1:T(4,128)(4,1)} %copy-done.2) | copy-start | bytes 39940
  57.3 24.1 %collective-permute-start.2 = (f32[13,256]{1,0:T(8,128)}, f32[13,256]{1,0:T(8,128)}, u32[]{:S(2)}, u32[]{:S(2)}) collective-permute-start(f32[13,256]{1,0:T(8,128)} %fusion.820), channel_id=1, source_target_pairs={{0,1},{1,0},{2,3},{3,2},{4,5},{5,4},{6,7},{7,6},{8,9},{9,8},{10,11... | collective-permute-start | bytes 39944 | tf_op jit(solution)/shard_map/ppermute | solution.py:172
  62.3 12.1 %all-to-all-start.2 = ((f32[32,1,1024]{2,1,0:T(1,128)}), f32[32,1,1024]{2,1,0:T(1,128)}, u32[]{:S(2)}, u32[]{:S(2)}) async-start(f32[32,1,1024]{2,1,0:T(1,128)} %copy.249), calls=%async_computation.2 | async-start | bytes 262144 | tf_op jit(solution)/shard_map/all_to_all | solution.py:209
  74.4 27.2 %copy-start.12 = (pred[16]{0:T(512)(128)(4,1)S(1)}, pred[16]{0:T(512)(128)(4,1)}, u32[]{:S(2)}) copy-start(pred[16]{0:T(512)(128)(4,1)} %copy-done.11) | copy-start | bytes 52
  74.4 27.2 %copy-start.14 = (pred[16]{0:T(512)(128)(4,1)S(1)}, pred[16]{0:T(512)(128)(4,1)}, u32[]{:S(2)}) copy-start(pred[16]{0:T(512)(128)(4,1)} %copy-done.13) | copy-start | bytes 52
  74.4 27.2 %copy-start.16 = (pred[16]{0:T(512)(128)(4,1)S(1)}, pred[16]{0:T(512)(128)(4,1)}, u32[]{:S(2)}) copy-start(pred[16]{0:T(512)(128)(4,1)} %copy-done.15) | copy-start | bytes 52
  74.4 27.2 %copy-start.18 = (pred[16]{0:T(512)(128)(4,1)S(1)}, pred[16]{0:T(512)(128)(4,1)}, u32[]{:S(2)}) copy-start(pred[16]{0:T(512)(128)(4,1)} %copy-done.17) | copy-start | bytes 52
  74.4 28.5 %copy-start.1 = (f32[64,340]{1,0:T(8,128)S(1)}, f32[64,340]{1,0:T(8,128)}, u32[]{:S(2)}) copy-start(f32[64,340]{1,0:T(8,128)} %mul.1837) | copy-start | bytes 261124
  85.3 14.1 %all-to-all-start.3 = ((f32[16,1,768]{2,1,0:T(1,128)}), f32[16,1,768]{2,1,0:T(1,128)S(1)}, u32[]{:S(2)}, u32[]{:S(2)}) async-start(f32[16,1,768]{2,1,0:T(1,128)} %broadcast_select_fusion.70), calls=%async_computation.3 | async-start | bytes 98304 | tf_op jit(solution)/shard_map/all_to_all | solution.py:118
  100.2 7.8 %copy-start.20 = (pred[32]{0:T(512)(128)(4,1)S(1)}, pred[32]{0:T(512)(128)(4,1)}, u32[]{:S(2)}) copy-start(pred[32]{0:T(512)(128)(4,1)} %copy-done.19) | copy-start | bytes 100
  100.2 7.8 %copy-start.22 = (pred[32]{0:T(512)(128)(4,1)S(1)}, pred[32]{0:T(512)(128)(4,1)}, u32[]{:S(2)}) copy-start(pred[32]{0:T(512)(128)(4,1)} %copy-done.21) | copy-start | bytes 100
  100.2 7.8 %copy-start.24 = (pred[32]{0:T(512)(128)(4,1)S(1)}, pred[32]{0:T(512)(128)(4,1)}, u32[]{:S(2)}) copy-start(pred[32]{0:T(512)(128)(4,1)} %copy-done.23) | copy-start | bytes 100
  100.3 7.8 %copy-start.26 = (pred[32]{0:T(512)(128)(4,1)S(1)}, pred[32]{0:T(512)(128)(4,1)}, u32[]{:S(2)}) copy-start(pred[32]{0:T(512)(128)(4,1)} %copy-done.25) | copy-start | bytes 100
  100.3 7.8 %copy-start.28 = (pred[32]{0:T(512)(128)(4,1)S(1)}, pred[32]{0:T(512)(128)(4,1)}, u32[]{:S(2)}) copy-start(pred[32]{0:T(512)(128)(4,1)} %copy-done.27) | copy-start | bytes 100
  100.3 7.8 %copy-start.30 = (pred[32]{0:T(512)(128)(4,1)S(1)}, pred[32]{0:T(512)(128)(4,1)}, u32[]{:S(2)}) copy-start(pred[32]{0:T(512)(128)(4,1)} %copy-done.29) | copy-start | bytes 100
  100.3 7.8 %copy-start.32 = (pred[32]{0:T(512)(128)(4,1)S(1)}, pred[32]{0:T(512)(128)(4,1)}, u32[]{:S(2)}) copy-start(pred[32]{0:T(512)(128)(4,1)} %copy-done.31) | copy-start | bytes 100
  100.3 7.8 %copy-start.34 = (pred[32]{0:T(512)(128)(4,1)S(1)}, pred[32]{0:T(512)(128)(4,1)}, u32[]{:S(2)}) copy-start(pred[32]{0:T(512)(128)(4,1)} %copy-done.33) | copy-start | bytes 100
  100.3 7.8 %copy-start.36 = (pred[32]{0:T(512)(128)(4,1)S(1)}, pred[32]{0:T(512)(128)(4,1)}, u32[]{:S(2)}) copy-start(pred[32]{0:T(512)(128)(4,1)} %copy-done.35) | copy-start | bytes 100
  100.3 7.8 %copy-start.38 = (pred[32]{0:T(512)(128)(4,1)S(1)}, pred[32]{0:T(512)(128)(4,1)}, u32[]{:S(2)}) copy-start(pred[32]{0:T(512)(128)(4,1)} %copy-done.37) | copy-start | bytes 100
  100.3 7.8 %copy-start.40 = (pred[32]{0:T(512)(128)(4,1)S(1)}, pred[32]{0:T(512)(128)(4,1)}, u32[]{:S(2)}) copy-start(pred[32]{0:T(512)(128)(4,1)} %copy-done.39) | copy-start | bytes 100
  100.3 7.8 %copy-start.42 = (pred[32]{0:T(512)(128)(4,1)S(1)}, pred[32]{0:T(512)(128)(4,1)}, u32[]{:S(2)}) copy-start(pred[32]{0:T(512)(128)(4,1)} %copy-done.41) | copy-start | bytes 100
  100.3 7.8 %copy-start.44 = (pred[32]{0:T(512)(128)(4,1)S(1)}, pred[32]{0:T(512)(128)(4,1)}, u32[]{:S(2)}) copy-start(pred[32]{0:T(512)(128)(4,1)} %copy-done.43) | copy-start | bytes 100
  100.4 7.8 %copy-start.46 = (pred[32]{0:T(512)(128)(4,1)S(1)}, pred[32]{0:T(512)(128)(4,1)}, u32[]{:S(2)}) copy-start(pred[32]{0:T(512)(128)(4,1)} %copy-done.45) | copy-start | bytes 100
  100.4 7.8 %copy-start.48 = (pred[32]{0:T(512)(128)(4,1)S(1)}, pred[32]{0:T(512)(128)(4,1)}, u32[]{:S(2)}) copy-start(pred[32]{0:T(512)(128)(4,1)} %copy-done.47) | copy-start | bytes 100
  100.4 7.8 %copy-start.50 = (pred[32]{0:T(512)(128)(4,1)S(1)}, pred[32]{0:T(512)(128)(4,1)}, u32[]{:S(2)}) copy-start(pred[32]{0:T(512)(128)(4,1)} %copy-done.49) | copy-start | bytes 100
  100.4 7.8 %copy-start.52 = (pred[32]{0:T(512)(128)(4,1)S(1)}, pred[32]{0:T(512)(128)(4,1)}, u32[]{:S(2)}) copy-start(pred[32]{0:T(512)(128)(4,1)} %copy-done.51) | copy-start | bytes 100
  100.4 7.8 %copy-start.54 = (pred[32]{0:T(512)(128)(4,1)S(1)}, pred[32]{0:T(512)(128)(4,1)}, u32[]{:S(2)}) copy-start(pred[32]{0:T(512)(128)(4,1)} %copy-done.53) | copy-start | bytes 100
  100.4 7.8 %copy-start.56 = (pred[32]{0:T(512)(128)(4,1)S(1)}, pred[32]{0:T(512)(128)(4,1)}, u32[]{:S(2)}) copy-start(pred[32]{0:T(512)(128)(4,1)} %copy-done.55) | copy-start | bytes 100
  100.4 7.8 %copy-start.58 = (pred[32]{0:T(512)(128)(4,1)S(1)}, pred[32]{0:T(512)(128)(4,1)}, u32[]{:S(2)}) copy-start(pred[32]{0:T(512)(128)(4,1)} %copy-done.57) | copy-start | bytes 100
  100.4 7.8 %copy-start.60 = (pred[32]{0:T(512)(128)(4,1)S(1)}, pred[32]{0:T(512)(128)(4,1)}, u32[]{:S(2)}) copy-start(pred[32]{0:T(512)(128)(4,1)} %copy-done.59) | copy-start | bytes 100
  101.5 12.8 %copy-start.96 = (pred[4]{0:T(512)(128)(4,1)S(1)}, pred[4]{0:T(512)(128)(4,1)}, u32[]{:S(2)}) copy-start(pred[4]{0:T(512)(128)(4,1)} %copy-done.95) | copy-start | bytes 16
  101.5 12.9 %copy-start.94 = (pred[4]{0:T(512)(128)(4,1)S(1)}, pred[4]{0:T(512)(128)(4,1)}, u32[]{:S(2)}) copy-start(pred[4]{0:T(512)(128)(4,1)} %copy-done.93) | copy-start | bytes 16
  101.5 13.1 %copy-start.92 = (pred[4]{0:T(512)(128)(4,1)S(1)}, pred[4]{0:T(512)(128)(4,1)}, u32[]{:S(2)}) copy-start(pred[4]{0:T(512)(128)(4,1)} %copy-done.91) | copy-start | bytes 16
  101.5 13.3 %copy-start.90 = (pred[4]{0:T(512)(128)(4,1)S(1)}, pred[4]{0:T(512)(128)(4,1)}, u32[]{:S(2)}) copy-start(pred[4]{0:T(512)(128)(4,1)} %copy-done.89) | copy-start | bytes 16
  101.5 13.4 %copy-start.83 = (s32[85]{0:T(128)S(1)}, s32[85]{0:T(128)}, u32[]{:S(2)}) copy-start(s32[85]{0:T(128)} %copy-done.82) | copy-start | bytes 1024
  102.6 26.3 %copy-start.79 = (pred[4]{0:T(512)(128)(4,1)S(1)}, pred[4]{0:T(512)(128)(4,1)}, u32[]{:S(2)}) copy-start(pred[4]{0:T(512)(128)(4,1)} %iota_compare_fusion.9) | copy-start | bytes 16
  111.4 11.0 %all-to-all-start.4 = ((f32[32,1,1026]{2,1,0:T(1,128)}), f32[32,1,1026]{2,1,0:T(1,128)S(1)}, u32[]{:S(2)}, u32[]{:S(2)}) async-start(f32[32,1,1026]{2,1,0:T(1,128)} %broadcast_select_fusion.62), calls=%async_computation.4 | async-start | bytes 294912 | tf_op jit(solution)/shard_map/all_to_all | solution.py:209
  115.7 13.1 %collective-permute-start.3 = (f32[13,256]{1,0:T(8,128)S(1)}, f32[13,256]{1,0:T(8,128)S(1)}, u32[]{:S(2)}, u32[]{:S(2)}) collective-permute-start(f32[13,256]{1,0:T(8,128)S(1)} %fusion.819), channel_id=1, source_target_pairs={{0,1},{1,0},{2,3},{3,2},{4,5},{5,4},{6,7},{7,6},{8,9},{9,8},{10,11... | collective-permute-start | bytes 39944 | tf_op jit(solution)/shard_map/ppermute | solution.py:172
  140.6 11.0 %all-to-all-start = ((f32[32,1,1028]{2,1,0:T(1,128)}), f32[32,1,1028]{2,1,0:T(1,128)S(1)}, u32[]{:S(2)}, u32[]{:S(2)}) async-start(f32[32,1,1028]{2,1,0:T(1,128)} %broadcast_select_fusion.118), calls=%async_computation | async-start | bytes 294912 | tf_op jit(solution)/shard_map/while/body/eval_jaxpr/all_to_all | solution.py:209
  143.2 14.6 %collective-permute-start = (f32[13,256]{1,0:T(8,128)S(1)}, f32[13,256]{1,0:T(8,128)S(1)}, u32[]{:S(2)}, u32[]{:S(2)}) collective-permute-start(f32[13,256]{1,0:T(8,128)S(1)} %fusion.871), channel_id=1, source_target_pairs={{0,1},{1,0},{2,3},{3,2},{4,5},{5,4},{6,7},{7,6},{8,9},{9,8},{10,11... | collective-permute-start | bytes 39944 | tf_op jit(solution)/shard_map/while/body/eval_jaxpr/ppermute | solution.py:172
  169.5 11.0 %all-to-all-start = ((f32[32,1,1028]{2,1,0:T(1,128)}), f32[32,1,1028]{2,1,0:T(1,128)S(1)}, u32[]{:S(2)}, u32[]{:S(2)}) async-start(f32[32,1,1028]{2,1,0:T(1,128)} %broadcast_select_fusion.118), calls=%async_computation | async-start | bytes 294912 | tf_op jit(solution)/shard_map/while/body/eval_jaxpr/all_to_all | solution.py:209
  172.1 14.6 %collective-permute-start = (f32[13,256]{1,0:T(8,128)S(1)}, f32[13,256]{1,0:T(8,128)S(1)}, u32[]{:S(2)}, u32[]{:S(2)}) collective-permute-start(f32[13,256]{1,0:T(8,128)S(1)} %fusion.871), channel_id=1, source_target_pairs={{0,1},{1,0},{2,3},{3,2},{4,5},{5,4},{6,7},{7,6},{8,9},{9,8},{10,11... | collective-permute-start | bytes 39944 | tf_op jit(solution)/shard_map/while/body/eval_jaxpr/ppermute | solution.py:172
  198.5 11.0 %all-to-all-start = ((f32[32,1,1028]{2,1,0:T(1,128)}), f32[32,1,1028]{2,1,0:T(1,128)S(1)}, u32[]{:S(2)}, u32[]{:S(2)}) async-start(f32[32,1,1028]{2,1,0:T(1,128)} %broadcast_select_fusion.118), calls=%async_computation | async-start | bytes 294912 | tf_op jit(solution)/shard_map/while/body/eval_jaxpr/all_to_all | solution.py:209
  201.1 14.6 %collective-permute-start = (f32[13,256]{1,0:T(8,128)S(1)}, f32[13,256]{1,0:T(8,128)S(1)}, u32[]{:S(2)}, u32[]{:S(2)}) collective-permute-start(f32[13,256]{1,0:T(8,128)S(1)} %fusion.871), channel_id=1, source_target_pairs={{0,1},{1,0},{2,3},{3,2},{4,5},{5,4},{6,7},{7,6},{8,9},{9,8},{10,11... | collective-permute-start | bytes 39944 | tf_op jit(solution)/shard_map/while/body/eval_jaxpr/ppermute | solution.py:172
  (46 other events, 155.6 us)

commit v8 on v6

--- a/solution.py
+++ b/solution.py
@@ -56,8 +56,7 @@
     return dict(
         pick_mass=gather_matrix(first, MASS_LINE).T,
         pick_stiff=gather_matrix(first, STIFF_LINE).T,
-        lanes_m=gather_matrix(second, MASS_LINE),
-        lanes_k=gather_matrix(second, STIFF_LINE),
+        lanes=jnp.concatenate([gather_matrix(second, STIFF_LINE), gather_matrix(second, MASS_LINE)], 0),
         scatter_second=gather_matrix(second, np.eye(4)).T,
         scatter_first=gather_matrix(first, np.eye(4)),
     )
@@ -77,11 +76,8 @@
     along_first_k = jnp.einsum("kx,dxy->dky", pick_stiff, v_mass, precision=HIGH) + jnp.einsum(
         "kx,dxy->dky", pick_mass, v_stiff, precision=HIGH
     )
-    lanes_m = mats["lanes_m"]
-    lanes_k = mats["lanes_k"]
-    flat_m = along_first_m.reshape(-1, second)
-    flat_k = along_first_k.reshape(-1, second)
-    element = jnp.dot(flat_m, lanes_k, precision=HIGH) + jnp.dot(flat_k, lanes_m, precision=HIGH)
+    flat = jnp.concatenate([along_first_m.reshape(-1, second), along_first_k.reshape(-1, second)], 1)
+    element = jnp.dot(flat, mats["lanes"], precision=HIGH)
     element = element.reshape(depth, 4, first_el, 4, second_el) * conduct.reshape(
         1, 1, first_el, 1, second_el
     )

time: 156 us -> 157 us (level)
  matrix products: 21.6 us -> 15.9 us
  other arithmetic: 33.8 us -> 38.6 us
    dot_general x12 -> x6, matrix products: 9.07 us -> 3.42 us  [local_products(): element = jnp.dot(flat, mats['lanes'], precision=HIGH)]
  transfers between devices with their start and end apart: 13 -> 13, of which waited for: 8 -> 9; matrix products, arithmetic and copies ran while one was open for 14% -> 16% of each run, Pallas kernels for 0% -> 0%
where the time goes in v8:
time: 157 us; the launch traced here: 156 us
  waiting for transfers between devices  41.2 us (26%)
  other arithmetic  38.6 us (25%)
  starting transfers between devices  36.5 us (23%)
  local copies, waits for them, and re-layouts  20.7 us (13%)
  matrix products  15.9 us (10%)
  between operations  2.03 us (1%)
    all_to_all x7, waiting for transfers between devices, plane_exchange(): got = lax.all_to_all(send, ('hx', 'hy'), 0, 0, tiled=True)  37.4 us
    all_to_all x7, starting transfers between devices, plane_exchange(): got = lax.all_to_all(send, ('hx', 'hy'), 0, 0, tiled=True)  35.5 us
    reduce_sum x2, other arithmetic, per_device(): current = jnp.sum(cond_nodes * gate_flat * (volts - reversal[:, None]), 0)  16.6 us
    select_n x7, other arithmetic, plane_exchange(): send = jnp.where(code_of[:, None] == code, table[code][None, :], send)  6.31 us
    ppermute x6, waiting for transfers between devices, torso_stage(): got = lax.ppermute(face, 'torso', [(0, 1), (1, 0)])  3.8 us
    select_n x44, local copies, waits for them, and re-layouts, plane_exchange(): received[offset] = jnp.where(valid, row[:pieces[offset].shape[0]], 0.0)  3.77 us
    dot_general x6, matrix products, local_products(): element = jnp.dot(flat, mats['lanes'], precision=HIGH)  3.42 us
    select_n x37, other arithmetic, plane_exchange(): received[offset] = jnp.where(valid, row[:pieces[offset].shape[0]], 0.0)  3.17 us
  transfers between devices with their start and end apart: 13, of which 9 were waited for; matrix products, arithmetic and copies ran while one was open for 16% of the time, Pallas kernels for 0%

profile of v8, /device:TPU:0, one launch (start us, length us, event | category | flops | bytes accessed | tf_op | source)
XLA Modules:
  0.0 155.9 jit_solution(1190112367640946932)
XLA Ops:
  0.7 0.8 copy.209
  2.9 0.7 mul.1097
  5.2 0.9 select_select_fusion.7
  6.2 0.6 convolution_multiply_fusion.3
  7.4 0.6 collective-permute-start.1
  8.1 0.6 slice_bitcast_fusion.22
  8.8 0.6 slice_bitcast_fusion.15
  9.4 0.7 broadcast_compare_fusion.11
  10.1 0.6 slice_bitcast_fusion.9
  10.7 0.6 compare_select_fusion
  13.2 0.7 all_to_all.31
  13.8 7.9 %all-to-all-start.1 = ((f32[16,1,1024]{2,1,0:T(1,128)}), f32[16,1,1024]{2,1,0:T(1,128)S(1)}, u32[]{:S(2)}, u32[]{:S(2)}) async-start(f32[16,1,1024]{2,1,0:T(1,128)} %all_to_all.31), calls=%async_computation.1 | async-start | bytes 131072 | tf_op jit(solution)/shard_map/all_to_all | solution.py:136
  21.8 7.9 %multiply_reduce_fusion.1 = (f32[4,13,256]{2,0,1:T(4,128)}, f32[40,4,13,256]{3,1,2,0:T(4,128)S(1)}) fusion(f32[40]{0:T(128)} %param.39, f32[4,13,256]{2,0,1:T(4,128)S(1)} %copy-done, f32[40]{0:T(128)} %get-tuple-element.830, f32[40]{0:T(128)} %get-tuple-element.829, f32[40]{0:T(128)} %get-tuple-element.831, f32[40]{0:T(128)} %get-tuple-element.832, ...), kind=kLoop, calls=%fused_computation.290 | loop fusion | flops 12766208 | bytes 4435616 | tf_op jit(solution)/shard_map/reduce_sum | solution.py:285
  29.8 0.6 broadcast_select_fusion.37
  30.5 0.7 fusion.453
  31.4 0.7 copy.207
  32.1 0.7 fusion.456
  33.2 0.7 copy.204
  33.9 0.9 fusion.272
  34.9 1.0 fusion.303
  35.9 1.0 fusion.304
  36.8 1.0 convolution_add_fusion.2
  37.8 0.6 convolution_multiply_fusion.2
  38.7 0.9 fusion.379
  39.6 0.6 fusion.369
  40.5 1.3 broadcast_multiply_fusion.1
  41.7 0.7 mul.1165
  42.4 0.7 mul.1166
  43.2 0.7 fusion.371
  44.5 0.8 select_select_fusion.9
  45.3 0.7 copy.220
  46.0 0.7 copy.213
  46.7 6.8 %all-to-all-start.2 = ((f32[16,1,1024]{2,1,0:T(1,128)}), f32[16,1,1024]{2,1,0:T(1,128)}, u32[]{:S(2)}, u32[]{:S(2)}) async-start(f32[16,1,1024]{2,1,0:T(1,128)} %copy.213), calls=%async_computation.2 | async-start | bytes 131072 | tf_op jit(solution)/shard_map/all_to_all | solution.py:136
  53.5 8.6 %multiply_reduce_fusion = (f32[4,13,256]{2,0,1:T(4,128)}, f32[40,4,13,256]{3,1,2,0:T(4,128)}) fusion(f32[4,13,256]{2,0,1:T(4,128)} %copy.220, f32[40]{0:T(128)} %param.39, f32[40]{0:T(128)} %get-tuple-element.830, f32[40]{0:T(128)} %get-tuple-element.829, f32[40]{0:T(128)} %get-tuple-element.831, f32[40]{0:T(128)} %get-tuple-element.832, ...), kind=kLoop, calls=%fused_computation.288 | loop fusion | flops 12766208 | bytes 4435616 | tf_op jit(solution)/shard_map/reduce_sum | solution.py:285
  62.1 0.8 broadcast_select_fusion.36
  64.0 0.9 fusion.275
  65.6 1.5 broadcast_select_fusion.30
  67.2 6.8 %all-to-all-start.3 = ((f32[16,1,768]{2,1,0:T(1,128)}), f32[16,1,768]{2,1,0:T(1,128)S(1)}, u32[]{:S(2)}, u32[]{:S(2)}) async-start(f32[16,1,768]{2,1,0:T(1,128)} %broadcast_select_fusion.30), calls=%async_computation.3 | async-start | bytes 98304 | tf_op jit(solution)/shard_map/all_to_all | solution.py:136
  74.0 7.4 %all-to-all-done.3 = f32[16,1,768]{2,1,0:T(1,128)S(1)} async-done(((f32[16,1,768]{2,1,0:T(1,128)}), f32[16,1,768]{2,1,0:T(1,128)S(1)}, u32[]{:S(2)}, u32[]{:S(2)}) %all-to-all-start.3) | async-done | bytes 49184 | tf_op jit(solution)/shard_map/all_to_all | solution.py:136
  82.3 1.0 multiply_bitcast_fusion.3
  83.3 1.0 fusion.301
  85.0 0.6 convolution_multiply_fusion.1
  86.6 0.7 copy.232
  88.3 1.0 broadcast_select_fusion.22
  89.3 3.5 %all-to-all-start.4 = ((f32[16,1,1026]{2,1,0:T(1,128)}), f32[16,1,1026]{2,1,0:T(1,128)S(1)}, u32[]{:S(2)}, u32[]{:S(2)}) async-start(f32[16,1,1026]{2,1,0:T(1,128)} %broadcast_select_fusion.22), calls=%async_computation.4 | async-start | bytes 147456 | tf_op jit(solution)/shard_map/all_to_all | solution.py:136
  92.8 7.5 %all-to-all-done.4 = f32[16,1,1026]{2,1,0:T(1,128)S(1)} async-done(((f32[16,1,1026]{2,1,0:T(1,128)}), f32[16,1,1026]{2,1,0:T(1,128)S(1)}, u32[]{:S(2)}, u32[]{:S(2)}) %all-to-all-start.4) | async-done | bytes 65696 | tf_op jit(solution)/shard_map/all_to_all | solution.py:136
  101.7 53.5 %while.33 = (s32[]{:T(128)}, f32[4,13,256]{2,1,0:T(8,128)S(1)}, f32[4,13,256]{2,1,0:T(8,128)S(1)}, f32[4,13,256]{2,1,0:T(8,128)S(1)}, f32[4,13,256]{2,1,0:T(8,12...) while((s32[]{:T(128)}, f32[4,13,256]{2,1,0:T(8,128)S(1)}, ...), condition=%wide.region_7.8_spmd.clone.clone.clone, body=%wide.region_4.7_spmd.clone.clone.clone.sunk | while | flops 213083744 | bytes 4259643 | solution.py:355
  102.7 0.6 convolution_multiply_fusion.5
  103.3 0.6 fusion.659
  104.6 1.1 collective-permute-done
  106.3 1.0 broadcast_select_fusion.66
  107.2 3.5 %all-to-all-start = ((f32[16,1,1028]{2,1,0:T(1,128)}), f32[16,1,1028]{2,1,0:T(1,128)S(1)}, u32[]{:S(2)}, u32[]{:S(2)}) async-start(f32[16,1,1028]{2,1,0:T(1,128)} %broadcast_select_fusion.66), calls=%async_computation | async-start | bytes 147456 | tf_op jit(solution)/shard_map/while/body/eval_jaxpr/all_to_all | solution.py:136
  110.8 7.5 %all-to-all-done = f32[16,1,1028]{2,1,0:T(1,128)S(1)} async-done(((f32[16,1,1028]{2,1,0:T(1,128)}), f32[16,1,1028]{2,1,0:T(1,128)S(1)}, u32[]{:S(2)}, u32[]{:S(2)}) %all-to-all-start) | async-done | bytes 65824 | tf_op jit(solution)/shard_map/while/body/eval_jaxpr/all_to_all | solution.py:136
  121.2 0.6 fusion.659
  122.4 1.1 collective-permute-done
  124.1 1.0 broadcast_select_fusion.66
  125.1 3.5 %all-to-all-start = ((f32[16,1,1028]{2,1,0:T(1,128)}), f32[16,1,1028]{2,1,0:T(1,128)S(1)}, u32[]{:S(2)}, u32[]{:S(2)}) async-start(f32[16,1,1028]{2,1,0:T(1,128)} %broadcast_select_fusion.66), calls=%async_computation | async-start | bytes 147456 | tf_op jit(solution)/shard_map/while/body/eval_jaxpr/all_to_all | solution.py:136
  128.6 7.5 %all-to-all-done = f32[16,1,1028]{2,1,0:T(1,128)S(1)} async-done(((f32[16,1,1028]{2,1,0:T(1,128)}), f32[16,1,1028]{2,1,0:T(1,128)S(1)}, u32[]{:S(2)}, u32[]{:S(2)}) %all-to-all-start) | async-done | bytes 65824 | tf_op jit(solution)/shard_map/while/body/eval_jaxpr/all_to_all | solution.py:136
  139.0 0.6 fusion.659
  140.3 1.1 collective-permute-done
  142.0 1.0 broadcast_select_fusion.66
  142.9 3.5 %all-to-all-start = ((f32[16,1,1028]{2,1,0:T(1,128)}), f32[16,1,1028]{2,1,0:T(1,128)S(1)}, u32[]{:S(2)}, u32[]{:S(2)}) async-start(f32[16,1,1028]{2,1,0:T(1,128)} %broadcast_select_fusion.66), calls=%async_computation | async-start | bytes 147456 | tf_op jit(solution)/shard_map/while/body/eval_jaxpr/all_to_all | solution.py:136
  146.5 7.5 %all-to-all-done = f32[16,1,1028]{2,1,0:T(1,128)S(1)} async-done(((f32[16,1,1028]{2,1,0:T(1,128)}), f32[16,1,1028]{2,1,0:T(1,128)S(1)}, u32[]{:S(2)}, u32[]{:S(2)}) %all-to-all-start) | async-done | bytes 65824 | tf_op jit(solution)/shard_map/while/body/eval_jaxpr/all_to_all | solution.py:136
  155.2 0.7 copy.233
  (438 shorter events, 24.4 us)
Async XLA Ops:
  1.7 5.4 %copy-start.9 = (s32[16]{0:T(128)}, s32[16]{0:T(128)S(1)}, u32[]{:S(2)}) copy-start(s32[16]{0:T(128)S(1)} %iota.909) | copy-start | bytes 196
  1.8 5.3 %copy-start.12 = (pred[16]{0:T(512)(128)(4,1)}, pred[16]{0:T(512)(128)(4,1)S(1)}, u32[]{:S(2)}) copy-start(pred[16]{0:T(512)(128)(4,1)S(1)} %iota.918) | copy-start | bytes 52
  2.0 5.1 %copy-start.14 = (pred[16]{0:T(512)(128)(4,1)}, pred[16]{0:T(512)(128)(4,1)S(1)}, u32[]{:S(2)}) copy-start(pred[16]{0:T(512)(128)(4,1)S(1)} %iota.915) | copy-start | bytes 52
  2.2 5.0 %copy-start.16 = (pred[16]{0:T(512)(128)(4,1)}, pred[16]{0:T(512)(128)(4,1)S(1)}, u32[]{:S(2)}) copy-start(pred[16]{0:T(512)(128)(4,1)S(1)} %iota.912) | copy-start | bytes 52
  2.3 4.8 %copy-start.18 = (pred[16]{0:T(512)(128)(4,1)}, pred[16]{0:T(512)(128)(4,1)S(1)}, u32[]{:S(2)}) copy-start(pred[16]{0:T(512)(128)(4,1)S(1)} %iota.904) | copy-start | bytes 52
  3.6 4.4 %copy-start.41 = (f32[3,40]{1,0:T(4,128)S(1)}, f32[3,40]{1,0:T(4,128)}, u32[]{:S(2)}) copy-start(f32[3,40]{1,0:T(4,128)} %param.38) | copy-start | bytes 1444
  3.6 5.1 %copy-start.39 = (f32[3,40]{1,0:T(4,128)S(1)}, f32[3,40]{1,0:T(4,128)}, u32[]{:S(2)}) copy-start(f32[3,40]{1,0:T(4,128)} %param.37) | copy-start | bytes 1444
  3.6 5.1 %copy-start.38 = (f32[4,40]{1,0:T(4,128)S(1)}, f32[4,40]{1,0:T(4,128)}, u32[]{:S(2)}) copy-start(f32[4,40]{1,0:T(4,128)} %param.40) | copy-start | bytes 1924
  3.7 5.1 %copy-start.40 = (f32[3,40]{1,0:T(4,128)S(1)}, f32[3,40]{1,0:T(4,128)}, u32[]{:S(2)}) copy-start(f32[3,40]{1,0:T(4,128)} %param.35) | copy-start | bytes 1444
  3.7 5.7 %copy-start.7 = (s32[4,13,256]{2,0,1:T(4,128)S(1)}, s32[4,13,256]{2,0,1:T(4,128)}, u32[]{:S(2)}) copy-start(s32[4,13,256]{2,0,1:T(4,128)} %param.34) | copy-start | bytes 159748
  3.7 5.7 %copy-start.8 = (s32[4,13,256]{2,0,1:T(4,128)S(1)}, s32[4,13,256]{2,0,1:T(4,128)}, u32[]{:S(2)}) copy-start(s32[4,13,256]{2,0,1:T(4,128)} %param.33) | copy-start | bytes 159748
  3.8 6.3 %copy-start.42 = (f32[3,40]{1,0:T(4,128)S(1)}, f32[3,40]{1,0:T(4,128)}, u32[]{:S(2)}) copy-start(f32[3,40]{1,0:T(4,128)} %param.36) | copy-start | bytes 1444
  4.2 3.2 %copy-start.36 = (s32[340]{0:T(512)}, s32[340]{0:T(512)S(1)}, u32[]{:S(2)}) copy-start(s32[340]{0:T(512)S(1)} %iota.926) | copy-start | bytes 4084
  4.4 3.0 %copy-start.43 = (pred[340]{0:T(512)(128)(4,1)}, pred[340]{0:T(512)(128)(4,1)S(1)}, u32[]{:S(2)}) copy-start(pred[340]{0:T(512)(128)(4,1)S(1)} %iota.935) | copy-start | bytes 1024
  4.6 2.8 %copy-start.45 = (pred[340]{0:T(512)(128)(4,1)}, pred[340]{0:T(512)(128)(4,1)S(1)}, u32[]{:S(2)}) copy-start(pred[340]{0:T(512)(128)(4,1)S(1)} %iota.932) | copy-start | bytes 1024
  4.7 2.7 %copy-start.47 = (pred[340]{0:T(512)(128)(4,1)}, pred[340]{0:T(512)(128)(4,1)S(1)}, u32[]{:S(2)}) copy-start(pred[340]{0:T(512)(128)(4,1)S(1)} %iota.929) | copy-start | bytes 1024
  4.9 3.1 %copy-start.49 = (pred[340]{0:T(512)(128)(4,1)}, pred[340]{0:T(512)(128)(4,1)S(1)}, u32[]{:S(2)}) copy-start(pred[340]{0:T(512)(128)(4,1)S(1)} %iota.921) | copy-start | bytes 1024
  4.9 16.9 %copy-start = (f32[4,13,256]{2,0,1:T(4,128)S(1)}, f32[4,13,256]{2,0,1:T(4,128)}, u32[]{:S(2)}) copy-start(f32[4,13,256]{2,0,1:T(4,128)} %param.31) | copy-start | bytes 159748
  7.4 5.0 %collective-permute-start.1 = (f32[13,256]{1,0:T(8,128)S(1)}, f32[13,256]{1,0:T(8,128)S(1)}, u32[]{:S(2)}, u32[]{:S(2)}) collective-permute-start(f32[13,256]{1,0:T(8,128)S(1)} %fusion.373), channel_id=1, source_target_pairs={{0,1},{1,0},{2,3},{3,2},{4,5},{5,4},{6,7},{7,6},{8,9},{9,8},{10,11... | collective-permute-start | bytes 39944 | tf_op jit(solution)/shard_map/ppermute | solution.py:103
  8.0 13.7 %copy-start.20 = (pred[16]{0:T(512)(128)(4,1)}, pred[16]{0:T(512)(128)(4,1)S(1)}, u32[]{:S(2)}) copy-start(pred[16]{0:T(512)(128)(4,1)S(1)} %get-tuple-element.652) | copy-start | bytes 52
  8.1 13.7 %copy-start.22 = (pred[16]{0:T(512)(128)(4,1)}, pred[16]{0:T(512)(128)(4,1)S(1)}, u32[]{:S(2)}) copy-start(pred[16]{0:T(512)(128)(4,1)S(1)} %get-tuple-element.815) | copy-start | bytes 52
  8.1 13.7 %copy-start.24 = (pred[16]{0:T(512)(128)(4,1)}, pred[16]{0:T(512)(128)(4,1)S(1)}, u32[]{:S(2)}) copy-start(pred[16]{0:T(512)(128)(4,1)S(1)} %get-tuple-element.816) | copy-start | bytes 52
  8.1 13.7 %copy-start.26 = (pred[16]{0:T(512)(128)(4,1)}, pred[16]{0:T(512)(128)(4,1)S(1)}, u32[]{:S(2)}) copy-start(pred[16]{0:T(512)(128)(4,1)S(1)} %get-tuple-element.817) | copy-start | bytes 52
  8.1 13.7 %copy-start.28 = (pred[16]{0:T(512)(128)(4,1)}, pred[16]{0:T(512)(128)(4,1)S(1)}, u32[]{:S(2)}) copy-start(pred[16]{0:T(512)(128)(4,1)S(1)} %get-tuple-element.818) | copy-start | bytes 52
  8.1 13.7 %copy-start.30 = (pred[16]{0:T(512)(128)(4,1)}, pred[16]{0:T(512)(128)(4,1)S(1)}, u32[]{:S(2)}) copy-start(pred[16]{0:T(512)(128)(4,1)S(1)} %get-tuple-element.819) | copy-start | bytes 52
  8.1 13.7 %copy-start.32 = (pred[16]{0:T(512)(128)(4,1)}, pred[16]{0:T(512)(128)(4,1)S(1)}, u32[]{:S(2)}) copy-start(pred[16]{0:T(512)(128)(4,1)S(1)} %get-tuple-element.820) | copy-start | bytes 52
  8.1 13.7 %copy-start.34 = (pred[16]{0:T(512)(128)(4,1)}, pred[16]{0:T(512)(128)(4,1)S(1)}, u32[]{:S(2)}) copy-start(pred[16]{0:T(512)(128)(4,1)S(1)} %get-tuple-element.821) | copy-start | bytes 52
  13.8 15.9 %all-to-all-start.1 = ((f32[16,1,1024]{2,1,0:T(1,128)}), f32[16,1,1024]{2,1,0:T(1,128)S(1)}, u32[]{:S(2)}, u32[]{:S(2)}) async-start(f32[16,1,1024]{2,1,0:T(1,128)} %all_to_all.31), calls=%async_computation.1 | async-start | bytes 131072 | tf_op jit(solution)/shard_map/all_to_all | solution.py:136
  34.8 18.6 %copy-start.4 = (pred[4,13,256]{2,0,1:T(4,128)(4,1)S(1)}, pred[4,13,256]{2,0,1:T(4,128)(4,1)}, u32[]{:S(2)}) copy-start(pred[4,13,256]{2,0,1:T(4,128)(4,1)} %get-tuple-element.755) | copy-start | bytes 39940
  40.3 2.9 %collective-permute-start.2 = (f32[13,256]{1,0:T(8,128)}, f32[13,256]{1,0:T(8,128)}, u32[]{:S(2)}, u32[]{:S(2)}) collective-permute-start(f32[13,256]{1,0:T(8,128)} %fusion.369), channel_id=1, source_target_pairs={{0,1},{1,0},{2,3},{3,2},{4,5},{5,4},{6,7},{7,6},{8,9},{9,8},{10,11... | collective-permute-start | bytes 39944 | tf_op jit(solution)/shard_map/ppermute | solution.py:103
  46.7 15.4 %all-to-all-start.2 = ((f32[16,1,1024]{2,1,0:T(1,128)}), f32[16,1,1024]{2,1,0:T(1,128)}, u32[]{:S(2)}, u32[]{:S(2)}) async-start(f32[16,1,1024]{2,1,0:T(1,128)} %copy.213), calls=%async_computation.2 | async-start | bytes 131072 | tf_op jit(solution)/shard_map/all_to_all | solution.py:136
  53.5 10.5 %copy-start.2 = (f32[256]{0:T(256)S(1)}, f32[256]{0:T(256)}, u32[]{:S(2)}) copy-start(f32[256]{0:T(256)} %compare_select_fusion) | copy-start | bytes 3076
  53.5 29.8 %copy-start.10 = (s32[16]{0:T(128)S(1)}, s32[16]{0:T(128)}, u32[]{:S(2)}) copy-start(s32[16]{0:T(128)} %copy-done.9) | copy-start | bytes 196
  62.1 22.2 %copy-start.13 = (pred[16]{0:T(512)(128)(4,1)S(1)}, pred[16]{0:T(512)(128)(4,1)}, u32[]{:S(2)}) copy-start(pred[16]{0:T(512)(128)(4,1)} %copy-done.12) | copy-start | bytes 52
  62.1 22.2 %copy-start.15 = (pred[16]{0:T(512)(128)(4,1)S(1)}, pred[16]{0:T(512)(128)(4,1)}, u32[]{:S(2)}) copy-start(pred[16]{0:T(512)(128)(4,1)} %copy-done.14) | copy-start | bytes 52
  62.1 22.2 %copy-start.17 = (pred[16]{0:T(512)(128)(4,1)S(1)}, pred[16]{0:T(512)(128)(4,1)}, u32[]{:S(2)}) copy-start(pred[16]{0:T(512)(128)(4,1)} %copy-done.16) | copy-start | bytes 52
  62.1 22.2 %copy-start.19 = (pred[16]{0:T(512)(128)(4,1)S(1)}, pred[16]{0:T(512)(128)(4,1)}, u32[]{:S(2)}) copy-start(pred[16]{0:T(512)(128)(4,1)} %copy-done.18) | copy-start | bytes 52
  62.1 22.8 %copy-start.1 = (f32[64,340]{1,0:T(8,128)S(1)}, f32[64,340]{1,0:T(8,128)}, u32[]{:S(2)}) copy-start(f32[64,340]{1,0:T(8,128)} %mul.1166) | copy-start | bytes 261124
  63.2 22.8 %copy-start.11 = (s32[16]{0:T(128)S(1)}, s32[16]{0:T(128)}, u32[]{:S(2)}) copy-start(s32[16]{0:T(128)} %copy-done.9) | copy-start | bytes 196
  64.0 22.2 %copy-start.5 = (f32[4,13]{1,0:T(4,128)S(1)}, f32[4,13]{1,0:T(4,128)}, u32[]{:S(2)}) copy-start(f32[4,13]{1,0:T(4,128)} %broadcast_multiply_fusion.1) | copy-start | bytes 628
  67.2 14.3 %all-to-all-start.3 = ((f32[16,1,768]{2,1,0:T(1,128)}), f32[16,1,768]{2,1,0:T(1,128)S(1)}, u32[]{:S(2)}, u32[]{:S(2)}) async-start(f32[16,1,768]{2,1,0:T(1,128)} %broadcast_select_fusion.30), calls=%async_computation.3 | async-start | bytes 98304 | tf_op jit(solution)/shard_map/all_to_all | solution.py:136
  84.9 3.4 %copy-start.21 = (pred[16]{0:T(512)(128)(4,1)S(1)}, pred[16]{0:T(512)(128)(4,1)}, u32[]{:S(2)}) copy-start(pred[16]{0:T(512)(128)(4,1)} %copy-done.20) | copy-start | bytes 52
  84.9 3.4 %copy-start.23 = (pred[16]{0:T(512)(128)(4,1)S(1)}, pred[16]{0:T(512)(128)(4,1)}, u32[]{:S(2)}) copy-start(pred[16]{0:T(512)(128)(4,1)} %copy-done.22) | copy-start | bytes 52
  84.9 3.4 %copy-start.25 = (pred[16]{0:T(512)(128)(4,1)S(1)}, pred[16]{0:T(512)(128)(4,1)}, u32[]{:S(2)}) copy-start(pred[16]{0:T(512)(128)(4,1)} %copy-done.24) | copy-start | bytes 52
  84.9 3.4 %copy-start.27 = (pred[16]{0:T(512)(128)(4,1)S(1)}, pred[16]{0:T(512)(128)(4,1)}, u32[]{:S(2)}) copy-start(pred[16]{0:T(512)(128)(4,1)} %copy-done.26) | copy-start | bytes 52
  84.9 3.4 %copy-start.29 = (pred[16]{0:T(512)(128)(4,1)S(1)}, pred[16]{0:T(512)(128)(4,1)}, u32[]{:S(2)}) copy-start(pred[16]{0:T(512)(128)(4,1)} %copy-done.28) | copy-start | bytes 52
  84.9 3.4 %copy-start.31 = (pred[16]{0:T(512)(128)(4,1)S(1)}, pred[16]{0:T(512)(128)(4,1)}, u32[]{:S(2)}) copy-start(pred[16]{0:T(512)(128)(4,1)} %copy-done.30) | copy-start | bytes 52
  84.9 3.4 %copy-start.33 = (pred[16]{0:T(512)(128)(4,1)S(1)}, pred[16]{0:T(512)(128)(4,1)}, u32[]{:S(2)}) copy-start(pred[16]{0:T(512)(128)(4,1)} %copy-done.32) | copy-start | bytes 52
  84.9 3.4 %copy-start.35 = (pred[16]{0:T(512)(128)(4,1)S(1)}, pred[16]{0:T(512)(128)(4,1)}, u32[]{:S(2)}) copy-start(pred[16]{0:T(512)(128)(4,1)} %copy-done.34) | copy-start | bytes 52
  85.5 16.0 %copy-start.3 = (f32[256]{0:T(256)S(1)}, f32[256]{0:T(256)}, u32[]{:S(2)}) copy-start(f32[256]{0:T(256)} %compare_select_fusion) | copy-start | bytes 3076
  85.6 16.1 %copy-start.6 = (f32[1,4,85]{2,1,0:T(4,128)S(1)}, f32[1,4,85]{2,1,0:T(4,128)}, u32[]{:S(2)}) copy-start(f32[1,4,85]{2,1,0:T(4,128)} %param.42) | copy-start | bytes 4084
  85.6 16.1 %copy-start.37 = (s32[340]{0:T(512)S(1)}, s32[340]{0:T(512)}, u32[]{:S(2)}) copy-start(s32[340]{0:T(512)} %copy-done.36) | copy-start | bytes 4084
  85.6 16.1 %copy-start.44 = (pred[340]{0:T(512)(128)(4,1)S(1)}, pred[340]{0:T(512)(128)(4,1)}, u32[]{:S(2)}) copy-start(pred[340]{0:T(512)(128)(4,1)} %copy-done.43) | copy-start | bytes 1024
  85.6 16.1 %copy-start.46 = (pred[340]{0:T(512)(128)(4,1)S(1)}, pred[340]{0:T(512)(128)(4,1)}, u32[]{:S(2)}) copy-start(pred[340]{0:T(512)(128)(4,1)} %copy-done.45) | copy-start | bytes 1024
  85.6 16.1 %copy-start.48 = (pred[340]{0:T(512)(128)(4,1)S(1)}, pred[340]{0:T(512)(128)(4,1)}, u32[]{:S(2)}) copy-start(pred[340]{0:T(512)(128)(4,1)} %copy-done.47) | copy-start | bytes 1024
  85.6 16.1 %copy-start.50 = (pred[340]{0:T(512)(128)(4,1)S(1)}, pred[340]{0:T(512)(128)(4,1)}, u32[]{:S(2)}) copy-start(pred[340]{0:T(512)(128)(4,1)} %copy-done.49) | copy-start | bytes 1024
  86.4 1.2 collective-permute-start.3
  89.3 11.0 %all-to-all-start.4 = ((f32[16,1,1026]{2,1,0:T(1,128)}), f32[16,1,1026]{2,1,0:T(1,128)S(1)}, u32[]{:S(2)}, u32[]{:S(2)}) async-start(f32[16,1,1026]{2,1,0:T(1,128)} %broadcast_select_fusion.22), calls=%async_computation.4 | async-start | bytes 147456 | tf_op jit(solution)/shard_map/all_to_all | solution.py:136
  104.4 1.2 collective-permute-start
  107.2 11.0 %all-to-all-start = ((f32[16,1,1028]{2,1,0:T(1,128)}), f32[16,1,1028]{2,1,0:T(1,128)S(1)}, u32[]{:S(2)}, u32[]{:S(2)}) async-start(f32[16,1,1028]{2,1,0:T(1,128)} %broadcast_select_fusion.66), calls=%async_computation | async-start | bytes 147456 | tf_op jit(solution)/shard_map/while/body/eval_jaxpr/all_to_all | solution.py:136
  122.3 1.2 collective-permute-start
  125.1 11.0 %all-to-all-start = ((f32[16,1,1028]{2,1,0:T(1,128)}), f32[16,1,1028]{2,1,0:T(1,128)S(1)}, u32[]{:S(2)}, u32[]{:S(2)}) async-start(f32[16,1,1028]{2,1,0:T(1,128)} %broadcast_select_fusion.66), calls=%async_computation | async-start | bytes 147456 | tf_op jit(solution)/shard_map/while/body/eval_jaxpr/all_to_all | solution.py:136
  140.1 1.2 collective-permute-start
  142.9 11.0 %all-to-all-start = ((f32[16,1,1028]{2,1,0:T(1,128)}), f32[16,1,1028]{2,1,0:T(1,128)S(1)}, u32[]{:S(2)}, u32[]{:S(2)}) async-start(f32[16,1,1028]{2,1,0:T(1,128)} %broadcast_select_fusion.66), calls=%async_computation | async-start | bytes 147456 | tf_op jit(solution)/shard_map/while/body/eval_jaxpr/all_to_all | solution.py:136

commit v9 on v6

--- a/solution.py
+++ b/solution.py
@@ -56,14 +56,14 @@
     return dict(
         pick_mass=gather_matrix(first, MASS_LINE).T,
         pick_stiff=gather_matrix(first, STIFF_LINE).T,
+        lanes_k=gather_matrix(second, STIFF_LINE),
         lanes_m=gather_matrix(second, MASS_LINE),
-        lanes_k=gather_matrix(second, STIFF_LINE),
         scatter_second=gather_matrix(second, np.eye(4)).T,
         scatter_first=gather_matrix(first, np.eye(4)),
     )
 
 
-def local_products(values, conduct, mats):
+def local_products(values, conduct, mats, merged=False):
     depth, first, second = values.shape
     first_el, second_el = conduct.shape[1], conduct.shape[2]
     mass_d = [[float(MASS_LINE[i, j]) for j in range(4)] for i in range(4)]
@@ -77,11 +77,15 @@
     along_first_k = jnp.einsum("kx,dxy->dky", pick_stiff, v_mass, precision=HIGH) + jnp.einsum(
         "kx,dxy->dky", pick_mass, v_stiff, precision=HIGH
     )
-    lanes_m = mats["lanes_m"]
-    lanes_k = mats["lanes_k"]
     flat_m = along_first_m.reshape(-1, second)
     flat_k = along_first_k.reshape(-1, second)
-    element = jnp.dot(flat_m, lanes_k, precision=HIGH) + jnp.dot(flat_k, lanes_m, precision=HIGH)
+    if merged:
+        lanes = jnp.concatenate([mats["lanes_k"], mats["lanes_m"]], 0)
+        element = jnp.dot(jnp.concatenate([flat_m, flat_k], 1), lanes, precision=HIGH)
+    else:
+        element = jnp.dot(flat_m, mats["lanes_k"], precision=HIGH) + jnp.dot(
+            flat_k, mats["lanes_m"], precision=HIGH
+        )
     element = element.reshape(depth, 4, first_el, 4, second_el) * conduct.reshape(
         1, 1, first_el, 1, second_el
     )
@@ -319,7 +323,7 @@
     zero_lanes = 0.0 * torso_weight[0, 0]
 
     def exchange(residual, extra):
-        local = local_products(residual, torso_cond, mats)
+        local = local_products(residual, torso_cond, mats, merged=True)
         terms = [
             torso_weight * residual * residual,
             residual * local + weighted_mass * residual * residual,

time: 156 us -> 160 us (1.026)
  other arithmetic: 33.8 us -> 39.2 us
  matrix products: 21.6 us -> 18.3 us
    dot_general x12 -> x8, matrix products: 9.07 us -> 5.92 us  [the longest x4 2.25 us: local_products(): jnp.dot(jnp.concatenate([flat_m, flat_k], 1), lanes, precision=HIGH)]
  transfers between devices with their start and end apart: 13 -> 13, of which waited for: 8 -> 9; matrix products, arithmetic and copies ran while one was open for 14% -> 16% of each run, Pallas kernels for 0% -> 0%
where the time goes in v9:
time: 160 us; the launch traced here: 159 us
  waiting for transfers between devices  41.2 us (26%)
  other arithmetic  39.2 us (25%)
  starting transfers between devices  36.7 us (23%)
  local copies, waits for them, and re-layouts  20.8 us (13%)
  matrix products  18.3 us (11%)
  between operations  2.07 us (1%)
    all_to_all x7, waiting for transfers between devices, plane_exchange(): got = lax.all_to_all(send, ('hx', 'hy'), 0, 0, tiled=True)  37.4 us
    all_to_all x7, starting transfers between devices, plane_exchange(): got = lax.all_to_all(send, ('hx', 'hy'), 0, 0, tiled=True)  35.7 us
    reduce_sum x2, other arithmetic, per_device(): current = jnp.sum(cond_nodes * gate_flat * (volts - reversal[:, None]), 0)  16.6 us
    select_n x7, other arithmetic, plane_exchange(): send = jnp.where(code_of[:, None] == code, table[code][None, :], send)  6.3 us
    ppermute x6, waiting for transfers between devices, torso_stage(): got = lax.ppermute(face, 'torso', [(0, 1), (1, 0)])  3.8 us
    select_n x44, local copies, waits for them, and re-layouts, plane_exchange(): received[offset] = jnp.where(valid, row[:pieces[offset].shape[0]], 0.0)  3.77 us
  transfers between devices with their start and end apart: 13, of which 9 were waited for; matrix products, arithmetic and copies ran while one was open for 16% of the time, Pallas kernels for 0%

profile of v9, /device:TPU:0, one launch (start us, length us, event | category | flops | bytes accessed | tf_op | source)
XLA Modules:
  0.0 159.1 jit_solution(8778495289341558870)
XLA Ops:
  0.7 0.8 copy.209
  2.9 0.7 mul.1105
  3.7 0.9 select_select_fusion.8
  6.7 0.6 collective-permute-start.1
  7.4 0.6 slice_bitcast_fusion.22
  8.8 0.6 slice_bitcast_fusion.15
  9.4 0.7 broadcast_compare_fusion.11
  10.1 0.6 slice_bitcast_fusion.9
  11.3 0.6 or_select_fusion.1
  11.9 0.9 select_select_fusion.7
  14.1 0.7 all_to_all.31
  14.8 7.9 %all-to-all-start.1 = ((f32[16,1,1024]{2,1,0:T(1,128)}), f32[16,1,1024]{2,1,0:T(1,128)S(1)}, u32[]{:S(2)}, u32[]{:S(2)}) async-start(f32[16,1,1024]{2,1,0:T(1,128)} %all_to_all.31), calls=%async_computation.1 | async-start | bytes 131072 | tf_op jit(solution)/shard_map/all_to_all | solution.py:144
  22.8 7.9 %multiply_reduce_fusion.1 = (f32[4,13,256]{2,0,1:T(4,128)}, f32[40,4,13,256]{3,1,2,0:T(4,128)S(1)}) fusion(f32[40]{0:T(128)} %param.39, f32[4,13,256]{2,0,1:T(4,128)S(1)} %copy-done.2, f32[40]{0:T(128)} %get-tuple-element.844, f32[40]{0:T(128)} %get-tuple-element.843, f32[40]{0:T(128)} %get-tuple-element.845, f32[40]{0:T(128)} %get-tuple-element.846, ...), kind=kLoop, calls=%fused_computation.290 | loop fusion | flops 12766208 | bytes 4435616 | tf_op jit(solution)/shard_map/reduce_sum | solution.py:293
  30.7 0.6 broadcast_select_fusion.37
  31.4 0.7 fusion.461
  32.4 0.7 copy.207
  33.1 0.6 fusion.464
  34.1 0.7 copy.204
  34.8 0.9 fusion.280
  35.8 0.9 fusion.312
  36.7 0.9 fusion.311
  37.7 1.4 fusion.616
  39.1 0.9 convolution_add_fusion.4
  40.1 1.4 fusion.232
  41.8 0.9 fusion.387
  42.7 0.6 fusion.377
  43.5 1.3 broadcast_multiply_fusion.1
  44.8 0.7 mul.1173
  45.5 0.7 mul.1174
  46.3 0.7 fusion.379
  47.6 0.8 select_select_fusion.11
  48.4 0.7 copy.220
  49.1 0.7 copy.213
  49.8 6.8 %all-to-all-start.2 = ((f32[16,1,1024]{2,1,0:T(1,128)}), f32[16,1,1024]{2,1,0:T(1,128)}, u32[]{:S(2)}, u32[]{:S(2)}) async-start(f32[16,1,1024]{2,1,0:T(1,128)} %copy.213), calls=%async_computation.2 | async-start | bytes 131072 | tf_op jit(solution)/shard_map/all_to_all | solution.py:144
  56.5 8.6 %multiply_reduce_fusion = (f32[4,13,256]{2,0,1:T(4,128)}, f32[40,4,13,256]{3,1,2,0:T(4,128)}) fusion(f32[4,13,256]{2,0,1:T(4,128)} %copy.220, f32[40]{0:T(128)} %param.39, f32[40]{0:T(128)} %get-tuple-element.844, f32[40]{0:T(128)} %get-tuple-element.843, f32[40]{0:T(128)} %get-tuple-element.845, f32[40]{0:T(128)} %get-tuple-element.846, ...), kind=kLoop, calls=%fused_computation.288 | loop fusion | flops 12766208 | bytes 4435616 | tf_op jit(solution)/shard_map/reduce_sum | solution.py:293
  65.2 0.8 broadcast_select_fusion.36
  67.0 0.9 fusion.283
  68.7 1.5 broadcast_select_fusion.30
  70.2 7.0 %all-to-all-start.3 = ((f32[16,1,768]{2,1,0:T(1,128)}), f32[16,1,768]{2,1,0:T(1,128)S(1)}, u32[]{:S(2)}, u32[]{:S(2)}) async-start(f32[16,1,768]{2,1,0:T(1,128)} %broadcast_select_fusion.30), calls=%async_computation.3 | async-start | bytes 98304 | tf_op jit(solution)/shard_map/all_to_all | solution.py:144
  77.3 7.5 %all-to-all-done.3 = f32[16,1,768]{2,1,0:T(1,128)S(1)} async-done(((f32[16,1,768]{2,1,0:T(1,128)}), f32[16,1,768]{2,1,0:T(1,128)S(1)}, u32[]{:S(2)}, u32[]{:S(2)}) %all-to-all-start.3) | async-done | bytes 49184 | tf_op jit(solution)/shard_map/all_to_all | solution.py:144
  85.5 1.0 multiply_bitcast_fusion.3
  86.5 0.9 fusion.309
  88.2 0.6 convolution_multiply_fusion.1
  89.8 0.7 copy.232
  91.5 1.0 broadcast_select_fusion.22
  92.5 3.5 %all-to-all-start.4 = ((f32[16,1,1026]{2,1,0:T(1,128)}), f32[16,1,1026]{2,1,0:T(1,128)S(1)}, u32[]{:S(2)}, u32[]{:S(2)}) async-start(f32[16,1,1026]{2,1,0:T(1,128)} %broadcast_select_fusion.22), calls=%async_computation.4 | async-start | bytes 147456 | tf_op jit(solution)/shard_map/all_to_all | solution.py:144
  96.0 7.5 %all-to-all-done.4 = f32[16,1,1026]{2,1,0:T(1,128)S(1)} async-done(((f32[16,1,1026]{2,1,0:T(1,128)}), f32[16,1,1026]{2,1,0:T(1,128)S(1)}, u32[]{:S(2)}, u32[]{:S(2)}) %all-to-all-start.4) | async-done | bytes 65696 | tf_op jit(solution)/shard_map/all_to_all | solution.py:144
  104.9 53.5 %while.33 = (s32[]{:T(128)}, f32[4,13,256]{2,1,0:T(8,128)S(1)}, f32[4,13,256]{2,1,0:T(8,128)S(1)}, f32[4,13,256]{2,1,0:T(8,128)S(1)}, f32[4,13,256]{2,1,0:T(8,12...) while((s32[]{:T(128)}, f32[4,13,256]{2,1,0:T(8,128)S(1)}, ...), condition=%wide.region_7.8_spmd.clone.clone.clone, body=%wide.region_4.7_spmd.clone.clone.clone.sunk | while | flops 213083744 | bytes 4259643 | solution.py:363
  106.5 0.6 fusion.675
  107.8 1.1 collective-permute-done
  109.5 1.0 broadcast_select_fusion.66
  110.4 3.5 %all-to-all-start = ((f32[16,1,1028]{2,1,0:T(1,128)}), f32[16,1,1028]{2,1,0:T(1,128)S(1)}, u32[]{:S(2)}, u32[]{:S(2)}) async-start(f32[16,1,1028]{2,1,0:T(1,128)} %broadcast_select_fusion.66), calls=%async_computation | async-start | bytes 147456 | tf_op jit(solution)/shard_map/while/body/eval_jaxpr/all_to_all | solution.py:144
  114.0 7.5 %all-to-all-done = f32[16,1,1028]{2,1,0:T(1,128)S(1)} async-done(((f32[16,1,1028]{2,1,0:T(1,128)}), f32[16,1,1028]{2,1,0:T(1,128)S(1)}, u32[]{:S(2)}, u32[]{:S(2)}) %all-to-all-start) | async-done | bytes 65824 | tf_op jit(solution)/shard_map/while/body/eval_jaxpr/all_to_all | solution.py:144
  124.4 0.6 fusion.675
  125.6 1.1 collective-permute-done
  127.3 1.0 broadcast_select_fusion.66
  128.3 3.5 %all-to-all-start = ((f32[16,1,1028]{2,1,0:T(1,128)}), f32[16,1,1028]{2,1,0:T(1,128)S(1)}, u32[]{:S(2)}, u32[]{:S(2)}) async-start(f32[16,1,1028]{2,1,0:T(1,128)} %broadcast_select_fusion.66), calls=%async_computation | async-start | bytes 147456 | tf_op jit(solution)/shard_map/while/body/eval_jaxpr/all_to_all | solution.py:144
  131.9 7.5 %all-to-all-done = f32[16,1,1028]{2,1,0:T(1,128)S(1)} async-done(((f32[16,1,1028]{2,1,0:T(1,128)}), f32[16,1,1028]{2,1,0:T(1,128)S(1)}, u32[]{:S(2)}, u32[]{:S(2)}) %all-to-all-start) | async-done | bytes 65824 | tf_op jit(solution)/shard_map/while/body/eval_jaxpr/all_to_all | solution.py:144
  142.2 0.6 fusion.675
  143.5 1.1 collective-permute-done
  145.2 1.0 broadcast_select_fusion.66
  146.1 3.5 %all-to-all-start = ((f32[16,1,1028]{2,1,0:T(1,128)}), f32[16,1,1028]{2,1,0:T(1,128)S(1)}, u32[]{:S(2)}, u32[]{:S(2)}) async-start(f32[16,1,1028]{2,1,0:T(1,128)} %broadcast_select_fusion.66), calls=%async_computation | async-start | bytes 147456 | tf_op jit(solution)/shard_map/while/body/eval_jaxpr/all_to_all | solution.py:144
  149.7 7.5 %all-to-all-done = f32[16,1,1028]{2,1,0:T(1,128)S(1)} async-done(((f32[16,1,1028]{2,1,0:T(1,128)}), f32[16,1,1028]{2,1,0:T(1,128)S(1)}, u32[]{:S(2)}, u32[]{:S(2)}) %all-to-all-start) | async-done | bytes 65824 | tf_op jit(solution)/shard_map/while/body/eval_jaxpr/all_to_all | solution.py:144
  158.4 0.7 copy.233
  (444 shorter events, 25.6 us)
Async XLA Ops:
  1.7 4.8 %copy-start.11 = (s32[16]{0:T(128)}, s32[16]{0:T(128)S(1)}, u32[]{:S(2)}) copy-start(s32[16]{0:T(128)S(1)} %iota.973) | copy-start | bytes 196
  1.8 4.6 %copy-start.13 = (pred[16]{0:T(512)(128)(4,1)}, pred[16]{0:T(512)(128)(4,1)S(1)}, u32[]{:S(2)}) copy-start(pred[16]{0:T(512)(128)(4,1)S(1)} %iota.982) | copy-start | bytes 52
  2.0 4.5 %copy-start.15 = (pred[16]{0:T(512)(128)(4,1)}, pred[16]{0:T(512)(128)(4,1)S(1)}, u32[]{:S(2)}) copy-start(pred[16]{0:T(512)(128)(4,1)S(1)} %iota.979) | copy-start | bytes 52
  2.1 4.3 %copy-start.17 = (pred[16]{0:T(512)(128)(4,1)}, pred[16]{0:T(512)(128)(4,1)S(1)}, u32[]{:S(2)}) copy-start(pred[16]{0:T(512)(128)(4,1)S(1)} %iota.976) | copy-start | bytes 52
  2.3 4.1 %copy-start.19 = (pred[16]{0:T(512)(128)(4,1)}, pred[16]{0:T(512)(128)(4,1)S(1)}, u32[]{:S(2)}) copy-start(pred[16]{0:T(512)(128)(4,1)S(1)} %iota.968) | copy-start | bytes 52
  4.7 3.3 %copy-start.40 = (f32[3,40]{1,0:T(4,128)S(1)}, f32[3,40]{1,0:T(4,128)}, u32[]{:S(2)}) copy-start(f32[3,40]{1,0:T(4,128)} %param.37) | copy-start | bytes 1444
  4.7 4.1 %copy-start.39 = (f32[4,40]{1,0:T(4,128)S(1)}, f32[4,40]{1,0:T(4,128)}, u32[]{:S(2)}) copy-start(f32[4,40]{1,0:T(4,128)} %param.40) | copy-start | bytes 1924
  4.7 4.1 %copy-start.41 = (f32[3,40]{1,0:T(4,128)S(1)}, f32[3,40]{1,0:T(4,128)}, u32[]{:S(2)}) copy-start(f32[3,40]{1,0:T(4,128)} %param.35) | copy-start | bytes 1444
  4.7 4.7 %copy-start.9 = (s32[4,13,256]{2,0,1:T(4,128)S(1)}, s32[4,13,256]{2,0,1:T(4,128)}, u32[]{:S(2)}) copy-start(s32[4,13,256]{2,0,1:T(4,128)} %param.34) | copy-start | bytes 159748
  4.7 4.7 %copy-start.10 = (s32[4,13,256]{2,0,1:T(4,128)S(1)}, s32[4,13,256]{2,0,1:T(4,128)}, u32[]{:S(2)}) copy-start(s32[4,13,256]{2,0,1:T(4,128)} %param.33) | copy-start | bytes 159748
  4.7 5.4 %copy-start.43 = (f32[3,40]{1,0:T(4,128)S(1)}, f32[3,40]{1,0:T(4,128)}, u32[]{:S(2)}) copy-start(f32[3,40]{1,0:T(4,128)} %param.36) | copy-start | bytes 1444
  4.8 6.6 %copy-start.1 = (f32[256,340]{0,1:T(8,128)}, f32[256,340]{0,1:T(8,128)S(1)}, u32[]{:S(2)}) copy-start(f32[256,340]{0,1:T(8,128)S(1)} %select_n.2963) | copy-start | bytes 1044484
  4.8 6.5 %copy-start = (f32[256,340]{0,1:T(8,128)}, f32[256,340]{0,1:T(8,128)S(1)}, u32[]{:S(2)}) copy-start(f32[256,340]{0,1:T(8,128)S(1)} %select_n.2996) | copy-start | bytes 1044484
  4.9 17.9 %copy-start.2 = (f32[4,13,256]{2,0,1:T(4,128)S(1)}, f32[4,13,256]{2,0,1:T(4,128)}, u32[]{:S(2)}) copy-start(f32[4,13,256]{2,0,1:T(4,128)} %param.31) | copy-start | bytes 159748
  6.7 6.7 %collective-permute-start.1 = (f32[13,256]{1,0:T(8,128)S(1)}, f32[13,256]{1,0:T(8,128)S(1)}, u32[]{:S(2)}, u32[]{:S(2)}) collective-permute-start(f32[13,256]{1,0:T(8,128)S(1)} %fusion.381), channel_id=1, source_target_pairs={{0,1},{1,0},{2,3},{3,2},{4,5},{5,4},{6,7},{7,6},{8,9},{9,8},{10,11... | collective-permute-start | bytes 39944 | tf_op jit(solution)/shard_map/ppermute | solution.py:111
  7.3 15.4 %copy-start.21 = (pred[16]{0:T(512)(128)(4,1)}, pred[16]{0:T(512)(128)(4,1)S(1)}, u32[]{:S(2)}) copy-start(pred[16]{0:T(512)(128)(4,1)S(1)} %get-tuple-element.663) | copy-start | bytes 52
  7.3 15.3 %copy-start.23 = (pred[16]{0:T(512)(128)(4,1)}, pred[16]{0:T(512)(128)(4,1)S(1)}, u32[]{:S(2)}) copy-start(pred[16]{0:T(512)(128)(4,1)S(1)} %get-tuple-element.829) | copy-start | bytes 52
  7.3 15.3 %copy-start.25 = (pred[16]{0:T(512)(128)(4,1)}, pred[16]{0:T(512)(128)(4,1)S(1)}, u32[]{:S(2)}) copy-start(pred[16]{0:T(512)(128)(4,1)S(1)} %get-tuple-element.830) | copy-start | bytes 52
  7.4 15.3 %copy-start.27 = (pred[16]{0:T(512)(128)(4,1)}, pred[16]{0:T(512)(128)(4,1)S(1)}, u32[]{:S(2)}) copy-start(pred[16]{0:T(512)(128)(4,1)S(1)} %get-tuple-element.831) | copy-start | bytes 52
  7.4 15.3 %copy-start.29 = (pred[16]{0:T(512)(128)(4,1)}, pred[16]{0:T(512)(128)(4,1)S(1)}, u32[]{:S(2)}) copy-start(pred[16]{0:T(512)(128)(4,1)S(1)} %get-tuple-element.832) | copy-start | bytes 52
  7.4 15.3 %copy-start.31 = (pred[16]{0:T(512)(128)(4,1)}, pred[16]{0:T(512)(128)(4,1)S(1)}, u32[]{:S(2)}) copy-start(pred[16]{0:T(512)(128)(4,1)S(1)} %get-tuple-element.833) | copy-start | bytes 52
  7.4 15.3 %copy-start.33 = (pred[16]{0:T(512)(128)(4,1)}, pred[16]{0:T(512)(128)(4,1)S(1)}, u32[]{:S(2)}) copy-start(pred[16]{0:T(512)(128)(4,1)S(1)} %get-tuple-element.834) | copy-start | bytes 52
  7.4 15.3 %copy-start.35 = (pred[16]{0:T(512)(128)(4,1)}, pred[16]{0:T(512)(128)(4,1)S(1)}, u32[]{:S(2)}) copy-start(pred[16]{0:T(512)(128)(4,1)S(1)} %get-tuple-element.835) | copy-start | bytes 52
  8.1 4.8 %copy-start.37 = (s32[340]{0:T(512)}, s32[340]{0:T(512)S(1)}, u32[]{:S(2)}) copy-start(s32[340]{0:T(512)S(1)} %iota.1004) | copy-start | bytes 4084
  8.3 14.5 %copy-start.44 = (pred[340]{0:T(512)(128)(4,1)}, pred[340]{0:T(512)(128)(4,1)S(1)}, u32[]{:S(2)}) copy-start(pred[340]{0:T(512)(128)(4,1)S(1)} %iota.1013) | copy-start | bytes 1024
  8.4 14.3 %copy-start.46 = (pred[340]{0:T(512)(128)(4,1)}, pred[340]{0:T(512)(128)(4,1)S(1)}, u32[]{:S(2)}) copy-start(pred[340]{0:T(512)(128)(4,1)S(1)} %iota.1010) | copy-start | bytes 1024
  8.6 4.3 %copy-start.48 = (pred[340]{0:T(512)(128)(4,1)}, pred[340]{0:T(512)(128)(4,1)S(1)}, u32[]{:S(2)}) copy-start(pred[340]{0:T(512)(128)(4,1)S(1)} %iota.1007) | copy-start | bytes 1024
  8.8 4.1 %copy-start.50 = (pred[340]{0:T(512)(128)(4,1)}, pred[340]{0:T(512)(128)(4,1)S(1)}, u32[]{:S(2)}) copy-start(pred[340]{0:T(512)(128)(4,1)S(1)} %iota.1000) | copy-start | bytes 1024
  14.8 15.9 %all-to-all-start.1 = ((f32[16,1,1024]{2,1,0:T(1,128)}), f32[16,1,1024]{2,1,0:T(1,128)S(1)}, u32[]{:S(2)}, u32[]{:S(2)}) async-start(f32[16,1,1024]{2,1,0:T(1,128)} %all_to_all.31), calls=%async_computation.1 | async-start | bytes 131072 | tf_op jit(solution)/shard_map/all_to_all | solution.py:144
  35.7 20.8 %copy-start.6 = (pred[4,13,256]{2,0,1:T(4,128)(4,1)S(1)}, pred[4,13,256]{2,0,1:T(4,128)(4,1)}, u32[]{:S(2)}) copy-start(pred[4,13,256]{2,0,1:T(4,128)(4,1)} %get-tuple-element.766) | copy-start | bytes 39940
  43.3 3.0 %collective-permute-start.2 = (f32[13,256]{1,0:T(8,128)}, f32[13,256]{1,0:T(8,128)}, u32[]{:S(2)}, u32[]{:S(2)}) collective-permute-start(f32[13,256]{1,0:T(8,128)} %fusion.377), channel_id=1, source_target_pairs={{0,1},{1,0},{2,3},{3,2},{4,5},{5,4},{6,7},{7,6},{8,9},{9,8},{10,11... | collective-permute-start | bytes 39944 | tf_op jit(solution)/shard_map/ppermute | solution.py:111
  49.8 15.4 %all-to-all-start.2 = ((f32[16,1,1024]{2,1,0:T(1,128)}), f32[16,1,1024]{2,1,0:T(1,128)}, u32[]{:S(2)}, u32[]{:S(2)}) async-start(f32[16,1,1024]{2,1,0:T(1,128)} %copy.213), calls=%async_computation.2 | async-start | bytes 131072 | tf_op jit(solution)/shard_map/all_to_all | solution.py:144
  56.5 10.5 %copy-start.4 = (f32[256]{0:T(256)S(1)}, f32[256]{0:T(256)}, u32[]{:S(2)}) copy-start(f32[256]{0:T(256)} %compare_select_fusion) | copy-start | bytes 3076
  65.2 22.3 %copy-start.12 = (s32[16]{0:T(128)S(1)}, s32[16]{0:T(128)}, u32[]{:S(2)}) copy-start(s32[16]{0:T(128)} %copy-done.11) | copy-start | bytes 196
  65.2 22.3 %copy-start.14 = (pred[16]{0:T(512)(128)(4,1)S(1)}, pred[16]{0:T(512)(128)(4,1)}, u32[]{:S(2)}) copy-start(pred[16]{0:T(512)(128)(4,1)} %copy-done.13) | copy-start | bytes 52
  65.2 22.3 %copy-start.16 = (pred[16]{0:T(512)(128)(4,1)S(1)}, pred[16]{0:T(512)(128)(4,1)}, u32[]{:S(2)}) copy-start(pred[16]{0:T(512)(128)(4,1)} %copy-done.15) | copy-start | bytes 52
  65.2 22.3 %copy-start.18 = (pred[16]{0:T(512)(128)(4,1)S(1)}, pred[16]{0:T(512)(128)(4,1)}, u32[]{:S(2)}) copy-start(pred[16]{0:T(512)(128)(4,1)} %copy-done.17) | copy-start | bytes 52
  65.2 22.3 %copy-start.20 = (pred[16]{0:T(512)(128)(4,1)S(1)}, pred[16]{0:T(512)(128)(4,1)}, u32[]{:S(2)}) copy-start(pred[16]{0:T(512)(128)(4,1)} %copy-done.19) | copy-start | bytes 52
  65.2 22.9 %copy-start.3 = (f32[64,340]{1,0:T(8,128)S(1)}, f32[64,340]{1,0:T(8,128)}, u32[]{:S(2)}) copy-start(f32[64,340]{1,0:T(8,128)} %mul.1174) | copy-start | bytes 261124
  67.0 22.4 %copy-start.7 = (f32[4,13]{1,0:T(4,128)S(1)}, f32[4,13]{1,0:T(4,128)}, u32[]{:S(2)}) copy-start(f32[4,13]{1,0:T(4,128)} %broadcast_multiply_fusion.1) | copy-start | bytes 628
  70.2 14.5 %all-to-all-start.3 = ((f32[16,1,768]{2,1,0:T(1,128)}), f32[16,1,768]{2,1,0:T(1,128)S(1)}, u32[]{:S(2)}, u32[]{:S(2)}) async-start(f32[16,1,768]{2,1,0:T(1,128)} %broadcast_select_fusion.30), calls=%async_computation.3 | async-start | bytes 98304 | tf_op jit(solution)/shard_map/all_to_all | solution.py:144
  88.1 3.4 %copy-start.22 = (pred[16]{0:T(512)(128)(4,1)S(1)}, pred[16]{0:T(512)(128)(4,1)}, u32[]{:S(2)}) copy-start(pred[16]{0:T(512)(128)(4,1)} %copy-done.21) | copy-start | bytes 52
  88.1 3.4 %copy-start.24 = (pred[16]{0:T(512)(128)(4,1)S(1)}, pred[16]{0:T(512)(128)(4,1)}, u32[]{:S(2)}) copy-start(pred[16]{0:T(512)(128)(4,1)} %copy-done.23) | copy-start | bytes 52
  88.1 3.4 %copy-start.26 = (pred[16]{0:T(512)(128)(4,1)S(1)}, pred[16]{0:T(512)(128)(4,1)}, u32[]{:S(2)}) copy-start(pred[16]{0:T(512)(128)(4,1)} %copy-done.25) | copy-start | bytes 52
  88.1 3.4 %copy-start.28 = (pred[16]{0:T(512)(128)(4,1)S(1)}, pred[16]{0:T(512)(128)(4,1)}, u32[]{:S(2)}) copy-start(pred[16]{0:T(512)(128)(4,1)} %copy-done.27) | copy-start | bytes 52
  88.1 3.4 %copy-start.30 = (pred[16]{0:T(512)(128)(4,1)S(1)}, pred[16]{0:T(512)(128)(4,1)}, u32[]{:S(2)}) copy-start(pred[16]{0:T(512)(128)(4,1)} %copy-done.29) | copy-start | bytes 52
  88.1 3.4 %copy-start.32 = (pred[16]{0:T(512)(128)(4,1)S(1)}, pred[16]{0:T(512)(128)(4,1)}, u32[]{:S(2)}) copy-start(pred[16]{0:T(512)(128)(4,1)} %copy-done.31) | copy-start | bytes 52
  88.2 3.4 %copy-start.34 = (pred[16]{0:T(512)(128)(4,1)S(1)}, pred[16]{0:T(512)(128)(4,1)}, u32[]{:S(2)}) copy-start(pred[16]{0:T(512)(128)(4,1)} %copy-done.33) | copy-start | bytes 52
  88.2 3.4 %copy-start.36 = (pred[16]{0:T(512)(128)(4,1)S(1)}, pred[16]{0:T(512)(128)(4,1)}, u32[]{:S(2)}) copy-start(pred[16]{0:T(512)(128)(4,1)} %copy-done.35) | copy-start | bytes 52
  88.8 16.0 %copy-start.5 = (f32[256]{0:T(256)S(1)}, f32[256]{0:T(256)}, u32[]{:S(2)}) copy-start(f32[256]{0:T(256)} %compare_select_fusion) | copy-start | bytes 3076
  88.8 16.1 %copy-start.8 = (f32[1,4,85]{2,1,0:T(4,128)S(1)}, f32[1,4,85]{2,1,0:T(4,128)}, u32[]{:S(2)}) copy-start(f32[1,4,85]{2,1,0:T(4,128)} %param.42) | copy-start | bytes 4084
  88.8 16.1 %copy-start.38 = (s32[340]{0:T(512)S(1)}, s32[340]{0:T(512)}, u32[]{:S(2)}) copy-start(s32[340]{0:T(512)} %copy-done.37) | copy-start | bytes 4084
  88.8 16.1 %copy-start.45 = (pred[340]{0:T(512)(128)(4,1)S(1)}, pred[340]{0:T(512)(128)(4,1)}, u32[]{:S(2)}) copy-start(pred[340]{0:T(512)(128)(4,1)} %copy-done.44) | copy-start | bytes 1024
  88.8 16.1 %copy-start.47 = (pred[340]{0:T(512)(128)(4,1)S(1)}, pred[340]{0:T(512)(128)(4,1)}, u32[]{:S(2)}) copy-start(pred[340]{0:T(512)(128)(4,1)} %copy-done.46) | copy-start | bytes 1024
  88.8 16.1 %copy-start.49 = (pred[340]{0:T(512)(128)(4,1)S(1)}, pred[340]{0:T(512)(128)(4,1)}, u32[]{:S(2)}) copy-start(pred[340]{0:T(512)(128)(4,1)} %copy-done.48) | copy-start | bytes 1024
  88.8 16.1 %copy-start.51 = (pred[340]{0:T(512)(128)(4,1)S(1)}, pred[340]{0:T(512)(128)(4,1)}, u32[]{:S(2)}) copy-start(pred[340]{0:T(512)(128)(4,1)} %copy-done.50) | copy-start | bytes 1024
  89.6 1.2 collective-permute-start.3
  92.5 11.0 %all-to-all-start.4 = ((f32[16,1,1026]{2,1,0:T(1,128)}), f32[16,1,1026]{2,1,0:T(1,128)S(1)}, u32[]{:S(2)}, u32[]{:S(2)}) async-start(f32[16,1,1026]{2,1,0:T(1,128)} %broadcast_select_fusion.22), calls=%async_computation.4 | async-start | bytes 147456 | tf_op jit(solution)/shard_map/all_to_all | solution.py:144
  107.6 1.2 collective-permute-start
  110.4 11.0 %all-to-all-start = ((f32[16,1,1028]{2,1,0:T(1,128)}), f32[16,1,1028]{2,1,0:T(1,128)S(1)}, u32[]{:S(2)}, u32[]{:S(2)}) async-start(f32[16,1,1028]{2,1,0:T(1,128)} %broadcast_select_fusion.66), calls=%async_computation | async-start | bytes 147456 | tf_op jit(solution)/shard_map/while/body/eval_jaxpr/all_to_all | solution.py:144
  125.5 1.2 collective-permute-start
  128.3 11.0 %all-to-all-start = ((f32[16,1,1028]{2,1,0:T(1,128)}), f32[16,1,1028]{2,1,0:T(1,128)S(1)}, u32[]{:S(2)}, u32[]{:S(2)}) async-start(f32[16,1,1028]{2,1,0:T(1,128)} %broadcast_select_fusion.66), calls=%async_computation | async-start | bytes 147456 | tf_op jit(solution)/shard_map/while/body/eval_jaxpr/all_to_all | solution.py:144
  143.3 1.2 collective-permute-start
  146.1 11.0 %all-to-all-start = ((f32[16,1,1028]{2,1,0:T(1,128)}), f32[16,1,1028]{2,1,0:T(1,128)S(1)}, u32[]{:S(2)}, u32[]{:S(2)}) async-start(f32[16,1,1028]{2,1,0:T(1,128)} %broadcast_select_fusion.66), calls=%async_computation | async-start | bytes 147456 | tf_op jit(solution)/shard_map/while/body/eval_jaxpr/all_to_all | solution.py:144
  (1 other events, 2.7 us)

commit v10 on v9

--- a/solution.py
+++ b/solution.py
@@ -58,6 +58,9 @@
         pick_stiff=gather_matrix(first, STIFF_LINE).T,
         lanes_k=gather_matrix(second, STIFF_LINE),
         lanes_m=gather_matrix(second, MASS_LINE),
+        lanes=jnp.stack([gather_matrix(second, STIFF_LINE), gather_matrix(second, MASS_LINE)]).reshape(
+            2 * second, -1
+        ),
         scatter_second=gather_matrix(second, np.eye(4)).T,
         scatter_first=gather_matrix(first, np.eye(4)),
     )
@@ -80,8 +83,7 @@
     flat_m = along_first_m.reshape(-1, second)
     flat_k = along_first_k.reshape(-1, second)
     if merged:
-        lanes = jnp.concatenate([mats["lanes_k"], mats["lanes_m"]], 0)
-        element = jnp.dot(jnp.concatenate([flat_m, flat_k], 1), lanes, precision=HIGH)
+        element = jnp.dot(jnp.concatenate([flat_m, flat_k], 1), mats["lanes"], precision=HIGH)
     else:
         element = jnp.dot(flat_m, mats["lanes_k"], precision=HIGH) + jnp.dot(
             flat_k, mats["lanes_m"], precision=HIGH

time: 160 us -> 154 us (0.963)
  other arithmetic: 39.2 us -> 33.1 us
  matrix products: 18.3 us -> 16.2 us
  local copies, waits for them, and re-layouts: 20.8 us -> 22.7 us
    dot_general x0 -> x3, local copies, waits for them, and re-layouts: none -> 3.27 us  [the longest x2 3.15 us: local_products(): jnp.dot(jnp.concatenate([flat_m, flat_k], 1), mats['lanes'], precision=HIGH)]
  transfers between devices with their start and end apart: 13 -> 13, of which waited for: 9 -> 10; matrix products, arithmetic and copies ran while one was open for 16% -> 16% of each run, Pallas kernels for 0% -> 0%
where the time goes in v10:
time: 154 us; the launch traced here: 153 us
  waiting for transfers between devices  41.3 us (27%)
  starting transfers between devices  36.6 us (24%)
  other arithmetic  33.1 us (21%)
  local copies, waits for them, and re-layouts  22.7 us (15%)
  matrix products  16.2 us (11%)
  between operations  2.26 us (1%)
    all_to_all x7, waiting for transfers between devices, plane_exchange(): got = lax.all_to_all(send, ('hx', 'hy'), 0, 0, tiled=True)  37.5 us
    all_to_all x7, starting transfers between devices, plane_exchange(): got = lax.all_to_all(send, ('hx', 'hy'), 0, 0, tiled=True)  35.5 us
    reduce_sum x2, other arithmetic, per_device(): current = jnp.sum(cond_nodes * gate_flat * (volts - reversal[:, None]), 0)  15.3 us
    select_n x7, other arithmetic, plane_exchange(): send = jnp.where(code_of[:, None] == code, table[code][None, :], send)  6.27 us
    ppermute x6, waiting for transfers between devices, torso_stage(): got = lax.ppermute(face, 'torso', [(0, 1), (1, 0)])  3.86 us
    select_n x44, local copies, waits for them, and re-layouts, plane_exchange(): received[offset] = jnp.where(valid, row[:pieces[offset].shape[0]], 0.0)  3.77 us
    dot_general x2, local copies, waits for them, and re-layouts, local_products(): jnp.dot(jnp.concatenate([flat_m, flat_k], 1), mats['lanes'], precision=HIGH)  3.15 us
  transfers between devices with their start and end apart: 13, of which 10 were waited for; matrix products, arithmetic and copies ran while one was open for 16% of the time, Pallas kernels for 0%

profile of v10, /device:TPU:0, one launch (start us, length us, event | category | flops | bytes accessed | tf_op | source)
XLA Modules:
  0.0 153.1 jit_solution(4416401087425646748)
XLA Ops:
  0.7 0.8 copy.216
  2.9 0.7 mul.1104
  3.7 0.9 select_select_fusion.8
  4.9 0.4 fusion.614
  5.6 0.4 fusion.233
  6.7 0.6 collective-permute-start.1
  7.4 0.6 slice_bitcast_fusion.22
  8.8 0.6 slice_bitcast_fusion.15
  9.4 0.7 broadcast_compare_fusion.11
  10.1 0.6 slice_bitcast_fusion.9
  10.9 1.8 %select_select_fusion.7 = (f32[1,256,340]{2,1,0:T(8,128)}, f32[1,256,340]{2,1,0:T(8,128)}) fusion(s32[340]{0:T(512)S(1)} %iota.1016, pred[340]{0:T(512)(128)(4,1)S(1)} %iota.1025, pred[340]{0:T(512)(128)(4,1)S(1)} %iota.1022, pred[340]{0:T(512)(128)(4,1)S(1)} %iota.1019, pred[340]{0:T(512)(128)(4,1)S(1)} %iota.1012), kind=kLoop, calls=%fused_computation.309 | loop fusion | flops 4613120 | bytes 699040 | tf_op jit(solution)/shard_map/jit(_where)/select_n | solution.py:51
  13.5 0.7 all_to_all.31
  14.1 7.9 %all-to-all-start.1 = ((f32[16,1,1024]{2,1,0:T(1,128)}), f32[16,1,1024]{2,1,0:T(1,128)S(1)}, u32[]{:S(2)}, u32[]{:S(2)}) async-start(f32[16,1,1024]{2,1,0:T(1,128)} %all_to_all.31), calls=%async_computation.1 | async-start | bytes 131072 | tf_op jit(solution)/shard_map/all_to_all | solution.py:146
  22.1 7.3 %multiply_reduce_fusion.1 = (f32[4,13,256]{2,0,1:T(4,128)S(1)}, f32[40,4,13,256]{3,1,2,0:T(4,128)S(1)}) fusion(f32[40]{0:T(128)} %param.39, f32[4,13,256]{2,0,1:T(4,128)S(1)} %copy-done.3, f32[40]{0:T(128)} %get-tuple-element.833, f32[40]{0:T(128)} %get-tuple-element.832, f32[40]{0:T(128)} %get-tuple-element.834, f32[40]{0:T(128)} %get-tuple-element.835, ...), kind=kLoop, calls=%fused_computation.290 | loop fusion | flops 12766208 | bytes 4435616 | tf_op jit(solution)/shard_map/reduce_sum | solution.py:295
  29.6 0.6 broadcast_select_fusion.37
  30.3 0.7 fusion.461
  31.3 0.7 copy.214
  32.0 0.7 fusion.464
  33.0 0.7 copy.211
  33.7 0.9 fusion.281
  34.7 1.0 fusion.312
  35.7 1.0 fusion.311
  36.7 0.4 fusion.616
  37.1 1.0 convolution_add_fusion.4
  38.1 0.4 fusion.232
  39.5 1.1 copy.232
  40.6 2.0 %reshape.5414 = f32[4,85,512,1,1]{2,1,0,3,4:T(8,128)} reshape(f32[340,512]{1,0:T(8,128)} %copy.232) | data formatting | bytes 1392640 | tf_op jit(solution)/shard_map/dot_general | solution.py:86
  43.3 0.8 select_select_fusion.11
  44.1 0.7 copy.227
  44.7 0.7 copy.220
  45.4 6.8 %all-to-all-start.2 = ((f32[16,1,1024]{2,1,0:T(1,128)}), f32[16,1,1024]{2,1,0:T(1,128)S(1)}, u32[]{:S(2)}, u32[]{:S(2)}) async-start(f32[16,1,1024]{2,1,0:T(1,128)} %copy.220), calls=%async_computation.2 | async-start | bytes 131072 | tf_op jit(solution)/shard_map/all_to_all | solution.py:146
  52.2 8.0 %multiply_reduce_fusion = (f32[4,13,256]{2,0,1:T(4,128)S(1)}, f32[40,4,13,256]{3,1,2,0:T(4,128)}) fusion(f32[4,13,256]{2,0,1:T(4,128)} %copy.227, f32[40]{0:T(128)} %param.39, f32[40]{0:T(128)} %get-tuple-element.833, f32[40]{0:T(128)} %get-tuple-element.832, f32[40]{0:T(128)} %get-tuple-element.834, f32[40]{0:T(128)} %get-tuple-element.835, ...), kind=kLoop, calls=%fused_computation.288 | loop fusion | flops 12766208 | bytes 4435616 | tf_op jit(solution)/shard_map/reduce_sum | solution.py:295
  62.1 1.5 broadcast_select_fusion.30
  63.7 6.9 %all-to-all-start.3 = ((f32[16,1,768]{2,1,0:T(1,128)}), f32[16,1,768]{2,1,0:T(1,128)S(1)}, u32[]{:S(2)}, u32[]{:S(2)}) async-start(f32[16,1,768]{2,1,0:T(1,128)} %broadcast_select_fusion.30), calls=%async_computation.3 | async-start | bytes 98304 | tf_op jit(solution)/shard_map/all_to_all | solution.py:146
  70.6 7.5 %all-to-all-done.3 = f32[16,1,768]{2,1,0:T(1,128)S(1)} async-done(((f32[16,1,768]{2,1,0:T(1,128)}), f32[16,1,768]{2,1,0:T(1,128)S(1)}, u32[]{:S(2)}, u32[]{:S(2)}) %all-to-all-start.3) | async-done | bytes 49184 | tf_op jit(solution)/shard_map/all_to_all | solution.py:146
  78.9 1.0 multiply_bitcast_fusion.3
  79.9 1.0 fusion.310
  81.6 1.0 convolution_multiply_fusion.1
  82.9 0.3 fusion.618
  83.7 0.7 copy.241
  84.4 0.5 collective-permute-done.3
  85.6 1.0 broadcast_select_fusion.22
  86.5 3.5 %all-to-all-start.4 = ((f32[16,1,1026]{2,1,0:T(1,128)}), f32[16,1,1026]{2,1,0:T(1,128)S(1)}, u32[]{:S(2)}, u32[]{:S(2)}) async-start(f32[16,1,1026]{2,1,0:T(1,128)} %broadcast_select_fusion.22), calls=%async_computation.4 | async-start | bytes 147456 | tf_op jit(solution)/shard_map/all_to_all | solution.py:146
  90.0 7.5 %all-to-all-done.4 = f32[16,1,1026]{2,1,0:T(1,128)S(1)} async-done(((f32[16,1,1026]{2,1,0:T(1,128)}), f32[16,1,1026]{2,1,0:T(1,128)S(1)}, u32[]{:S(2)}, u32[]{:S(2)}) %all-to-all-start.4) | async-done | bytes 65696 | tf_op jit(solution)/shard_map/all_to_all | solution.py:146
  98.9 53.5 %while.33 = (s32[]{:T(128)}, f32[4,13,256]{2,1,0:T(8,128)S(1)}, f32[4,13,256]{2,1,0:T(8,128)S(1)}, f32[4,13,256]{2,1,0:T(8,128)S(1)}, f32[4,13,256]{2,1,0:T(8,12...) while((s32[]{:T(128)}, f32[4,13,256]{2,1,0:T(8,128)S(1)}, ...), condition=%wide.region_7.8_spmd.clone.clone.clone, body=%wide.region_4.7_spmd.clone.clone.clone.sunk | while | flops 213083744 | bytes 4259643 | solution.py:365
  99.9 0.5 convolution_multiply_fusion.3
  100.5 0.6 fusion.675
  101.8 1.1 collective-permute-done
  103.5 1.0 broadcast_select_fusion.66
  104.4 3.5 %all-to-all-start = ((f32[16,1,1028]{2,1,0:T(1,128)}), f32[16,1,1028]{2,1,0:T(1,128)S(1)}, u32[]{:S(2)}, u32[]{:S(2)}) async-start(f32[16,1,1028]{2,1,0:T(1,128)} %broadcast_select_fusion.66), calls=%async_computation | async-start | bytes 147456 | tf_op jit(solution)/shard_map/while/body/eval_jaxpr/all_to_all | solution.py:146
  108.0 7.5 %all-to-all-done = f32[16,1,1028]{2,1,0:T(1,128)S(1)} async-done(((f32[16,1,1028]{2,1,0:T(1,128)}), f32[16,1,1028]{2,1,0:T(1,128)S(1)}, u32[]{:S(2)}, u32[]{:S(2)}) %all-to-all-start) | async-done | bytes 65824 | tf_op jit(solution)/shard_map/while/body/eval_jaxpr/all_to_all | solution.py:146
  117.8 0.6 convolution_multiply_fusion.3
  118.4 0.6 fusion.675
  119.6 1.1 collective-permute-done
  121.3 1.0 broadcast_select_fusion.66
  122.3 3.5 %all-to-all-start = ((f32[16,1,1028]{2,1,0:T(1,128)}), f32[16,1,1028]{2,1,0:T(1,128)S(1)}, u32[]{:S(2)}, u32[]{:S(2)}) async-start(f32[16,1,1028]{2,1,0:T(1,128)} %broadcast_select_fusion.66), calls=%async_computation | async-start | bytes 147456 | tf_op jit(solution)/shard_map/while/body/eval_jaxpr/all_to_all | solution.py:146
  125.9 7.5 %all-to-all-done = f32[16,1,1028]{2,1,0:T(1,128)S(1)} async-done(((f32[16,1,1028]{2,1,0:T(1,128)}), f32[16,1,1028]{2,1,0:T(1,128)S(1)}, u32[]{:S(2)}, u32[]{:S(2)}) %all-to-all-start) | async-done | bytes 65824 | tf_op jit(solution)/shard_map/while/body/eval_jaxpr/all_to_all | solution.py:146
  135.6 0.6 convolution_multiply_fusion.3
  136.2 0.6 fusion.675
  137.5 1.1 collective-permute-done
  139.2 1.0 broadcast_select_fusion.66
  140.1 3.5 %all-to-all-start = ((f32[16,1,1028]{2,1,0:T(1,128)}), f32[16,1,1028]{2,1,0:T(1,128)S(1)}, u32[]{:S(2)}, u32[]{:S(2)}) async-start(f32[16,1,1028]{2,1,0:T(1,128)} %broadcast_select_fusion.66), calls=%async_computation | async-start | bytes 147456 | tf_op jit(solution)/shard_map/while/body/eval_jaxpr/all_to_all | solution.py:146
  143.7 7.5 %all-to-all-done = f32[16,1,1028]{2,1,0:T(1,128)S(1)} async-done(((f32[16,1,1028]{2,1,0:T(1,128)}), f32[16,1,1028]{2,1,0:T(1,128)S(1)}, u32[]{:S(2)}, u32[]{:S(2)}) %all-to-all-start) | async-done | bytes 65824 | tf_op jit(solution)/shard_map/while/body/eval_jaxpr/all_to_all | solution.py:146
  152.4 0.7 copy.242
  (458 shorter events, 22.1 us)
Async XLA Ops:
  1.8 4.6 %copy-start.9 = (pred[16]{0:T(512)(128)(4,1)}, pred[16]{0:T(512)(128)(4,1)S(1)}, u32[]{:S(2)}) copy-start(pred[16]{0:T(512)(128)(4,1)S(1)} %iota.994) | copy-start | bytes 52
  2.0 4.4 %copy-start.12 = (pred[16]{0:T(512)(128)(4,1)}, pred[16]{0:T(512)(128)(4,1)S(1)}, u32[]{:S(2)}) copy-start(pred[16]{0:T(512)(128)(4,1)S(1)} %iota.991) | copy-start | bytes 52
  2.1 4.3 %copy-start.15 = (pred[16]{0:T(512)(128)(4,1)}, pred[16]{0:T(512)(128)(4,1)S(1)}, u32[]{:S(2)}) copy-start(pred[16]{0:T(512)(128)(4,1)S(1)} %iota.988) | copy-start | bytes 52
  2.3 4.1 %copy-start.18 = (pred[16]{0:T(512)(128)(4,1)}, pred[16]{0:T(512)(128)(4,1)S(1)}, u32[]{:S(2)}) copy-start(pred[16]{0:T(512)(128)(4,1)S(1)} %iota.980) | copy-start | bytes 52
  4.7 4.1 %copy-start.44 = (f32[4,40]{1,0:T(4,128)S(1)}, f32[4,40]{1,0:T(4,128)}, u32[]{:S(2)}) copy-start(f32[4,40]{1,0:T(4,128)} %param.40) | copy-start | bytes 1924
  4.7 4.1 %copy-start.46 = (f32[3,40]{1,0:T(4,128)S(1)}, f32[3,40]{1,0:T(4,128)}, u32[]{:S(2)}) copy-start(f32[3,40]{1,0:T(4,128)} %param.35) | copy-start | bytes 1444
  4.7 4.7 %copy-start.7 = (s32[4,13,256]{2,0,1:T(4,128)S(1)}, s32[4,13,256]{2,0,1:T(4,128)}, u32[]{:S(2)}) copy-start(s32[4,13,256]{2,0,1:T(4,128)} %param.34) | copy-start | bytes 159748
  4.7 4.7 %copy-start.8 = (s32[4,13,256]{2,0,1:T(4,128)S(1)}, s32[4,13,256]{2,0,1:T(4,128)}, u32[]{:S(2)}) copy-start(s32[4,13,256]{2,0,1:T(4,128)} %param.33) | copy-start | bytes 159748
  4.7 5.4 %copy-start.48 = (f32[3,40]{1,0:T(4,128)S(1)}, f32[3,40]{1,0:T(4,128)}, u32[]{:S(2)}) copy-start(f32[3,40]{1,0:T(4,128)} %param.36) | copy-start | bytes 1444
  4.9 17.3 %copy-start.3 = (f32[4,13,256]{2,0,1:T(4,128)S(1)}, f32[4,13,256]{2,0,1:T(4,128)}, u32[]{:S(2)}) copy-start(f32[4,13,256]{2,0,1:T(4,128)} %param.31) | copy-start | bytes 159748
  6.7 6.1 %collective-permute-start.1 = (f32[13,256]{1,0:T(8,128)S(1)}, f32[13,256]{1,0:T(8,128)S(1)}, u32[]{:S(2)}, u32[]{:S(2)}) collective-permute-start(f32[13,256]{1,0:T(8,128)S(1)} %fusion.381), channel_id=1, source_target_pairs={{0,1},{1,0},{2,3},{3,2},{4,5},{5,4},{6,7},{7,6},{8,9},{9,8},{10,11... | collective-permute-start | bytes 39944 | tf_op jit(solution)/shard_map/ppermute | solution.py:113
  7.2 14.8 %copy-start.21 = (pred[16]{0:T(512)(128)(4,1)}, pred[16]{0:T(512)(128)(4,1)S(1)}, u32[]{:S(2)}) copy-start(pred[16]{0:T(512)(128)(4,1)S(1)} %get-tuple-element.652) | copy-start | bytes 52
  7.3 14.7 %copy-start.24 = (pred[16]{0:T(512)(128)(4,1)}, pred[16]{0:T(512)(128)(4,1)S(1)}, u32[]{:S(2)}) copy-start(pred[16]{0:T(512)(128)(4,1)S(1)} %get-tuple-element.818) | copy-start | bytes 52
  7.3 14.7 %copy-start.27 = (pred[16]{0:T(512)(128)(4,1)}, pred[16]{0:T(512)(128)(4,1)S(1)}, u32[]{:S(2)}) copy-start(pred[16]{0:T(512)(128)(4,1)S(1)} %get-tuple-element.819) | copy-start | bytes 52
  7.3 14.7 %copy-start.30 = (pred[16]{0:T(512)(128)(4,1)}, pred[16]{0:T(512)(128)(4,1)S(1)}, u32[]{:S(2)}) copy-start(pred[16]{0:T(512)(128)(4,1)S(1)} %get-tuple-element.820) | copy-start | bytes 52
  7.3 14.7 %copy-start.33 = (pred[16]{0:T(512)(128)(4,1)}, pred[16]{0:T(512)(128)(4,1)S(1)}, u32[]{:S(2)}) copy-start(pred[16]{0:T(512)(128)(4,1)S(1)} %get-tuple-element.821) | copy-start | bytes 52
  7.3 14.7 %copy-start.36 = (pred[16]{0:T(512)(128)(4,1)}, pred[16]{0:T(512)(128)(4,1)S(1)}, u32[]{:S(2)}) copy-start(pred[16]{0:T(512)(128)(4,1)S(1)} %get-tuple-element.822) | copy-start | bytes 52
  7.3 14.7 %copy-start.38 = (pred[16]{0:T(512)(128)(4,1)}, pred[16]{0:T(512)(128)(4,1)S(1)}, u32[]{:S(2)}) copy-start(pred[16]{0:T(512)(128)(4,1)S(1)} %get-tuple-element.823) | copy-start | bytes 52
  7.4 14.7 %copy-start.40 = (pred[16]{0:T(512)(128)(4,1)}, pred[16]{0:T(512)(128)(4,1)S(1)}, u32[]{:S(2)}) copy-start(pred[16]{0:T(512)(128)(4,1)S(1)} %get-tuple-element.824) | copy-start | bytes 52
  8.2 13.9 %copy-start.49 = (pred[340]{0:T(512)(128)(4,1)}, pred[340]{0:T(512)(128)(4,1)S(1)}, u32[]{:S(2)}) copy-start(pred[340]{0:T(512)(128)(4,1)S(1)} %iota.1025) | copy-start | bytes 1024
  8.4 13.7 %copy-start.51 = (pred[340]{0:T(512)(128)(4,1)}, pred[340]{0:T(512)(128)(4,1)S(1)}, u32[]{:S(2)}) copy-start(pred[340]{0:T(512)(128)(4,1)S(1)} %iota.1022) | copy-start | bytes 1024
  8.6 13.6 %copy-start.53 = (pred[340]{0:T(512)(128)(4,1)}, pred[340]{0:T(512)(128)(4,1)S(1)}, u32[]{:S(2)}) copy-start(pred[340]{0:T(512)(128)(4,1)S(1)} %iota.1019) | copy-start | bytes 1024
  8.7 13.4 %copy-start.55 = (pred[340]{0:T(512)(128)(4,1)}, pred[340]{0:T(512)(128)(4,1)S(1)}, u32[]{:S(2)}) copy-start(pred[340]{0:T(512)(128)(4,1)S(1)} %iota.1012) | copy-start | bytes 1024
  10.1 19.4 %copy-start.4 = (pred[4,13,256]{2,0,1:T(4,128)(4,1)}, pred[4,13,256]{2,0,1:T(4,128)(4,1)S(1)}, u32[]{:S(2)}) copy-start(pred[4,13,256]{2,0,1:T(4,128)(4,1)S(1)} %get-tuple-element.755) | copy-start | bytes 39940
  14.1 15.4 %all-to-all-start.1 = ((f32[16,1,1024]{2,1,0:T(1,128)}), f32[16,1,1024]{2,1,0:T(1,128)S(1)}, u32[]{:S(2)}, u32[]{:S(2)}) async-start(f32[16,1,1024]{2,1,0:T(1,128)} %all_to_all.31), calls=%async_computation.1 | async-start | bytes 131072 | tf_op jit(solution)/shard_map/all_to_all | solution.py:146
  29.6 9.3 %copy-start.10 = (pred[16]{0:T(512)(128)(4,1)S(1)}, pred[16]{0:T(512)(128)(4,1)}, u32[]{:S(2)}) copy-start(pred[16]{0:T(512)(128)(4,1)} %copy-done.9) | copy-start | bytes 52
  29.6 9.3 %copy-start.13 = (pred[16]{0:T(512)(128)(4,1)S(1)}, pred[16]{0:T(512)(128)(4,1)}, u32[]{:S(2)}) copy-start(pred[16]{0:T(512)(128)(4,1)} %copy-done.12) | copy-start | bytes 52
  29.6 9.3 %copy-start.16 = (pred[16]{0:T(512)(128)(4,1)S(1)}, pred[16]{0:T(512)(128)(4,1)}, u32[]{:S(2)}) copy-start(pred[16]{0:T(512)(128)(4,1)} %copy-done.15) | copy-start | bytes 52
  29.6 9.3 %copy-start.19 = (pred[16]{0:T(512)(128)(4,1)S(1)}, pred[16]{0:T(512)(128)(4,1)}, u32[]{:S(2)}) copy-start(pred[16]{0:T(512)(128)(4,1)} %copy-done.18) | copy-start | bytes 52
  33.7 5.6 %copy-start.1 = (f32[1,256,340]{2,1,0:T(8,128)S(1)}, f32[1,256,340]{2,1,0:T(8,128)}, u32[]{:S(2)}) copy-start(f32[1,256,340]{2,1,0:T(8,128)} %get-tuple-element.785) | copy-start | bytes 1044484
  33.7 5.6 %copy-start.2 = (f32[1,256,340]{2,1,0:T(8,128)S(1)}, f32[1,256,340]{2,1,0:T(8,128)}, u32[]{:S(2)}) copy-start(f32[1,256,340]{2,1,0:T(8,128)} %get-tuple-element.786) | copy-start | bytes 1044484
  39.1 3.5 %collective-permute-start.2 = (f32[13,256]{1,0:T(8,128)S(1)}, f32[13,256]{1,0:T(8,128)S(1)}, u32[]{:S(2)}, u32[]{:S(2)}) collective-permute-start(f32[13,256]{1,0:T(8,128)S(1)} %fusion.377), channel_id=1, source_target_pairs={{0,1},{1,0},{2,3},{3,2},{4,5},{5,4},{6,7},{7,6},{8,9},{9,8},{10,11... | collective-permute-start | bytes 39944 | tf_op jit(solution)/shard_map/ppermute | solution.py:113
  39.4 3.9 %copy-start.28 = (pred[16]{0:T(512)(128)(4,1)S(1)}, pred[16]{0:T(512)(128)(4,1)}, u32[]{:S(2)}) copy-start(pred[16]{0:T(512)(128)(4,1)} %copy-done.27) | copy-start | bytes 52
  39.4 3.9 %copy-start.31 = (pred[16]{0:T(512)(128)(4,1)S(1)}, pred[16]{0:T(512)(128)(4,1)}, u32[]{:S(2)}) copy-start(pred[16]{0:T(512)(128)(4,1)} %copy-done.30) | copy-start | bytes 52
  39.5 12.7 %copy-start.5 = (pred[4,13,256]{2,0,1:T(4,128)(4,1)S(1)}, pred[4,13,256]{2,0,1:T(4,128)(4,1)}, u32[]{:S(2)}) copy-start(pred[4,13,256]{2,0,1:T(4,128)(4,1)} %copy-done.4) | copy-start | bytes 39940
  45.4 14.8 %all-to-all-start.2 = ((f32[16,1,1024]{2,1,0:T(1,128)}), f32[16,1,1024]{2,1,0:T(1,128)S(1)}, u32[]{:S(2)}, u32[]{:S(2)}) async-start(f32[16,1,1024]{2,1,0:T(1,128)} %copy.220), calls=%async_computation.2 | async-start | bytes 131072 | tf_op jit(solution)/shard_map/all_to_all | solution.py:146
  60.2 20.7 %copy-start.11 = (pred[16]{0:T(512)(128)(4,1)S(1)}, pred[16]{0:T(512)(128)(4,1)}, u32[]{:S(2)}) copy-start(pred[16]{0:T(512)(128)(4,1)} %copy-done.9) | copy-start | bytes 52
  60.2 20.7 %copy-start.14 = (pred[16]{0:T(512)(128)(4,1)S(1)}, pred[16]{0:T(512)(128)(4,1)}, u32[]{:S(2)}) copy-start(pred[16]{0:T(512)(128)(4,1)} %copy-done.12) | copy-start | bytes 52
  60.2 20.7 %copy-start.17 = (pred[16]{0:T(512)(128)(4,1)S(1)}, pred[16]{0:T(512)(128)(4,1)}, u32[]{:S(2)}) copy-start(pred[16]{0:T(512)(128)(4,1)} %copy-done.15) | copy-start | bytes 52
  60.2 20.7 %copy-start.20 = (pred[16]{0:T(512)(128)(4,1)S(1)}, pred[16]{0:T(512)(128)(4,1)}, u32[]{:S(2)}) copy-start(pred[16]{0:T(512)(128)(4,1)} %copy-done.18) | copy-start | bytes 52
  60.2 21.3 %copy-start = (f32[4,85,512,1,1]{2,1,0,3,4:T(8,128)S(1)}, f32[4,85,512,1,1]{2,1,0,3,4:T(8,128)}, u32[]{:S(2)}) copy-start(f32[4,85,512,1,1]{2,1,0,3,4:T(8,128)} %reshape.5414) | copy-start | bytes 2088964
  60.2 21.3 %copy-start.6 = (f32[1,4,85]{2,1,0:T(4,128)S(1)}, f32[1,4,85]{2,1,0:T(4,128)}, u32[]{:S(2)}) copy-start(f32[1,4,85]{2,1,0:T(4,128)} %param.42) | copy-start | bytes 4084
  63.7 14.4 %all-to-all-start.3 = ((f32[16,1,768]{2,1,0:T(1,128)}), f32[16,1,768]{2,1,0:T(1,128)S(1)}, u32[]{:S(2)}, u32[]{:S(2)}) async-start(f32[16,1,768]{2,1,0:T(1,128)} %broadcast_select_fusion.30), calls=%async_computation.3 | async-start | bytes 98304 | tf_op jit(solution)/shard_map/all_to_all | solution.py:146
  79.9 5.6 %copy-start.23 = (pred[16]{0:T(512)(128)(4,1)S(1)}, pred[16]{0:T(512)(128)(4,1)}, u32[]{:S(2)}) copy-start(pred[16]{0:T(512)(128)(4,1)} %copy-done.21) | copy-start | bytes 52
  79.9 5.6 %copy-start.26 = (pred[16]{0:T(512)(128)(4,1)S(1)}, pred[16]{0:T(512)(128)(4,1)}, u32[]{:S(2)}) copy-start(pred[16]{0:T(512)(128)(4,1)} %copy-done.24) | copy-start | bytes 52
  79.9 5.6 %copy-start.29 = (pred[16]{0:T(512)(128)(4,1)S(1)}, pred[16]{0:T(512)(128)(4,1)}, u32[]{:S(2)}) copy-start(pred[16]{0:T(512)(128)(4,1)} %copy-done.27) | copy-start | bytes 52
  79.9 5.6 %copy-start.32 = (pred[16]{0:T(512)(128)(4,1)S(1)}, pred[16]{0:T(512)(128)(4,1)}, u32[]{:S(2)}) copy-start(pred[16]{0:T(512)(128)(4,1)} %copy-done.30) | copy-start | bytes 52
  79.9 5.6 %copy-start.35 = (pred[16]{0:T(512)(128)(4,1)S(1)}, pred[16]{0:T(512)(128)(4,1)}, u32[]{:S(2)}) copy-start(pred[16]{0:T(512)(128)(4,1)} %copy-done.33) | copy-start | bytes 52
  79.9 5.6 %copy-start.37 = (pred[16]{0:T(512)(128)(4,1)S(1)}, pred[16]{0:T(512)(128)(4,1)}, u32[]{:S(2)}) copy-start(pred[16]{0:T(512)(128)(4,1)} %copy-done.36) | copy-start | bytes 52
  79.9 5.6 %copy-start.39 = (pred[16]{0:T(512)(128)(4,1)S(1)}, pred[16]{0:T(512)(128)(4,1)}, u32[]{:S(2)}) copy-start(pred[16]{0:T(512)(128)(4,1)} %copy-done.38) | copy-start | bytes 52
  79.9 5.6 %copy-start.41 = (pred[16]{0:T(512)(128)(4,1)S(1)}, pred[16]{0:T(512)(128)(4,1)}, u32[]{:S(2)}) copy-start(pred[16]{0:T(512)(128)(4,1)} %copy-done.40) | copy-start | bytes 52
  81.6 17.2 %copy-start.43 = (s32[340]{0:T(512)S(1)}, s32[340]{0:T(512)}, u32[]{:S(2)}) copy-start(s32[340]{0:T(512)} %copy-done.42) | copy-start | bytes 4084
  81.6 17.2 %copy-start.50 = (pred[340]{0:T(512)(128)(4,1)S(1)}, pred[340]{0:T(512)(128)(4,1)}, u32[]{:S(2)}) copy-start(pred[340]{0:T(512)(128)(4,1)} %copy-done.49) | copy-start | bytes 1024
  81.6 17.2 %copy-start.52 = (pred[340]{0:T(512)(128)(4,1)S(1)}, pred[340]{0:T(512)(128)(4,1)}, u32[]{:S(2)}) copy-start(pred[340]{0:T(512)(128)(4,1)} %copy-done.51) | copy-start | bytes 1024
  81.6 17.2 %copy-start.54 = (pred[340]{0:T(512)(128)(4,1)S(1)}, pred[340]{0:T(512)(128)(4,1)}, u32[]{:S(2)}) copy-start(pred[340]{0:T(512)(128)(4,1)} %copy-done.53) | copy-start | bytes 1024
  81.6 17.2 %copy-start.56 = (pred[340]{0:T(512)(128)(4,1)S(1)}, pred[340]{0:T(512)(128)(4,1)}, u32[]{:S(2)}) copy-start(pred[340]{0:T(512)(128)(4,1)} %copy-done.55) | copy-start | bytes 1024
  83.7 1.2 collective-permute-start.3
  86.5 11.0 %all-to-all-start.4 = ((f32[16,1,1026]{2,1,0:T(1,128)}), f32[16,1,1026]{2,1,0:T(1,128)S(1)}, u32[]{:S(2)}, u32[]{:S(2)}) async-start(f32[16,1,1026]{2,1,0:T(1,128)} %broadcast_select_fusion.22), calls=%async_computation.4 | async-start | bytes 147456 | tf_op jit(solution)/shard_map/all_to_all | solution.py:146
  101.6 1.2 collective-permute-start
  104.4 11.0 %all-to-all-start = ((f32[16,1,1028]{2,1,0:T(1,128)}), f32[16,1,1028]{2,1,0:T(1,128)S(1)}, u32[]{:S(2)}, u32[]{:S(2)}) async-start(f32[16,1,1028]{2,1,0:T(1,128)} %broadcast_select_fusion.66), calls=%async_computation | async-start | bytes 147456 | tf_op jit(solution)/shard_map/while/body/eval_jaxpr/all_to_all | solution.py:146
  119.5 1.2 collective-permute-start
  122.3 11.0 %all-to-all-start = ((f32[16,1,1028]{2,1,0:T(1,128)}), f32[16,1,1028]{2,1,0:T(1,128)S(1)}, u32[]{:S(2)}, u32[]{:S(2)}) async-start(f32[16,1,1028]{2,1,0:T(1,128)} %broadcast_select_fusion.66), calls=%async_computation | async-start | bytes 147456 | tf_op jit(solution)/shard_map/while/body/eval_jaxpr/all_to_all | solution.py:146
  137.3 1.2 collective-permute-start
  140.1 11.0 %all-to-all-start = ((f32[16,1,1028]{2,1,0:T(1,128)}), f32[16,1,1028]{2,1,0:T(1,128)S(1)}, u32[]{:S(2)}, u32[]{:S(2)}) async-start(f32[16,1,1028]{2,1,0:T(1,128)} %broadcast_select_fusion.66), calls=%async_computation | async-start | bytes 147456 | tf_op jit(solution)/shard_map/while/body/eval_jaxpr/all_to_all | solution.py:146
  (6 other events, 20.4 us)

commit v11 on v10

--- a/solution.py
+++ b/solution.py
@@ -362,7 +362,9 @@
         return (solution, residual, direction, image, norm_next, curvature)
 
     state = (solution, residual, direction, image, norm_now, curvature)
-    solution = lax.fori_loop(1, ITERS, later_turn, state)[0]
+    for turn_index in range(1, ITERS):
+        state = later_turn(turn_index, state)
+    solution = state[0]
     return (potential, new_gating, solution)
 
 

time: 154 us -> 163 us (1.058)
  blocking collectives: 0 us -> 20.3 us
  waiting for transfers between devices: 41.3 us -> 26.6 us
  other arithmetic: 33.1 us -> 43.2 us
  starting transfers between devices: 36.6 us -> 29.5 us
    all_to_all x0 -> x2, blocking collectives: none -> 20.3 us  [plane_exchange(): got = lax.all_to_all(send, ('hx', 'hy'), 0, 0, tiled=True)]
    all_to_all x7 -> x5, waiting for transfers between devices: 37.5 us -> 22 us  [plane_exchange(): got = lax.all_to_all(send, ('hx', 'hy'), 0, 0, tiled=True)]
    select_n x2, other arithmetic: 2.7 us -> 12.7 us  [gather_matrix(): out = jnp.where((offset == a) & (local == j), jnp.float32(line[a, j]), out)]
    all_to_all x7 -> x5, starting transfers between devices: 35.5 us -> 28.5 us  [plane_exchange(): got = lax.all_to_all(send, ('hx', 'hy'), 0, 0, tiled=True)]
    unnamed x0 -> x1, other arithmetic: none -> 2.56 us
    unnamed x121 -> x109, local copies, waits for them, and re-layouts: 2.41 us -> 4.66 us
    select_n x7, other arithmetic: 6.27 us -> 4.3 us  [plane_exchange(): send = jnp.where(code_of[:, None] == code, table[code][None, :], send)]
    dot_general x2 -> x1, local copies, waits for them, and re-layouts: 3.15 us -> 1.18 us  [local_products(): jnp.dot(jnp.concatenate([flat_m, flat_k], 1), mats['lanes'], precision=HIGH)]
  transfers between devices with their start and end apart: 13 -> 11, of which waited for: 10 -> 8; matrix products, arithmetic and copies ran while one was open for 16% -> 23% of each run, Pallas kernels for 0% -> 0%
where the time goes in v11:
time: 163 us; the launch traced here: 162 us
  other arithmetic  43.2 us (27%)
  starting transfers between devices  29.5 us (18%)
  waiting for transfers between devices  26.6 us (16%)
  local copies, waits for them, and re-layouts  21.8 us (13%)
  blocking collectives  20.3 us (12%)
  matrix products  17.4 us (11%)
  between operations  2.72 us (2%)
    all_to_all x5, starting transfers between devices, plane_exchange(): got = lax.all_to_all(send, ('hx', 'hy'), 0, 0, tiled=True)  28.5 us
    all_to_all x5, waiting for transfers between devices, plane_exchange(): got = lax.all_to_all(send, ('hx', 'hy'), 0, 0, tiled=True)  22 us
    all_to_all x2, blocking collectives, plane_exchange(): got = lax.all_to_all(send, ('hx', 'hy'), 0, 0, tiled=True)  20.3 us
    reduce_sum x2, other arithmetic, per_device(): current = jnp.sum(cond_nodes * gate_flat * (volts - reversal[:, None]), 0)  15.3 us
    select_n x2, other arithmetic, gather_matrix(): out = jnp.where((offset == a) & (local == j), jnp.float32(line[a, j]), out)  12.7 us
    unnamed x109, local copies, waits for them, and re-layouts  4.66 us
    ppermute x6, waiting for transfers between devices, torso_stage(): got = lax.ppermute(face, 'torso', [(0, 1), (1, 0)])  4.63 us
    select_n x7, other arithmetic, plane_exchange(): send = jnp.where(code_of[:, None] == code, table[code][None, :], send)  4.3 us
  transfers between devices with their start and end apart: 11, of which 8 were waited for; matrix products, arithmetic and copies ran while one was open for 23% of the time, Pallas kernels for 0%

profile of v11, /device:TPU:0, one launch (start us, length us, event | category | flops | bytes accessed | tf_op | source)
XLA Modules:
  0.0 161.6 jit_solution(11170501058535432136)
XLA Ops:
  0.7 0.8 copy.274
  2.9 0.7 mul.1352
  3.7 0.9 select_select_fusion.3
  4.9 0.4 fusion.633
  5.6 0.4 fusion.1
  6.0 0.3 fusion.634
  6.7 0.6 collective-permute-start
  7.4 0.6 slice_bitcast_fusion.26
  8.7 0.6 slice_bitcast_fusion.19
  9.3 0.7 broadcast_compare_fusion.3
  10.0 0.6 slice_bitcast_fusion.13
  10.8 11.8 %and_select_fusion.31 = (f32[1,256,340]{1,0,2:T(1,128)}, f32[1,256,340]{1,0,2:T(1,128)}) fusion(pred[340]{0:T(512)(128)(4,1)S(1)} %iota.1266, pred[340]{0:T(512)(128)(4,1)S(1)} %iota.1273, pred[340]{0:T(512)(128)(4,1)S(1)} %iota.1276, pred[340]{0:T(512)(128)(4,1)S(1)} %iota.1279, s32[340]{0:T(512)S(1)} %iota.1270), kind=kLoop, calls=%fused_computation.61 | loop fusion | flops 4613120 | bytes 699040 | tf_op jit(solution)/shard_map/jit(_where)/select_n | solution.py:51
  23.5 0.7 all_to_all.40
  24.1 7.9 %all-to-all-start = ((f32[16,1,1024]{2,1,0:T(1,128)}), f32[16,1,1024]{2,1,0:T(1,128)S(1)}, u32[]{:S(2)}, u32[]{:S(2)}) async-start(f32[16,1,1024]{2,1,0:T(1,128)} %all_to_all.40), calls=%async_computation | async-start | bytes 131072 | tf_op jit(solution)/shard_map/all_to_all | solution.py:146
  32.1 7.3 %multiply_reduce_fusion.1 = (f32[4,13,256]{2,0,1:T(4,128)S(1)}, f32[40,4,13,256]{3,1,2,0:T(4,128)S(1)}) fusion(f32[40]{0:T(128)} %param.45, f32[4,13,256]{2,0,1:T(4,128)S(1)} %copy-done, f32[40]{0:T(128)} %get-tuple-element.449, f32[40]{0:T(128)} %get-tuple-element.448, f32[40]{0:T(128)} %get-tuple-element.450, f32[40]{0:T(128)} %get-tuple-element.451, ...), kind=kLoop, calls=%fused_computation.2 | loop fusion | flops 12766208 | bytes 4435616 | tf_op jit(solution)/shard_map/reduce_sum | solution.py:295
  39.6 0.6 broadcast_select_fusion.49
  40.3 0.7 fusion.344
  41.2 0.7 copy.272
  42.0 0.7 fusion.349
  43.0 0.7 copy.269
  43.7 0.9 fusion.82
  44.6 0.9 fusion.140
  45.6 0.9 fusion.139
  46.5 0.4 fusion.635
  47.0 1.0 convolution_add_fusion.6
  47.9 0.4 fusion
  48.4 0.3 fusion.636
  48.8 0.8 fusion.233
  49.8 2.6 %maximum_bitcast_fusion = f32[340,2,256]{2,1,0:T(2,128)} fusion(f32[1,256,340]{1,0,2:T(1,128)} %get-tuple-element.375, f32[1,256,340]{1,0,2:T(1,128)} %get-tuple-element.374), kind=kLoop, calls=%fused_computation.66 | loop fusion | flops 174080 | bytes 1392640
  52.4 1.3 pad.573
  53.8 0.9 copy.376
  54.7 1.2 reshape.6653
  56.7 0.7 copy.278
  57.4 6.7 %all-to-all-start.1 = ((f32[16,1,1024]{2,1,0:T(1,128)}), f32[16,1,1024]{2,1,0:T(1,128)S(1)}, u32[]{:S(2)}, u32[]{:S(2)}) async-start(f32[16,1,1024]{2,1,0:T(1,128)} %copy.278), calls=%async_computation.1 | async-start | bytes 131072 | tf_op jit(solution)/shard_map/all_to_all | solution.py:146
  64.2 7.9 %multiply_reduce_fusion = (f32[4,13,256]{2,0,1:T(4,128)S(1)}, f32[40,4,13,256]{3,1,2,0:T(4,128)}) fusion(f32[4,13,256]{2,0,1:T(4,128)S(1)} %copy.285, f32[40]{0:T(128)} %param.45, f32[40]{0:T(128)} %get-tuple-element.449, f32[40]{0:T(128)} %get-tuple-element.448, f32[40]{0:T(128)} %get-tuple-element.450, f32[40]{0:T(128)} %get-tuple-element.451, ...), kind=kLoop, calls=%fused_computation | loop fusion | flops 12766208 | bytes 4435616 | tf_op jit(solution)/shard_map/reduce_sum | solution.py:295
  74.1 1.5 broadcast_select_fusion.38
  75.6 6.9 %all-to-all-start.2 = ((f32[16,1,768]{2,1,0:T(1,128)}), f32[16,1,768]{2,1,0:T(1,128)S(1)}, u32[]{:S(2)}, u32[]{:S(2)}) async-start(f32[16,1,768]{2,1,0:T(1,128)} %broadcast_select_fusion.38), calls=%async_computation.2 | async-start | bytes 98304 | tf_op jit(solution)/shard_map/all_to_all | solution.py:146
  82.5 7.5 %all-to-all-done.2 = f32[16,1,768]{2,1,0:T(1,128)S(1)} async-done(((f32[16,1,768]{2,1,0:T(1,128)}), f32[16,1,768]{2,1,0:T(1,128)S(1)}, u32[]{:S(2)}, u32[]{:S(2)}) %all-to-all-start.2) | async-done | bytes 49184 | tf_op jit(solution)/shard_map/all_to_all | solution.py:146
  90.8 1.0 multiply_bitcast_fusion.3
  91.9 0.9 fusion.138
  93.5 1.0 convolution_multiply_fusion.3
  94.7 0.3 fusion.637
  95.6 1.2 collective-permute-done.2
  97.4 1.0 broadcast_select_fusion.6
  98.4 3.5 %all-to-all-start.3 = ((f32[16,1,1026]{2,1,0:T(1,128)}), f32[16,1,1026]{2,1,0:T(1,128)S(1)}, u32[]{:S(2)}, u32[]{:S(2)}) async-start(f32[16,1,1026]{2,1,0:T(1,128)} %broadcast_select_fusion.6), calls=%async_computation.3 | async-start | bytes 147456 | tf_op jit(solution)/shard_map/all_to_all | solution.py:146
  101.9 7.5 %all-to-all-done.3 = f32[16,1,1026]{2,1,0:T(1,128)S(1)} async-done(((f32[16,1,1026]{2,1,0:T(1,128)}), f32[16,1,1026]{2,1,0:T(1,128)S(1)}, u32[]{:S(2)}, u32[]{:S(2)}) %all-to-all-start.3) | async-done | bytes 65696 | tf_op jit(solution)/shard_map/all_to_all | solution.py:146
  111.7 1.0 convolution_multiply_fusion.2
  112.9 0.3 fusion.638
  113.8 1.2 collective-permute-done.3
  115.5 0.3 broadcast_select_fusion.28
  115.9 10.2 %all_to_all.60 = f32[16,1,1028]{2,1,0:T(1,128)S(1)} all-to-all(f32[16,1,1028]{2,1,0:T(1,128)S(1)} %broadcast_select_fusion.28), channel_id=1, replica_groups=mesh['hx'=4,'hy'=4,'torso'=2] {'hx','hy'}, dimensions={0} | all-to-all | bytes 131584 | tf_op jit(solution)/shard_map/all_to_all | solution.py:146
  128.3 1.0 convolution_multiply_fusion.1
  129.5 0.3 fusion.639
  130.4 1.2 collective-permute-done.4
  132.1 0.3 broadcast_select_fusion.27
  132.4 10.2 %all_to_all.61 = f32[16,1,1028]{2,1,0:T(1,128)S(1)} all-to-all(f32[16,1,1028]{2,1,0:T(1,128)S(1)} %broadcast_select_fusion.27), channel_id=1, replica_groups=mesh['hx'=4,'hy'=4,'torso'=2] {'hx','hy'}, dimensions={0} | all-to-all | bytes 131584 | tf_op jit(solution)/shard_map/all_to_all | solution.py:146
  144.8 1.0 convolution_multiply_fusion
  146.1 0.3 fusion.640
  147.0 1.2 collective-permute-done.5
  148.7 1.0 broadcast_select_fusion.26
  149.7 3.5 %all-to-all-start.6 = ((f32[16,1,1028]{2,1,0:T(1,128)}), f32[16,1,1028]{2,1,0:T(1,128)S(1)}, u32[]{:S(2)}, u32[]{:S(2)}) async-start(f32[16,1,1028]{2,1,0:T(1,128)} %broadcast_select_fusion.26), calls=%async_computation.6 | async-start | bytes 147456 | tf_op jit(solution)/shard_map/all_to_all | solution.py:146
  153.2 0.7 copy.325
  153.9 6.9 %all-to-all-done.6 = f32[16,1,1028]{2,1,0:T(1,128)S(1)} async-done(((f32[16,1,1028]{2,1,0:T(1,128)}), f32[16,1,1028]{2,1,0:T(1,128)S(1)}, u32[]{:S(2)}, u32[]{:S(2)}) %all-to-all-start.6) | async-done | bytes 65824 | tf_op jit(solution)/shard_map/all_to_all | solution.py:146
  160.9 0.7 copy.326
  (427 shorter events, 20.4 us)
Async XLA Ops:
  1.7 4.7 %copy-start.28 = (s32[16]{0:T(128)}, s32[16]{0:T(128)S(1)}, u32[]{:S(2)}) copy-start(s32[16]{0:T(128)S(1)} %iota.1239) | copy-start | bytes 196
  1.8 4.6 %copy-start.31 = (pred[16]{0:T(512)(128)(4,1)}, pred[16]{0:T(512)(128)(4,1)S(1)}, u32[]{:S(2)}) copy-start(pred[16]{0:T(512)(128)(4,1)S(1)} %iota.1248) | copy-start | bytes 52
  2.0 4.4 %copy-start.34 = (pred[16]{0:T(512)(128)(4,1)}, pred[16]{0:T(512)(128)(4,1)S(1)}, u32[]{:S(2)}) copy-start(pred[16]{0:T(512)(128)(4,1)S(1)} %iota.1245) | copy-start | bytes 52
  2.1 4.3 %copy-start.37 = (pred[16]{0:T(512)(128)(4,1)}, pred[16]{0:T(512)(128)(4,1)S(1)}, u32[]{:S(2)}) copy-start(pred[16]{0:T(512)(128)(4,1)S(1)} %iota.1242) | copy-start | bytes 52
  2.3 4.1 %copy-start.40 = (pred[16]{0:T(512)(128)(4,1)}, pred[16]{0:T(512)(128)(4,1)S(1)}, u32[]{:S(2)}) copy-start(pred[16]{0:T(512)(128)(4,1)S(1)} %iota.1234) | copy-start | bytes 52
  4.6 2.6 %copy-start.45 = (f32[3,40]{1,0:T(4,128)S(1)}, f32[3,40]{1,0:T(4,128)}, u32[]{:S(2)}) copy-start(f32[3,40]{1,0:T(4,128)} %param.44) | copy-start | bytes 1444
  4.7 3.3 %copy-start.43 = (f32[3,40]{1,0:T(4,128)S(1)}, f32[3,40]{1,0:T(4,128)}, u32[]{:S(2)}) copy-start(f32[3,40]{1,0:T(4,128)} %param.43) | copy-start | bytes 1444
  4.7 4.1 %copy-start.42 = (f32[4,40]{1,0:T(4,128)S(1)}, f32[4,40]{1,0:T(4,128)}, u32[]{:S(2)}) copy-start(f32[4,40]{1,0:T(4,128)} %param.46) | copy-start | bytes 1924
  4.7 4.0 %copy-start.44 = (f32[3,40]{1,0:T(4,128)S(1)}, f32[3,40]{1,0:T(4,128)}, u32[]{:S(2)}) copy-start(f32[3,40]{1,0:T(4,128)} %param.41) | copy-start | bytes 1444
  4.7 4.6 %copy-start.4 = (s32[4,13,256]{2,0,1:T(4,128)S(1)}, s32[4,13,256]{2,0,1:T(4,128)}, u32[]{:S(2)}) copy-start(s32[4,13,256]{2,0,1:T(4,128)} %param.40) | copy-start | bytes 159748
  4.7 4.6 %copy-start.5 = (s32[4,13,256]{2,0,1:T(4,128)S(1)}, s32[4,13,256]{2,0,1:T(4,128)}, u32[]{:S(2)}) copy-start(s32[4,13,256]{2,0,1:T(4,128)} %param.39) | copy-start | bytes 159748
  4.7 5.3 %copy-start.46 = (f32[3,40]{1,0:T(4,128)S(1)}, f32[3,40]{1,0:T(4,128)}, u32[]{:S(2)}) copy-start(f32[3,40]{1,0:T(4,128)} %param.42) | copy-start | bytes 1444
  4.9 27.2 %copy-start = (f32[4,13,256]{2,0,1:T(4,128)S(1)}, f32[4,13,256]{2,0,1:T(4,128)}, u32[]{:S(2)}) copy-start(f32[4,13,256]{2,0,1:T(4,128)} %param.37) | copy-start | bytes 159748
  6.7 16.1 %collective-permute-start = (f32[13,256]{1,0:T(8,128)S(1)}, f32[13,256]{1,0:T(8,128)S(1)}, u32[]{:S(2)}, u32[]{:S(2)}) collective-permute-start(f32[13,256]{1,0:T(8,128)S(1)} %fusion.221), channel_id=1, source_target_pairs={{0,1},{1,0},{2,3},{3,2},{4,5},{5,4},{6,7},{7,6},{8,9},{9,8},{10,11... | collective-permute-start | bytes 39944 | tf_op jit(solution)/shard_map/ppermute | solution.py:113
  7.3 24.7 %copy-start.7 = (pred[16]{0:T(512)(128)(4,1)}, pred[16]{0:T(512)(128)(4,1)S(1)}, u32[]{:S(2)}) copy-start(pred[16]{0:T(512)(128)(4,1)S(1)} %get-tuple-element.434) | copy-start | bytes 52
  7.3 24.7 %copy-start.10 = (pred[16]{0:T(512)(128)(4,1)}, pred[16]{0:T(512)(128)(4,1)S(1)}, u32[]{:S(2)}) copy-start(pred[16]{0:T(512)(128)(4,1)S(1)} %get-tuple-element.435) | copy-start | bytes 52
  7.3 24.7 %copy-start.13 = (pred[16]{0:T(512)(128)(4,1)}, pred[16]{0:T(512)(128)(4,1)S(1)}, u32[]{:S(2)}) copy-start(pred[16]{0:T(512)(128)(4,1)S(1)} %get-tuple-element.436) | copy-start | bytes 52
  7.3 24.7 %copy-start.16 = (pred[16]{0:T(512)(128)(4,1)}, pred[16]{0:T(512)(128)(4,1)S(1)}, u32[]{:S(2)}) copy-start(pred[16]{0:T(512)(128)(4,1)S(1)} %get-tuple-element.437) | copy-start | bytes 52
  7.3 24.7 %copy-start.19 = (pred[16]{0:T(512)(128)(4,1)}, pred[16]{0:T(512)(128)(4,1)S(1)}, u32[]{:S(2)}) copy-start(pred[16]{0:T(512)(128)(4,1)S(1)} %get-tuple-element.438) | copy-start | bytes 52
  7.3 24.7 %copy-start.22 = (pred[16]{0:T(512)(128)(4,1)}, pred[16]{0:T(512)(128)(4,1)S(1)}, u32[]{:S(2)}) copy-start(pred[16]{0:T(512)(128)(4,1)S(1)} %get-tuple-element.439) | copy-start | bytes 52
  7.4 24.7 %copy-start.25 = (pred[16]{0:T(512)(128)(4,1)}, pred[16]{0:T(512)(128)(4,1)S(1)}, u32[]{:S(2)}) copy-start(pred[16]{0:T(512)(128)(4,1)S(1)} %get-tuple-element.440) | copy-start | bytes 52
  10.0 29.4 %copy-start.1 = (pred[4,13,256]{2,0,1:T(4,128)(4,1)}, pred[4,13,256]{2,0,1:T(4,128)(4,1)S(1)}, u32[]{:S(2)}) copy-start(pred[4,13,256]{2,0,1:T(4,128)(4,1)S(1)} %get-tuple-element.337) | copy-start | bytes 39940
  24.1 15.4 %all-to-all-start = ((f32[16,1,1024]{2,1,0:T(1,128)}), f32[16,1,1024]{2,1,0:T(1,128)S(1)}, u32[]{:S(2)}, u32[]{:S(2)}) async-start(f32[16,1,1024]{2,1,0:T(1,128)} %all_to_all.40), calls=%async_computation | async-start | bytes 131072 | tf_op jit(solution)/shard_map/all_to_all | solution.py:146
  39.6 9.2 %copy-start.29 = (s32[16]{0:T(128)S(1)}, s32[16]{0:T(128)}, u32[]{:S(2)}) copy-start(s32[16]{0:T(128)} %copy-done.28) | copy-start | bytes 196
  39.6 9.2 %copy-start.32 = (pred[16]{0:T(512)(128)(4,1)S(1)}, pred[16]{0:T(512)(128)(4,1)}, u32[]{:S(2)}) copy-start(pred[16]{0:T(512)(128)(4,1)} %copy-done.31) | copy-start | bytes 52
  39.6 9.2 %copy-start.35 = (pred[16]{0:T(512)(128)(4,1)S(1)}, pred[16]{0:T(512)(128)(4,1)}, u32[]{:S(2)}) copy-start(pred[16]{0:T(512)(128)(4,1)} %copy-done.34) | copy-start | bytes 52
  39.6 9.2 %copy-start.38 = (pred[16]{0:T(512)(128)(4,1)S(1)}, pred[16]{0:T(512)(128)(4,1)}, u32[]{:S(2)}) copy-start(pred[16]{0:T(512)(128)(4,1)} %copy-done.37) | copy-start | bytes 52
  49.6 6.3 %collective-permute-start.1 = (f32[13,256]{1,0:T(8,128)S(1)}, f32[13,256]{1,0:T(8,128)S(1)}, u32[]{:S(2)}, u32[]{:S(2)}) collective-permute-start(f32[13,256]{1,0:T(8,128)S(1)} %fusion.217), channel_id=1, source_target_pairs={{0,1},{1,0},{2,3},{3,2},{4,5},{5,4},{6,7},{7,6},{8,9},{9,8},{10,11... | collective-permute-start | bytes 39944 | tf_op jit(solution)/shard_map/ppermute | solution.py:113
  52.4 4.1 %copy-start.8 = (pred[16]{0:T(512)(128)(4,1)S(1)}, pred[16]{0:T(512)(128)(4,1)}, u32[]{:S(2)}) copy-start(pred[16]{0:T(512)(128)(4,1)} %copy-done.7) | copy-start | bytes 52
  52.4 4.1 %copy-start.11 = (pred[16]{0:T(512)(128)(4,1)S(1)}, pred[16]{0:T(512)(128)(4,1)}, u32[]{:S(2)}) copy-start(pred[16]{0:T(512)(128)(4,1)} %copy-done.10) | copy-start | bytes 52
  52.4 4.2 %copy-start.14 = (pred[16]{0:T(512)(128)(4,1)S(1)}, pred[16]{0:T(512)(128)(4,1)}, u32[]{:S(2)}) copy-start(pred[16]{0:T(512)(128)(4,1)} %copy-done.13) | copy-start | bytes 52
  52.4 4.2 %copy-start.17 = (pred[16]{0:T(512)(128)(4,1)S(1)}, pred[16]{0:T(512)(128)(4,1)}, u32[]{:S(2)}) copy-start(pred[16]{0:T(512)(128)(4,1)} %copy-done.16) | copy-start | bytes 52
  52.4 4.2 %copy-start.20 = (pred[16]{0:T(512)(128)(4,1)S(1)}, pred[16]{0:T(512)(128)(4,1)}, u32[]{:S(2)}) copy-start(pred[16]{0:T(512)(128)(4,1)} %copy-done.19) | copy-start | bytes 52
  52.4 4.2 %copy-start.23 = (pred[16]{0:T(512)(128)(4,1)S(1)}, pred[16]{0:T(512)(128)(4,1)}, u32[]{:S(2)}) copy-start(pred[16]{0:T(512)(128)(4,1)} %copy-done.22) | copy-start | bytes 52
  52.4 4.2 %copy-start.26 = (pred[16]{0:T(512)(128)(4,1)S(1)}, pred[16]{0:T(512)(128)(4,1)}, u32[]{:S(2)}) copy-start(pred[16]{0:T(512)(128)(4,1)} %copy-done.25) | copy-start | bytes 52
  53.8 10.4 %copy-start.2 = (pred[4,13,256]{2,0,1:T(4,128)(4,1)S(1)}, pred[4,13,256]{2,0,1:T(4,128)(4,1)}, u32[]{:S(2)}) copy-start(pred[4,13,256]{2,0,1:T(4,128)(4,1)} %copy-done.1) | copy-start | bytes 39940
  53.8 10.4 %copy-start.3 = (pred[4,13,256]{2,0,1:T(4,128)(4,1)S(1)}, pred[4,13,256]{2,0,1:T(4,128)(4,1)}, u32[]{:S(2)}) copy-start(pred[4,13,256]{2,0,1:T(4,128)(4,1)} %get-tuple-element.338) | copy-start | bytes 39940
  57.4 14.8 %all-to-all-start.1 = ((f32[16,1,1024]{2,1,0:T(1,128)}), f32[16,1,1024]{2,1,0:T(1,128)S(1)}, u32[]{:S(2)}, u32[]{:S(2)}) async-start(f32[16,1,1024]{2,1,0:T(1,128)} %copy.278), calls=%async_computation.1 | async-start | bytes 131072 | tf_op jit(solution)/shard_map/all_to_all | solution.py:146
  72.1 20.7 %copy-start.30 = (s32[16]{0:T(128)S(1)}, s32[16]{0:T(128)}, u32[]{:S(2)}) copy-start(s32[16]{0:T(128)} %copy-done.28) | copy-start | bytes 196
  72.1 20.7 %copy-start.33 = (pred[16]{0:T(512)(128)(4,1)S(1)}, pred[16]{0:T(512)(128)(4,1)}, u32[]{:S(2)}) copy-start(pred[16]{0:T(512)(128)(4,1)} %copy-done.31) | copy-start | bytes 52
  72.1 20.7 %copy-start.36 = (pred[16]{0:T(512)(128)(4,1)S(1)}, pred[16]{0:T(512)(128)(4,1)}, u32[]{:S(2)}) copy-start(pred[16]{0:T(512)(128)(4,1)} %copy-done.34) | copy-start | bytes 52
  72.1 20.7 %copy-start.39 = (pred[16]{0:T(512)(128)(4,1)S(1)}, pred[16]{0:T(512)(128)(4,1)}, u32[]{:S(2)}) copy-start(pred[16]{0:T(512)(128)(4,1)} %copy-done.37) | copy-start | bytes 52
  72.2 20.7 %copy-start.41 = (pred[16]{0:T(512)(128)(4,1)S(1)}, pred[16]{0:T(512)(128)(4,1)}, u32[]{:S(2)}) copy-start(pred[16]{0:T(512)(128)(4,1)} %copy-done.40) | copy-start | bytes 52
  72.2 21.3 %copy-start.6 = (f32[1,4,85]{2,1,0:T(4,128)S(1)}, f32[1,4,85]{2,1,0:T(4,128)}, u32[]{:S(2)}) copy-start(f32[1,4,85]{2,1,0:T(4,128)} %param.48) | copy-start | bytes 4084
  75.6 14.4 %all-to-all-start.2 = ((f32[16,1,768]{2,1,0:T(1,128)}), f32[16,1,768]{2,1,0:T(1,128)S(1)}, u32[]{:S(2)}, u32[]{:S(2)}) async-start(f32[16,1,768]{2,1,0:T(1,128)} %broadcast_select_fusion.38), calls=%async_computation.2 | async-start | bytes 98304 | tf_op jit(solution)/shard_map/all_to_all | solution.py:146
  91.8 5.6 %copy-start.9 = (pred[16]{0:T(512)(128)(4,1)S(1)}, pred[16]{0:T(512)(128)(4,1)}, u32[]{:S(2)}) copy-start(pred[16]{0:T(512)(128)(4,1)} %copy-done.7) | copy-start | bytes 52
  91.8 5.6 %copy-start.12 = (pred[16]{0:T(512)(128)(4,1)S(1)}, pred[16]{0:T(512)(128)(4,1)}, u32[]{:S(2)}) copy-start(pred[16]{0:T(512)(128)(4,1)} %copy-done.10) | copy-start | bytes 52
  91.8 5.6 %copy-start.15 = (pred[16]{0:T(512)(128)(4,1)S(1)}, pred[16]{0:T(512)(128)(4,1)}, u32[]{:S(2)}) copy-start(pred[16]{0:T(512)(128)(4,1)} %copy-done.13) | copy-start | bytes 52
  91.8 5.6 %copy-start.18 = (pred[16]{0:T(512)(128)(4,1)S(1)}, pred[16]{0:T(512)(128)(4,1)}, u32[]{:S(2)}) copy-start(pred[16]{0:T(512)(128)(4,1)} %copy-done.16) | copy-start | bytes 52
  91.8 5.6 %copy-start.21 = (pred[16]{0:T(512)(128)(4,1)S(1)}, pred[16]{0:T(512)(128)(4,1)}, u32[]{:S(2)}) copy-start(pred[16]{0:T(512)(128)(4,1)} %copy-done.19) | copy-start | bytes 52
  91.8 5.6 %copy-start.24 = (pred[16]{0:T(512)(128)(4,1)S(1)}, pred[16]{0:T(512)(128)(4,1)}, u32[]{:S(2)}) copy-start(pred[16]{0:T(512)(128)(4,1)} %copy-done.22) | copy-start | bytes 52
  91.8 5.6 %copy-start.27 = (pred[16]{0:T(512)(128)(4,1)S(1)}, pred[16]{0:T(512)(128)(4,1)}, u32[]{:S(2)}) copy-start(pred[16]{0:T(512)(128)(4,1)} %copy-done.25) | copy-start | bytes 52
  95.5 1.2 collective-permute-start.2
  98.4 11.0 %all-to-all-start.3 = ((f32[16,1,1026]{2,1,0:T(1,128)}), f32[16,1,1026]{2,1,0:T(1,128)S(1)}, u32[]{:S(2)}, u32[]{:S(2)}) async-start(f32[16,1,1026]{2,1,0:T(1,128)} %broadcast_select_fusion.6), calls=%async_computation.3 | async-start | bytes 147456 | tf_op jit(solution)/shard_map/all_to_all | solution.py:146
  113.7 1.2 collective-permute-start.3
  130.3 1.2 collective-permute-start.4
  146.9 1.2 collective-permute-start.5
  149.7 11.0 %all-to-all-start.6 = ((f32[16,1,1028]{2,1,0:T(1,128)}), f32[16,1,1028]{2,1,0:T(1,128)S(1)}, u32[]{:S(2)}, u32[]{:S(2)}) async-start(f32[16,1,1028]{2,1,0:T(1,128)} %broadcast_select_fusion.26), calls=%async_computation.6 | async-start | bytes 147456 | tf_op jit(solution)/shard_map/all_to_all | solution.py:146

commit v12 on v10

--- a/solution.py
+++ b/solution.py
@@ -56,6 +56,9 @@
     return dict(
         pick_mass=gather_matrix(first, MASS_LINE).T,
         pick_stiff=gather_matrix(first, STIFF_LINE).T,
+        pick_both=jnp.stack([gather_matrix(first, MASS_LINE).T, gather_matrix(first, STIFF_LINE).T]).reshape(
+            -1, first
+        ),
         lanes_k=gather_matrix(second, STIFF_LINE),
         lanes_m=gather_matrix(second, MASS_LINE),
         lanes=jnp.stack([gather_matrix(second, STIFF_LINE), gather_matrix(second, MASS_LINE)]).reshape(
@@ -76,10 +79,17 @@
     v_stiff = jnp.stack([sum(stiff_d[i][j] * rows[j] for j in range(4)) for i in range(4)])
     pick_mass = mats["pick_mass"]
     pick_stiff = mats["pick_stiff"]
-    along_first_m = jnp.einsum("kx,dxy->dky", pick_mass, v_mass, precision=HIGH)
-    along_first_k = jnp.einsum("kx,dxy->dky", pick_stiff, v_mass, precision=HIGH) + jnp.einsum(
-        "kx,dxy->dky", pick_mass, v_stiff, precision=HIGH
-    )
+    if merged:
+        both = jnp.einsum("kx,dxy->dky", mats["pick_both"], v_mass, precision=HIGH)
+        along_first_m = both[:, : pick_mass.shape[0]]
+        along_first_k = both[:, pick_mass.shape[0] :] + jnp.einsum(
+            "kx,dxy->dky", pick_mass, v_stiff, precision=HIGH
+        )
+    else:
+        along_first_m = jnp.einsum("kx,dxy->dky", pick_mass, v_mass, precision=HIGH)
+        along_first_k = jnp.einsum("kx,dxy->dky", pick_stiff, v_mass, precision=HIGH) + jnp.einsum(
+            "kx,dxy->dky", pick_mass, v_stiff, precision=HIGH
+        )
     flat_m = along_first_m.reshape(-1, second)
     flat_k = along_first_k.reshape(-1, second)
     if merged:

time: 154 us -> 158 us (1.026)
  matrix products: 16.2 us -> 17.9 us
  other arithmetic: 33.1 us -> 34.7 us
    dot_general x0 -> x4, matrix products: none -> 1.93 us  [local_products(): both = jnp.einsum('kx,dxy->dky', mats['pick_both'], v_mass, precision=HIGH)]
    dot_general x6 -> x2, matrix products: 3.01 us -> 1.22 us  [local_products(): jnp.einsum('kx,dxy->dky', pick_stiff, v_mass, precision=HIGH)]
  transfers between devices with their start and end apart: 13 -> 13, of which waited for: 10 -> 9; matrix products, arithmetic and copies ran while one was open for 16% -> 17% of each run, Pallas kernels for 0% -> 0%
where the time goes in v12:
time: 158 us; the launch traced here: 157 us
  waiting for transfers between devices  41.2 us (26%)
  starting transfers between devices  36.8 us (23%)
  other arithmetic  34.7 us (22%)
  local copies, waits for them, and re-layouts  23.5 us (15%)
  matrix products  17.9 us (11%)
  between operations  2.31 us (1%)
    all_to_all x7, waiting for transfers between devices, plane_exchange(): got = lax.all_to_all(send, ('hx', 'hy'), 0, 0, tiled=True)  37.4 us
    all_to_all x7, starting transfers between devices, plane_exchange(): got = lax.all_to_all(send, ('hx', 'hy'), 0, 0, tiled=True)  35.7 us
    reduce_sum x2, other arithmetic, per_device(): current = jnp.sum(cond_nodes * gate_flat * (volts - reversal[:, None]), 0)  15.9 us
    select_n x7, other arithmetic, plane_exchange(): send = jnp.where(code_of[:, None] == code, table[code][None, :], send)  6.28 us
    select_n x44, local copies, waits for them, and re-layouts, plane_exchange(): received[offset] = jnp.where(valid, row[:pieces[offset].shape[0]], 0.0)  3.77 us
    ppermute x6, waiting for transfers between devices, torso_stage(): got = lax.ppermute(face, 'torso', [(0, 1), (1, 0)])  3.77 us
  transfers between devices with their start and end apart: 13, of which 9 were waited for; matrix products, arithmetic and copies ran while one was open for 17% of the time, Pallas kernels for 0%

profile of v12, /device:TPU:0, one launch (start us, length us, event | category | flops | bytes accessed | tf_op | source)
XLA Modules:
  0.0 157.1 jit_solution(15362647584870776160)
XLA Ops:
  0.7 0.8 copy.208
  2.9 0.7 mul.1102
  3.7 0.9 select_select_fusion.5
  6.6 0.6 collective-permute-start.1
  7.3 0.7 and_select_fusion.34
  9.5 0.6 slice_bitcast_fusion.15
  10.1 0.7 broadcast_compare_fusion.11
  10.8 0.6 slice_bitcast_fusion.9
  11.5 0.7 broadcast_multiply_fusion.1
  12.2 0.9 select_select_fusion.4
  13.2 0.5 compare_select_fusion
  14.5 0.7 all_to_all.31
  15.2 7.9 %all-to-all-start.1 = ((f32[16,1,1024]{2,1,0:T(1,128)}), f32[16,1,1024]{2,1,0:T(1,128)S(1)}, u32[]{:S(2)}, u32[]{:S(2)}) async-start(f32[16,1,1024]{2,1,0:T(1,128)} %all_to_all.31), calls=%async_computation.1 | async-start | bytes 131072 | tf_op jit(solution)/shard_map/all_to_all | solution.py:156
  23.2 7.9 %multiply_reduce_fusion.1 = (f32[4,13,256]{2,0,1:T(4,128)}, f32[40,4,13,256]{3,1,2,0:T(4,128)S(1)}) fusion(f32[40]{0:T(128)} %param.39, f32[4,13,256]{2,0,1:T(4,128)S(1)} %copy-done.3, f32[40]{0:T(128)} %get-tuple-element.788, f32[40]{0:T(128)} %get-tuple-element.787, f32[40]{0:T(128)} %get-tuple-element.789, f32[40]{0:T(128)} %get-tuple-element.790, ...), kind=kLoop, calls=%fused_computation.270 | loop fusion | flops 12766208 | bytes 4435616 | tf_op jit(solution)/shard_map/reduce_sum | solution.py:305
  31.1 0.6 broadcast_select_fusion.37
  31.8 0.7 fusion.443
  32.8 0.7 copy.206
  33.5 0.6 fusion.446
  34.5 0.7 copy.203
  35.2 1.0 fusion.261
  36.2 0.9 fusion.298
  37.1 0.9 fusion.297
  38.1 1.4 fusion.577
  39.5 0.9 convolution_add_fusion.2
  40.5 1.4 fusion.212
  42.3 0.9 fusion.373
  43.5 1.1 copy.222
  44.6 2.0 %reshape.6239 = f32[4,85,512,1,1]{2,1,0,3,4:T(8,128)} reshape(f32[340,512]{1,0:T(8,128)} %copy.222) | data formatting | bytes 1392640 | tf_op jit(solution)/shard_map/dot_general | solution.py:96
  46.7 0.7 reshape.6236
  48.0 0.8 select_select_fusion.8
  48.8 0.7 copy.219
  49.4 0.7 copy.212
  50.1 6.7 %all-to-all-start.2 = ((f32[16,1,1024]{2,1,0:T(1,128)}), f32[16,1,1024]{2,1,0:T(1,128)S(1)}, u32[]{:S(2)}, u32[]{:S(2)}) async-start(f32[16,1,1024]{2,1,0:T(1,128)} %copy.212), calls=%async_computation.2 | async-start | bytes 131072 | tf_op jit(solution)/shard_map/all_to_all | solution.py:156
  56.9 8.0 %multiply_reduce_fusion = (f32[4,13,256]{2,0,1:T(4,128)S(1)}, f32[40,4,13,256]{3,1,2,0:T(4,128)}) fusion(f32[4,13,256]{2,0,1:T(4,128)} %copy.219, f32[40]{0:T(128)} %param.39, f32[40]{0:T(128)} %get-tuple-element.788, f32[40]{0:T(128)} %get-tuple-element.787, f32[40]{0:T(128)} %get-tuple-element.789, f32[40]{0:T(128)} %get-tuple-element.790, ...), kind=kLoop, calls=%fused_computation.268 | loop fusion | flops 12766208 | bytes 4435616 | tf_op jit(solution)/shard_map/reduce_sum | solution.py:305
  66.9 1.5 broadcast_select_fusion.30
  68.5 7.0 %all-to-all-start.3 = ((f32[16,1,768]{2,1,0:T(1,128)}), f32[16,1,768]{2,1,0:T(1,128)S(1)}, u32[]{:S(2)}, u32[]{:S(2)}) async-start(f32[16,1,768]{2,1,0:T(1,128)} %broadcast_select_fusion.30), calls=%async_computation.3 | async-start | bytes 98304 | tf_op jit(solution)/shard_map/all_to_all | solution.py:156
  75.5 7.5 %all-to-all-done.3 = f32[16,1,768]{2,1,0:T(1,128)S(1)} async-done(((f32[16,1,768]{2,1,0:T(1,128)}), f32[16,1,768]{2,1,0:T(1,128)S(1)}, u32[]{:S(2)}, u32[]{:S(2)}) %all-to-all-start.3) | async-done | bytes 49184 | tf_op jit(solution)/shard_map/all_to_all | solution.py:156
  83.8 1.0 multiply_bitcast_fusion.3
  84.9 1.0 convolution_bitcast_fusion.2
  86.3 1.0 convolution_multiply_fusion.1
  88.5 0.7 copy.231
  90.3 1.0 broadcast_select_fusion.22
  91.2 3.5 %all-to-all-start.4 = ((f32[16,1,1026]{2,1,0:T(1,128)}), f32[16,1,1026]{2,1,0:T(1,128)S(1)}, u32[]{:S(2)}, u32[]{:S(2)}) async-start(f32[16,1,1026]{2,1,0:T(1,128)} %broadcast_select_fusion.22), calls=%async_computation.4 | async-start | bytes 147456 | tf_op jit(solution)/shard_map/all_to_all | solution.py:156
  94.8 7.5 %all-to-all-done.4 = f32[16,1,1026]{2,1,0:T(1,128)S(1)} async-done(((f32[16,1,1026]{2,1,0:T(1,128)}), f32[16,1,1026]{2,1,0:T(1,128)S(1)}, u32[]{:S(2)}, u32[]{:S(2)}) %all-to-all-start.4) | async-done | bytes 65696 | tf_op jit(solution)/shard_map/all_to_all | solution.py:156
  103.6 52.9 %while.32 = (s32[]{:T(128)}, f32[4,13,256]{2,1,0:T(8,128)S(1)}, f32[4,13,256]{2,1,0:T(8,128)S(1)}, f32[4,13,256]{2,1,0:T(8,128)S(1)}, f32[4,13,256]{2,1,0:T(8,12...) while((s32[]{:T(128)}, f32[4,13,256]{2,1,0:T(8,128)S(1)}, ...), condition=%wide.region_7.8_spmd.clone.clone, body=%wide.region_4.7_spmd.clone.clone.sunk | while | flops 213028416 | bytes 4338883 | solution.py:375
  104.4 0.6 convolution_multiply_fusion.3
  105.0 0.6 fusion.635
  106.2 1.1 collective-permute-done
  107.9 1.0 broadcast_select_fusion.66
  108.9 3.5 %all-to-all-start = ((f32[16,1,1028]{2,1,0:T(1,128)}), f32[16,1,1028]{2,1,0:T(1,128)S(1)}, u32[]{:S(2)}, u32[]{:S(2)}) async-start(f32[16,1,1028]{2,1,0:T(1,128)} %broadcast_select_fusion.66), calls=%async_computation | async-start | bytes 147456 | tf_op jit(solution)/shard_map/while/body/eval_jaxpr/all_to_all | solution.py:156
  112.5 7.5 %all-to-all-done = f32[16,1,1028]{2,1,0:T(1,128)S(1)} async-done(((f32[16,1,1028]{2,1,0:T(1,128)}), f32[16,1,1028]{2,1,0:T(1,128)S(1)}, u32[]{:S(2)}, u32[]{:S(2)}) %all-to-all-start) | async-done | bytes 65824 | tf_op jit(solution)/shard_map/while/body/eval_jaxpr/all_to_all | solution.py:156
  122.0 0.6 convolution_multiply_fusion.3
  122.6 0.6 fusion.635
  123.9 1.1 collective-permute-done
  125.6 1.0 broadcast_select_fusion.66
  126.5 3.5 %all-to-all-start = ((f32[16,1,1028]{2,1,0:T(1,128)}), f32[16,1,1028]{2,1,0:T(1,128)S(1)}, u32[]{:S(2)}, u32[]{:S(2)}) async-start(f32[16,1,1028]{2,1,0:T(1,128)} %broadcast_select_fusion.66), calls=%async_computation | async-start | bytes 147456 | tf_op jit(solution)/shard_map/while/body/eval_jaxpr/all_to_all | solution.py:156
  130.1 7.5 %all-to-all-done = f32[16,1,1028]{2,1,0:T(1,128)S(1)} async-done(((f32[16,1,1028]{2,1,0:T(1,128)}), f32[16,1,1028]{2,1,0:T(1,128)S(1)}, u32[]{:S(2)}, u32[]{:S(2)}) %all-to-all-start) | async-done | bytes 65824 | tf_op jit(solution)/shard_map/while/body/eval_jaxpr/all_to_all | solution.py:156
  139.7 0.6 convolution_multiply_fusion.3
  140.2 0.6 fusion.635
  141.5 1.1 collective-permute-done
  143.2 1.0 broadcast_select_fusion.66
  144.2 3.5 %all-to-all-start = ((f32[16,1,1028]{2,1,0:T(1,128)}), f32[16,1,1028]{2,1,0:T(1,128)S(1)}, u32[]{:S(2)}, u32[]{:S(2)}) async-start(f32[16,1,1028]{2,1,0:T(1,128)} %broadcast_select_fusion.66), calls=%async_computation | async-start | bytes 147456 | tf_op jit(solution)/shard_map/while/body/eval_jaxpr/all_to_all | solution.py:156
  147.7 7.5 %all-to-all-done = f32[16,1,1028]{2,1,0:T(1,128)S(1)} async-done(((f32[16,1,1028]{2,1,0:T(1,128)}), f32[16,1,1028]{2,1,0:T(1,128)S(1)}, u32[]{:S(2)}, u32[]{:S(2)}) %all-to-all-start) | async-done | bytes 65824 | tf_op jit(solution)/shard_map/while/body/eval_jaxpr/all_to_all | solution.py:156
  156.5 0.7 copy.232
  (474 shorter events, 23.1 us)
Async XLA Ops:
  1.7 5.6 %copy-start.12 = (s32[16]{0:T(128)}, s32[16]{0:T(128)S(1)}, u32[]{:S(2)}) copy-start(s32[16]{0:T(128)S(1)} %iota.927) | copy-start | bytes 196
  1.8 5.5 %copy-start.14 = (pred[16]{0:T(512)(128)(4,1)}, pred[16]{0:T(512)(128)(4,1)S(1)}, u32[]{:S(2)}) copy-start(pred[16]{0:T(512)(128)(4,1)S(1)} %iota.936) | copy-start | bytes 52
  4.7 5.4 %copy-start.10 = (s32[4,13,256]{2,0,1:T(4,128)S(1)}, s32[4,13,256]{2,0,1:T(4,128)}, u32[]{:S(2)}) copy-start(s32[4,13,256]{2,0,1:T(4,128)} %param.34) | copy-start | bytes 159748
  4.7 6.1 %copy-start.54 = (f32[3,40]{1,0:T(4,128)S(1)}, f32[3,40]{1,0:T(4,128)}, u32[]{:S(2)}) copy-start(f32[3,40]{1,0:T(4,128)} %param.36) | copy-start | bytes 1444
  4.8 8.3 %copy-start.1 = (f32[256,340]{0,1:T(8,128)}, f32[256,340]{0,1:T(8,128)S(1)}, u32[]{:S(2)}) copy-start(f32[256,340]{0,1:T(8,128)S(1)} %select_n.3347) | copy-start | bytes 1044484
  4.8 8.3 %copy-start = (f32[256,340]{0,1:T(8,128)}, f32[256,340]{0,1:T(8,128)S(1)}, u32[]{:S(2)}) copy-start(f32[256,340]{0,1:T(8,128)S(1)} %select_n.3380) | copy-start | bytes 1044484
  6.1 17.1 %copy-start.3 = (f32[4,13,256]{2,0,1:T(4,128)S(1)}, f32[4,13,256]{2,0,1:T(4,128)}, u32[]{:S(2)}) copy-start(f32[4,13,256]{2,0,1:T(4,128)} %param.31) | copy-start | bytes 159748
  6.6 7.1 %collective-permute-start.1 = (f32[13,256]{1,0:T(8,128)S(1)}, f32[13,256]{1,0:T(8,128)S(1)}, u32[]{:S(2)}, u32[]{:S(2)}) collective-permute-start(f32[13,256]{1,0:T(8,128)S(1)} %fusion.367), channel_id=1, source_target_pairs={{0,1},{1,0},{2,3},{3,2},{4,5},{5,4},{6,7},{7,6},{8,9},{9,8},{10,11... | collective-permute-start | bytes 39944 | tf_op jit(solution)/shard_map/ppermute | solution.py:123
  7.2 15.8 %copy-start.24 = (pred[16]{0:T(512)(128)(4,1)}, pred[16]{0:T(512)(128)(4,1)S(1)}, u32[]{:S(2)}) copy-start(pred[16]{0:T(512)(128)(4,1)S(1)} %get-tuple-element.605) | copy-start | bytes 52
  8.1 15.0 %copy-start.28 = (pred[16]{0:T(512)(128)(4,1)}, pred[16]{0:T(512)(128)(4,1)S(1)}, u32[]{:S(2)}) copy-start(pred[16]{0:T(512)(128)(4,1)S(1)} %get-tuple-element.773) | copy-start | bytes 52
  8.1 15.0 %copy-start.32 = (pred[16]{0:T(512)(128)(4,1)}, pred[16]{0:T(512)(128)(4,1)S(1)}, u32[]{:S(2)}) copy-start(pred[16]{0:T(512)(128)(4,1)S(1)} %get-tuple-element.774) | copy-start | bytes 52
  8.1 15.0 %copy-start.36 = (pred[16]{0:T(512)(128)(4,1)}, pred[16]{0:T(512)(128)(4,1)S(1)}, u32[]{:S(2)}) copy-start(pred[16]{0:T(512)(128)(4,1)S(1)} %get-tuple-element.775) | copy-start | bytes 52
  8.1 15.0 %copy-start.39 = (pred[16]{0:T(512)(128)(4,1)}, pred[16]{0:T(512)(128)(4,1)S(1)}, u32[]{:S(2)}) copy-start(pred[16]{0:T(512)(128)(4,1)S(1)} %get-tuple-element.776) | copy-start | bytes 52
  8.1 15.0 %copy-start.42 = (pred[16]{0:T(512)(128)(4,1)}, pred[16]{0:T(512)(128)(4,1)S(1)}, u32[]{:S(2)}) copy-start(pred[16]{0:T(512)(128)(4,1)S(1)} %get-tuple-element.777) | copy-start | bytes 52
  8.1 15.0 %copy-start.44 = (pred[16]{0:T(512)(128)(4,1)}, pred[16]{0:T(512)(128)(4,1)S(1)}, u32[]{:S(2)}) copy-start(pred[16]{0:T(512)(128)(4,1)S(1)} %get-tuple-element.778) | copy-start | bytes 52
  8.1 15.0 %copy-start.46 = (pred[16]{0:T(512)(128)(4,1)}, pred[16]{0:T(512)(128)(4,1)S(1)}, u32[]{:S(2)}) copy-start(pred[16]{0:T(512)(128)(4,1)S(1)} %get-tuple-element.779) | copy-start | bytes 52
  9.0 14.2 %copy-start.55 = (pred[340]{0:T(512)(128)(4,1)}, pred[340]{0:T(512)(128)(4,1)S(1)}, u32[]{:S(2)}) copy-start(pred[340]{0:T(512)(128)(4,1)S(1)} %iota.973) | copy-start | bytes 1024
  9.1 14.0 %copy-start.57 = (pred[340]{0:T(512)(128)(4,1)}, pred[340]{0:T(512)(128)(4,1)S(1)}, u32[]{:S(2)}) copy-start(pred[340]{0:T(512)(128)(4,1)S(1)} %iota.970) | copy-start | bytes 1024
  15.2 15.9 %all-to-all-start.1 = ((f32[16,1,1024]{2,1,0:T(1,128)}), f32[16,1,1024]{2,1,0:T(1,128)S(1)}, u32[]{:S(2)}, u32[]{:S(2)}) async-start(f32[16,1,1024]{2,1,0:T(1,128)} %all_to_all.31), calls=%async_computation.1 | async-start | bytes 131072 | tf_op jit(solution)/shard_map/all_to_all | solution.py:156
  35.2 8.3 %copy-start.22 = (f32[1,16,13]{1,0,2:T(1,128)S(1)}, f32[1,16,13]{1,0,2:T(1,128)}, u32[]{:S(2)}) copy-start(f32[1,16,13]{1,0,2:T(1,128)} %get-tuple-element.741) | copy-start | bytes 2500
  35.2 8.3 %copy-start.23 = (f32[1,16,13]{1,0,2:T(1,128)S(1)}, f32[1,16,13]{1,0,2:T(1,128)}, u32[]{:S(2)}) copy-start(f32[1,16,13]{1,0,2:T(1,128)} %get-tuple-element.742) | copy-start | bytes 2500
  41.9 6.1 %copy-start.25 = (pred[16]{0:T(512)(128)(4,1)S(1)}, pred[16]{0:T(512)(128)(4,1)}, u32[]{:S(2)}) copy-start(pred[16]{0:T(512)(128)(4,1)} %copy-done.24) | copy-start | bytes 52
  41.9 6.1 %copy-start.29 = (pred[16]{0:T(512)(128)(4,1)S(1)}, pred[16]{0:T(512)(128)(4,1)}, u32[]{:S(2)}) copy-start(pred[16]{0:T(512)(128)(4,1)} %copy-done.28) | copy-start | bytes 52
  41.9 6.1 %copy-start.33 = (pred[16]{0:T(512)(128)(4,1)S(1)}, pred[16]{0:T(512)(128)(4,1)}, u32[]{:S(2)}) copy-start(pred[16]{0:T(512)(128)(4,1)} %copy-done.32) | copy-start | bytes 52
  41.9 6.1 %copy-start.37 = (pred[16]{0:T(512)(128)(4,1)S(1)}, pred[16]{0:T(512)(128)(4,1)}, u32[]{:S(2)}) copy-start(pred[16]{0:T(512)(128)(4,1)} %copy-done.36) | copy-start | bytes 52
  41.9 6.1 %copy-start.40 = (pred[16]{0:T(512)(128)(4,1)S(1)}, pred[16]{0:T(512)(128)(4,1)}, u32[]{:S(2)}) copy-start(pred[16]{0:T(512)(128)(4,1)} %copy-done.39) | copy-start | bytes 52
  42.3 14.6 %copy-start.5 = (pred[4,13,256]{2,0,1:T(4,128)(4,1)S(1)}, pred[4,13,256]{2,0,1:T(4,128)(4,1)}, u32[]{:S(2)}) copy-start(pred[4,13,256]{2,0,1:T(4,128)(4,1)} %get-tuple-element.708) | copy-start | bytes 39940
  43.2 4.2 %collective-permute-start.2 = (f32[13,256]{1,0:T(8,128)S(1)}, f32[13,256]{1,0:T(8,128)S(1)}, u32[]{:S(2)}, u32[]{:S(2)}) collective-permute-start(f32[13,256]{1,0:T(8,128)S(1)} %fusion.363), channel_id=1, source_target_pairs={{0,1},{1,0},{2,3},{3,2},{4,5},{5,4},{6,7},{7,6},{8,9},{9,8},{10,11... | collective-permute-start | bytes 39944 | tf_op jit(solution)/shard_map/ppermute | solution.py:123
  43.5 13.4 %copy-start.6 = (f32[2,16,13]{1,0,2:T(2,128)}, f32[2,16,13]{1,0,2:T(2,128)S(1)}, u32[]{:S(2)}) copy-start(f32[2,16,13]{1,0,2:T(2,128)S(1)} %pad_maximum_fusion.27) | copy-start | bytes 4996
  50.1 14.9 %all-to-all-start.2 = ((f32[16,1,1024]{2,1,0:T(1,128)}), f32[16,1,1024]{2,1,0:T(1,128)S(1)}, u32[]{:S(2)}, u32[]{:S(2)}) async-start(f32[16,1,1024]{2,1,0:T(1,128)} %copy.212), calls=%async_computation.2 | async-start | bytes 131072 | tf_op jit(solution)/shard_map/all_to_all | solution.py:156
  56.9 9.2 %copy-start.4 = (f32[256]{0:T(256)S(1)}, f32[256]{0:T(256)}, u32[]{:S(2)}) copy-start(f32[256]{0:T(256)} %compare_select_fusion) | copy-start | bytes 3076
  56.9 10.0 %copy-start.26 = (pred[16]{0:T(512)(128)(4,1)S(1)}, pred[16]{0:T(512)(128)(4,1)}, u32[]{:S(2)}) copy-start(pred[16]{0:T(512)(128)(4,1)} %copy-done.24) | copy-start | bytes 52
  56.9 10.0 %copy-start.30 = (pred[16]{0:T(512)(128)(4,1)S(1)}, pred[16]{0:T(512)(128)(4,1)}, u32[]{:S(2)}) copy-start(pred[16]{0:T(512)(128)(4,1)} %copy-done.28) | copy-start | bytes 52
  56.9 10.0 %copy-start.34 = (pred[16]{0:T(512)(128)(4,1)S(1)}, pred[16]{0:T(512)(128)(4,1)}, u32[]{:S(2)}) copy-start(pred[16]{0:T(512)(128)(4,1)} %copy-done.32) | copy-start | bytes 52
  64.9 20.9 %copy-start.13 = (s32[16]{0:T(128)S(1)}, s32[16]{0:T(128)}, u32[]{:S(2)}) copy-start(s32[16]{0:T(128)} %copy-done.12) | copy-start | bytes 196
  64.9 20.9 %copy-start.15 = (pred[16]{0:T(512)(128)(4,1)S(1)}, pred[16]{0:T(512)(128)(4,1)}, u32[]{:S(2)}) copy-start(pred[16]{0:T(512)(128)(4,1)} %copy-done.14) | copy-start | bytes 52
  65.0 20.9 %copy-start.17 = (pred[16]{0:T(512)(128)(4,1)S(1)}, pred[16]{0:T(512)(128)(4,1)}, u32[]{:S(2)}) copy-start(pred[16]{0:T(512)(128)(4,1)} %copy-done.16) | copy-start | bytes 52
  65.0 20.9 %copy-start.19 = (pred[16]{0:T(512)(128)(4,1)S(1)}, pred[16]{0:T(512)(128)(4,1)}, u32[]{:S(2)}) copy-start(pred[16]{0:T(512)(128)(4,1)} %copy-done.18) | copy-start | bytes 52
  65.0 20.9 %copy-start.21 = (pred[16]{0:T(512)(128)(4,1)S(1)}, pred[16]{0:T(512)(128)(4,1)}, u32[]{:S(2)}) copy-start(pred[16]{0:T(512)(128)(4,1)} %copy-done.20) | copy-start | bytes 52
  65.0 21.3 %copy-start.2 = (f32[4,85,512,1,1]{2,1,0,3,4:T(8,128)S(1)}, f32[4,85,512,1,1]{2,1,0,3,4:T(8,128)}, u32[]{:S(2)}) copy-start(f32[4,85,512,1,1]{2,1,0,3,4:T(8,128)} %reshape.6239) | copy-start | bytes 2088964
  65.0 21.3 %copy-start.9 = (f32[1,4,85]{2,1,0:T(4,128)S(1)}, f32[1,4,85]{2,1,0:T(4,128)}, u32[]{:S(2)}) copy-start(f32[1,4,85]{2,1,0:T(4,128)} %param.42) | copy-start | bytes 4084
  68.4 19.7 %copy-start.8 = (f32[4,13]{1,0:T(4,128)S(1)}, f32[4,13]{1,0:T(4,128)}, u32[]{:S(2)}) copy-start(f32[4,13]{1,0:T(4,128)} %broadcast_multiply_fusion.1) | copy-start | bytes 628
  68.5 14.5 %all-to-all-start.3 = ((f32[16,1,768]{2,1,0:T(1,128)}), f32[16,1,768]{2,1,0:T(1,128)S(1)}, u32[]{:S(2)}, u32[]{:S(2)}) async-start(f32[16,1,768]{2,1,0:T(1,128)} %broadcast_select_fusion.30), calls=%async_computation.3 | async-start | bytes 98304 | tf_op jit(solution)/shard_map/all_to_all | solution.py:156
  84.8 5.4 %copy-start.27 = (pred[16]{0:T(512)(128)(4,1)S(1)}, pred[16]{0:T(512)(128)(4,1)}, u32[]{:S(2)}) copy-start(pred[16]{0:T(512)(128)(4,1)} %copy-done.24) | copy-start | bytes 52
  84.8 5.4 %copy-start.31 = (pred[16]{0:T(512)(128)(4,1)S(1)}, pred[16]{0:T(512)(128)(4,1)}, u32[]{:S(2)}) copy-start(pred[16]{0:T(512)(128)(4,1)} %copy-done.28) | copy-start | bytes 52
  84.8 5.4 %copy-start.35 = (pred[16]{0:T(512)(128)(4,1)S(1)}, pred[16]{0:T(512)(128)(4,1)}, u32[]{:S(2)}) copy-start(pred[16]{0:T(512)(128)(4,1)} %copy-done.32) | copy-start | bytes 52
  84.8 5.4 %copy-start.38 = (pred[16]{0:T(512)(128)(4,1)S(1)}, pred[16]{0:T(512)(128)(4,1)}, u32[]{:S(2)}) copy-start(pred[16]{0:T(512)(128)(4,1)} %copy-done.36) | copy-start | bytes 52
  84.8 5.4 %copy-start.41 = (pred[16]{0:T(512)(128)(4,1)S(1)}, pred[16]{0:T(512)(128)(4,1)}, u32[]{:S(2)}) copy-start(pred[16]{0:T(512)(128)(4,1)} %copy-done.39) | copy-start | bytes 52
  84.8 5.4 %copy-start.43 = (pred[16]{0:T(512)(128)(4,1)S(1)}, pred[16]{0:T(512)(128)(4,1)}, u32[]{:S(2)}) copy-start(pred[16]{0:T(512)(128)(4,1)} %copy-done.42) | copy-start | bytes 52
  84.8 5.4 %copy-start.45 = (pred[16]{0:T(512)(128)(4,1)S(1)}, pred[16]{0:T(512)(128)(4,1)}, u32[]{:S(2)}) copy-start(pred[16]{0:T(512)(128)(4,1)} %copy-done.44) | copy-start | bytes 52
  84.8 5.4 %copy-start.47 = (pred[16]{0:T(512)(128)(4,1)S(1)}, pred[16]{0:T(512)(128)(4,1)}, u32[]{:S(2)}) copy-start(pred[16]{0:T(512)(128)(4,1)} %copy-done.46) | copy-start | bytes 52
  86.3 17.2 %copy-start.49 = (s32[340]{0:T(512)S(1)}, s32[340]{0:T(512)}, u32[]{:S(2)}) copy-start(s32[340]{0:T(512)} %copy-done.48) | copy-start | bytes 4084
  86.3 17.2 %copy-start.56 = (pred[340]{0:T(512)(128)(4,1)S(1)}, pred[340]{0:T(512)(128)(4,1)}, u32[]{:S(2)}) copy-start(pred[340]{0:T(512)(128)(4,1)} %copy-done.55) | copy-start | bytes 1024
  86.3 17.2 %copy-start.58 = (pred[340]{0:T(512)(128)(4,1)S(1)}, pred[340]{0:T(512)(128)(4,1)}, u32[]{:S(2)}) copy-start(pred[340]{0:T(512)(128)(4,1)} %copy-done.57) | copy-start | bytes 1024
  86.3 17.2 %copy-start.60 = (pred[340]{0:T(512)(128)(4,1)S(1)}, pred[340]{0:T(512)(128)(4,1)}, u32[]{:S(2)}) copy-start(pred[340]{0:T(512)(128)(4,1)} %copy-done.59) | copy-start | bytes 1024
  86.3 17.2 %copy-start.62 = (pred[340]{0:T(512)(128)(4,1)S(1)}, pred[340]{0:T(512)(128)(4,1)}, u32[]{:S(2)}) copy-start(pred[340]{0:T(512)(128)(4,1)} %copy-done.61) | copy-start | bytes 1024
  88.4 1.2 collective-permute-start.3
  91.2 11.0 %all-to-all-start.4 = ((f32[16,1,1026]{2,1,0:T(1,128)}), f32[16,1,1026]{2,1,0:T(1,128)S(1)}, u32[]{:S(2)}, u32[]{:S(2)}) async-start(f32[16,1,1026]{2,1,0:T(1,128)} %broadcast_select_fusion.22), calls=%async_computation.4 | async-start | bytes 147456 | tf_op jit(solution)/shard_map/all_to_all | solution.py:156
  106.1 1.2 collective-permute-start
  108.9 11.0 %all-to-all-start = ((f32[16,1,1028]{2,1,0:T(1,128)}), f32[16,1,1028]{2,1,0:T(1,128)S(1)}, u32[]{:S(2)}, u32[]{:S(2)}) async-start(f32[16,1,1028]{2,1,0:T(1,128)} %broadcast_select_fusion.66), calls=%async_computation | async-start | bytes 147456 | tf_op jit(solution)/shard_map/while/body/eval_jaxpr/all_to_all | solution.py:156
  123.7 1.2 collective-permute-start
  126.5 11.0 %all-to-all-start = ((f32[16,1,1028]{2,1,0:T(1,128)}), f32[16,1,1028]{2,1,0:T(1,128)S(1)}, u32[]{:S(2)}, u32[]{:S(2)}) async-start(f32[16,1,1028]{2,1,0:T(1,128)} %broadcast_select_fusion.66), calls=%async_computation | async-start | bytes 147456 | tf_op jit(solution)/shard_map/while/body/eval_jaxpr/all_to_all | solution.py:156
  141.4 1.2 collective-permute-start
  144.2 11.0 %all-to-all-start = ((f32[16,1,1028]{2,1,0:T(1,128)}), f32[16,1,1028]{2,1,0:T(1,128)S(1)}, u32[]{:S(2)}, u32[]{:S(2)}) async-start(f32[16,1,1028]{2,1,0:T(1,128)} %broadcast_select_fusion.66), calls=%async_computation | async-start | bytes 147456 | tf_op jit(solution)/shard_map/while/body/eval_jaxpr/all_to_all | solution.py:156
  (12 other events, 54.5 us)

commit v13 on v10

--- a/solution.py
+++ b/solution.py
@@ -288,7 +288,7 @@
     gate_flat = gating.reshape(gating.shape[0], -1)
     mats = element_matrices(first_len, second_len)
     for repeat in range(STEPS):
-        diffusion, _, tied = face_sums(local_products(potential, heart_cond, mats), tie=potential)
+        diffusion, _, tied = face_sums(local_products(potential, heart_cond, mats, merged=True), tie=potential)
         volts = tied.reshape(1, -1)
         inf_value = jax.nn.sigmoid((volts - half_nodes) * slope_nodes)
         gate_flat = inf_value + (gate_flat - inf_value) * decay_nodes

time: 154 us -> 139 us (0.903)
  local copies, waits for them, and re-layouts: 22.7 us -> 15.6 us
  other arithmetic: 33.1 us -> 26.6 us
  matrix products: 16.2 us -> 13.8 us
    dot_general x2, local copies, waits for them, and re-layouts: 3.15 us -> 0.33 us  [local_products(): jnp.dot(jnp.concatenate([flat_m, flat_k], 1), mats['lanes'], precision=HIGH)]
    dot_general x4 -> x6, matrix products: 2.69 us -> 4.78 us  [local_products(): jnp.dot(jnp.concatenate([flat_m, flat_k], 1), mats['lanes'], precision=HIGH)]
    select_n x37, other arithmetic: 2.42 us -> 0.47 us  [plane_exchange(): received[offset] = jnp.where(valid, row[:pieces[offset].shape[0]], 0.0)]
    broadcast_in_dim x3, local copies, waits for them, and re-layouts: 1.81 us -> 0.02 us  [node_table(): out = jnp.where(labels == kind, matrix[kind][:, None], out)]
    dot_general x4 -> x0, matrix products: 1.71 us -> none  [the longest x2 0.86 us: local_products(): jnp.dot(flat_k, mats['lanes_m'], precision=HIGH)]
  transfers between devices with their start and end apart: 13 -> 13, of which waited for: 10 -> 11; matrix products, arithmetic and copies ran while one was open for 16% -> 12% of each run, Pallas kernels for 0% -> 0%
where the time goes in v13:
time: 139 us; the launch traced here: 138 us
  waiting for transfers between devices  42.7 us (31%)
  starting transfers between devices  36.9 us (27%)
  other arithmetic  26.6 us (19%)
  local copies, waits for them, and re-layouts  15.6 us (11%)
  matrix products  13.8 us (10%)
  between operations  1.81 us (1%)
    all_to_all x7, waiting for transfers between devices, plane_exchange(): got = lax.all_to_all(send, ('hx', 'hy'), 0, 0, tiled=True)  37.4 us
    all_to_all x7, starting transfers between devices, plane_exchange(): got = lax.all_to_all(send, ('hx', 'hy'), 0, 0, tiled=True)  36 us
    reduce_sum x2, other arithmetic, per_device(): current = jnp.sum(cond_nodes * gate_flat * (volts - reversal[:, None]), 0)  15.8 us
    ppermute x6, waiting for transfers between devices, torso_stage(): got = lax.ppermute(face, 'torso', [(0, 1), (1, 0)])  5.3 us
    select_n x7, other arithmetic, plane_exchange(): send = jnp.where(code_of[:, None] == code, table[code][None, :], send)  4.91 us
    dot_general x6, matrix products, local_products(): jnp.dot(jnp.concatenate([flat_m, flat_k], 1), mats['lanes'], precision=HIGH)  4.78 us
    select_n x44, local copies, waits for them, and re-layouts, plane_exchange(): received[offset] = jnp.where(valid, row[:pieces[offset].shape[0]], 0.0)  3.77 us
    dot_general x6, matrix products, local_products(): jnp.dot(element.reshape(-1, 4 * second_el), scatter_second, precision=HIGH)  2.92 us
  transfers between devices with their start and end apart: 13, of which 11 were waited for; matrix products, arithmetic and copies ran while one was open for 12% of the time, Pallas kernels for 0%

profile of v13, /device:TPU:0, one launch (start us, length us, event | category | flops | bytes accessed | tf_op | source)
XLA Modules:
  0.0 138.3 jit_solution(17932793721084856898)
XLA Ops:
  0.7 0.8 copy.224
  2.3 0.3 fusion.306
  2.6 0.3 convolution_bitcast_fusion.2
  2.9 0.3 select_select_fusion.8
  3.9 0.9 select_select_fusion.7
  5.4 0.3 fusion.234
  5.8 1.0 convolution_multiply_fusion.3
  7.0 0.3 fusion.608
  7.6 0.6 collective-permute-start.1
  8.7 0.4 collective-permute-done.1
  9.7 0.7 all_to_all.31
  10.4 8.2 %all-to-all-start.1 = ((f32[16,1,1024]{2,1,0:T(1,128)}), f32[16,1,1024]{2,1,0:T(1,128)S(1)}, u32[]{:S(2)}, u32[]{:S(2)}) async-start(f32[16,1,1024]{2,1,0:T(1,128)} %all_to_all.31), calls=%async_computation.1 | async-start | bytes 131072 | tf_op jit(solution)/shard_map/all_to_all | solution.py:146
  18.6 7.9 %multiply_reduce_fusion.1 = (f32[4,13,256]{2,0,1:T(4,128)S(1)}, f32[40,4,13,256]{3,1,2,0:T(4,128)}) fusion(f32[40]{0:T(128)S(1)} %copy-done.6, f32[4,13,256]{2,0,1:T(4,128)S(1)} %copy-done, f32[40]{0:T(128)S(1)} %get-tuple-element.830, f32[40]{0:T(128)S(1)} %get-tuple-element.829, f32[40]{0:T(128)S(1)} %get-tuple-element.831, f32[40]{0:T(128)S(1)} %get-tuple-element.832, ...), kind=kLoop, calls=%fused_computation.290 | loop fusion | flops 12766208 | bytes 4435616 | tf_op jit(solution)/shard_map/reduce_sum | solution.py:295
  27.7 0.3 fusion.305
  28.0 0.3 convolution_bitcast_fusion.1
  28.2 0.3 fusion.233
  28.6 1.0 convolution_multiply_fusion.2
  29.8 0.3 fusion.609
  30.5 1.1 collective-permute-done.2
  32.4 0.7 copy.229
  33.1 6.9 %all-to-all-start.2 = ((f32[16,1,1024]{2,1,0:T(1,128)}), f32[16,1,1024]{2,1,0:T(1,128)S(1)}, u32[]{:S(2)}, u32[]{:S(2)}) async-start(f32[16,1,1024]{2,1,0:T(1,128)} %copy.229), calls=%async_computation.2 | async-start | bytes 131072 | tf_op jit(solution)/shard_map/all_to_all | solution.py:146
  40.0 7.9 %multiply_reduce_fusion = (f32[4,13,256]{2,0,1:T(4,128)S(1)}, f32[40,4,13,256]{3,1,2,0:T(4,128)}) fusion(f32[4,13,256]{2,0,1:T(4,128)S(1)} %copy.236, f32[40]{0:T(128)S(1)} %copy-done.6, f32[40]{0:T(128)S(1)} %get-tuple-element.830, f32[40]{0:T(128)S(1)} %get-tuple-element.829, f32[40]{0:T(128)S(1)} %get-tuple-element.831, f32[40]{0:T(128)S(1)} %get-tuple-element.832, ...), kind=kLoop, calls=%fused_computation.288 | loop fusion | flops 12766208 | bytes 4435616 | tf_op jit(solution)/shard_map/reduce_sum | solution.py:295
  49.8 0.8 broadcast_select_fusion.30
  50.6 6.9 %all-to-all-start.3 = ((f32[16,1,768]{2,1,0:T(1,128)}), f32[16,1,768]{2,1,0:T(1,128)S(1)}, u32[]{:S(2)}, u32[]{:S(2)}) async-start(f32[16,1,768]{2,1,0:T(1,128)} %broadcast_select_fusion.30), calls=%async_computation.3 | async-start | bytes 98304 | tf_op jit(solution)/shard_map/all_to_all | solution.py:146
  57.5 7.4 %all-to-all-done.3 = f32[16,1,768]{2,1,0:T(1,128)S(1)} async-done(((f32[16,1,768]{2,1,0:T(1,128)}), f32[16,1,768]{2,1,0:T(1,128)S(1)}, u32[]{:S(2)}, u32[]{:S(2)}) %all-to-all-start.3) | async-done | bytes 49184 | tf_op jit(solution)/shard_map/all_to_all | solution.py:146
  66.1 0.3 fusion.304
  66.4 0.3 convolution_bitcast_fusion
  66.7 0.3 fusion.232
  67.0 1.0 convolution_multiply_fusion.1
  68.2 0.3 fusion.610
  69.1 0.7 copy.249
  69.8 0.5 collective-permute-done.3
  70.8 1.0 broadcast_select_fusion.22
  71.8 3.5 %all-to-all-start.4 = ((f32[16,1,1026]{2,1,0:T(1,128)}), f32[16,1,1026]{2,1,0:T(1,128)S(1)}, u32[]{:S(2)}, u32[]{:S(2)}) async-start(f32[16,1,1026]{2,1,0:T(1,128)} %broadcast_select_fusion.22), calls=%async_computation.4 | async-start | bytes 147456 | tf_op jit(solution)/shard_map/all_to_all | solution.py:146
  75.3 7.5 %all-to-all-done.4 = f32[16,1,1026]{2,1,0:T(1,128)S(1)} async-done(((f32[16,1,1026]{2,1,0:T(1,128)}), f32[16,1,1026]{2,1,0:T(1,128)S(1)}, u32[]{:S(2)}, u32[]{:S(2)}) %all-to-all-start.4) | async-done | bytes 65696 | tf_op jit(solution)/shard_map/all_to_all | solution.py:146
  84.1 53.5 %while.33 = (s32[]{:T(128)}, f32[4,13,256]{2,1,0:T(8,128)S(1)}, f32[4,13,256]{2,1,0:T(8,128)S(1)}, f32[4,13,256]{2,1,0:T(8,128)S(1)}, f32[4,13,256]{2,1,0:T(8,12...) while((s32[]{:T(128)}, f32[4,13,256]{2,1,0:T(8,128)S(1)}, ...), condition=%wide.region_7.8_spmd.clone.clone.clone, body=%wide.region_4.7_spmd.clone.clone.clone.sunk | while | flops 213083744 | bytes 4259643 | solution.py:365
  84.2 0.3 fusion.657
  84.5 0.3 fusion.658
  84.9 0.3 convolution_add_fusion.5
  85.2 0.6 convolution_multiply_fusion.5
  85.7 0.6 fusion.659
  87.0 1.1 collective-permute-done
  88.7 1.0 broadcast_select_fusion.66
  89.7 3.5 %all-to-all-start = ((f32[16,1,1028]{2,1,0:T(1,128)}), f32[16,1,1028]{2,1,0:T(1,128)S(1)}, u32[]{:S(2)}, u32[]{:S(2)}) async-start(f32[16,1,1028]{2,1,0:T(1,128)} %broadcast_select_fusion.66), calls=%async_computation | async-start | bytes 147456 | tf_op jit(solution)/shard_map/while/body/eval_jaxpr/all_to_all | solution.py:146
  93.2 7.5 %all-to-all-done = f32[16,1,1028]{2,1,0:T(1,128)S(1)} async-done(((f32[16,1,1028]{2,1,0:T(1,128)}), f32[16,1,1028]{2,1,0:T(1,128)S(1)}, u32[]{:S(2)}, u32[]{:S(2)}) %all-to-all-start) | async-done | bytes 65824 | tf_op jit(solution)/shard_map/while/body/eval_jaxpr/all_to_all | solution.py:146
  102.0 0.3 fusion.657
  102.3 0.3 fusion.658
  102.7 0.3 convolution_add_fusion.5
  103.0 0.6 convolution_multiply_fusion.5
  103.6 0.6 fusion.659
  104.9 1.1 collective-permute-done
  106.5 1.0 broadcast_select_fusion.66
  107.5 3.5 %all-to-all-start = ((f32[16,1,1028]{2,1,0:T(1,128)}), f32[16,1,1028]{2,1,0:T(1,128)S(1)}, u32[]{:S(2)}, u32[]{:S(2)}) async-start(f32[16,1,1028]{2,1,0:T(1,128)} %broadcast_select_fusion.66), calls=%async_computation | async-start | bytes 147456 | tf_op jit(solution)/shard_map/while/body/eval_jaxpr/all_to_all | solution.py:146
  111.1 7.5 %all-to-all-done = f32[16,1,1028]{2,1,0:T(1,128)S(1)} async-done(((f32[16,1,1028]{2,1,0:T(1,128)}), f32[16,1,1028]{2,1,0:T(1,128)S(1)}, u32[]{:S(2)}, u32[]{:S(2)}) %all-to-all-start) | async-done | bytes 65824 | tf_op jit(solution)/shard_map/while/body/eval_jaxpr/all_to_all | solution.py:146
  119.9 0.3 fusion.657
  120.2 0.3 fusion.658
  120.6 0.3 convolution_add_fusion.5
  120.9 0.6 convolution_multiply_fusion.5
  121.4 0.6 fusion.659
  122.7 1.1 collective-permute-done
  124.4 1.0 broadcast_select_fusion.66
  125.4 3.5 %all-to-all-start = ((f32[16,1,1028]{2,1,0:T(1,128)}), f32[16,1,1028]{2,1,0:T(1,128)S(1)}, u32[]{:S(2)}, u32[]{:S(2)}) async-start(f32[16,1,1028]{2,1,0:T(1,128)} %broadcast_select_fusion.66), calls=%async_computation | async-start | bytes 147456 | tf_op jit(solution)/shard_map/while/body/eval_jaxpr/all_to_all | solution.py:146
  128.9 7.5 %all-to-all-done = f32[16,1,1028]{2,1,0:T(1,128)S(1)} async-done(((f32[16,1,1028]{2,1,0:T(1,128)}), f32[16,1,1028]{2,1,0:T(1,128)S(1)}, u32[]{:S(2)}, u32[]{:S(2)}) %all-to-all-start) | async-done | bytes 65824 | tf_op jit(solution)/shard_map/while/body/eval_jaxpr/all_to_all | solution.py:146
  137.7 0.7 copy.250
  (370 shorter events, 18.5 us)
Async XLA Ops:
  4.9 0.9 copy-start.5
  5.2 3.0 %copy-start.10 = (f32[3,40]{1,0:T(4,128)S(1)}, f32[3,40]{1,0:T(4,128)}, u32[]{:S(2)}) copy-start(f32[3,40]{1,0:T(4,128)} %param.38) | copy-start | bytes 1444
  5.2 3.0 %copy-start.8 = (f32[3,40]{1,0:T(4,128)S(1)}, f32[3,40]{1,0:T(4,128)}, u32[]{:S(2)}) copy-start(f32[3,40]{1,0:T(4,128)} %param.37) | copy-start | bytes 1444
  5.3 3.0 %copy-start.7 = (f32[4,40]{1,0:T(4,128)S(1)}, f32[4,40]{1,0:T(4,128)}, u32[]{:S(2)}) copy-start(f32[4,40]{1,0:T(4,128)} %param.40) | copy-start | bytes 1924
  5.3 3.0 %copy-start.9 = (f32[3,40]{1,0:T(4,128)S(1)}, f32[3,40]{1,0:T(4,128)}, u32[]{:S(2)}) copy-start(f32[3,40]{1,0:T(4,128)} %param.35) | copy-start | bytes 1444
  5.3 3.1 %copy-start.2 = (s32[4,13,256]{2,0,1:T(4,128)S(1)}, s32[4,13,256]{2,0,1:T(4,128)}, u32[]{:S(2)}) copy-start(s32[4,13,256]{2,0,1:T(4,128)} %param.34) | copy-start | bytes 159748
  5.3 3.1 %copy-start.3 = (s32[4,13,256]{2,0,1:T(4,128)S(1)}, s32[4,13,256]{2,0,1:T(4,128)}, u32[]{:S(2)}) copy-start(s32[4,13,256]{2,0,1:T(4,128)} %param.33) | copy-start | bytes 159748
  5.4 3.1 %copy-start.11 = (f32[3,40]{1,0:T(4,128)S(1)}, f32[3,40]{1,0:T(4,128)}, u32[]{:S(2)}) copy-start(f32[3,40]{1,0:T(4,128)} %param.36) | copy-start | bytes 1444
  5.7 12.9 %copy-start = (f32[4,13,256]{2,0,1:T(4,128)S(1)}, f32[4,13,256]{2,0,1:T(4,128)}, u32[]{:S(2)}) copy-start(f32[4,13,256]{2,0,1:T(4,128)} %param.31) | copy-start | bytes 159748
  5.7 12.9 %copy-start.6 = (f32[40]{0:T(128)S(1)}, f32[40]{0:T(128)}, u32[]{:S(2)}) copy-start(f32[40]{0:T(128)} %param.39) | copy-start | bytes 484
  7.6 1.4 %collective-permute-start.1 = (f32[13,256]{1,0:T(8,128)S(1)}, f32[13,256]{1,0:T(8,128)S(1)}, u32[]{:S(2)}, u32[]{:S(2)}) collective-permute-start(f32[13,256]{1,0:T(8,128)S(1)} %fusion.373), channel_id=1, source_target_pairs={{0,1},{1,0},{2,3},{3,2},{4,5},{5,4},{6,7},{7,6},{8,9},{9,8},{10,11... | collective-permute-start | bytes 39944 | tf_op jit(solution)/shard_map/ppermute | solution.py:113
  10.4 16.1 %all-to-all-start.1 = ((f32[16,1,1024]{2,1,0:T(1,128)}), f32[16,1,1024]{2,1,0:T(1,128)S(1)}, u32[]{:S(2)}, u32[]{:S(2)}) async-start(f32[16,1,1024]{2,1,0:T(1,128)} %all_to_all.31), calls=%async_computation.1 | async-start | bytes 131072 | tf_op jit(solution)/shard_map/all_to_all | solution.py:146
  30.4 1.2 collective-permute-start.2
  33.1 14.8 %all-to-all-start.2 = ((f32[16,1,1024]{2,1,0:T(1,128)}), f32[16,1,1024]{2,1,0:T(1,128)S(1)}, u32[]{:S(2)}, u32[]{:S(2)}) async-start(f32[16,1,1024]{2,1,0:T(1,128)} %copy.229), calls=%async_computation.2 | async-start | bytes 131072 | tf_op jit(solution)/shard_map/all_to_all | solution.py:146
  40.0 25.8 %copy-start.4 = (s32[13,256]{1,0:T(8,128)S(1)}, s32[13,256]{1,0:T(8,128)}, u32[]{:S(2)}) copy-start(s32[13,256]{1,0:T(8,128)} %param.43) | copy-start | bytes 39940
  47.9 19.1 %copy-start.1 = (f32[1,4,85]{2,1,0:T(4,128)S(1)}, f32[1,4,85]{2,1,0:T(4,128)}, u32[]{:S(2)}) copy-start(f32[1,4,85]{2,1,0:T(4,128)} %param.42) | copy-start | bytes 4084
  50.6 14.4 %all-to-all-start.3 = ((f32[16,1,768]{2,1,0:T(1,128)}), f32[16,1,768]{2,1,0:T(1,128)S(1)}, u32[]{:S(2)}, u32[]{:S(2)}) async-start(f32[16,1,768]{2,1,0:T(1,128)} %broadcast_select_fusion.30), calls=%async_computation.3 | async-start | bytes 98304 | tf_op jit(solution)/shard_map/all_to_all | solution.py:146
  69.0 1.2 collective-permute-start.3
  71.8 11.0 %all-to-all-start.4 = ((f32[16,1,1026]{2,1,0:T(1,128)}), f32[16,1,1026]{2,1,0:T(1,128)S(1)}, u32[]{:S(2)}, u32[]{:S(2)}) async-start(f32[16,1,1026]{2,1,0:T(1,128)} %broadcast_select_fusion.22), calls=%async_computation.4 | async-start | bytes 147456 | tf_op jit(solution)/shard_map/all_to_all | solution.py:146
  86.9 1.2 collective-permute-start
  89.7 11.0 %all-to-all-start = ((f32[16,1,1028]{2,1,0:T(1,128)}), f32[16,1,1028]{2,1,0:T(1,128)S(1)}, u32[]{:S(2)}, u32[]{:S(2)}) async-start(f32[16,1,1028]{2,1,0:T(1,128)} %broadcast_select_fusion.66), calls=%async_computation | async-start | bytes 147456 | tf_op jit(solution)/shard_map/while/body/eval_jaxpr/all_to_all | solution.py:146
  104.7 1.2 collective-permute-start
  107.5 11.0 %all-to-all-start = ((f32[16,1,1028]{2,1,0:T(1,128)}), f32[16,1,1028]{2,1,0:T(1,128)S(1)}, u32[]{:S(2)}, u32[]{:S(2)}) async-start(f32[16,1,1028]{2,1,0:T(1,128)} %broadcast_select_fusion.66), calls=%async_computation | async-start | bytes 147456 | tf_op jit(solution)/shard_map/while/body/eval_jaxpr/all_to_all | solution.py:146
  122.6 1.2 collective-permute-start
  125.4 11.0 %all-to-all-start = ((f32[16,1,1028]{2,1,0:T(1,128)}), f32[16,1,1028]{2,1,0:T(1,128)S(1)}, u32[]{:S(2)}, u32[]{:S(2)}) async-start(f32[16,1,1028]{2,1,0:T(1,128)} %broadcast_select_fusion.66), calls=%async_computation | async-start | bytes 147456 | tf_op jit(solution)/shard_map/while/body/eval_jaxpr/all_to_all | solution.py:146
